TPU v7x, 32 devices: a whole 2x2x4 slice. The times are simulated.
32 devices in a mesh: rep: 4 (over y, core), exp: 8 (over z, x).
Axes of the slice: x: 2, y: 2, z: 4, core: 2. Of those that a mesh axis runs over, the one named last changes fastest.
Arguments:
- tokens: bfloat16 [8192, 1024], P(('rep', 'exp')), may hold values from -6 to 6
- cotangent: bfloat16 [8192, 1024], P(('rep', 'exp')), may hold values from -6 to 6
- expert_ids: int32 [8192, 8], P(('rep', 'exp')), may hold values from 0 to 15, as said below
- combine: bfloat16 [8192, 8], P(('rep', 'exp')), may hold values from 0.049804688 to 0.34960938
- gate_weight: bfloat16 [4, 16, 1024, 384], P('rep', 'exp'), may hold values from -0.1875 to 0.1875
- up_weight: bfloat16 [4, 16, 1024, 384], P('rep', 'exp'), may hold values from -0.1875 to 0.1875
- down_weight: bfloat16 [4, 16, 384, 1024], P('rep', 'exp'), may hold values from -0.625 to 0.625
- moment1: float32 [4, 16, 384, 1024], P('rep', 'exp'), may hold values from -4 to 4
- moment2: float32 [4, 16, 384, 1024], P('rep', 'exp'), may hold values from 0.01 to 1
- round_k: int32 [8], P('exp'), may hold values from 0 to 1
Outputs:
- mixed: bfloat16 [8192, 1024], P(('rep', 'exp'))
- input_grad: bfloat16 [8192, 1024], P(('rep', 'exp'))
- gate_grad: bfloat16 [4, 16, 1024, 384], P('rep', 'exp')
- up_grad: bfloat16 [4, 16, 1024, 384], P('rep', 'exp')
- new_down: bfloat16 [4, 16, 384, 1024], P('rep', 'exp')
- new_moment1: float32 [4, 16, 384, 1024], P('rep', 'exp')
- new_moment2: float32 [4, 16, 384, 1024], P('rep', 'exp')
Inputs may be any that keep to these rules, and one draw needn't show every extreme that they name: `expert_ids`: each row names 8 different experts. Of the 256 rows of one device, at most 256 name any one expert, and at most 384 name one of the two experts 2i and 2i + 1; in every draw one expert is named by exactly 256 rows of every device, and one such pair of experts by exactly 384.
All inputs are finite; a program needn't handle non-finite values.
Results may differ from a plain program's by a relative error of at most 0.0064.
Values may be sent and summed in bfloat16 or wider, within the bound.
No kernel may reach another device: no remote copies, remote signals or barrier semaphores. Data moves between devices by JAX's collectives and lax.ppermute only.
A program may use at most 192 MiB of HBM per device.

v0:
```python
from functools import partial

import jax
import jax.numpy as jnp
from jax import lax
from jax.sharding import PartitionSpec as P

ROUNDS = 2


beta_one = 0.9
beta_two = 0.999
learn_rate = 0.01
decay_rate = 0.1
adam_eps = 1e-08
step_count = 100.0


def for_sending(value):

    def short(part):
        return part.astype(jnp.bfloat16) if part.dtype == jnp.float32 else part

    return jax.tree.map(short, value)


def shifted(value, axis, by):
    size = lax.axis_size(axis)
    return lax.ppermute(value, axis, [(i, (i + by) % size) for i in range(size)])


def slot_table(expert_ids, experts, capacity):
    slot_total = expert_ids.shape[0]
    one_hot = (expert_ids[:, None] == jnp.arange(experts, dtype=jnp.int32)[None, :]).astype(
        jnp.int32
    )
    earlier = jnp.cumsum(one_hot, axis=0) - one_hot
    position = jnp.sum(earlier * one_hot, axis=1)
    target = expert_ids * capacity + position
    filler = jnp.full((experts * capacity,), slot_total, jnp.int32)
    row_table = filler.at[target].set(jnp.arange(slot_total, dtype=jnp.int32))
    return (row_table.reshape(experts, capacity), target)


def forward_part(expert_rows, gate_matrix, up_matrix, down_matrix):
    gate_value = jnp.einsum(
        "serd,edh->serh", expert_rows, gate_matrix, preferred_element_type=jnp.float32
    )
    up_value = jnp.einsum(
        "serd,edh->serh", expert_rows, up_matrix, preferred_element_type=jnp.float32
    )
    sigmoid_gate = jax.nn.sigmoid(gate_value)
    active = gate_value * sigmoid_gate
    hidden = (active * up_value).astype(jnp.bfloat16)
    expert_out = jnp.einsum(
        "serh,ehd->serd", hidden, down_matrix, preferred_element_type=jnp.float32
    ).astype(jnp.bfloat16)
    return (gate_value, up_value, sigmoid_gate, active, hidden, expert_out)


def backward_part(
    expert_rows, cot_rows, weight_rows, forward_state, gate_matrix, up_matrix, down_matrix
):
    gate_value, up_value, sigmoid_gate, active, hidden, expert_out = forward_state
    slot_cot = (weight_rows.astype(jnp.float32)[..., None] * cot_rows.astype(jnp.float32)).astype(
        jnp.bfloat16
    )
    hidden_cot = jnp.einsum(
        "serd,ehd->serh", slot_cot, down_matrix, preferred_element_type=jnp.float32
    )
    gate_cot = (
        hidden_cot * up_value * sigmoid_gate * (1.0 + gate_value * (1.0 - sigmoid_gate))
    ).astype(jnp.bfloat16)
    up_cot = (hidden_cot * active).astype(jnp.bfloat16)
    down_grad = jnp.einsum("serh,serd->ehd", hidden, slot_cot, preferred_element_type=jnp.float32)
    gate_grad = jnp.einsum(
        "serd,serh->edh", expert_rows, gate_cot, preferred_element_type=jnp.float32
    ).astype(jnp.bfloat16)
    up_grad = jnp.einsum(
        "serd,serh->edh", expert_rows, up_cot, preferred_element_type=jnp.float32
    ).astype(jnp.bfloat16)
    input_cot = (
        jnp.einsum("serh,edh->serd", gate_cot, gate_matrix, preferred_element_type=jnp.float32)
        + jnp.einsum("serh,edh->serd", up_cot, up_matrix, preferred_element_type=jnp.float32)
    ).astype(jnp.bfloat16)
    return (input_cot, gate_grad, up_grad, down_grad)


def from_peer(down_shard, hops):
    return jax.tree.map(
        lambda part, own: part.astype(own.dtype),
        shifted(for_sending(down_shard), "rep", hops),
        down_shard,
    )


def per_device(
    tokens,
    cotangent,
    expert_ids,
    combine,
    gate_weight,
    up_weight,
    down_weight,
    moment1,
    moment2,
    round_k,
):
    token_count, top_count = expert_ids.shape
    local_experts = gate_weight.shape[1]
    model_width = tokens.shape[1]
    devices_exp = lax.axis_size("exp")
    experts = local_experts * devices_exp
    capacity = 2 * token_count * top_count // experts
    flat_ids = expert_ids.reshape(-1)
    slots_per = local_experts * capacity
    row_table, target = slot_table(flat_ids, experts, capacity)
    row_table = row_table.reshape(devices_exp, slots_per)
    source_rows = row_table // top_count
    zero_row = jnp.zeros((1, model_width), jnp.bfloat16)
    send_rows = jnp.concatenate([tokens, zero_row])[source_rows]
    send_cot = jnp.concatenate([cotangent, zero_row])[source_rows]
    send_weight = jnp.concatenate([combine.reshape(-1), jnp.zeros((1,), jnp.bfloat16)])[row_table]

    def to_expert(received):
        return received.reshape((devices_exp, local_experts, capacity) + received.shape[2:])

    def from_expert(results):
        flat_results = results.reshape(devices_exp, local_experts * capacity, model_width)
        return flat_results

    gate_matrix = gate_weight[0]
    up_matrix = up_weight[0]
    down_matrix = down_weight[0]
    recv_rows = lax.all_to_all(send_rows, "exp", split_axis=0, concat_axis=0, tiled=True)
    expert_rows = to_expert(recv_rows)
    forward_state = forward_part(expert_rows, gate_matrix, up_matrix, down_matrix)
    out_back = lax.all_to_all(
        from_expert(forward_state[5]), "exp", split_axis=0, concat_axis=0, tiled=True
    )
    recv_cot, recv_weight = (
        lax.all_to_all(send_cot, "exp", split_axis=0, concat_axis=0, tiled=True),
        lax.all_to_all(send_weight, "exp", split_axis=0, concat_axis=0, tiled=True),
    )
    backward_state = backward_part(
        expert_rows,
        to_expert(recv_cot),
        to_expert(recv_weight),
        forward_state,
        gate_matrix,
        up_matrix,
        down_matrix,
    )
    cot_back = lax.all_to_all(
        from_expert(backward_state[0]), "exp", split_axis=0, concat_axis=0, tiled=True
    )
    slot_out = out_back.reshape(devices_exp * slots_per, model_width)[target].reshape(
        token_count, top_count, model_width
    )
    mixed = jnp.sum(
        combine.astype(jnp.float32)[:, :, None] * slot_out.astype(jnp.float32), axis=1
    ).astype(jnp.bfloat16)
    slot_input = cot_back.reshape(devices_exp * slots_per, model_width)[target].reshape(
        token_count, top_count, model_width
    )
    input_grad = jnp.sum(slot_input.astype(jnp.float32), axis=1).astype(jnp.bfloat16)
    input_cot, gate_grad, up_grad, down_grad = backward_state
    peer_down = lax.switch(
        round_k[0],
        [partial(from_peer, hops=1 << bit_index) for bit_index in range(ROUNDS)],
        down_weight,
    )
    bias_one = 1.0 - beta_one**step_count
    bias_two = 1.0 - beta_two**step_count
    first = beta_one * moment1[0] + (1.0 - beta_one) * down_grad
    second = beta_two * moment2[0] + (1.0 - beta_two) * down_grad * down_grad
    own_down = down_matrix.astype(jnp.float32)
    averaged = (own_down + peer_down[0].astype(jnp.float32)) * 0.5
    update = first / bias_one / (jnp.sqrt(second / bias_two) + adam_eps)
    new_down = (averaged - learn_rate * (update + decay_rate * own_down)).astype(jnp.bfloat16)
    return (
        mixed,
        input_grad,
        gate_grad[None],
        up_grad[None],
        new_down[None],
        first[None],
        second[None],
    )


def solution(mesh):
    return jax.shard_map(
        per_device,
        mesh=mesh,
        in_specs=(
            P(("rep", "exp"), None),
            P(("rep", "exp"), None),
            P(("rep", "exp"), None),
            P(("rep", "exp"), None),
            P("rep", "exp", None, None),
            P("rep", "exp", None, None),
            P("rep", "exp", None, None),
            P("rep", "exp", None, None),
            P("rep", "exp", None, None),
            P("exp"),
        ),
        out_specs=(
            P(("rep", "exp"), None),
            P(("rep", "exp"), None),
            P("rep", "exp", None, None),
            P("rep", "exp", None, None),
            P("rep", "exp", None, None),
            P("rep", "exp", None, None),
            P("rep", "exp", None, None),
        ),
        check_vma=False,
    )
```

profile of v0, /device:TPU:0, one launch (start us, length us, event | category | flops | bytes accessed | tf_op | source)
XLA Modules:
  0.0 876.2 jit_solution(2876099313697591255)
XLA Ops:
  0.6 0.0 copy-start
  0.6 0.8 broadcast_multiply_fusion
  1.5 0.8 copy.37
  2.3 0.1 eq.29
  2.4 0.1 eq.25
  2.5 0.8 copy.42
  3.3 0.1 reshape.211
  3.5 0.1 copy.36
  3.6 0.1 mul.104
  3.7 4.5 reduce-window.6
  8.3 0.4 slice_reduce_fusion
  8.7 0.2 reduce-window.9
  8.9 0.1 broadcast_add_fusion
  9.0 0.1 fusion.53
  9.1 8.1 scatter_custom_fusion
  17.2 0.0 copy-start.5
  17.3 25.6 %gather_fusion.2 = bf16[4096]{0:T(1024)(128)(2,1)S(1)} fusion(bf16[2049]{0:T(1024)(128)(2,1)S(1)} %pad_maximum_fusion, s32[4096]{0:T(1024)S(1)} %broadcast_clamp_fusion), kind=kCustom, calls=%fused_computation.2 | custom fusion | bytes 32768 | tf_op jit(solution)/shard_map/gather | solution.py:123
  42.9 0.5 broadcast.190
  43.4 0.7 reduce.5
  44.1 0.6 reshape.280
  44.7 7.3 all-to-all-start.2
  52.0 0.0 copy-done.5
  52.1 18.2 %gather_fusion = bf16[4096,1024]{1,0:T(8,128)(2,1)} fusion(bf16[257,1024]{1,0:T(8,128)(2,1)S(1)} %concatenate.9, s32[4096]{0:T(1024)S(1)} %broadcast_clamp_fusion.1), kind=kCustom, calls=%fused_computation | custom fusion | bytes 16793600 | tf_op jit(solution)/shard_map/gather | solution.py:121
  70.3 0.0 all-to-all-done.2
  70.3 6.1 all-to-all-start
  76.4 0.0 copy-done.6
  76.5 18.2 %gather_fusion.3 = bf16[4096,1024]{1,0:T(8,128)(2,1)} fusion(bf16[257,1024]{1,0:T(8,128)(2,1)S(1)} %concatenate.11, s32[4096]{0:T(1024)S(1)} %broadcast_clamp_fusion.1), kind=kCustom, calls=%fused_computation.3 | custom fusion | bytes 16793600 | tf_op jit(solution)/shard_map/gather | solution.py:122
  94.7 164.4 %all-to-all-done = bf16[8,512,1024]{2,1,0:T(8,128)(2,1)} async-done(((bf16[8,512,1024]{2,1,0:T(8,128)(2,1)}), bf16[8,512,1024]{2,1,0:T(8,128)(2,1)}, u32[]{:S(2)}, u32[]{:S(2)}) %all-to-all-start) | async-done | bytes 8388640 | tf_op jit(solution)/shard_map/all_to_all | solution.py:135
  259.0 5.3 all-to-all-start.3
  264.4 0.0 copy-done.4
  264.5 9.6 %fusion.7 = f32[2,8,256,384]{3,2,1,0:T(8,128)} fusion(bf16[8,2,256,1024]{3,2,1,0:T(8,128)(2,1)} %bitcast.6, bf16[1,2,1024,384]{3,2,1,0:T(8,128)(2,1)S(1)} %copy-done.4), kind=kOutput, calls=%fused_computation.17 | convolution fusion | flops 3221225472 | bytes 16252928 | tf_op jit(solution)/shard_map/serd,edh->serh/dot_general | solution.py:49
  274.0 0.0 copy-done
  274.0 9.7 %fusion.9 = f32[2,8,256,384]{3,2,1,0:T(8,128)} fusion(bf16[8,2,256,1024]{3,2,1,0:T(8,128)(2,1)} %bitcast.6, bf16[1,2,1024,384]{3,2,1,0:T(8,128)(2,1)S(1)} %copy-done), kind=kOutput, calls=%fused_computation.19 | convolution fusion | flops 3221225472 | bytes 16252928 | tf_op jit(solution)/shard_map/serd,edh->serh/dot_general | solution.py:46
  283.7 162.6 %all-to-all-done.3 = bf16[8,512,1024]{2,1,0:T(8,128)(2,1)} async-done(((bf16[8,512,1024]{2,1,0:T(8,128)(2,1)}), bf16[8,512,1024]{2,1,0:T(8,128)(2,1)}, u32[]{:S(2)}, u32[]{:S(2)}) %all-to-all-start.3) | async-done | bytes 8388640 | tf_op jit(solution)/shard_map/all_to_all | solution.py:142
  446.3 13.5 %fusion.14 = (bf16[8,2,256,384]{3,2,0,1:T(8,128)(2,1)}, bf16[8,2,256,384]{3,2,0,1:T(8,128)(2,1)}, bf16[8,2,256,384]{3,2,0,1:T(8,128)(2,1)S(1)}) fusion(f32[2,8,256,384]{3,2,1,0:T(8,128)} %fusion.9, f32[2,8,256,384]{3,2,1,0:T(8,128)} %fusion.7, bf16[1,2,384,1024]{3,2,1,0:T(8,128)(2,1)} %param.18, bf16[8,2,256,1024]{3,2,1,0:T(8,128)(2,1)} %bitcast.45, ...), kind=kOutput, calls=%fused_computation.26 | convolution fusion | flops 3257401344 | bytes 31997952 | tf_op jit(solution)/shard_map/serd,ehd->serh/dot_general | solution.py:68
  459.8 1.7 copy-done.14
  461.4 0.0 copy-done.9
  461.4 6.6 convert_bitcast_fusion
  468.1 7.9 copy.41
  476.0 5.2 all-to-all-start.1
  481.2 10.0 %fusion.37 = f32[2,8,256,1024]{3,2,1,0:T(8,128)} fusion(bf16[8,2,256,384]{3,2,0,1:T(8,128)(2,1)} %get-tuple-element.19, bf16[1,2,1024,384]{3,2,1,0:T(8,128)(2,1)S(1)} %copy-done), kind=kOutput, calls=%fused_computation.56 | convolution fusion | flops 3221225472 | bytes 21495808 | tf_op jit(solution)/shard_map/serh,edh->serd/dot_general | solution.py:83
  491.2 11.2 %fusion.1 = bf16[8,2,256,1024]{3,2,0,1:T(8,128)(2,1)} fusion(f32[2,8,256,1024]{3,2,1,0:T(8,128)} %fusion.37, bf16[8,2,256,384]{3,2,0,1:T(8,128)(2,1)} %get-tuple-element.18, bf16[1,2,1024,384]{3,2,1,0:T(8,128)(2,1)S(1)} %copy-done.4), kind=kOutput, calls=%fused_computation.9 | convolution fusion | flops 3229614080 | bytes 29884416 | tf_op jit(solution)/shard_map/serh,edh->serd/dot_general | solution.py:84
  502.4 8.0 copy.45
  510.3 153.0 %all-to-all-done.1 = bf16[8,512,1024]{2,1,0:T(8,128)(2,1)} async-done(((bf16[8,512,1024]{2,1,0:T(8,128)(2,1)}), bf16[8,512,1024]{2,1,0:T(8,128)(2,1)}, u32[]{:S(2)}, u32[]{:S(2)}) %all-to-all-start.1) | async-done | bytes 8388640 | tf_op jit(solution)/shard_map/all_to_all | solution.py:138
  663.3 5.1 all-to-all-start.4
  668.5 0.0 copy-done.7
  668.5 0.1 copy.35
  669.3 0.0 copy-done.10
  669.3 21.1 %conditional.4 = (bf16[2,384,1024]{2,1,0:T(8,128)(2,1)}) conditional(s32[]{:T(128)} %bitcast.36, bf16[1,2,384,1024]{3,2,1,0:T(8,128)(2,1)S(1)} %copy-done.10, bf16[1,2,384,1024]{3,2,1,0:T(8,128)(2,1)S(1)} %copy-done.10), branch_computations={%region_6.7_spmd, %region_7.8_spmd} | conditional | bytes 12582988
  669.3 0.1 collective-permute-start
  669.4 19.8 %collective-permute-done = bf16[1,2,384,1024]{3,2,1,0:T(8,128)(2,1)S(1)} collective-permute-done((bf16[1,2,384,1024]{3,2,1,0:T(8,128)(2,1)S(1)}, bf16[1,2,384,1024]{3,2,1,0:T(8,128)(2,1)S(1)}, u32[]{:S(2)}, u32[]{:S(2)}) %collective-permute-start) | collective-permute-done | bytes 1572896 | tf_op jit(solution)/shard_map/cond/branch_0_fun/ppermute | solution.py:29
  689.2 1.1 copy-done.12
  690.3 10.1 %fusion.46 = bf16[1,2,1024,384]{3,2,1,0:T(8,128)(2,1)} fusion(bf16[8,2,256,1024]{3,2,1,0:T(8,128)(2,1)} %bitcast.6, bf16[8,2,256,384]{3,2,0,1:T(8,128)(2,1)} %get-tuple-element.18), kind=kOutput, calls=%fused_computation.63 | convolution fusion | flops 3222011904 | bytes 13107200 | tf_op jit(solution)/shard_map/serd,serh->edh/dot_general | solution.py:79
  700.4 0.0 copy-done.3
  700.4 9.2 %fusion.43 = bf16[1,2,1024,384]{3,2,1,0:T(8,128)(2,1)} fusion(bf16[8,2,256,1024]{3,2,1,0:T(8,128)(2,1)} %bitcast.6, bf16[8,2,256,384]{3,2,0,1:T(8,128)(2,1)S(1)} %copy-done.3), kind=kOutput, calls=%fused_computation.62 | convolution fusion | flops 3222011904 | bytes 13107200 | tf_op jit(solution)/shard_map/serd,serh->edh/dot_general | solution.py:76
  709.7 0.0 copy-done.8
  709.7 0.0 copy-done.11
  709.7 12.0 %fusion.50 = (f32[1,2,384,1024]{3,2,1,0:T(8,128)}, bf16[1,2,384,1024]{3,2,1,0:T(8,128)(2,1)}, f32[1,2,384,1024]{3,2,1,0:T(8,128)}) fusion(f32[1,2,384,1024]{3,2,1,0:T(8,128)S(1)} %copy-done.8, f32[1,2,384,1024]{3,2,1,0:T(8,128)} %param.19, bf16[2,384,1024]{2,1,0:T(8,128)(2,1)} %get-tuple-element.26, bf16[1,2,384,1024]{3,2,1,0:T(8,128)(2,1)S(1)} %copy-done.11, ...), kind=kOutput, calls=%fused_computation.65 | convolution fusion | flops 3249537024 | bytes 28852224 | tf_op jit(solution)/shard_map/serh,serd->ehd/dot_general | solution.py:75
  721.7 15.4 %gather_fusion.1 = bf16[2048,1024]{1,0:T(8,128)(2,1)} fusion(bf16[4096,1024]{1,0:T(8,128)(2,1)} %bitcast.20, s32[2048]{0:T(1024)S(1)} %broadcast_clamp_fusion.2), kind=kCustom, calls=%fused_computation.1 | custom fusion | bytes 8396800 | tf_op jit(solution)/shard_map/gather | solution.py:157
  737.1 113.6 %all-to-all-done.4 = bf16[8,512,1024]{2,1,0:T(8,128)(2,1)} async-done(((bf16[8,512,1024]{2,1,0:T(8,128)(2,1)}), bf16[8,512,1024]{2,1,0:T(8,128)(2,1)}, u32[]{:S(2)}, u32[]{:S(2)}) %all-to-all-start.4) | async-done | bytes 8388640 | tf_op jit(solution)/shard_map/all_to_all | solution.py:154
  850.7 15.5 %gather_fusion.4 = bf16[2048,1024]{1,0:T(8,128)(2,1)} fusion(bf16[4096,1024]{1,0:T(8,128)(2,1)} %bitcast.30, s32[2048]{0:T(1024)S(1)} %broadcast_clamp_fusion.2), kind=kCustom, calls=%fused_computation.4 | custom fusion | bytes 8396800 | tf_op jit(solution)/shard_map/gather | solution.py:163
  866.2 0.0 copy-start.1
  866.2 6.5 bitcast_reduce_fusion
  872.7 3.3 fusion.2
  (30 shorter events, 0.3 us)
Async XLA Ops:
  0.6 273.4 %copy-start = (bf16[1,2,1024,384]{3,2,1,0:T(8,128)(2,1)S(1)}, bf16[1,2,1024,384]{3,2,1,0:T(8,128)(2,1)}, u32[]{:S(2)}) copy-start(bf16[1,2,1024,384]{3,2,1,0:T(8,128)(2,1)} %param.16) | copy-start | bytes 4718596
  17.2 34.8 %copy-start.5 = (bf16[256,1024]{1,0:T(8,128)(2,1)S(1)}, bf16[256,1024]{1,0:T(8,128)(2,1)}, u32[]{:S(2)}) copy-start(bf16[256,1024]{1,0:T(8,128)(2,1)} %param.12) | copy-start | bytes 1572868
  44.7 25.6 %all-to-all-start.2 = ((bf16[8,2,256]{2,1,0:T(2,128)(2,1)}), bf16[8,2,256]{2,1,0:T(2,128)(2,1)S(1)}, u32[]{:S(2)}, u32[]{:S(2)}) async-start(bf16[8,2,256]{2,1,0:T(2,128)(2,1)} %reshape.280), calls=%async_computation.2 | async-start | bytes 16384 | tf_op jit(solution)/shard_map/all_to_all | solution.py:143
  70.3 6.1 copy-start.6
  70.3 188.7 %all-to-all-start = ((bf16[8,512,1024]{2,1,0:T(8,128)(2,1)}), bf16[8,512,1024]{2,1,0:T(8,128)(2,1)}, u32[]{:S(2)}, u32[]{:S(2)}) async-start(bf16[8,512,1024]{2,1,0:T(8,128)(2,1)} %bitcast.168), calls=%async_computation | async-start | bytes 16777216 | tf_op jit(solution)/shard_map/all_to_all | solution.py:135
  259.0 5.4 copy-start.4
  259.0 187.3 %all-to-all-start.3 = ((bf16[8,512,1024]{2,1,0:T(8,128)(2,1)}), bf16[8,512,1024]{2,1,0:T(8,128)(2,1)}, u32[]{:S(2)}, u32[]{:S(2)}) async-start(bf16[8,512,1024]{2,1,0:T(8,128)(2,1)} %bitcast.167), calls=%async_computation.3 | async-start | bytes 16777216 | tf_op jit(solution)/shard_map/all_to_all | solution.py:142
  446.3 15.1 %copy-start.9 = (bf16[1,2,384,1024]{3,2,1,0:T(8,128)(2,1)S(1)}, bf16[1,2,384,1024]{3,2,1,0:T(8,128)(2,1)}, u32[]{:S(2)}) copy-start(bf16[1,2,384,1024]{3,2,1,0:T(8,128)(2,1)} %param.18) | copy-start | bytes 4718596
  459.8 1.7 copy-start.14
  476.0 187.3 %all-to-all-start.1 = ((bf16[8,512,1024]{2,1,0:T(8,128)(2,1)}), bf16[8,512,1024]{2,1,0:T(8,128)(2,1)}, u32[]{:S(2)}, u32[]{:S(2)}) async-start(bf16[8,512,1024]{2,1,0:T(8,128)(2,1)} %bitcast.170), calls=%async_computation.1 | async-start | bytes 16777216 | tf_op jit(solution)/shard_map/all_to_all | solution.py:138
  663.3 5.2 copy-start.7
  663.3 5.9 copy-start.10
  663.3 187.3 %all-to-all-start.4 = ((bf16[8,512,1024]{2,1,0:T(8,128)(2,1)}), bf16[8,512,1024]{2,1,0:T(8,128)(2,1)}, u32[]{:S(2)}, u32[]{:S(2)}) async-start(bf16[8,512,1024]{2,1,0:T(8,128)(2,1)} %bitcast.169), calls=%async_computation.4 | async-start | bytes 16777216 | tf_op jit(solution)/shard_map/all_to_all | solution.py:154
  669.3 19.9 %collective-permute-start = (bf16[1,2,384,1024]{3,2,1,0:T(8,128)(2,1)S(1)}, bf16[1,2,384,1024]{3,2,1,0:T(8,128)(2,1)S(1)}, u32[]{:S(2)}, u32[]{:S(2)}) collective-permute-start(bf16[1,2,384,1024]{3,2,1,0:T(8,128)(2,1)S(1)} %param), channel_id=1, source_target_pairs={{0,8},{8,16},{16,24},{24,0},{1,9},{9,17},{17,25},{25,1},{2,10},{10... | collective-permute-start | bytes 4718600 | tf_op jit(solution)/shard_map/cond/branch_0_fun/ppermute | solution.py:29
  689.2 1.1 copy-start.12
  690.3 10.1 %copy-start.3 = (bf16[8,2,256,384]{3,2,0,1:T(8,128)(2,1)S(1)}, bf16[8,2,256,384]{3,2,0,1:T(8,128)(2,1)}, u32[]{:S(2)}) copy-start(bf16[8,2,256,384]{3,2,0,1:T(8,128)(2,1)} %get-tuple-element.19) | copy-start | bytes 9437188
  700.4 9.2 %copy-start.8 = (f32[1,2,384,1024]{3,2,1,0:T(8,128)S(1)}, f32[1,2,384,1024]{3,2,1,0:T(8,128)}, u32[]{:S(2)}) copy-start(f32[1,2,384,1024]{3,2,1,0:T(8,128)} %param.20) | copy-start | bytes 9437188
  700.4 9.2 %copy-start.11 = (bf16[1,2,384,1024]{3,2,1,0:T(8,128)(2,1)S(1)}, bf16[1,2,384,1024]{3,2,1,0:T(8,128)(2,1)}, u32[]{:S(2)}) copy-start(bf16[1,2,384,1024]{3,2,1,0:T(8,128)(2,1)} %param.18) | copy-start | bytes 4718596
  866.2 6.5 copy-start.2
  866.2 9.8 %copy-start.1 = (bf16[1,2,1024,384]{3,2,1,0:T(8,128)(2,1)S(1)}, bf16[1,2,1024,384]{3,2,1,0:T(8,128)(2,1)}, u32[]{:S(2)}) copy-start(bf16[1,2,1024,384]{3,2,1,0:T(8,128)(2,1)} %param.16) | copy-start | bytes 4718596
where the time goes:
time: 881 us; the launch traced here: 876 us
  waiting for transfers between devices  613 us (70%)
  local copies, waits for them, and re-layouts  124 us (14%)
  matrix products  91.9 us (10%)
  starting transfers between devices  29 us (3%)
  other arithmetic  16.3 us (2%)
    all_to_all x1, waiting for transfers between devices, per_device(): lax.all_to_all(send_rows, 'exp', split_axis=0, concat_axis=0, tiled=True)  164 us
    all_to_all x1, waiting for transfers between devices, per_device(): lax.all_to_all(send_cot, 'exp', split_axis=0, concat_axis=0, tiled=True)  163 us
    all_to_all x1, waiting for transfers between devices, per_device(): lax.all_to_all(from_expert(forward_state[5]), 'exp', split_axis=0, concat...  153 us
    all_to_all x1, waiting for transfers between devices, per_device(): lax.all_to_all(from_expert(backward_state[0]), 'exp', split_axis=0, conca...  114 us
    gather x1, local copies, waits for them, and re-layouts, per_device(): jnp.concatenate([combine.reshape(-1), jnp.zeros((1,), jnp.bfloat16)])  25.6 us
    ppermute x1, waiting for transfers between devices, shifted(): lax.ppermute(value, axis, [(i, (i + by) % size) for i in range(size)])  19.8 us
    gather x1, local copies, waits for them, and re-layouts, per_device(): send_rows = jnp.concatenate([tokens, zero_row])[source_rows]  18.2 us
    gather x1, local copies, waits for them, and re-layouts, per_device(): send_cot = jnp.concatenate([cotangent, zero_row])[source_rows]  18.2 us
  transfers between devices with their start and end apart: 6, of which 5 were waited for; matrix products, arithmetic and copies ran while one was open for 15% of the time, Pallas kernels for 0%

commit v1 on v0

v1 whole, which is shorter than its diff:
```python
import jax
import jax.numpy as jnp
from jax import lax
from jax.sharding import PartitionSpec as P

ROUNDS = 2
CHUNK_ROWS = 2048


beta_one = 0.9
beta_two = 0.999
learn_rate = 0.01
decay_rate = 0.1
adam_eps = 1e-08
step_count = 100.0


def shifted(value, axis, by):
    size = lax.axis_size(axis)
    return lax.ppermute(value, axis, [(i, (i + by) % size) for i in range(size)])


def dense_weights(expert_ids, combine, experts):
    expert_iota = jnp.arange(experts, dtype=jnp.int32)
    hit = expert_ids[:, :, None] == expert_iota[None, None, :]
    picked = jnp.where(hit, combine.astype(jnp.float32)[:, :, None], 0.0)
    return jnp.sum(picked, axis=1).astype(jnp.bfloat16)


def per_device(
    tokens,
    cotangent,
    expert_ids,
    combine,
    gate_weight,
    up_weight,
    down_weight,
    moment1,
    moment2,
    round_k,
):
    local_experts = gate_weight.shape[1]
    devices_exp = lax.axis_size("exp")
    experts = local_experts * devices_exp
    my_exp = lax.axis_index("exp")

    weight_table = dense_weights(expert_ids, combine, experts)
    group_weight = lax.all_gather(weight_table, "exp", axis=0, tiled=True)
    group_tokens = lax.all_gather(tokens, "exp", axis=0, tiled=True)
    group_cot = lax.all_gather(cotangent, "exp", axis=0, tiled=True)
    local_weight = lax.dynamic_slice_in_dim(
        group_weight, my_exp * local_experts, local_experts, axis=1
    ).astype(jnp.float32)
    local_weight = jnp.transpose(local_weight)[:, :, None]

    gate_matrix = gate_weight[0]
    up_matrix = up_weight[0]
    down_matrix = down_weight[0]

    def chunk_pass(chunk_tokens, chunk_cot, chunk_weight):
        gate_value = jnp.einsum(
            "td,edh->eth", chunk_tokens, gate_matrix, preferred_element_type=jnp.float32
        )
        up_value = jnp.einsum(
            "td,edh->eth", chunk_tokens, up_matrix, preferred_element_type=jnp.float32
        )
        sigmoid_gate = jax.nn.sigmoid(gate_value)
        active = gate_value * sigmoid_gate
        hidden = (active * up_value).astype(jnp.bfloat16)
        expert_out = jnp.einsum(
            "eth,ehd->etd", hidden, down_matrix, preferred_element_type=jnp.float32
        ).astype(jnp.bfloat16)
        mixed_part = jnp.sum(chunk_weight * expert_out.astype(jnp.float32), axis=0)
        slot_cot = (chunk_weight * chunk_cot.astype(jnp.float32)[None]).astype(jnp.bfloat16)
        hidden_cot = jnp.einsum(
            "etd,ehd->eth", slot_cot, down_matrix, preferred_element_type=jnp.float32
        )
        gate_cot = (
            hidden_cot * up_value * sigmoid_gate * (1.0 + gate_value * (1.0 - sigmoid_gate))
        ).astype(jnp.bfloat16)
        up_cot = (hidden_cot * active).astype(jnp.bfloat16)
        down_grad = jnp.einsum(
            "eth,etd->ehd", hidden, slot_cot, preferred_element_type=jnp.float32
        )
        gate_grad = jnp.einsum(
            "td,eth->edh", chunk_tokens, gate_cot, preferred_element_type=jnp.float32
        )
        up_grad = jnp.einsum(
            "td,eth->edh", chunk_tokens, up_cot, preferred_element_type=jnp.float32
        )
        input_cot = (
            jnp.einsum("eth,edh->etd", gate_cot, gate_matrix, preferred_element_type=jnp.float32)
            + jnp.einsum("eth,edh->etd", up_cot, up_matrix, preferred_element_type=jnp.float32)
        ).astype(jnp.bfloat16)
        input_part = jnp.sum(input_cot.astype(jnp.float32), axis=0)
        return mixed_part, input_part, gate_grad, up_grad, down_grad

    group_count = group_tokens.shape[0]
    chunk = min(group_count, CHUNK_ROWS)
    chunks = group_count // chunk
    if chunks == 1:
        mixed_part, input_part, gate_grad, up_grad, down_grad = chunk_pass(
            group_tokens, group_cot, local_weight
        )
    else:

        def step(carry, packed):
            parts = chunk_pass(*packed)
            grads = tuple(acc + part for acc, part in zip(carry, parts[2:]))
            return grads, parts[:2]

        zeros = (
            jnp.zeros(gate_matrix.shape, jnp.float32),
            jnp.zeros(up_matrix.shape, jnp.float32),
            jnp.zeros(down_matrix.shape, jnp.float32),
        )
        packed = (
            group_tokens.reshape(chunks, chunk, -1),
            group_cot.reshape(chunks, chunk, -1),
            jnp.transpose(local_weight.reshape(local_experts, chunks, chunk, 1), (1, 0, 2, 3)),
        )
        (gate_grad, up_grad, down_grad), (mixed_parts, input_parts) = lax.scan(
            step, zeros, packed
        )
        mixed_part = mixed_parts.reshape(group_count, -1)
        input_part = input_parts.reshape(group_count, -1)
    gate_grad = gate_grad.astype(jnp.bfloat16)
    up_grad = up_grad.astype(jnp.bfloat16)
    mixed = lax.psum_scatter(mixed_part, "exp", scatter_dimension=0, tiled=True).astype(
        jnp.bfloat16
    )
    input_grad = lax.psum_scatter(
        input_part, "exp", scatter_dimension=0, tiled=True
    ).astype(jnp.bfloat16)

    peers = [shifted(down_weight, "rep", 1 << bit_index) for bit_index in range(ROUNDS)]
    peer_down = peers[0]
    for bit_index in range(1, ROUNDS):
        peer_down = jnp.where(round_k[0] == bit_index, peers[bit_index], peer_down)
    bias_one = 1.0 - beta_one**step_count
    bias_two = 1.0 - beta_two**step_count
    first = beta_one * moment1[0] + (1.0 - beta_one) * down_grad
    second = beta_two * moment2[0] + (1.0 - beta_two) * down_grad * down_grad
    own_down = down_matrix.astype(jnp.float32)
    averaged = (own_down + peer_down[0].astype(jnp.float32)) * 0.5
    update = first / bias_one / (jnp.sqrt(second / bias_two) + adam_eps)
    new_down = (averaged - learn_rate * (update + decay_rate * own_down)).astype(jnp.bfloat16)
    return (
        mixed,
        input_grad,
        gate_grad[None],
        up_grad[None],
        new_down[None],
        first[None],
        second[None],
    )


def solution(mesh):
    return jax.shard_map(
        per_device,
        mesh=mesh,
        in_specs=(
            P(("rep", "exp"), None),
            P(("rep", "exp"), None),
            P(("rep", "exp"), None),
            P(("rep", "exp"), None),
            P("rep", "exp", None, None),
            P("rep", "exp", None, None),
            P("rep", "exp", None, None),
            P("rep", "exp", None, None),
            P("rep", "exp", None, None),
            P("exp"),
        ),
        out_specs=(
            P(("rep", "exp"), None),
            P(("rep", "exp"), None),
            P("rep", "exp", None, None),
            P("rep", "exp", None, None),
            P("rep", "exp", None, None),
            P("rep", "exp", None, None),
            P("rep", "exp", None, None),
        ),
        check_vma=False,
    )
```

time: 881 us -> 506 us (0.57)
  waiting for transfers between devices: 613 us -> 350 us
  local copies, waits for them, and re-layouts: 124 us -> 4.57 us
  blocking collectives: 0 us -> 32.6 us
  starting transfers between devices: 29 us -> 1.85 us
  between operations: 1.77 us -> 14.5 us
    all_to_all x5 -> x0, waiting for transfers between devices: 594 us -> none  [the longest x1 164 us: per_device(): lax.all_to_all(send_rows, 'exp', split_axis=0, concat_axis=0, tiled=True)]
    reduce_scatter x0 -> x2, waiting for transfers between devices: none -> 219 us  [the longest x1 150 us: per_device(): lax.psum_scatter(input_part, 'exp', scatter_dimension=0, tiled=True)]
    all_gather x0 -> x2, waiting for transfers between devices: none -> 111 us  [the longest x1 67.4 us: per_device(): group_tokens = lax.all_gather(tokens, 'exp', axis=0, tiled=True)]
    gather x5 -> x0, local copies, waits for them, and re-layouts: 92.9 us -> none  [the longest x1 25.6 us: per_device(): jnp.concatenate([combine.reshape(-1), jnp.zeros((1,), jnp.bfloat16)])]
    all_gather x0 -> x1, blocking collectives: none -> 32.6 us  [per_device(): group_weight = lax.all_gather(weight_table, 'exp', axis=0, tiled=True)]
    all_to_all x5 -> x0, starting transfers between devices: 29 us -> none  [the longest x1 7.25 us: per_device(): lax.all_to_all(send_weight, 'exp', split_axis=0, concat_axis=0, tiled=True)]
    convert_element_type x4 -> x0, local copies, waits for them, and re-layouts: 16 us -> none  [the longest x1 7.95 us: backward_part(): input_cot = (jnp.einsum('serh,edh->serd', gate_cot, gate_matrix, preferre...]
    convert_element_type x2 -> x4, other arithmetic: 0.06 us -> 11.3 us  [the longest x1 6.47 us: chunk_pass(): chunk_cot.astype(jnp.float32)[None]]
  transfers between devices with their start and end apart: 6 -> 6, of which waited for: 5 -> 6; matrix products, arithmetic and copies ran while one was open for 15% -> 13% of each run, Pallas kernels for 0% -> 0%
where the time goes in v1:
time: 506 us; the launch traced here: 505 us
  waiting for transfers between devices  350 us (69%)
  matrix products  89.8 us (18%)
  blocking collectives  32.6 us (6%)
  between operations  14.5 us (3%)
  other arithmetic  12.1 us (2%)
    reduce_scatter x1, waiting for transfers between devices, per_device(): lax.psum_scatter(input_part, 'exp', scatter_dimension=0, tiled=True)  150 us
    reduce_scatter x1, waiting for transfers between devices, per_device(): lax.psum_scatter(mixed_part, 'exp', scatter_dimension=0, tiled=True)  68.6 us
    all_gather x1, waiting for transfers between devices, per_device(): group_tokens = lax.all_gather(tokens, 'exp', axis=0, tiled=True)  67.4 us
    all_gather x1, waiting for transfers between devices, per_device(): group_cot = lax.all_gather(cotangent, 'exp', axis=0, tiled=True)  43.9 us
    all_gather x1, blocking collectives, per_device(): group_weight = lax.all_gather(weight_table, 'exp', axis=0, tiled=True)  32.6 us
    ppermute x2, waiting for transfers between devices, shifted(): lax.ppermute(value, axis, [(i, (i + by) % size) for i in range(size)])  18.7 us
    dot_general x1, matrix products, chunk_pass(): jnp.einsum('eth,etd->ehd', hidden, slot_cot, preferred_element_type=jnp.f...  15.9 us
    dot_general x1, matrix products, chunk_pass(): jnp.einsum('eth,edh->etd', up_cot, up_matrix, preferred_element_type=jnp....  12.9 us
  transfers between devices with their start and end apart: 6, of which 6 were waited for; matrix products, arithmetic and copies ran while one was open for 13% of the time, Pallas kernels for 0%

profile of v1, /device:TPU:0, one launch (start us, length us, event | category | flops | bytes accessed | tf_op | source)
XLA Modules:
  0.0 505.2 jit_solution(15658487517615227164)
XLA Ops:
  7.2 0.0 copy-start
  7.2 0.0 all-gather.5.cloned.1.call-start
  7.2 0.7 all-gather.5.cloned.1.call-update
  7.9 0.0 all-gather.3.cloned.1.call-start
  8.0 0.7 all-gather.3.cloned.1.call-update
  8.7 0.0 reduce-scatter.3.cloned.1.call-start
  8.7 0.7 convert_element_type.64
  9.4 0.7 select_reduce_fusion
  10.1 32.6 %all_gather.9 = bf16[2048,16]{0,1:T(8,128)(2,1)S(1)} all-gather(bf16[256,16]{0,1:T(8,128)(2,1)S(1)} %select_reduce_fusion), channel_id=1, replica_groups=mesh['rep'=4,'exp'=8] {'exp'}, dimensions={0}, use_global_device_ids=true | all-gather | bytes 73728 | tf_op jit(solution)/shard_map/all_gather | solution.py:48
  42.8 0.0 copy-start.3
  42.8 43.9 %all-gather.5.cloned.1.call-done = bf16[2048,1024]{1,0:T(8,128)(2,1)} async-done(((bf16[256,1024]{1,0:T(8,128)(2,1)}), bf16[2048,1024]{1,0:T(8,128)(2,1)}) %all-gather.5.cloned.1.call-update) | async-done | bytes 4194320 | tf_op jit(solution)/shard_map/all_gather | solution.py:50
  86.7 6.5 %convert_element_type.70 = f32[2048,1024]{1,0:T(8,128)} convert(bf16[2048,1024]{1,0:T(8,128)(2,1)} %all-gather.5.cloned.1.call-done) | non-fusion elementwise | flops 2097152 | bytes 12582912 | tf_op jit(solution)/shard_map/convert_element_type | solution.py:74
  93.1 67.4 %all-gather.3.cloned.1.call-done = bf16[2048,1024]{1,0:T(8,128)(2,1)} async-done(((bf16[256,1024]{1,0:T(8,128)(2,1)}), bf16[2048,1024]{1,0:T(8,128)(2,1)}) %all-gather.3.cloned.1.call-update) | async-done | bytes 4194320 | tf_op jit(solution)/shard_map/all_gather | solution.py:49
  160.5 0.0 copy-done.3
  160.5 0.0 copy-start.4
  160.5 7.7 %fusion.18 = f32[2,384,2048]{2,1,0:T(8,128)} fusion(bf16[2048,1024]{1,0:T(8,128)(2,1)} %all-gather.3.cloned.1.call-done, bf16[1,2,1024,384]{3,2,1,0:T(8,128)(2,1)S(1)} %copy-done.3), kind=kOutput, calls=%fused_computation.29 | convolution fusion | flops 3221225472 | bytes 12058624 | tf_op jit(solution)/shard_map/td,edh->eth/dot_general | solution.py:64
  168.2 0.0 copy-done
  168.2 0.0 copy-done.4
  168.2 0.0 copy-start.5
  168.2 5.5 %fusion.20 = f32[2,384,2048]{2,1,0:T(8,128)} fusion(bf16[2048,1024]{1,0:T(8,128)(2,1)S(1)} %copy-done.4, bf16[1,2,1024,384]{3,2,1,0:T(8,128)(2,1)S(1)} %copy-done), kind=kOutput, calls=%fused_computation.31 | convolution fusion | flops 3221225472 | bytes 12058624 | tf_op jit(solution)/shard_map/td,edh->eth/dot_general | solution.py:61
  173.7 0.0 copy-done.5
  173.7 12.6 %multiply_convert_fusion.3 = (bf16[2,2048,384]{1,2,0:T(8,128)(2,1)}, bf16[2,2048,384]{1,2,0:T(8,128)(2,1)}, bf16[2,2048,384]{1,2,0:T(8,128)(2,1)}) fusion(f32[2,384,2048]{2,1,0:T(8,128)} %fusion.20, f32[2,384,2048]{2,1,0:T(8,128)} %fusion.18, bf16[1,2,384,1024]{3,2,1,0:T(8,128)(2,1)S(1)} %copy-done.5, f32[2048,1024]{1,0:T(8,128)} %convert_element_type.70, ...), kind=kOutput, calls=%fused_computation.23 | convolution fusion | flops 3253207040 | bytes 31997952 | tf_op jit(solution)/shard_map/etd,ehd->eth/dot_general | solution.py:75
  186.3 10.9 %multiply_reduce_fusion = f32[2048,1024]{1,0:T(8,128)} fusion(f32[2,2048]{1,0:T(2,128)S(1)} %convert_bitcast_fusion, bf16[2,2048,384]{1,2,0:T(8,128)(2,1)} %get-tuple-element.23, bf16[1,2,384,1024]{3,2,1,0:T(8,128)(2,1)S(1)} %copy-done.5), kind=kOutput, calls=%fused_computation.3 | convolution fusion | flops 3235905536 | bytes 13123584 | tf_op jit(solution)/shard_map/eth,ehd->etd/dot_general | solution.py:70
  197.1 0.0 reduce-scatter.3.cloned.1.call-update
  197.1 0.2 reduce-scatter.5.cloned.1.call-start
  197.4 0.0 copy-start.2
  197.4 11.0 %fusion.38 = f32[2,2048,1024]{2,1,0:T(8,128)} fusion(bf16[2,2048,384]{1,2,0:T(8,128)(2,1)} %get-tuple-element.22, bf16[1,2,1024,384]{3,2,1,0:T(8,128)(2,1)S(1)} %copy-done), kind=kOutput, calls=%fused_computation.48 | convolution fusion | flops 3221225472 | bytes 21495808 | tf_op jit(solution)/shard_map/eth,edh->etd/dot_general | solution.py:92
  208.3 0.0 copy-done.2
  208.3 12.9 %convert_reduce_fusion = f32[2048,1024]{1,0:T(8,128)} fusion(f32[2,2048,1024]{2,1,0:T(8,128)} %fusion.38, bf16[2,2048,384]{1,2,0:T(8,128)(2,1)S(1)} %copy-done.2, bf16[1,2,1024,384]{3,2,1,0:T(8,128)(2,1)S(1)} %copy-done.3), kind=kOutput, calls=%fused_computation | convolution fusion | flops 3235905536 | bytes 29884416 | tf_op jit(solution)/shard_map/eth,edh->etd/dot_general | solution.py:93
  221.3 0.0 copy-start.6
  221.3 0.0 reduce-scatter.5.cloned.1.call-update
  221.3 1.4 copy-done.6
  222.7 0.0 collective-permute-start.1
  222.7 1.5 collective-permute-start
  224.9 6.6 %fusion.45 = bf16[1,2,1024,384]{2,3,1,0:T(8,128)(2,1)S(1)} fusion(bf16[2,2048,384]{1,2,0:T(8,128)(2,1)} %get-tuple-element.22, bf16[2048,1024]{1,0:T(8,128)(2,1)} %all-gather.3.cloned.1.call-done), kind=kOutput, calls=%fused_computation.53 | convolution fusion | flops 3222011904 | bytes 8912896 | tf_op jit(solution)/shard_map/td,eth->edh/dot_general | solution.py:85
  231.5 1.6 copy.35
  233.1 6.7 %fusion.42 = bf16[1,2,1024,384]{2,3,1,0:T(8,128)(2,1)S(1)} fusion(bf16[2,2048,384]{1,2,0:T(8,128)(2,1)} %get-tuple-element.21, bf16[2048,1024]{1,0:T(8,128)(2,1)} %all-gather.3.cloned.1.call-done), kind=kOutput, calls=%fused_computation.52 | convolution fusion | flops 3222011904 | bytes 8912896 | tf_op jit(solution)/shard_map/td,eth->edh/dot_general | solution.py:88
  239.8 1.6 copy.36
  241.4 17.6 %collective-permute-done.1 = bf16[1,2,384,1024]{3,2,1,0:T(8,128)(2,1)} collective-permute-done((bf16[1,2,384,1024]{3,2,1,0:T(8,128)(2,1)S(1)}, bf16[1,2,384,1024]{3,2,1,0:T(8,128)(2,1)}, u32[]{:S(2)}, u32[]{:S(2)}) %collective-permute-start.1) | collective-permute-done | bytes 1572896 | tf_op jit(solution)/shard_map/ppermute | solution.py:20
  259.0 1.1 collective-permute-done
  260.1 0.0 copy-start.1
  260.1 15.9 %fusion.49 = (f32[1,2,384,1024]{3,2,1,0:T(8,128)}, bf16[1,2,384,1024]{3,2,1,0:T(8,128)(2,1)}, f32[1,2,384,1024]{3,2,1,0:T(8,128)}) fusion(f32[1,2,384,1024]{3,2,1,0:T(8,128)} %param.18, f32[1,2,384,1024]{3,2,1,0:T(8,128)} %param.17, bf16[1,2,384,1024]{3,2,1,0:T(8,128)(2,1)} %collective-permute-done, bf16[1,2,384,1024]{3,2,1,0:T(8,128)(2,1)} %collective-permute-done.1, ...), kind=kOutput, calls=%fused_computation.55 | convolution fusion | flops 3246129152 | bytes 30425088 | tf_op jit(solution)/shard_map/eth,etd->ehd/dot_general | solution.py:82
  276.0 68.6 %reduce-scatter.3.cloned.1.call-done = f32[256,1024]{1,0:T(8,128)} async-done(((f32[2048,1024]{1,0:T(8,128)}), f32[256,1024]{1,0:T(8,128)}) %reduce-scatter.3.cloned.1.call-update) | async-done | bytes 1048592 | tf_op jit(solution)/shard_map/reduce_scatter | solution.py:129
  344.6 2.1 convert_element_type.69
  346.7 149.9 %reduce-scatter.5.cloned.1.call-done = f32[256,1024]{1,0:T(8,128)} async-done(((f32[2048,1024]{1,0:T(8,128)}), f32[256,1024]{1,0:T(8,128)}) %reduce-scatter.5.cloned.1.call-update) | async-done | bytes 1048592 | tf_op jit(solution)/shard_map/reduce_scatter | solution.py:132
  496.6 2.1 convert_element_type.76
  498.7 0.0 copy-done.1
  (1 shorter events, 0.0 us)
Async XLA Ops:
  7.2 161.0 %copy-start = (bf16[1,2,1024,384]{3,2,1,0:T(8,128)(2,1)S(1)}, bf16[1,2,1024,384]{3,2,1,0:T(8,128)(2,1)}, u32[]{:S(2)}) copy-start(bf16[1,2,1024,384]{3,2,1,0:T(8,128)(2,1)} %param.14) | copy-start | bytes 4718596
  7.2 79.5 %all-gather.5.cloned.1.call-start = ((), (), s32[]{:S(2)}) async-start(), calls=%async_computation.4 | async-start | bytes 4718592 | tf_op jit(solution)/shard_map/all_gather | solution.py:50
  7.9 152.6 %all-gather.3.cloned.1.call-start = ((), (), s32[]{:S(2)}) async-start(), calls=%async_computation.2 | async-start | bytes 4718592 | tf_op jit(solution)/shard_map/all_gather | solution.py:49
  8.7 336.0 %reduce-scatter.3.cloned.1.call-start = ((), (), s32[]{:S(2)}) async-start(), calls=%async_computation.3 | async-start | bytes 9437184 | tf_op jit(solution)/shard_map/reduce_scatter | solution.py:129
  42.8 117.7 %copy-start.3 = (bf16[1,2,1024,384]{3,2,1,0:T(8,128)(2,1)S(1)}, bf16[1,2,1024,384]{3,2,1,0:T(8,128)(2,1)}, u32[]{:S(2)}) copy-start(bf16[1,2,1024,384]{3,2,1,0:T(8,128)(2,1)} %param.15) | copy-start | bytes 4718596
  160.5 7.7 %copy-start.4 = (bf16[2048,1024]{1,0:T(8,128)(2,1)S(1)}, bf16[2048,1024]{1,0:T(8,128)(2,1)}, u32[]{:S(2)}) copy-start(bf16[2048,1024]{1,0:T(8,128)(2,1)} %all-gather.3.cloned.1.call-done) | copy-start | bytes 12582916
  168.2 5.5 %copy-start.5 = (bf16[1,2,384,1024]{3,2,1,0:T(8,128)(2,1)S(1)}, bf16[1,2,384,1024]{3,2,1,0:T(8,128)(2,1)}, u32[]{:S(2)}) copy-start(bf16[1,2,384,1024]{3,2,1,0:T(8,128)(2,1)} %param.16) | copy-start | bytes 4718596
  197.1 299.5 %reduce-scatter.5.cloned.1.call-start = ((), (), s32[]{:S(2)}) async-start(), calls=%async_computation.5 | async-start | bytes 9437184 | tf_op jit(solution)/shard_map/reduce_scatter | solution.py:132
  197.4 11.0 %copy-start.2 = (bf16[2,2048,384]{1,2,0:T(8,128)(2,1)S(1)}, bf16[2,2048,384]{1,2,0:T(8,128)(2,1)}, u32[]{:S(2)}) copy-start(bf16[2,2048,384]{1,2,0:T(8,128)(2,1)} %get-tuple-element.21) | copy-start | bytes 9437188
  221.3 1.4 copy-start.6
  222.7 36.2 %collective-permute-start.1 = (bf16[1,2,384,1024]{3,2,1,0:T(8,128)(2,1)S(1)}, bf16[1,2,384,1024]{3,2,1,0:T(8,128)(2,1)}, u32[]{:S(2)}, u32[]{:S(2)}) collective-permute-start(bf16[1,2,384,1024]{3,2,1,0:T(8,128)(2,1)S(1)} %copy-done.6), channel_id=1, source_target_pairs={{0,8},{8,16},{16,24},{24,0},{1,9},{9,17},{17,25},{25,1},{2,10},{10... | collective-permute-start | bytes 4718600 | tf_op jit(solution)/shard_map/ppermute | solution.py:20
  222.7 37.3 %collective-permute-start = (bf16[1,2,384,1024]{3,2,1,0:T(8,128)(2,1)S(1)}, bf16[1,2,384,1024]{3,2,1,0:T(8,128)(2,1)}, u32[]{:S(2)}, u32[]{:S(2)}) collective-permute-start(bf16[1,2,384,1024]{3,2,1,0:T(8,128)(2,1)S(1)} %copy-done.6), channel_id=1, source_target_pairs={{0,16},{8,24},{16,0},{24,8},{1,17},{9,25},{17,1},{25,9},{2,18},{10... | collective-permute-start | bytes 4718600 | tf_op jit(solution)/shard_map/ppermute | solution.py:20
  260.1 238.6 %copy-start.1 = (bf16[1,2,1024,384]{3,2,1,0:T(8,128)(2,1)S(1)}, bf16[1,2,1024,384]{3,2,1,0:T(8,128)(2,1)}, u32[]{:S(2)}) copy-start(bf16[1,2,1024,384]{3,2,1,0:T(8,128)(2,1)} %param.14) | copy-start | bytes 4718596
Sparse Core Ops, SparseCore 0:
  10.1 76.4 all-gather.4
  88.8 71.6 all-gather.2
  197.3 147.3 reduce-scatter.2
  348.5 148.0 reduce-scatter.4

commit v2 on v1

--- a/solution.py
+++ b/solution.py
@@ -18,6 +18,10 @@
 def shifted(value, axis, by):
     size = lax.axis_size(axis)
     return lax.ppermute(value, axis, [(i, (i + by) % size) for i in range(size)])
+
+
+def as_bf16(value):
+    return lax.reduce_precision(value, exponent_bits=8, mantissa_bits=7)
 
 
 def dense_weights(expert_ids, combine, experts):
@@ -44,9 +48,22 @@
     experts = local_experts * devices_exp
     my_exp = lax.axis_index("exp")
 
+    token_count, model_width = tokens.shape
     weight_table = dense_weights(expert_ids, combine, experts)
-    group_weight = lax.all_gather(weight_table, "exp", axis=0, tiled=True)
-    group_tokens = lax.all_gather(tokens, "exp", axis=0, tiled=True)
+    weight_rows = -(-(token_count * experts) // model_width)
+    weight_rows = -(-weight_rows // 8) * 8
+    weight_flat = jnp.pad(
+        weight_table.reshape(-1), (0, weight_rows * model_width - token_count * experts)
+    )
+    packed_tokens = jnp.concatenate([tokens, weight_flat.reshape(weight_rows, model_width)])
+    gathered = lax.all_gather(packed_tokens, "exp", axis=0, tiled=False)
+    group_tokens = gathered[:, :token_count].reshape(devices_exp * token_count, model_width)
+    group_weight = (
+        gathered[:, token_count:]
+        .reshape(devices_exp, -1)[:, : token_count * experts]
+        .reshape(devices_exp * token_count, experts)
+    )
+    _, cotangent = lax.optimization_barrier((gathered, cotangent))
     group_cot = lax.all_gather(cotangent, "exp", axis=0, tiled=True)
     local_weight = lax.dynamic_slice_in_dim(
         group_weight, my_exp * local_experts, local_experts, axis=1
@@ -67,10 +84,10 @@
         sigmoid_gate = jax.nn.sigmoid(gate_value)
         active = gate_value * sigmoid_gate
         hidden = (active * up_value).astype(jnp.bfloat16)
-        expert_out = jnp.einsum(
-            "eth,ehd->etd", hidden, down_matrix, preferred_element_type=jnp.float32
-        ).astype(jnp.bfloat16)
-        mixed_part = jnp.sum(chunk_weight * expert_out.astype(jnp.float32), axis=0)
+        expert_out = as_bf16(
+            jnp.einsum("eth,ehd->etd", hidden, down_matrix, preferred_element_type=jnp.float32)
+        )
+        mixed_part = jnp.sum(chunk_weight * expert_out, axis=0)
         slot_cot = (chunk_weight * chunk_cot.astype(jnp.float32)[None]).astype(jnp.bfloat16)
         hidden_cot = jnp.einsum(
             "etd,ehd->eth", slot_cot, down_matrix, preferred_element_type=jnp.float32
@@ -88,11 +105,11 @@
         up_grad = jnp.einsum(
             "td,eth->edh", chunk_tokens, up_cot, preferred_element_type=jnp.float32
         )
-        input_cot = (
+        input_cot = as_bf16(
             jnp.einsum("eth,edh->etd", gate_cot, gate_matrix, preferred_element_type=jnp.float32)
             + jnp.einsum("eth,edh->etd", up_cot, up_matrix, preferred_element_type=jnp.float32)
-        ).astype(jnp.bfloat16)
-        input_part = jnp.sum(input_cot.astype(jnp.float32), axis=0)
+        )
+        input_part = jnp.sum(input_cot, axis=0)
         return mixed_part, input_part, gate_grad, up_grad, down_grad
 
     group_count = group_tokens.shape[0]

time: 506 us -> 500 us (0.988)
  blocking collectives: 32.6 us -> 0 us
  waiting for transfers between devices: 350 us -> 367 us
  local copies, waits for them, and re-layouts: 4.57 us -> 13 us
    all_gather x1 -> x0, blocking collectives: 32.6 us -> none  [per_device(): group_weight = lax.all_gather(weight_table, 'exp', axis=0, tiled=True)]
    all_gather x1, waiting for transfers between devices: 67.4 us -> 77.8 us  [per_device(): gathered = lax.all_gather(packed_tokens, 'exp', axis=0, tiled=False)]
    all_gather x1, waiting for transfers between devices: 43.9 us -> 52.6 us  [per_device(): group_cot = lax.all_gather(cotangent, 'exp', axis=0, tiled=True)]
  transfers between devices with their start and end apart: 6 -> 6, of which waited for: 6 -> 6; matrix products, arithmetic and copies ran while one was open for 13% -> 16% of each run, Pallas kernels for 0% -> 0%
where the time goes in v2:
time: 500 us; the launch traced here: 499 us
  waiting for transfers between devices  367 us (73%)
  matrix products  92.1 us (18%)
  between operations  14.5 us (3%)
  local copies, waits for them, and re-layouts  13 us (3%)
  other arithmetic  11 us (2%)
    reduce_scatter x1, waiting for transfers between devices, per_device(): lax.psum_scatter(input_part, 'exp', scatter_dimension=0, tiled=True)  150 us
    all_gather x1, waiting for transfers between devices, per_device(): gathered = lax.all_gather(packed_tokens, 'exp', axis=0, tiled=False)  77.8 us
    reduce_scatter x1, waiting for transfers between devices, per_device(): lax.psum_scatter(mixed_part, 'exp', scatter_dimension=0, tiled=True)  68 us
    all_gather x1, waiting for transfers between devices, per_device(): group_cot = lax.all_gather(cotangent, 'exp', axis=0, tiled=True)  52.6 us
    ppermute x2, waiting for transfers between devices, shifted(): lax.ppermute(value, axis, [(i, (i + by) % size) for i in range(size)])  18.2 us
    dot_general x1, matrix products, chunk_pass(): jnp.einsum('eth,etd->ehd', hidden, slot_cot, preferred_element_type=jnp.f...  16.2 us
    dot_general x1, matrix products, chunk_pass(): jnp.einsum('etd,ehd->eth', slot_cot, down_matrix, preferred_element_type=...  14.9 us
    dot_general x1, matrix products, chunk_pass(): jnp.einsum('eth,edh->etd', up_cot, up_matrix, preferred_element_type=jnp....  13.7 us
  transfers between devices with their start and end apart: 6, of which 6 were waited for; matrix products, arithmetic and copies ran while one was open for 16% of the time, Pallas kernels for 0%

profile of v2, /device:TPU:0, one launch (start us, length us, event | category | flops | bytes accessed | tf_op | source)
XLA Modules:
  0.0 499.1 jit_solution(6284070337207461421)
XLA Ops:
  7.2 0.0 copy-start
  7.2 0.0 all-gather.6.cloned.1.call-start
  7.2 0.8 convert_element_type.58
  8.0 0.7 select_reduce_fusion
  8.7 0.1 copy.32
  8.9 0.1 convert_element_type.60
  9.0 1.9 pad_maximum_fusion
  10.9 0.0 all-gather.6.cloned.1.call-update
  10.9 0.0 all-gather.4.cloned.1.call-start
  11.0 77.8 %all-gather.6.cloned.1.call-done = bf16[2112,1024]{1,0:T(8,128)(2,1)} async-done(((bf16[264,1024]{1,0:T(8,128)(2,1)}), bf16[2112,1024]{1,0:T(8,128)(2,1)}) %all-gather.6.cloned.1.call-update) | async-done | bytes 4325392 | tf_op jit(solution)/shard_map/all_gather | solution.py:59
  88.8 0.0 all-gather.4.cloned.1.call-update
  88.8 0.0 reduce-scatter.3.cloned.1.call-start
  88.8 4.6 slice.14
  93.4 0.9 slice_bitcast_fusion
  94.3 0.1 copy.42
  94.4 0.4 reshape.43
  94.8 0.2 convert_bitcast_fusion
  95.1 0.3 copy.33
  95.4 0.0 copy-start.3
  95.4 9.2 %fusion.23 = f32[2048,2,384]{2,0,1:T(8,128)} fusion(bf16[2048,1024,1]{1,0,2:T(8,128)(2,1)} %bitcast.106, bf16[1,2,1024,384]{3,2,1,0:T(8,128)(2,1)} %param.15), kind=kOutput, calls=%fused_computation.38 | convolution fusion | flops 3221225472 | bytes 12058624 | tf_op jit(solution)/shard_map/td,edh->eth/dot_general | solution.py:81
  104.6 0.0 copy-done
  104.6 0.0 copy-done.3
  104.6 5.3 %fusion.27 = f32[2048,2,384]{2,0,1:T(8,128)} fusion(bf16[2048,1024,1]{1,0,2:T(8,128)(2,1)S(1)} %bitcast.109, bf16[1,2,1024,384]{3,2,1,0:T(8,128)(2,1)S(1)} %copy-done), kind=kOutput, calls=%fused_computation.42 | convolution fusion | flops 3221225472 | bytes 12058624 | tf_op jit(solution)/shard_map/td,edh->eth/dot_general | solution.py:78
  109.9 0.0 copy-start.5
  109.9 52.6 %all-gather.4.cloned.1.call-done = bf16[2048,1024]{1,0:T(8,128)(2,1)} async-done(((bf16[256,1024]{1,0:T(8,128)(2,1)}), bf16[2048,1024]{1,0:T(8,128)(2,1)}) %all-gather.4.cloned.1.call-update) | async-done | bytes 4194320 | tf_op jit(solution)/shard_map/all_gather | solution.py:67
  162.6 3.2 convert_element_type.63
  165.8 0.0 copy-done.5
  165.8 0.0 copy-start.2
  165.8 14.9 %multiply_convert_fusion.3 = (bf16[2,2048,384]{2,1,0:T(8,128)(2,1)}, bf16[2,2048,384]{2,1,0:T(8,128)(2,1)}, bf16[2,2048,384]{2,1,0:T(8,128)(2,1)S(1)}) fusion(f32[2048,2,384]{2,0,1:T(8,128)} %fusion.27, f32[2048,2,384]{2,0,1:T(8,128)} %fusion.23, bf16[1,2,384,1024]{3,2,1,0:T(8,128)(2,1)S(1)} %copy-done.5, f32[2048,1024]{1,0:T(8,128)S(1)} %convert_element_type.63, ...), kind=kOutput, calls=%fused_computation.22 | convolution fusion | flops 3253207040 | bytes 31997952 | tf_op jit(solution)/shard_map/etd,ehd->eth/dot_general | solution.py:92
  180.6 0.0 copy-done.2
  180.6 0.0 copy-start.7
  180.7 1.6 copy-done.7
  182.3 8.8 %multiply_reduce_fusion = f32[2048,1024]{1,0:T(8,128)} fusion(f32[2,2048]{1,0:T(2,128)S(1)} %copy.33, bf16[2,2048,384]{2,1,0:T(8,128)(2,1)S(1)} %get-tuple-element.32, bf16[1,2,384,1024]{3,2,1,0:T(8,128)(2,1)S(1)} %copy-done.5), kind=kOutput, calls=%fused_computation.2 | convolution fusion | flops 3231711232 | bytes 13123584 | tf_op jit(solution)/shard_map/eth,ehd->etd/dot_general | solution.py:88
  191.1 0.0 reduce-scatter.3.cloned.1.call-update
  191.1 0.2 reduce-scatter.5.cloned.1.call-start
  191.4 0.0 copy-start.4
  191.4 10.4 %fusion.25 = f32[2,2048,1024]{2,1,0:T(8,128)} fusion(bf16[2,2048,384]{2,1,0:T(8,128)(2,1)} %get-tuple-element.31, bf16[1,2,1024,384]{3,2,1,0:T(8,128)(2,1)S(1)} %copy-done), kind=kOutput, calls=%fused_computation.40 | convolution fusion | flops 3221225472 | bytes 21495808 | tf_op jit(solution)/shard_map/eth,edh->etd/dot_general | solution.py:109
  201.8 0.0 copy-done.4
  201.8 13.7 %reduce-precision_reduce_fusion = f32[2048,1024]{1,0:T(8,128)} fusion(f32[2,2048,1024]{2,1,0:T(8,128)} %fusion.25, bf16[2,2048,384]{2,1,0:T(8,128)(2,1)} %get-tuple-element.30, bf16[1,2,1024,384]{3,2,1,0:T(8,128)(2,1)S(1)} %copy-done.4), kind=kOutput, calls=%fused_computation | convolution fusion | flops 3231711232 | bytes 29884416 | tf_op jit(solution)/shard_map/eth,edh->etd/dot_general | solution.py:110
  215.5 0.0 copy-start.6
  215.5 0.0 reduce-scatter.5.cloned.1.call-update
  215.5 1.4 copy-done.6
  216.9 0.0 collective-permute-start.1
  216.9 1.5 collective-permute-start
  219.1 6.7 %fusion.30 = bf16[1,2,1024,384]{2,3,1,0:T(8,128)(2,1)S(1)} fusion(bf16[2,2048,384]{2,1,0:T(8,128)(2,1)} %get-tuple-element.31, bf16[2048,1024,1]{1,0,2:T(8,128)(2,1)} %bitcast.107), kind=kOutput, calls=%fused_computation.45 | convolution fusion | flops 3222011904 | bytes 8912896 | tf_op jit(solution)/shard_map/td,eth->edh/dot_general | solution.py:102
  225.8 1.8 copy.37
  227.6 6.8 %fusion.31 = bf16[1,2,1024,384]{2,3,1,0:T(8,128)(2,1)S(1)} fusion(bf16[2,2048,384]{2,1,0:T(8,128)(2,1)} %get-tuple-element.30, bf16[2048,1024,1]{1,0,2:T(8,128)(2,1)} %bitcast.108), kind=kOutput, calls=%fused_computation.46 | convolution fusion | flops 3222011904 | bytes 8912896 | tf_op jit(solution)/shard_map/td,eth->edh/dot_general | solution.py:105
  234.5 1.6 copy.38
  236.1 17.1 %collective-permute-done.1 = bf16[1,2,384,1024]{3,2,1,0:T(8,128)(2,1)} collective-permute-done((bf16[1,2,384,1024]{3,2,1,0:T(8,128)(2,1)S(1)}, bf16[1,2,384,1024]{3,2,1,0:T(8,128)(2,1)}, u32[]{:S(2)}, u32[]{:S(2)}) %collective-permute-start.1) | collective-permute-done | bytes 1572896 | tf_op jit(solution)/shard_map/ppermute | solution.py:20
  253.2 1.1 collective-permute-done
  254.3 0.0 copy-start.1
  254.3 16.2 %fusion.33 = (f32[1,2,384,1024]{3,2,1,0:T(8,128)}, bf16[1,2,384,1024]{3,2,1,0:T(8,128)(2,1)}, f32[1,2,384,1024]{3,2,1,0:T(8,128)}) fusion(f32[1,2,384,1024]{3,2,1,0:T(8,128)} %param.18, f32[1,2,384,1024]{3,2,1,0:T(8,128)} %param.17, bf16[1,2,384,1024]{3,2,1,0:T(8,128)(2,1)} %collective-permute-done, bf16[1,2,384,1024]{3,2,1,0:T(8,128)(2,1)} %collective-permute-done.1, ...), kind=kOutput, calls=%fused_computation.49 | convolution fusion | flops 3246129152 | bytes 30425088 | tf_op jit(solution)/shard_map/eth,etd->ehd/dot_general | solution.py:99
  270.5 68.0 %reduce-scatter.3.cloned.1.call-done = f32[256,1024]{1,0:T(8,128)} async-done(((f32[2048,1024]{1,0:T(8,128)}), f32[256,1024]{1,0:T(8,128)}) %reduce-scatter.3.cloned.1.call-update) | async-done | bytes 1048592 | tf_op jit(solution)/shard_map/reduce_scatter | solution.py:146
  338.5 2.1 convert_element_type.62
  340.6 149.9 %reduce-scatter.5.cloned.1.call-done = f32[256,1024]{1,0:T(8,128)} async-done(((f32[2048,1024]{1,0:T(8,128)}), f32[256,1024]{1,0:T(8,128)}) %reduce-scatter.5.cloned.1.call-update) | async-done | bytes 1048592 | tf_op jit(solution)/shard_map/reduce_scatter | solution.py:149
  490.5 2.1 convert_element_type.67
  492.6 0.0 copy-done.1
  (3 shorter events, 0.0 us)
Async XLA Ops:
  7.2 97.5 %copy-start = (bf16[1,2,1024,384]{3,2,1,0:T(8,128)(2,1)S(1)}, bf16[1,2,1024,384]{3,2,1,0:T(8,128)(2,1)}, u32[]{:S(2)}) copy-start(bf16[1,2,1024,384]{3,2,1,0:T(8,128)(2,1)} %param.14) | copy-start | bytes 4718596
  7.2 81.6 %all-gather.6.cloned.1.call-start = ((), (), s32[]{:S(2)}) async-start(), calls=%async_computation.5 | async-start | bytes 4866048 | tf_op jit(solution)/shard_map/all_gather | solution.py:59
  10.9 151.6 %all-gather.4.cloned.1.call-start = ((), (), s32[]{:S(2)}) async-start(), calls=%async_computation.3 | async-start | bytes 4718592 | tf_op jit(solution)/shard_map/all_gather | solution.py:67
  88.8 249.7 %reduce-scatter.3.cloned.1.call-start = ((), (), s32[]{:S(2)}) async-start(), calls=%async_computation.2 | async-start | bytes 9437184 | tf_op jit(solution)/shard_map/reduce_scatter | solution.py:146
  95.4 9.3 %copy-start.3 = (bf16[8,256,1024]{2,1,0:T(8,128)(2,1)S(1)}, bf16[8,256,1024]{2,1,0:T(8,128)(2,1)}, u32[]{:S(2)}) copy-start(bf16[8,256,1024]{2,1,0:T(8,128)(2,1)} %slice.14) | copy-start | bytes 12582916
  109.9 55.8 %copy-start.5 = (bf16[1,2,384,1024]{3,2,1,0:T(8,128)(2,1)S(1)}, bf16[1,2,384,1024]{3,2,1,0:T(8,128)(2,1)}, u32[]{:S(2)}) copy-start(bf16[1,2,384,1024]{3,2,1,0:T(8,128)(2,1)} %param.16) | copy-start | bytes 4718596
  165.8 14.9 %copy-start.2 = (f32[2048,1024]{1,0:T(8,128)}, f32[2048,1024]{1,0:T(8,128)S(1)}, u32[]{:S(2)}) copy-start(f32[2048,1024]{1,0:T(8,128)S(1)} %convert_element_type.63) | copy-start | bytes 25165828
  180.6 1.6 copy-start.7
  191.1 299.3 %reduce-scatter.5.cloned.1.call-start = ((), (), s32[]{:S(2)}) async-start(), calls=%async_computation.4 | async-start | bytes 9437184 | tf_op jit(solution)/shard_map/reduce_scatter | solution.py:149
  191.4 10.4 %copy-start.4 = (bf16[1,2,1024,384]{3,2,1,0:T(8,128)(2,1)S(1)}, bf16[1,2,1024,384]{3,2,1,0:T(8,128)(2,1)}, u32[]{:S(2)}) copy-start(bf16[1,2,1024,384]{3,2,1,0:T(8,128)(2,1)} %param.15) | copy-start | bytes 4718596
  215.5 1.4 copy-start.6
  216.9 36.2 %collective-permute-start.1 = (bf16[1,2,384,1024]{3,2,1,0:T(8,128)(2,1)S(1)}, bf16[1,2,384,1024]{3,2,1,0:T(8,128)(2,1)}, u32[]{:S(2)}, u32[]{:S(2)}) collective-permute-start(bf16[1,2,384,1024]{3,2,1,0:T(8,128)(2,1)S(1)} %copy-done.6), channel_id=1, source_target_pairs={{0,8},{8,16},{16,24},{24,0},{1,9},{9,17},{17,25},{25,1},{2,10},{10... | collective-permute-start | bytes 4718600 | tf_op jit(solution)/shard_map/ppermute | solution.py:20
  216.9 37.3 %collective-permute-start = (bf16[1,2,384,1024]{3,2,1,0:T(8,128)(2,1)S(1)}, bf16[1,2,384,1024]{3,2,1,0:T(8,128)(2,1)}, u32[]{:S(2)}, u32[]{:S(2)}) collective-permute-start(bf16[1,2,384,1024]{3,2,1,0:T(8,128)(2,1)S(1)} %copy-done.6), channel_id=1, source_target_pairs={{0,16},{8,24},{16,0},{24,8},{1,17},{9,25},{17,1},{25,9},{2,18},{10... | collective-permute-start | bytes 4718600 | tf_op jit(solution)/shard_map/ppermute | solution.py:20
  254.3 238.3 %copy-start.1 = (bf16[1,2,1024,384]{3,2,1,0:T(8,128)(2,1)S(1)}, bf16[1,2,1024,384]{3,2,1,0:T(8,128)(2,1)}, u32[]{:S(2)}) copy-start(bf16[1,2,1024,384]{3,2,1,0:T(8,128)(2,1)} %param.14) | copy-start | bytes 4718596
Sparse Core Ops, SparseCore 0:
  11.0 77.6 all-gather.5
  90.9 71.6 all-gather.3
  191.3 147.1 reduce-scatter.2
  342.4 148.0 reduce-scatter.4

commit v3 on v2

--- a/solution.py
+++ b/solution.py
@@ -5,6 +5,7 @@
 
 ROUNDS = 2
 CHUNK_ROWS = 2048
+RING_MAX = 8
 
 
 beta_one = 0.9
@@ -29,6 +30,58 @@
     hit = expert_ids[:, :, None] == expert_iota[None, None, :]
     picked = jnp.where(hit, combine.astype(jnp.float32)[:, :, None], 0.0)
     return jnp.sum(picked, axis=1).astype(jnp.bfloat16)
+
+
+def ring_order(size):
+    return list(range(0, size, 2)) + list(range(size - 1 - size % 2, 0, -2))
+
+
+def ring_pairs(ring, step):
+    size = len(ring)
+    return [(ring[q], ring[(q + step) % size]) for q in range(size)]
+
+
+def ring_all_gather(shard, axis, ring):
+    size = len(ring)
+    ahead = size // 2
+    behind = size - 1 - ahead
+    got = {0: shard}
+    current = shard
+    for step in range(ahead):
+        current = lax.ppermute(current, axis, ring_pairs(ring, 1))
+        got[-(step + 1)] = current
+    current = shard
+    for step in range(behind):
+        current = lax.ppermute(current, axis, ring_pairs(ring, -1))
+        got[step + 1] = current
+    return jnp.concatenate([got[offset] for offset in range(-ahead, behind + 1)])
+
+
+def ring_reduce_scatter(part, axis, ring):
+    size = len(ring)
+    ahead = size // 2
+    behind = size - 1 - ahead
+    blocks = part.reshape((size, part.shape[0] // size) + part.shape[1:])
+
+    def block_at(offset):
+        return blocks[(offset + ahead) % size]
+
+    result = block_at(0)
+    if ahead:
+        send = block_at(ahead)
+        for step in range(ahead):
+            received = lax.ppermute(send, axis, ring_pairs(ring, 1))
+            if step < ahead - 1:
+                send = received + block_at(ahead - step - 1)
+        result = result + received
+    if behind:
+        send = block_at(-behind)
+        for step in range(behind):
+            received = lax.ppermute(send, axis, ring_pairs(ring, -1))
+            if step < behind - 1:
+                send = received + block_at(-behind + step + 1)
+        result = result + received
+    return result
 
 
 def per_device(
@@ -56,7 +109,20 @@
         weight_table.reshape(-1), (0, weight_rows * model_width - token_count * experts)
     )
     packed_tokens = jnp.concatenate([tokens, weight_flat.reshape(weight_rows, model_width)])
-    gathered = lax.all_gather(packed_tokens, "exp", axis=0, tiled=False)
+    ring = ring_order(devices_exp)
+    use_ring = devices_exp <= RING_MAX
+
+    def gather(value):
+        if use_ring:
+            return ring_all_gather(value, "exp", ring)
+        return lax.all_gather(value, "exp", axis=0, tiled=True)
+
+    def reduce_scatter(value):
+        if use_ring:
+            return ring_reduce_scatter(value, "exp", ring)
+        return lax.psum_scatter(value, "exp", scatter_dimension=0, tiled=True)
+
+    gathered = gather(packed_tokens[None])
     group_tokens = gathered[:, :token_count].reshape(devices_exp * token_count, model_width)
     group_weight = (
         gathered[:, token_count:]
@@ -64,7 +130,7 @@
         .reshape(devices_exp * token_count, experts)
     )
     _, cotangent = lax.optimization_barrier((gathered, cotangent))
-    group_cot = lax.all_gather(cotangent, "exp", axis=0, tiled=True)
+    group_cot = gather(cotangent)
     local_weight = lax.dynamic_slice_in_dim(
         group_weight, my_exp * local_experts, local_experts, axis=1
     ).astype(jnp.float32)
@@ -143,12 +209,8 @@
         input_part = input_parts.reshape(group_count, -1)
     gate_grad = gate_grad.astype(jnp.bfloat16)
     up_grad = up_grad.astype(jnp.bfloat16)
-    mixed = lax.psum_scatter(mixed_part, "exp", scatter_dimension=0, tiled=True).astype(
-        jnp.bfloat16
-    )
-    input_grad = lax.psum_scatter(
-        input_part, "exp", scatter_dimension=0, tiled=True
-    ).astype(jnp.bfloat16)
+    mixed = reduce_scatter(mixed_part).astype(jnp.bfloat16)
+    input_grad = reduce_scatter(input_part).astype(jnp.bfloat16)
 
     peers = [shifted(down_weight, "rep", 1 << bit_index) for bit_index in range(ROUNDS)]
     peer_down = peers[0]

time: 500 us -> 346 us (0.69); the launches traced: 499 us -> 340 us
  waiting for transfers between devices: 367 us -> 170 us
  starting transfers between devices: 1.89 us -> 34.8 us
  other arithmetic: 11 us -> 29.8 us
  between operations: 14.5 us -> 1.78 us
  matrix products: 92.1 us -> 81 us
  local copies, waits for them, and re-layouts: 13 us -> 22.6 us
    reduce_scatter x2 -> x0, waiting for transfers between devices: 218 us -> none  [the longest x1 150 us: per_device(): lax.psum_scatter(input_part, 'exp', scatter_dimension=0, tiled=True)]
    ppermute x0 -> x28, waiting for transfers between devices: none -> 170 us  [the longest x8 97.6 us: ring_reduce_scatter(): received = lax.ppermute(send, axis, ring_pairs(ring, 1))]
    all_gather x2 -> x0, waiting for transfers between devices: 130 us -> none  [the longest x1 77.8 us: per_device(): gathered = lax.all_gather(packed_tokens, 'exp', axis=0, tiled=False)]
    ppermute x0 -> x28, starting transfers between devices: none -> 33.2 us  [the longest x8 12.9 us: ring_reduce_scatter(): received = lax.ppermute(send, axis, ring_pairs(ring, 1))]
    add x0 -> x6, other arithmetic: none -> 19.3 us  [ring_reduce_scatter(): send = received + block_at(ahead - step - 1)]
    ppermute x2, waiting for transfers between devices: 18.2 us -> 0.01 us  [shifted(): lax.ppermute(value, axis, [(i, (i + by) % size) for i in range(size)])]
    unnamed x20 -> x37, local copies, waits for them, and re-layouts: 7.4 us -> 13.7 us
  transfers between devices with their start and end apart: 6 -> 30, of which waited for: 6 -> 18; matrix products, arithmetic and copies ran while one was open for 16% -> 37% of each run, Pallas kernels for 0% -> 0%
where the time goes in v3:
time: 346 us; the launch traced here: 340 us
  waiting for transfers between devices  170 us (49%)
  matrix products  81 us (23%)
  starting transfers between devices  34.8 us (10%)
  other arithmetic  29.8 us (9%)
  local copies, waits for them, and re-layouts  22.6 us (7%)
    ppermute x8, waiting for transfers between devices, ring_reduce_scatter(): received = lax.ppermute(send, axis, ring_pairs(ring, 1))  97.6 us
    ppermute x8, waiting for transfers between devices, ring_all_gather(): current = lax.ppermute(current, axis, ring_pairs(ring, 1))  57.2 us
    add x6, other arithmetic, ring_reduce_scatter(): send = received + block_at(ahead - step - 1)  19.3 us
    dot_general x1, matrix products, chunk_pass(): jnp.einsum('eth,edh->etd', up_cot, up_matrix, preferred_element_type=jnp....  16.4 us
    ppermute x6, waiting for transfers between devices, ring_all_gather(): current = lax.ppermute(current, axis, ring_pairs(ring, -1))  15.2 us
    dot_general x1, matrix products, chunk_pass(): jnp.einsum('etd,ehd->eth', slot_cot, down_matrix, preferred_element_type=...  14.5 us
    unnamed x37, local copies, waits for them, and re-layouts  13.7 us
    dot_general x1, matrix products, chunk_pass(): jnp.einsum('eth,etd->ehd', hidden, slot_cot, preferred_element_type=jnp.f...  13.2 us
  transfers between devices with their start and end apart: 30, of which 18 were waited for; matrix products, arithmetic and copies ran while one was open for 37% of the time, Pallas kernels for 0%

profile of v3, /device:TPU:0, one launch (start us, length us, event | category | flops | bytes accessed | tf_op | source)
XLA Modules:
  0.0 339.9 jit_solution(8247734213519576026)
XLA Ops:
  2.5 1.1 maximum_bitcast_fusion
  3.6 3.1 collective-permute-start
  6.6 12.2 %collective-permute-done = bf16[1,264,1024]{2,1,0:T(8,128)(2,1)S(1)} collective-permute-done((bf16[1,264,1024]{2,1,0:T(8,128)(2,1)S(1)}, bf16[1,264,1024]{2,1,0:T(8,128)(2,1)S(1)}, u32[]{:S(2)}, u32[]{:S(2)}) %collective-permute-start) | collective-permute-done | bytes 540704 | tf_op jit(solution)/shard_map/ppermute | solution.py:51
  18.8 1.8 collective-permute-start.1
  20.9 11.4 %collective-permute-done.1 = bf16[1,264,1024]{2,1,0:T(8,128)(2,1)S(1)} collective-permute-done((bf16[1,264,1024]{2,1,0:T(8,128)(2,1)S(1)}, bf16[1,264,1024]{2,1,0:T(8,128)(2,1)S(1)}, u32[]{:S(2)}, u32[]{:S(2)}) %collective-permute-start.1) | collective-permute-done | bytes 540704 | tf_op jit(solution)/shard_map/ppermute | solution.py:51
  32.3 1.5 collective-permute-start.2
  34.3 10.5 %collective-permute-done.2 = bf16[1,264,1024]{2,1,0:T(8,128)(2,1)S(1)} collective-permute-done((bf16[1,264,1024]{2,1,0:T(8,128)(2,1)S(1)}, bf16[1,264,1024]{2,1,0:T(8,128)(2,1)S(1)}, u32[]{:S(2)}, u32[]{:S(2)}) %collective-permute-start.2) | collective-permute-done | bytes 540704 | tf_op jit(solution)/shard_map/ppermute | solution.py:51
  44.8 1.4 collective-permute-start.3
  46.9 9.6 %collective-permute-done.3 = bf16[1,264,1024]{2,1,0:T(8,128)(2,1)S(1)} collective-permute-done((bf16[1,264,1024]{2,1,0:T(8,128)(2,1)S(1)}, bf16[1,264,1024]{2,1,0:T(8,128)(2,1)S(1)}, u32[]{:S(2)}, u32[]{:S(2)}) %collective-permute-start.3) | collective-permute-done | bytes 540704 | tf_op jit(solution)/shard_map/ppermute | solution.py:51
  63.2 1.2 collective-permute-start.14
  64.4 10.9 %collective-permute-done.14 = bf16[256,1024]{1,0:T(8,128)(2,1)} collective-permute-done((bf16[256,1024]{1,0:T(8,128)(2,1)}, bf16[256,1024]{1,0:T(8,128)(2,1)}, u32[]{:S(2)}, u32[]{:S(2)}) %collective-permute-start.14) | collective-permute-done | bytes 524320 | tf_op jit(solution)/shard_map/ppermute | solution.py:51
  75.3 1.2 collective-permute-start.15
  76.5 1.6 collective-permute-start.28
  78.0 4.6 %slice.94 = bf16[8,256,1024]{2,1,0:T(8,128)(2,1)} slice(bf16[8,264,1024]{2,1,0:T(8,128)(2,1)} %constant_dynamic-update-slice_fusion), slice={[0:8], [0:256], [0:1024]} | slice | bytes 8388608 | tf_op jit(solution)/shard_map/slice | solution.py:126
  83.1 0.9 slice_bitcast_fusion
  85.1 1.5 collective-permute-start.16
  86.6 5.8 %fusion.23 = f32[2048,2,384]{2,0,1:T(8,128)S(1)} fusion(bf16[2048,1024,1]{1,0,2:T(8,128)(2,1)} %bitcast.107, bf16[1,2,1024,384]{3,2,1,0:T(8,128)(2,1)} %param.15), kind=kOutput, calls=%fused_computation.38 | convolution fusion | flops 3221225472 | bytes 12058624 | tf_op jit(solution)/shard_map/td,edh->eth/dot_general | solution.py:147
  92.4 4.6 %collective-permute-done.18 = bf16[256,1024]{1,0:T(8,128)(2,1)} collective-permute-done((bf16[256,1024]{1,0:T(8,128)(2,1)}, bf16[256,1024]{1,0:T(8,128)(2,1)}, u32[]{:S(2)}, u32[]{:S(2)}) %collective-permute-start.18) | collective-permute-done | bytes 524320 | tf_op jit(solution)/shard_map/ppermute | solution.py:55
  97.1 0.9 collective-permute-start.19
  97.9 1.6 collective-permute-done.16
  99.6 1.1 collective-permute-start.17
  100.7 5.3 %fusion.27 = f32[2048,2,384]{2,0,1:T(8,128)} fusion(bf16[2048,1024,1]{1,0,2:T(8,128)(2,1)S(1)} %bitcast.108, bf16[1,2,1024,384]{3,2,1,0:T(8,128)(2,1)S(1)} %copy-done), kind=kOutput, calls=%fused_computation.42 | convolution fusion | flops 3221225472 | bytes 12058624 | tf_op jit(solution)/shard_map/td,edh->eth/dot_general | solution.py:144
  106.0 4.6 %collective-permute-done.19 = bf16[256,1024]{1,0:T(8,128)(2,1)S(1)} collective-permute-done((bf16[256,1024]{1,0:T(8,128)(2,1)}, bf16[256,1024]{1,0:T(8,128)(2,1)S(1)}, u32[]{:S(2)}, u32[]{:S(2)}) %collective-permute-start.19) | collective-permute-done | bytes 524320 | tf_op jit(solution)/shard_map/ppermute | solution.py:55
  110.6 1.7 collective-permute-start.20
  113.2 1.1 constant_dynamic-update-slice_fusion.13
  114.3 1.1 constant_dynamic-update-slice_fusion.12
  115.4 1.1 constant_dynamic-update-slice_fusion.11
  116.5 1.1 constant_dynamic-update-slice_fusion.10
  117.6 6.0 %collective-permute-done.20 = bf16[256,1024]{1,0:T(8,128)(2,1)S(1)} collective-permute-done((bf16[256,1024]{1,0:T(8,128)(2,1)S(1)}, bf16[256,1024]{1,0:T(8,128)(2,1)S(1)}, u32[]{:S(2)}, u32[]{:S(2)}) %collective-permute-start.20) | collective-permute-done | bytes 524320 | tf_op jit(solution)/shard_map/ppermute | solution.py:55
  123.7 1.0 convert_element_type.67
  124.7 14.5 %multiply_convert_fusion.3 = (bf16[2,2048,384]{2,1,0:T(8,128)(2,1)}, bf16[2,2048,384]{2,1,0:T(8,128)(2,1)}, bf16[2,2048,384]{2,1,0:T(8,128)(2,1)}) fusion(f32[2048,2,384]{2,0,1:T(8,128)} %fusion.27, f32[2048,2,384]{2,0,1:T(8,128)S(1)} %fusion.23, bf16[1,2,384,1024]{3,2,1,0:T(8,128)(2,1)} %param.16, f32[2048,1024]{1,0:T(8,128)S(1)} %convert_element_type.67, ...), kind=kOutput, calls=%fused_computation.22 | convolution fusion | flops 3253207040 | bytes 31997952 | tf_op jit(solution)/shard_map/etd,ehd->eth/dot_general | solution.py:158
  139.2 8.4 %multiply_reduce_fusion = f32[2048,1024]{1,0:T(8,128)S(1)} fusion(f32[2,2048]{1,0:T(2,128)S(1)} %copy.33, bf16[2,2048,384]{2,1,0:T(8,128)(2,1)} %get-tuple-element.32, bf16[1,2,384,1024]{3,2,1,0:T(8,128)(2,1)} %param.16), kind=kOutput, calls=%fused_computation.2 | convolution fusion | flops 3231711232 | bytes 13123584 | tf_op jit(solution)/shard_map/eth,ehd->etd/dot_general | solution.py:154
  147.6 1.1 slice.96
  148.7 1.7 collective-permute-start.7
  150.5 10.3 %fusion.25 = f32[2,2048,1024]{2,1,0:T(8,128)} fusion(bf16[2,2048,384]{2,1,0:T(8,128)(2,1)} %get-tuple-element.31, bf16[1,2,1024,384]{3,2,1,0:T(8,128)(2,1)S(1)} %copy-done), kind=kOutput, calls=%fused_computation.40 | convolution fusion | flops 3221225472 | bytes 21495808 | tf_op jit(solution)/shard_map/eth,edh->etd/dot_general | solution.py:175
  160.8 16.4 %reduce-precision_reduce_fusion = f32[2048,1024]{1,0:T(8,128)} fusion(f32[2,2048,1024]{2,1,0:T(8,128)} %fusion.25, bf16[2,2048,384]{2,1,0:T(8,128)(2,1)} %get-tuple-element.30, bf16[1,2,1024,384]{3,2,1,0:T(8,128)(2,1)} %param.15), kind=kOutput, calls=%fused_computation | convolution fusion | flops 3231711232 | bytes 29884416 | tf_op jit(solution)/shard_map/eth,edh->etd/dot_general | solution.py:176
  177.1 1.3 slice.104
  178.5 1.6 collective-permute-start.21
  180.8 1.8 slice_add_fusion.10
  182.6 1.6 collective-permute-start.8
  184.7 19.9 %collective-permute-done.21 = f32[256,1024]{1,0:T(8,128)S(1)} collective-permute-done((f32[256,1024]{1,0:T(8,128)S(1)}, f32[256,1024]{1,0:T(8,128)S(1)}, u32[]{:S(2)}, u32[]{:S(2)}) %collective-permute-start.21) | collective-permute-done | bytes 1048608 | tf_op jit(solution)/shard_map/ppermute | solution.py:73
  204.6 1.8 slice_add_fusion.4
  206.4 1.6 collective-permute-start.22
  208.7 13.2 %fusion.37 = (f32[1,2,384,1024]{3,2,1,0:T(8,128)}, bf16[1,2,384,1024]{3,2,1,0:T(8,128)(2,1)}, f32[1,2,384,1024]{3,2,1,0:T(8,128)}) fusion(f32[1,2,384,1024]{3,2,1,0:T(8,128)} %param.18, f32[1,2,384,1024]{3,2,1,0:T(8,128)} %param.17, bf16[1,2,384,1024]{3,2,1,0:T(8,128)(2,1)} %collective-permute-done.28, ...), kind=kOutput, calls=%fused_computation.65 | convolution fusion | flops 3246129152 | bytes 30425088 | tf_op jit(solution)/shard_map/eth,etd->ehd/dot_general | solution.py:165
  221.9 5.3 %collective-permute-done.8 = f32[256,1024]{1,0:T(8,128)} collective-permute-done((f32[256,1024]{1,0:T(8,128)S(1)}, f32[256,1024]{1,0:T(8,128)}, u32[]{:S(2)}, u32[]{:S(2)}) %collective-permute-start.8) | collective-permute-done | bytes 1048608 | tf_op jit(solution)/shard_map/ppermute | solution.py:73
  227.2 4.3 %slice_add_fusion.9 = (f32[256,1024]{1,0:T(8,128)}, f32[256,1024]{1,0:T(8,128)}) fusion(f32[256,1024]{1,0:T(8,128)} %collective-permute-done.8, f32[2048,1024]{1,0:T(8,128)} %copy-done.2, f32[256,1024]{1,0:T(8,128)} %collective-permute-done.11), kind=kLoop, calls=%fused_computation.58 | loop fusion | flops 524288 | bytes 6291456 | tf_op jit(solution)/shard_map/add | solution.py:75
  231.5 1.6 collective-permute-start.9
  233.5 16.1 %collective-permute-done.22 = f32[256,1024]{1,0:T(8,128)S(1)} collective-permute-done((f32[256,1024]{1,0:T(8,128)S(1)}, f32[256,1024]{1,0:T(8,128)S(1)}, u32[]{:S(2)}, u32[]{:S(2)}) %collective-permute-start.22) | collective-permute-done | bytes 1048608 | tf_op jit(solution)/shard_map/ppermute | solution.py:73
  249.6 3.6 %slice_add_fusion.3 = (f32[256,1024]{1,0:T(8,128)}, f32[256,1024]{1,0:T(8,128)}) fusion(f32[256,1024]{1,0:T(8,128)S(1)} %collective-permute-done.22, f32[2048,1024]{1,0:T(8,128)} %reduce-precision_reduce_fusion, f32[256,1024]{1,0:T(8,128)} %collective-permute-done.25), kind=kLoop, calls=%fused_computation.50 | loop fusion | flops 524288 | bytes 6291456 | tf_op jit(solution)/shard_map/add | solution.py:75
  253.2 1.6 collective-permute-start.23
  255.2 3.6 %fusion.30 = bf16[1,2,1024,384]{2,3,1,0:T(8,128)(2,1)S(1)} fusion(bf16[2,2048,384]{2,1,0:T(8,128)(2,1)S(1)} %copy-done.8, bf16[2048,1024,1]{1,0,2:T(8,128)(2,1)S(1)} %bitcast.109), kind=kOutput, calls=%fused_computation.45 | convolution fusion | flops 3222011904 | bytes 8912896 | tf_op jit(solution)/shard_map/td,eth->edh/dot_general | solution.py:168
  258.8 1.6 copy.37
  260.3 11.8 %collective-permute-done.9 = f32[256,1024]{1,0:T(8,128)} collective-permute-done((f32[256,1024]{1,0:T(8,128)}, f32[256,1024]{1,0:T(8,128)}, u32[]{:S(2)}, u32[]{:S(2)}) %collective-permute-start.9) | collective-permute-done | bytes 1048608 | tf_op jit(solution)/shard_map/ppermute | solution.py:73
  272.1 4.2 %slice_add_fusion.8 = (f32[256,1024]{1,0:T(8,128)}, f32[256,1024]{1,0:T(8,128)}) fusion(f32[256,1024]{1,0:T(8,128)} %collective-permute-done.9, f32[2048,1024]{1,0:T(8,128)} %copy-done.2, f32[256,1024]{1,0:T(8,128)} %collective-permute-done.12), kind=kLoop, calls=%fused_computation.57 | loop fusion | flops 524288 | bytes 6291456 | tf_op jit(solution)/shard_map/add | solution.py:75
  276.3 1.6 collective-permute-start.10
  278.4 16.1 %collective-permute-done.23 = f32[256,1024]{1,0:T(8,128)S(1)} collective-permute-done((f32[256,1024]{1,0:T(8,128)}, f32[256,1024]{1,0:T(8,128)S(1)}, u32[]{:S(2)}, u32[]{:S(2)}) %collective-permute-start.23) | collective-permute-done | bytes 1048608 | tf_op jit(solution)/shard_map/ppermute | solution.py:73
  294.5 3.6 %slice_add_fusion.2 = (f32[256,1024]{1,0:T(8,128)}, f32[256,1024]{1,0:T(8,128)}) fusion(f32[256,1024]{1,0:T(8,128)S(1)} %collective-permute-done.23, f32[2048,1024]{1,0:T(8,128)} %reduce-precision_reduce_fusion, f32[256,1024]{1,0:T(8,128)} %collective-permute-done.26), kind=kLoop, calls=%fused_computation.49 | loop fusion | flops 524288 | bytes 6291456 | tf_op jit(solution)/shard_map/add | solution.py:75
  298.1 1.6 collective-permute-start.24
  300.4 3.6 %fusion.31 = bf16[1,2,1024,384]{2,3,1,0:T(8,128)(2,1)S(1)} fusion(bf16[2,2048,384]{2,1,0:T(8,128)(2,1)S(1)} %copy-done.7, bf16[2048,1024,1]{1,0,2:T(8,128)(2,1)S(1)} %bitcast.110), kind=kOutput, calls=%fused_computation.46 | convolution fusion | flops 3222011904 | bytes 8912896 | tf_op jit(solution)/shard_map/td,eth->edh/dot_general | solution.py:171
  303.9 1.6 copy.38
  305.5 11.6 %collective-permute-done.10 = f32[256,1024]{1,0:T(8,128)} collective-permute-done((f32[256,1024]{1,0:T(8,128)}, f32[256,1024]{1,0:T(8,128)}, u32[]{:S(2)}, u32[]{:S(2)}) %collective-permute-start.10) | collective-permute-done | bytes 1048608 | tf_op jit(solution)/shard_map/ppermute | solution.py:73
  317.1 2.9 fusion.35
  320.0 16.8 %collective-permute-done.24 = f32[256,1024]{1,0:T(8,128)} collective-permute-done((f32[256,1024]{1,0:T(8,128)}, f32[256,1024]{1,0:T(8,128)}, u32[]{:S(2)}, u32[]{:S(2)}) %collective-permute-start.24) | collective-permute-done | bytes 1048608 | tf_op jit(solution)/shard_map/ppermute | solution.py:73
  336.8 2.9 fusion.33
  (68 shorter events, 15.6 us)
Async XLA Ops:
  0.6 100.1 %copy-start = (bf16[1,2,1024,384]{3,2,1,0:T(8,128)(2,1)S(1)}, bf16[1,2,1024,384]{3,2,1,0:T(8,128)(2,1)}, u32[]{:S(2)}) copy-start(bf16[1,2,1024,384]{3,2,1,0:T(8,128)(2,1)} %param.14) | copy-start | bytes 4718596
  0.6 59.2 %copy-start.9 = (bf16[256,1024]{1,0:T(8,128)(2,1)S(1)}, bf16[256,1024]{1,0:T(8,128)(2,1)}, u32[]{:S(2)}) copy-start(bf16[256,1024]{1,0:T(8,128)(2,1)} %param.10) | copy-start | bytes 1572868
  3.6 15.3 %collective-permute-start = (bf16[1,264,1024]{2,1,0:T(8,128)(2,1)S(1)}, bf16[1,264,1024]{2,1,0:T(8,128)(2,1)S(1)}, u32[]{:S(2)}, u32[]{:S(2)}) collective-permute-start(bf16[1,264,1024]{2,1,0:T(8,128)(2,1)S(1)} %maximum_bitcast_fusion), channel_id=1, source_target_pairs={{0,2},{2,4},{4,6},{6,7},{7,5},{5,3},{3,1},{1,0},{8,10},{10,12},{12... | collective-permute-start | bytes 1622024 | tf_op jit(solution)/shard_map/ppermute | solution.py:51
  18.8 13.5 %collective-permute-start.1 = (bf16[1,264,1024]{2,1,0:T(8,128)(2,1)S(1)}, bf16[1,264,1024]{2,1,0:T(8,128)(2,1)S(1)}, u32[]{:S(2)}, u32[]{:S(2)}) collective-permute-start(bf16[1,264,1024]{2,1,0:T(8,128)(2,1)S(1)} %collective-permute-done), channel_id=1, source_target_pairs={{0,2},{2,4},{4,6},{6,7},{7,5},{5,3},{3,1},{1,0},{8,10},{10,12},{12... | collective-permute-start | bytes 1622024 | tf_op jit(solution)/shard_map/ppermute | solution.py:51
  20.7 13.1 %collective-permute-start.4 = (bf16[1,264,1024]{2,1,0:T(8,128)(2,1)S(1)}, bf16[1,264,1024]{2,1,0:T(8,128)(2,1)S(1)}, u32[]{:S(2)}, u32[]{:S(2)}) collective-permute-start(bf16[1,264,1024]{2,1,0:T(8,128)(2,1)S(1)} %maximum_bitcast_fusion), channel_id=1, source_target_pairs={{0,1},{2,0},{4,2},{6,4},{7,6},{5,7},{3,5},{1,3},{8,9},{10,8},{12,1... | collective-permute-start | bytes 1622024 | tf_op jit(solution)/shard_map/ppermute | solution.py:55
  32.3 12.5 %collective-permute-start.2 = (bf16[1,264,1024]{2,1,0:T(8,128)(2,1)S(1)}, bf16[1,264,1024]{2,1,0:T(8,128)(2,1)S(1)}, u32[]{:S(2)}, u32[]{:S(2)}) collective-permute-start(bf16[1,264,1024]{2,1,0:T(8,128)(2,1)S(1)} %collective-permute-done.1), channel_id=1, source_target_pairs={{0,2},{2,4},{4,6},{6,7},{7,5},{5,3},{3,1},{1,0},{8,10},{10,12},{12... | collective-permute-start | bytes 1622024 | tf_op jit(solution)/shard_map/ppermute | solution.py:51
  33.8 12.4 %collective-permute-start.5 = (bf16[1,264,1024]{2,1,0:T(8,128)(2,1)S(1)}, bf16[1,264,1024]{2,1,0:T(8,128)(2,1)S(1)}, u32[]{:S(2)}, u32[]{:S(2)}) collective-permute-start(bf16[1,264,1024]{2,1,0:T(8,128)(2,1)S(1)} %collective-permute-done.4), channel_id=1, source_target_pairs={{0,1},{2,0},{4,2},{6,4},{7,6},{5,7},{3,5},{1,3},{8,9},{10,8},{12,1... | collective-permute-start | bytes 1622024 | tf_op jit(solution)/shard_map/ppermute | solution.py:55
  44.8 11.6 %collective-permute-start.3 = (bf16[1,264,1024]{2,1,0:T(8,128)(2,1)S(1)}, bf16[1,264,1024]{2,1,0:T(8,128)(2,1)S(1)}, u32[]{:S(2)}, u32[]{:S(2)}) collective-permute-start(bf16[1,264,1024]{2,1,0:T(8,128)(2,1)S(1)} %collective-permute-done.2), channel_id=1, source_target_pairs={{0,2},{2,4},{4,6},{6,7},{7,5},{5,3},{3,1},{1,0},{8,10},{10,12},{12... | collective-permute-start | bytes 1622024 | tf_op jit(solution)/shard_map/ppermute | solution.py:51
  46.2 16.1 %collective-permute-start.6 = (bf16[1,264,1024]{2,1,0:T(8,128)(2,1)S(1)}, bf16[1,264,1024]{2,1,0:T(8,128)(2,1)S(1)}, u32[]{:S(2)}, u32[]{:S(2)}) collective-permute-start(bf16[1,264,1024]{2,1,0:T(8,128)(2,1)S(1)} %collective-permute-done.5), channel_id=1, source_target_pairs={{0,1},{2,0},{4,2},{6,4},{7,6},{5,7},{3,5},{1,3},{8,9},{10,8},{12,1... | collective-permute-start | bytes 1622024 | tf_op jit(solution)/shard_map/ppermute | solution.py:55
  63.2 12.1 %collective-permute-start.14 = (bf16[256,1024]{1,0:T(8,128)(2,1)}, bf16[256,1024]{1,0:T(8,128)(2,1)}, u32[]{:S(2)}, u32[]{:S(2)}) collective-permute-start(bf16[256,1024]{1,0:T(8,128)(2,1)} %param.11), channel_id=1, source_target_pairs={{0,2},{2,4},{4,6},{6,7},{7,5},{5,3},{3,1},{1,0},{8,10},{10,12},{12... | collective-permute-start | bytes 1572872 | tf_op jit(solution)/shard_map/ppermute | solution.py:51
  75.3 9.8 %collective-permute-start.15 = (bf16[256,1024]{1,0:T(8,128)(2,1)}, bf16[256,1024]{1,0:T(8,128)(2,1)}, u32[]{:S(2)}, u32[]{:S(2)}) collective-permute-start(bf16[256,1024]{1,0:T(8,128)(2,1)} %collective-permute-done.14), channel_id=1, source_target_pairs={{0,2},{2,4},{4,6},{6,7},{7,5},{5,3},{3,1},{1,0},{8,10},{10,12},{12... | collective-permute-start | bytes 1572872 | tf_op jit(solution)/shard_map/ppermute | solution.py:51
  76.5 131.6 %collective-permute-start.29 = (bf16[1,2,384,1024]{3,2,1,0:T(8,128)(2,1)}, bf16[1,2,384,1024]{3,2,1,0:T(8,128)(2,1)}, u32[]{:S(2)}, u32[]{:S(2)}) collective-permute-start(bf16[1,2,384,1024]{3,2,1,0:T(8,128)(2,1)} %param.16), channel_id=1, source_target_pairs={{0,8},{8,16},{16,24},{24,0},{1,9},{9,17},{17,25},{25,1},{2,10},{10... | collective-permute-start | bytes 4718600 | tf_op jit(solution)/shard_map/ppermute | solution.py:21
  76.5 132.2 %collective-permute-start.28 = (bf16[1,2,384,1024]{3,2,1,0:T(8,128)(2,1)}, bf16[1,2,384,1024]{3,2,1,0:T(8,128)(2,1)}, u32[]{:S(2)}, u32[]{:S(2)}) collective-permute-start(bf16[1,2,384,1024]{3,2,1,0:T(8,128)(2,1)} %param.16), channel_id=1, source_target_pairs={{0,16},{8,24},{16,0},{24,8},{1,17},{9,25},{17,1},{25,9},{2,18},{10... | collective-permute-start | bytes 4718600 | tf_op jit(solution)/shard_map/ppermute | solution.py:21
  82.6 14.5 %collective-permute-start.18 = (bf16[256,1024]{1,0:T(8,128)(2,1)}, bf16[256,1024]{1,0:T(8,128)(2,1)}, u32[]{:S(2)}, u32[]{:S(2)}) collective-permute-start(bf16[256,1024]{1,0:T(8,128)(2,1)} %param.11), channel_id=1, source_target_pairs={{0,1},{2,0},{4,2},{6,4},{7,6},{5,7},{3,5},{1,3},{8,9},{10,8},{12,1... | collective-permute-start | bytes 1572872 | tf_op jit(solution)/shard_map/ppermute | solution.py:55
  85.1 14.5 %collective-permute-start.16 = (bf16[256,1024]{1,0:T(8,128)(2,1)}, bf16[256,1024]{1,0:T(8,128)(2,1)S(1)}, u32[]{:S(2)}, u32[]{:S(2)}) collective-permute-start(bf16[256,1024]{1,0:T(8,128)(2,1)} %collective-permute-done.15), channel_id=1, source_target_pairs={{0,2},{2,4},{4,6},{6,7},{7,5},{5,3},{3,1},{1,0},{8,10},{10,12},{12... | collective-permute-start | bytes 1572872 | tf_op jit(solution)/shard_map/ppermute | solution.py:51
  86.6 14.1 %copy-start.4 = (bf16[8,256,1024]{2,1,0:T(8,128)(2,1)S(1)}, bf16[8,256,1024]{2,1,0:T(8,128)(2,1)}, u32[]{:S(2)}) copy-start(bf16[8,256,1024]{2,1,0:T(8,128)(2,1)} %slice.94) | copy-start | bytes 12582916
  97.1 13.5 %collective-permute-start.19 = (bf16[256,1024]{1,0:T(8,128)(2,1)}, bf16[256,1024]{1,0:T(8,128)(2,1)S(1)}, u32[]{:S(2)}, u32[]{:S(2)}) collective-permute-start(bf16[256,1024]{1,0:T(8,128)(2,1)} %collective-permute-done.18), channel_id=1, source_target_pairs={{0,1},{2,0},{4,2},{6,4},{7,6},{5,7},{3,5},{1,3},{8,9},{10,8},{12,1... | collective-permute-start | bytes 1572872 | tf_op jit(solution)/shard_map/ppermute | solution.py:55
  99.6 13.6 %collective-permute-start.17 = (bf16[256,1024]{1,0:T(8,128)(2,1)S(1)}, bf16[256,1024]{1,0:T(8,128)(2,1)S(1)}, u32[]{:S(2)}, u32[]{:S(2)}) collective-permute-start(bf16[256,1024]{1,0:T(8,128)(2,1)S(1)} %collective-permute-done.16), channel_id=1, source_target_pairs={{0,2},{2,4},{4,6},{6,7},{7,5},{5,3},{3,1},{1,0},{8,10},{10,12},{12... | collective-permute-start | bytes 1572872 | tf_op jit(solution)/shard_map/ppermute | solution.py:51
  110.6 13.0 %collective-permute-start.20 = (bf16[256,1024]{1,0:T(8,128)(2,1)S(1)}, bf16[256,1024]{1,0:T(8,128)(2,1)S(1)}, u32[]{:S(2)}, u32[]{:S(2)}) collective-permute-start(bf16[256,1024]{1,0:T(8,128)(2,1)S(1)} %collective-permute-done.19), channel_id=1, source_target_pairs={{0,1},{2,0},{4,2},{6,4},{7,6},{5,7},{3,5},{1,3},{8,9},{10,8},{12,1... | collective-permute-start | bytes 1572872 | tf_op jit(solution)/shard_map/ppermute | solution.py:55
  124.7 14.5 %copy-start.3 = (f32[2048,1024]{1,0:T(8,128)}, f32[2048,1024]{1,0:T(8,128)S(1)}, u32[]{:S(2)}) copy-start(f32[2048,1024]{1,0:T(8,128)S(1)} %convert_element_type.67) | copy-start | bytes 25165828
  147.6 13.2 %copy-start.2 = (f32[2048,1024]{1,0:T(8,128)}, f32[2048,1024]{1,0:T(8,128)S(1)}, u32[]{:S(2)}) copy-start(f32[2048,1024]{1,0:T(8,128)S(1)} %multiply_reduce_fusion) | copy-start | bytes 25165828
  148.7 32.0 %collective-permute-start.7 = (f32[256,1024]{1,0:T(8,128)}, f32[256,1024]{1,0:T(8,128)S(1)}, u32[]{:S(2)}, u32[]{:S(2)}) collective-permute-start(f32[256,1024]{1,0:T(8,128)} %slice.96), channel_id=1, source_target_pairs={{0,2},{2,4},{4,6},{6,7},{7,5},{5,3},{3,1},{1,0},{8,10},{10,12},{12... | collective-permute-start | bytes 3145736 | tf_op jit(solution)/shard_map/ppermute | solution.py:73
  178.5 26.1 %collective-permute-start.21 = (f32[256,1024]{1,0:T(8,128)S(1)}, f32[256,1024]{1,0:T(8,128)S(1)}, u32[]{:S(2)}, u32[]{:S(2)}) collective-permute-start(f32[256,1024]{1,0:T(8,128)S(1)} %slice.104), channel_id=1, source_target_pairs={{0,2},{2,4},{4,6},{6,7},{7,5},{5,3},{3,1},{1,0},{8,10},{10,12},{12... | collective-permute-start | bytes 3145736 | tf_op jit(solution)/shard_map/ppermute | solution.py:73
  182.6 44.6 %collective-permute-start.8 = (f32[256,1024]{1,0:T(8,128)S(1)}, f32[256,1024]{1,0:T(8,128)}, u32[]{:S(2)}, u32[]{:S(2)}) collective-permute-start(f32[256,1024]{1,0:T(8,128)S(1)} %get-tuple-element.43), channel_id=1, source_target_pairs={{0,2},{2,4},{4,6},{6,7},{7,5},{5,3},{3,1},{1,0},{8,10},{10,12},{12... | collective-permute-start | bytes 3145736 | tf_op jit(solution)/shard_map/ppermute | solution.py:73
  184.2 43.0 %collective-permute-start.11 = (f32[256,1024]{1,0:T(8,128)S(1)}, f32[256,1024]{1,0:T(8,128)}, u32[]{:S(2)}, u32[]{:S(2)}) collective-permute-start(f32[256,1024]{1,0:T(8,128)S(1)} %get-tuple-element.44), channel_id=1, source_target_pairs={{0,1},{2,0},{4,2},{6,4},{7,6},{5,7},{3,5},{1,3},{8,9},{10,8},{12,1... | collective-permute-start | bytes 3145736 | tf_op jit(solution)/shard_map/ppermute | solution.py:80
  206.4 43.2 %collective-permute-start.22 = (f32[256,1024]{1,0:T(8,128)S(1)}, f32[256,1024]{1,0:T(8,128)S(1)}, u32[]{:S(2)}, u32[]{:S(2)}) collective-permute-start(f32[256,1024]{1,0:T(8,128)S(1)} %get-tuple-element.37), channel_id=1, source_target_pairs={{0,2},{2,4},{4,6},{6,7},{7,5},{5,3},{3,1},{1,0},{8,10},{10,12},{12... | collective-permute-start | bytes 3145736 | tf_op jit(solution)/shard_map/ppermute | solution.py:73
  208.0 41.5 %collective-permute-start.25 = (f32[256,1024]{1,0:T(8,128)S(1)}, f32[256,1024]{1,0:T(8,128)}, u32[]{:S(2)}, u32[]{:S(2)}) collective-permute-start(f32[256,1024]{1,0:T(8,128)S(1)} %get-tuple-element.38), channel_id=1, source_target_pairs={{0,1},{2,0},{4,2},{6,4},{7,6},{5,7},{3,5},{1,3},{8,9},{10,8},{12,1... | collective-permute-start | bytes 3145736 | tf_op jit(solution)/shard_map/ppermute | solution.py:80
  227.2 28.0 %copy-start.8 = (bf16[2,2048,384]{2,1,0:T(8,128)(2,1)S(1)}, bf16[2,2048,384]{2,1,0:T(8,128)(2,1)}, u32[]{:S(2)}) copy-start(bf16[2,2048,384]{2,1,0:T(8,128)(2,1)} %get-tuple-element.31) | copy-start | bytes 9437188
  231.5 23.8 %copy-start.5 = (bf16[8,256,1024]{2,1,0:T(8,128)(2,1)S(1)}, bf16[8,256,1024]{2,1,0:T(8,128)(2,1)}, u32[]{:S(2)}) copy-start(bf16[8,256,1024]{2,1,0:T(8,128)(2,1)} %slice.94) | copy-start | bytes 12582916
  231.5 40.7 %collective-permute-start.9 = (f32[256,1024]{1,0:T(8,128)}, f32[256,1024]{1,0:T(8,128)}, u32[]{:S(2)}, u32[]{:S(2)}) collective-permute-start(f32[256,1024]{1,0:T(8,128)} %get-tuple-element.41), channel_id=1, source_target_pairs={{0,2},{2,4},{4,6},{6,7},{7,5},{5,3},{3,1},{1,0},{8,10},{10,12},{12... | collective-permute-start | bytes 3145736 | tf_op jit(solution)/shard_map/ppermute | solution.py:73
  233.0 39.1 %collective-permute-start.12 = (f32[256,1024]{1,0:T(8,128)}, f32[256,1024]{1,0:T(8,128)}, u32[]{:S(2)}, u32[]{:S(2)}) collective-permute-start(f32[256,1024]{1,0:T(8,128)} %get-tuple-element.42), channel_id=1, source_target_pairs={{0,1},{2,0},{4,2},{6,4},{7,6},{5,7},{3,5},{1,3},{8,9},{10,8},{12,1... | collective-permute-start | bytes 3145736 | tf_op jit(solution)/shard_map/ppermute | solution.py:80
  253.2 41.3 %collective-permute-start.23 = (f32[256,1024]{1,0:T(8,128)}, f32[256,1024]{1,0:T(8,128)S(1)}, u32[]{:S(2)}, u32[]{:S(2)}) collective-permute-start(f32[256,1024]{1,0:T(8,128)} %get-tuple-element.35), channel_id=1, source_target_pairs={{0,2},{2,4},{4,6},{6,7},{7,5},{5,3},{3,1},{1,0},{8,10},{10,12},{12... | collective-permute-start | bytes 3145736 | tf_op jit(solution)/shard_map/ppermute | solution.py:73
  254.8 39.7 %collective-permute-start.26 = (f32[256,1024]{1,0:T(8,128)}, f32[256,1024]{1,0:T(8,128)}, u32[]{:S(2)}, u32[]{:S(2)}) collective-permute-start(f32[256,1024]{1,0:T(8,128)} %get-tuple-element.36), channel_id=1, source_target_pairs={{0,1},{2,0},{4,2},{6,4},{7,6},{5,7},{3,5},{1,3},{8,9},{10,8},{12,1... | collective-permute-start | bytes 3145736 | tf_op jit(solution)/shard_map/ppermute | solution.py:80
  272.1 28.2 %copy-start.7 = (bf16[2,2048,384]{2,1,0:T(8,128)(2,1)S(1)}, bf16[2,2048,384]{2,1,0:T(8,128)(2,1)}, u32[]{:S(2)}) copy-start(bf16[2,2048,384]{2,1,0:T(8,128)(2,1)} %get-tuple-element.30) | copy-start | bytes 9437188
  276.3 24.0 %copy-start.6 = (bf16[8,256,1024]{2,1,0:T(8,128)(2,1)S(1)}, bf16[8,256,1024]{2,1,0:T(8,128)(2,1)}, u32[]{:S(2)}) copy-start(bf16[8,256,1024]{2,1,0:T(8,128)(2,1)} %slice.94) | copy-start | bytes 12582916
  276.3 40.7 %collective-permute-start.10 = (f32[256,1024]{1,0:T(8,128)}, f32[256,1024]{1,0:T(8,128)}, u32[]{:S(2)}, u32[]{:S(2)}) collective-permute-start(f32[256,1024]{1,0:T(8,128)} %get-tuple-element.39), channel_id=1, source_target_pairs={{0,2},{2,4},{4,6},{6,7},{7,5},{5,3},{3,1},{1,0},{8,10},{10,12},{12... | collective-permute-start | bytes 3145736 | tf_op jit(solution)/shard_map/ppermute | solution.py:73
  277.9 39.2 %collective-permute-start.13 = (f32[256,1024]{1,0:T(8,128)}, f32[256,1024]{1,0:T(8,128)}, u32[]{:S(2)}, u32[]{:S(2)}) collective-permute-start(f32[256,1024]{1,0:T(8,128)} %get-tuple-element.40), channel_id=1, source_target_pairs={{0,1},{2,0},{4,2},{6,4},{7,6},{5,7},{3,5},{1,3},{8,9},{10,8},{12,1... | collective-permute-start | bytes 3145736 | tf_op jit(solution)/shard_map/ppermute | solution.py:80
  298.1 38.7 %collective-permute-start.24 = (f32[256,1024]{1,0:T(8,128)}, f32[256,1024]{1,0:T(8,128)}, u32[]{:S(2)}, u32[]{:S(2)}) collective-permute-start(f32[256,1024]{1,0:T(8,128)} %get-tuple-element.33), channel_id=1, source_target_pairs={{0,2},{2,4},{4,6},{6,7},{7,5},{5,3},{3,1},{1,0},{8,10},{10,12},{12... | collective-permute-start | bytes 3145736 | tf_op jit(solution)/shard_map/ppermute | solution.py:73
  299.7 37.1 %collective-permute-start.27 = (f32[256,1024]{1,0:T(8,128)}, f32[256,1024]{1,0:T(8,128)}, u32[]{:S(2)}, u32[]{:S(2)}) collective-permute-start(f32[256,1024]{1,0:T(8,128)} %get-tuple-element.34), channel_id=1, source_target_pairs={{0,1},{2,0},{4,2},{6,4},{7,6},{5,7},{3,5},{1,3},{8,9},{10,8},{12,1... | collective-permute-start | bytes 3145736 | tf_op jit(solution)/shard_map/ppermute | solution.py:80
  303.9 35.7 %copy-start.1 = (bf16[1,2,1024,384]{3,2,1,0:T(8,128)(2,1)S(1)}, bf16[1,2,1024,384]{3,2,1,0:T(8,128)(2,1)}, u32[]{:S(2)}) copy-start(bf16[1,2,1024,384]{3,2,1,0:T(8,128)(2,1)} %param.14) | copy-start | bytes 4718596

commit v4 on v3

--- a/solution.py
+++ b/solution.py
@@ -41,19 +41,35 @@
     return [(ring[q], ring[(q + step) % size]) for q in range(size)]
 
 
+def paired_shift(ahead_value, behind_value, axis, ring):
+    if behind_value is None:
+        return lax.ppermute(ahead_value, axis, ring_pairs(ring, 1)), None
+    if ahead_value is None:
+        return None, lax.ppermute(behind_value, axis, ring_pairs(ring, -1))
+    ahead_value, behind_value = lax.optimization_barrier((ahead_value, behind_value))
+    ahead_value = lax.ppermute(ahead_value, axis, ring_pairs(ring, 1))
+    behind_value = lax.ppermute(behind_value, axis, ring_pairs(ring, -1))
+    return lax.optimization_barrier((ahead_value, behind_value))
+
+
 def ring_all_gather(shard, axis, ring):
     size = len(ring)
     ahead = size // 2
     behind = size - 1 - ahead
     got = {0: shard}
-    current = shard
-    for step in range(ahead):
-        current = lax.ppermute(current, axis, ring_pairs(ring, 1))
-        got[-(step + 1)] = current
-    current = shard
-    for step in range(behind):
-        current = lax.ppermute(current, axis, ring_pairs(ring, -1))
-        got[step + 1] = current
+    ahead_value = shard
+    behind_value = shard
+    for step in range(max(ahead, behind)):
+        ahead_value, behind_value = paired_shift(
+            ahead_value if step < ahead else None,
+            behind_value if step < behind else None,
+            axis,
+            ring,
+        )
+        if step < ahead:
+            got[-(step + 1)] = ahead_value
+        if step < behind:
+            got[step + 1] = behind_value
     return jnp.concatenate([got[offset] for offset in range(-ahead, behind + 1)])
 
 
@@ -67,20 +83,23 @@
         return blocks[(offset + ahead) % size]
 
     result = block_at(0)
-    if ahead:
-        send = block_at(ahead)
-        for step in range(ahead):
-            received = lax.ppermute(send, axis, ring_pairs(ring, 1))
-            if step < ahead - 1:
-                send = received + block_at(ahead - step - 1)
-        result = result + received
-    if behind:
-        send = block_at(-behind)
-        for step in range(behind):
-            received = lax.ppermute(send, axis, ring_pairs(ring, -1))
-            if step < behind - 1:
-                send = received + block_at(-behind + step + 1)
-        result = result + received
+    ahead_value = block_at(ahead) if ahead else None
+    behind_value = block_at(-behind) if behind else None
+    for step in range(max(ahead, behind)):
+        ahead_value, behind_value = paired_shift(
+            ahead_value if step < ahead else None,
+            behind_value if step < behind else None,
+            axis,
+            ring,
+        )
+        if step < ahead - 1:
+            ahead_value = ahead_value + block_at(ahead - step - 1)
+        elif step == ahead - 1:
+            result = result + ahead_value
+        if step < behind - 1:
+            behind_value = behind_value + block_at(-behind + step + 1)
+        elif step == behind - 1:
+            result = result + behind_value
     return result
 
 

time: 346 us -> 342 us (0.988)
    unnamed x37 -> x45, local copies, waits for them, and re-layouts: 13.7 us -> 14.3 us
  transfers between devices with their start and end apart: 30 -> 30, of which waited for: 18 -> 23; matrix products, arithmetic and copies ran while one was open for 37% -> 36% of each run, Pallas kernels for 0% -> 0%
where the time goes in v4:
time: 342 us; the launch traced here: 337 us
  waiting for transfers between devices  170 us (50%)
  matrix products  80.8 us (24%)
  starting transfers between devices  31.8 us (9%)
  other arithmetic  29.2 us (9%)
  local copies, waits for them, and re-layouts  23.8 us (7%)
    ppermute x12, waiting for transfers between devices, paired_shift(): ahead_value = lax.ppermute(ahead_value, axis, ring_pairs(ring, 1))  106 us
    ppermute x4, waiting for transfers between devices, paired_shift(): return (lax.ppermute(ahead_value, axis, ring_pairs(ring, 1)), None)  44.4 us
    ppermute x12, waiting for transfers between devices, paired_shift(): behind_value = lax.ppermute(behind_value, axis, ring_pairs(ring, -1))  19.6 us
    ppermute x12, starting transfers between devices, paired_shift(): ahead_value = lax.ppermute(ahead_value, axis, ring_pairs(ring, 1))  17.9 us
    dot_general x1, matrix products, chunk_pass(): jnp.einsum('eth,edh->etd', up_cot, up_matrix, preferred_element_type=jnp....  16.4 us
    dot_general x1, matrix products, chunk_pass(): jnp.einsum('etd,ehd->eth', slot_cot, down_matrix, preferred_element_type=...  14.6 us
    unnamed x45, local copies, waits for them, and re-layouts  14.3 us
    dot_general x1, matrix products, chunk_pass(): jnp.einsum('eth,etd->ehd', hidden, slot_cot, preferred_element_type=jnp.f...  13.2 us
  transfers between devices with their start and end apart: 30, of which 23 were waited for; matrix products, arithmetic and copies ran while one was open for 36% of the time, Pallas kernels for 0%

profile of v4, /device:TPU:0, one launch (start us, length us, event | category | flops | bytes accessed | tf_op | source)
XLA Modules:
  0.0 337.4 jit_solution(43571048106554654)
XLA Ops:
  2.5 1.1 maximum_bitcast_fusion
  3.6 3.1 collective-permute-start
  6.7 12.2 %collective-permute-done = bf16[1,264,1024]{2,1,0:T(8,128)(2,1)S(1)} collective-permute-done((bf16[1,264,1024]{2,1,0:T(8,128)(2,1)S(1)}, bf16[1,264,1024]{2,1,0:T(8,128)(2,1)S(1)}, u32[]{:S(2)}, u32[]{:S(2)}) %collective-permute-start) | collective-permute-done | bytes 540704 | tf_op jit(solution)/shard_map/ppermute | solution.py:50
  18.8 1.5 collective-permute-done.1
  20.4 1.6 collective-permute-start.2
  22.4 10.8 %collective-permute-done.2 = bf16[1,264,1024]{2,1,0:T(8,128)(2,1)S(1)} collective-permute-done((bf16[1,264,1024]{2,1,0:T(8,128)(2,1)S(1)}, bf16[1,264,1024]{2,1,0:T(8,128)(2,1)S(1)}, u32[]{:S(2)}, u32[]{:S(2)}) %collective-permute-start.2) | collective-permute-done | bytes 540704 | tf_op jit(solution)/shard_map/ppermute | solution.py:50
  33.2 1.3 collective-permute-done.3
  34.5 1.6 collective-permute-start.4
  36.5 9.6 %collective-permute-done.4 = bf16[1,264,1024]{2,1,0:T(8,128)(2,1)S(1)} collective-permute-done((bf16[1,264,1024]{2,1,0:T(8,128)(2,1)S(1)}, bf16[1,264,1024]{2,1,0:T(8,128)(2,1)S(1)}, u32[]{:S(2)}, u32[]{:S(2)}) %collective-permute-start.4) | collective-permute-done | bytes 540704 | tf_op jit(solution)/shard_map/ppermute | solution.py:50
  46.1 1.3 collective-permute-done.5
  47.4 1.5 collective-permute-start.6
  48.9 8.9 %collective-permute-done.6 = bf16[1,264,1024]{2,1,0:T(8,128)(2,1)S(1)} collective-permute-done((bf16[1,264,1024]{2,1,0:T(8,128)(2,1)S(1)}, bf16[1,264,1024]{2,1,0:T(8,128)(2,1)S(1)}, u32[]{:S(2)}, u32[]{:S(2)}) %collective-permute-start.6) | collective-permute-done | bytes 540704 | tf_op jit(solution)/shard_map/ppermute | solution.py:46
  64.6 1.5 collective-permute-start.14
  66.6 8.2 %collective-permute-done.14 = bf16[256,1024]{1,0:T(8,128)(2,1)} collective-permute-done((bf16[256,1024]{1,0:T(8,128)(2,1)S(1)}, bf16[256,1024]{1,0:T(8,128)(2,1)}, u32[]{:S(2)}, u32[]{:S(2)}) %collective-permute-start.14) | collective-permute-done | bytes 524320 | tf_op jit(solution)/shard_map/ppermute | solution.py:50
  74.9 1.4 collective-permute-done.15
  76.2 2.9 collective-permute-start.16
  79.1 1.6 collective-permute-start.28
  80.7 4.6 %slice.94 = bf16[8,256,1024]{2,1,0:T(8,128)(2,1)} slice(bf16[8,264,1024]{2,1,0:T(8,128)(2,1)} %constant_dynamic-update-slice_fusion), slice={[0:8], [0:256], [0:1024]} | slice | bytes 8388608 | tf_op jit(solution)/shard_map/slice | solution.py:145
  87.2 1.4 collective-permute-done.17
  89.4 1.2 collective-permute-start.19
  90.6 5.8 %fusion.23 = f32[2048,2,384]{2,0,1:T(8,128)S(1)} fusion(bf16[2048,1024,1]{1,0,2:T(8,128)(2,1)} %bitcast.107, bf16[1,2,1024,384]{3,2,1,0:T(8,128)(2,1)} %param.15), kind=kOutput, calls=%fused_computation.38 | convolution fusion | flops 3221225472 | bytes 12058624 | tf_op jit(solution)/shard_map/td,edh->eth/dot_general | solution.py:166
  96.4 5.2 %collective-permute-done.18 = bf16[256,1024]{1,0:T(8,128)(2,1)S(1)} collective-permute-done((bf16[256,1024]{1,0:T(8,128)(2,1)}, bf16[256,1024]{1,0:T(8,128)(2,1)S(1)}, u32[]{:S(2)}, u32[]{:S(2)}) %collective-permute-start.18) | collective-permute-done | bytes 524320 | tf_op jit(solution)/shard_map/ppermute | solution.py:50
  101.6 1.7 collective-permute-done.19
  103.4 1.3 collective-permute-start.20
  104.7 5.3 %fusion.27 = f32[2048,2,384]{2,0,1:T(8,128)} fusion(bf16[2048,1024,1]{1,0,2:T(8,128)(2,1)S(1)} %bitcast.108, bf16[1,2,1024,384]{3,2,1,0:T(8,128)(2,1)S(1)} %copy-done), kind=kOutput, calls=%fused_computation.42 | convolution fusion | flops 3221225472 | bytes 12058624 | tf_op jit(solution)/shard_map/td,edh->eth/dot_general | solution.py:163
  110.0 6.9 %collective-permute-done.20 = bf16[256,1024]{1,0:T(8,128)(2,1)S(1)} collective-permute-done((bf16[256,1024]{1,0:T(8,128)(2,1)S(1)}, bf16[256,1024]{1,0:T(8,128)(2,1)S(1)}, u32[]{:S(2)}, u32[]{:S(2)}) %collective-permute-start.20) | collective-permute-done | bytes 524320 | tf_op jit(solution)/shard_map/ppermute | solution.py:46
  117.0 1.1 constant_dynamic-update-slice_fusion.13
  118.1 1.1 constant_dynamic-update-slice_fusion.12
  120.3 1.1 constant_dynamic-update-slice_fusion.9
  122.5 14.6 %multiply_convert_fusion.3 = (bf16[2,2048,384]{2,1,0:T(8,128)(2,1)}, bf16[2,2048,384]{2,1,0:T(8,128)(2,1)}, bf16[2,2048,384]{2,1,0:T(8,128)(2,1)}) fusion(f32[2048,2,384]{2,0,1:T(8,128)} %fusion.27, f32[2048,2,384]{2,0,1:T(8,128)S(1)} %fusion.23, bf16[1,2,384,1024]{3,2,1,0:T(8,128)(2,1)} %param.16, f32[2048,1024]{1,0:T(8,128)S(1)} %convert_element_type.67, ...), kind=kOutput, calls=%fused_computation.22 | convolution fusion | flops 3253207040 | bytes 31997952 | tf_op jit(solution)/shard_map/etd,ehd->eth/dot_general | solution.py:177
  137.0 8.4 %multiply_reduce_fusion = f32[2048,1024]{1,0:T(8,128)S(1)} fusion(f32[2,2048]{1,0:T(2,128)S(1)} %copy.33, bf16[2,2048,384]{2,1,0:T(8,128)(2,1)} %get-tuple-element.128, bf16[1,2,384,1024]{3,2,1,0:T(8,128)(2,1)} %param.16), kind=kOutput, calls=%fused_computation.2 | convolution fusion | flops 3231711232 | bytes 13123584 | tf_op jit(solution)/shard_map/eth,ehd->etd/dot_general | solution.py:173
  145.4 1.4 fusion.39
  147.7 1.3 collective-permute-start.8
  149.6 8.1 %fusion.25 = f32[2,2048,1024]{2,1,0:T(8,128)} fusion(bf16[2,2048,384]{2,1,0:T(8,128)(2,1)S(1)} %copy-done.7, bf16[1,2,1024,384]{3,2,1,0:T(8,128)(2,1)S(1)} %copy-done), kind=kOutput, calls=%fused_computation.40 | convolution fusion | flops 3221225472 | bytes 21495808 | tf_op jit(solution)/shard_map/eth,edh->etd/dot_general | solution.py:194
  157.8 16.4 %reduce-precision_reduce_fusion = f32[2048,1024]{1,0:T(8,128)} fusion(f32[2,2048,1024]{2,1,0:T(8,128)} %fusion.25, bf16[2,2048,384]{2,1,0:T(8,128)(2,1)} %get-tuple-element.126, bf16[1,2,1024,384]{3,2,1,0:T(8,128)(2,1)} %param.15), kind=kOutput, calls=%fused_computation | convolution fusion | flops 3231711232 | bytes 29884416 | tf_op jit(solution)/shard_map/eth,edh->etd/dot_general | solution.py:195
  174.1 1.7 fusion.38
  176.7 1.2 collective-permute-start.22
  178.5 2.6 slice_add_fusion.9
  182.1 19.8 %collective-permute-done.21 = f32[256,1024]{1,0:T(8,128)S(1)} collective-permute-done((f32[256,1024]{1,0:T(8,128)S(1)}, f32[256,1024]{1,0:T(8,128)S(1)}, u32[]{:S(2)}, u32[]{:S(2)}) %collective-permute-start.21) | collective-permute-done | bytes 1048608 | tf_op jit(solution)/shard_map/ppermute | solution.py:50
  201.9 2.9 slice_add_fusion.3
  204.8 2.0 collective-permute-start.23
  207.1 13.2 %fusion.37 = (f32[1,2,384,1024]{3,2,1,0:T(8,128)}, bf16[1,2,384,1024]{3,2,1,0:T(8,128)(2,1)}, f32[1,2,384,1024]{3,2,1,0:T(8,128)}) fusion(f32[1,2,384,1024]{3,2,1,0:T(8,128)} %param.18, f32[1,2,384,1024]{3,2,1,0:T(8,128)} %param.17, bf16[1,2,384,1024]{3,2,1,0:T(8,128)(2,1)} %collective-permute-done.28, ...), kind=kOutput, calls=%fused_computation.65 | convolution fusion | flops 3246129152 | bytes 30425088 | tf_op jit(solution)/shard_map/eth,etd->ehd/dot_general | solution.py:184
  220.3 4.1 %collective-permute-done.9 = f32[256,1024]{1,0:T(8,128)S(1)} collective-permute-done((f32[256,1024]{1,0:T(8,128)S(1)}, f32[256,1024]{1,0:T(8,128)S(1)}, u32[]{:S(2)}, u32[]{:S(2)}) %collective-permute-start.9) | collective-permute-done | bytes 1048608 | tf_op jit(solution)/shard_map/ppermute | solution.py:50
  224.4 3.7 %collective-permute-done.10 = f32[256,1024]{1,0:T(8,128)} collective-permute-done((f32[256,1024]{1,0:T(8,128)S(1)}, f32[256,1024]{1,0:T(8,128)}, u32[]{:S(2)}, u32[]{:S(2)}) %collective-permute-start.10) | collective-permute-done | bytes 1048608 | tf_op jit(solution)/shard_map/ppermute | solution.py:51
  228.1 3.8 %slice_add_fusion.7 = (f32[256,1024]{1,0:T(8,128)}, f32[256,1024]{1,0:T(8,128)}) fusion(f32[256,1024]{1,0:T(8,128)} %collective-permute-done.10, f32[2048,1024]{1,0:T(8,128)} %copy-done.2, f32[256,1024]{1,0:T(8,128)S(1)} %collective-permute-done.9), kind=kLoop, calls=%fused_computation.56 | loop fusion | flops 524288 | bytes 6291456 | tf_op jit(solution)/shard_map/add | solution.py:100
  232.8 1.2 collective-permute-start.12
  234.0 12.9 %collective-permute-done.23 = f32[256,1024]{1,0:T(8,128)S(1)} collective-permute-done((f32[256,1024]{1,0:T(8,128)}, f32[256,1024]{1,0:T(8,128)S(1)}, u32[]{:S(2)}, u32[]{:S(2)}) %collective-permute-start.23) | collective-permute-done | bytes 1048608 | tf_op jit(solution)/shard_map/ppermute | solution.py:50
  246.9 3.7 %collective-permute-done.24 = f32[256,1024]{1,0:T(8,128)} collective-permute-done((f32[256,1024]{1,0:T(8,128)S(1)}, f32[256,1024]{1,0:T(8,128)}, u32[]{:S(2)}, u32[]{:S(2)}) %collective-permute-start.24) | collective-permute-done | bytes 1048608 | tf_op jit(solution)/shard_map/ppermute | solution.py:51
  250.6 3.6 %slice_add_fusion.1 = (f32[256,1024]{1,0:T(8,128)}, f32[256,1024]{1,0:T(8,128)}) fusion(f32[256,1024]{1,0:T(8,128)} %collective-permute-done.24, f32[2048,1024]{1,0:T(8,128)} %reduce-precision_reduce_fusion, f32[256,1024]{1,0:T(8,128)S(1)} %collective-permute-done.23), kind=kLoop, calls=%fused_computation.48 | loop fusion | flops 524288 | bytes 6291456 | tf_op jit(solution)/shard_map/add | solution.py:100
  255.1 1.2 collective-permute-start.26
  256.3 3.6 %fusion.30 = bf16[1,2,1024,384]{2,3,1,0:T(8,128)(2,1)S(1)} fusion(bf16[2,2048,384]{2,1,0:T(8,128)(2,1)S(1)} %copy-done.8, bf16[2048,1024,1]{1,0,2:T(8,128)(2,1)S(1)} %bitcast.109), kind=kOutput, calls=%fused_computation.45 | convolution fusion | flops 3222011904 | bytes 8912896 | tf_op jit(solution)/shard_map/td,eth->edh/dot_general | solution.py:187
  259.8 1.6 copy.37
  261.4 8.1 %collective-permute-done.11 = f32[256,1024]{1,0:T(8,128)} collective-permute-done((f32[256,1024]{1,0:T(8,128)}, f32[256,1024]{1,0:T(8,128)}, u32[]{:S(2)}, u32[]{:S(2)}) %collective-permute-start.11) | collective-permute-done | bytes 1048608 | tf_op jit(solution)/shard_map/ppermute | solution.py:50
  269.5 3.5 %collective-permute-done.12 = f32[256,1024]{1,0:T(8,128)S(1)} collective-permute-done((f32[256,1024]{1,0:T(8,128)}, f32[256,1024]{1,0:T(8,128)S(1)}, u32[]{:S(2)}, u32[]{:S(2)}) %collective-permute-start.12) | collective-permute-done | bytes 1048608 | tf_op jit(solution)/shard_map/ppermute | solution.py:51
  273.0 3.1 slice_add_fusion.6
  276.9 15.0 %collective-permute-done.25 = f32[256,1024]{1,0:T(8,128)} collective-permute-done((f32[256,1024]{1,0:T(8,128)}, f32[256,1024]{1,0:T(8,128)}, u32[]{:S(2)}, u32[]{:S(2)}) %collective-permute-start.25) | collective-permute-done | bytes 1048608 | tf_op jit(solution)/shard_map/ppermute | solution.py:50
  291.9 2.7 slice_add_fusion
  294.6 1.1 collective-permute-start.27
  295.7 5.4 %fusion.31 = bf16[1,2,1024,384]{2,3,1,0:T(8,128)(2,1)S(1)} fusion(bf16[2,2048,384]{2,1,0:T(8,128)(2,1)} %get-tuple-element.126, bf16[2048,1024,1]{1,0,2:T(8,128)(2,1)S(1)} %bitcast.110), kind=kOutput, calls=%fused_computation.46 | convolution fusion | flops 3222011904 | bytes 8912896 | tf_op jit(solution)/shard_map/td,eth->edh/dot_general | solution.py:190
  301.2 1.6 copy.38
  302.7 11.6 %collective-permute-done.13 = f32[256,1024]{1,0:T(8,128)} collective-permute-done((f32[256,1024]{1,0:T(8,128)}, f32[256,1024]{1,0:T(8,128)}, u32[]{:S(2)}, u32[]{:S(2)}) %collective-permute-start.13) | collective-permute-done | bytes 1048608 | tf_op jit(solution)/shard_map/ppermute | solution.py:46
  314.4 2.9 fusion.35
  317.3 17.0 %collective-permute-done.27 = f32[256,1024]{1,0:T(8,128)} collective-permute-done((f32[256,1024]{1,0:T(8,128)}, f32[256,1024]{1,0:T(8,128)}, u32[]{:S(2)}, u32[]{:S(2)}) %collective-permute-start.27) | collective-permute-done | bytes 1048608 | tf_op jit(solution)/shard_map/ppermute | solution.py:46
  334.2 2.9 fusion.33
  (76 shorter events, 21.1 us)
Async XLA Ops:
  0.6 104.0 %copy-start = (bf16[1,2,1024,384]{3,2,1,0:T(8,128)(2,1)S(1)}, bf16[1,2,1024,384]{3,2,1,0:T(8,128)(2,1)}, u32[]{:S(2)}) copy-start(bf16[1,2,1024,384]{3,2,1,0:T(8,128)(2,1)} %param.14) | copy-start | bytes 4718596
  0.6 60.6 %copy-start.9 = (bf16[256,1024]{1,0:T(8,128)(2,1)S(1)}, bf16[256,1024]{1,0:T(8,128)(2,1)}, u32[]{:S(2)}) copy-start(bf16[256,1024]{1,0:T(8,128)(2,1)} %param.10) | copy-start | bytes 1572868
  3.6 61.0 %copy-start.12 = (bf16[256,1024]{1,0:T(8,128)(2,1)S(1)}, bf16[256,1024]{1,0:T(8,128)(2,1)}, u32[]{:S(2)}) copy-start(bf16[256,1024]{1,0:T(8,128)(2,1)} %param.11) | copy-start | bytes 1572868
  3.6 15.3 %collective-permute-start = (bf16[1,264,1024]{2,1,0:T(8,128)(2,1)S(1)}, bf16[1,264,1024]{2,1,0:T(8,128)(2,1)S(1)}, u32[]{:S(2)}, u32[]{:S(2)}) collective-permute-start(bf16[1,264,1024]{2,1,0:T(8,128)(2,1)S(1)} %maximum_bitcast_fusion), channel_id=1, source_target_pairs={{0,2},{2,4},{4,6},{6,7},{7,5},{5,3},{3,1},{1,0},{8,10},{10,12},{12... | collective-permute-start | bytes 1622024 | tf_op jit(solution)/shard_map/ppermute | solution.py:50
  6.7 13.7 %collective-permute-start.1 = (bf16[1,264,1024]{2,1,0:T(8,128)(2,1)S(1)}, bf16[1,264,1024]{2,1,0:T(8,128)(2,1)S(1)}, u32[]{:S(2)}, u32[]{:S(2)}) collective-permute-start(bf16[1,264,1024]{2,1,0:T(8,128)(2,1)S(1)} %maximum_bitcast_fusion), channel_id=1, source_target_pairs={{0,1},{2,0},{4,2},{6,4},{7,6},{5,7},{3,5},{1,3},{8,9},{10,8},{12,1... | collective-permute-start | bytes 1622024 | tf_op jit(solution)/shard_map/ppermute | solution.py:51
  20.4 12.8 %collective-permute-start.2 = (bf16[1,264,1024]{2,1,0:T(8,128)(2,1)S(1)}, bf16[1,264,1024]{2,1,0:T(8,128)(2,1)S(1)}, u32[]{:S(2)}, u32[]{:S(2)}) collective-permute-start(bf16[1,264,1024]{2,1,0:T(8,128)(2,1)S(1)} %collective-permute-done), channel_id=1, source_target_pairs={{0,2},{2,4},{4,6},{6,7},{7,5},{5,3},{3,1},{1,0},{8,10},{10,12},{12... | collective-permute-start | bytes 1622024 | tf_op jit(solution)/shard_map/ppermute | solution.py:50
  22.0 12.5 %collective-permute-start.3 = (bf16[1,264,1024]{2,1,0:T(8,128)(2,1)S(1)}, bf16[1,264,1024]{2,1,0:T(8,128)(2,1)S(1)}, u32[]{:S(2)}, u32[]{:S(2)}) collective-permute-start(bf16[1,264,1024]{2,1,0:T(8,128)(2,1)S(1)} %collective-permute-done.1), channel_id=1, source_target_pairs={{0,1},{2,0},{4,2},{6,4},{7,6},{5,7},{3,5},{1,3},{8,9},{10,8},{12,1... | collective-permute-start | bytes 1622024 | tf_op jit(solution)/shard_map/ppermute | solution.py:51
  34.5 11.6 %collective-permute-start.4 = (bf16[1,264,1024]{2,1,0:T(8,128)(2,1)S(1)}, bf16[1,264,1024]{2,1,0:T(8,128)(2,1)S(1)}, u32[]{:S(2)}, u32[]{:S(2)}) collective-permute-start(bf16[1,264,1024]{2,1,0:T(8,128)(2,1)S(1)} %collective-permute-done.2), channel_id=1, source_target_pairs={{0,2},{2,4},{4,6},{6,7},{7,5},{5,3},{3,1},{1,0},{8,10},{10,12},{12... | collective-permute-start | bytes 1622024 | tf_op jit(solution)/shard_map/ppermute | solution.py:50
  36.1 11.3 %collective-permute-start.5 = (bf16[1,264,1024]{2,1,0:T(8,128)(2,1)S(1)}, bf16[1,264,1024]{2,1,0:T(8,128)(2,1)S(1)}, u32[]{:S(2)}, u32[]{:S(2)}) collective-permute-start(bf16[1,264,1024]{2,1,0:T(8,128)(2,1)S(1)} %collective-permute-done.3), channel_id=1, source_target_pairs={{0,1},{2,0},{4,2},{6,4},{7,6},{5,7},{3,5},{1,3},{8,9},{10,8},{12,1... | collective-permute-start | bytes 1622024 | tf_op jit(solution)/shard_map/ppermute | solution.py:51
  47.4 10.4 %collective-permute-start.6 = (bf16[1,264,1024]{2,1,0:T(8,128)(2,1)S(1)}, bf16[1,264,1024]{2,1,0:T(8,128)(2,1)S(1)}, u32[]{:S(2)}, u32[]{:S(2)}) collective-permute-start(bf16[1,264,1024]{2,1,0:T(8,128)(2,1)S(1)} %collective-permute-done.4), channel_id=1, source_target_pairs={{0,2},{2,4},{4,6},{6,7},{7,5},{5,3},{3,1},{1,0},{8,10},{10,12},{12... | collective-permute-start | bytes 1622024 | tf_op jit(solution)/shard_map/ppermute | solution.py:46
  64.6 10.3 %collective-permute-start.14 = (bf16[256,1024]{1,0:T(8,128)(2,1)S(1)}, bf16[256,1024]{1,0:T(8,128)(2,1)}, u32[]{:S(2)}, u32[]{:S(2)}) collective-permute-start(bf16[256,1024]{1,0:T(8,128)(2,1)S(1)} %copy-done.12), channel_id=1, source_target_pairs={{0,2},{2,4},{4,6},{6,7},{7,5},{5,3},{3,1},{1,0},{8,10},{10,12},{12... | collective-permute-start | bytes 1572872 | tf_op jit(solution)/shard_map/ppermute | solution.py:50
  66.1 10.1 %collective-permute-start.15 = (bf16[256,1024]{1,0:T(8,128)(2,1)S(1)}, bf16[256,1024]{1,0:T(8,128)(2,1)}, u32[]{:S(2)}, u32[]{:S(2)}) collective-permute-start(bf16[256,1024]{1,0:T(8,128)(2,1)S(1)} %copy-done.12), channel_id=1, source_target_pairs={{0,1},{2,0},{4,2},{6,4},{7,6},{5,7},{3,5},{1,3},{8,9},{10,8},{12,1... | collective-permute-start | bytes 1572872 | tf_op jit(solution)/shard_map/ppermute | solution.py:51
  76.2 11.0 %collective-permute-start.16 = (bf16[256,1024]{1,0:T(8,128)(2,1)}, bf16[256,1024]{1,0:T(8,128)(2,1)}, u32[]{:S(2)}, u32[]{:S(2)}) collective-permute-start(bf16[256,1024]{1,0:T(8,128)(2,1)} %collective-permute-done.14), channel_id=1, source_target_pairs={{0,2},{2,4},{4,6},{6,7},{7,5},{5,3},{3,1},{1,0},{8,10},{10,12},{12... | collective-permute-start | bytes 1572872 | tf_op jit(solution)/shard_map/ppermute | solution.py:50
  79.1 9.5 %collective-permute-start.17 = (bf16[256,1024]{1,0:T(8,128)(2,1)}, bf16[256,1024]{1,0:T(8,128)(2,1)}, u32[]{:S(2)}, u32[]{:S(2)}) collective-permute-start(bf16[256,1024]{1,0:T(8,128)(2,1)} %collective-permute-done.15), channel_id=1, source_target_pairs={{0,1},{2,0},{4,2},{6,4},{7,6},{5,7},{3,5},{1,3},{8,9},{10,8},{12,1... | collective-permute-start | bytes 1572872 | tf_op jit(solution)/shard_map/ppermute | solution.py:51
  79.1 127.8 %collective-permute-start.29 = (bf16[1,2,384,1024]{3,2,1,0:T(8,128)(2,1)}, bf16[1,2,384,1024]{3,2,1,0:T(8,128)(2,1)}, u32[]{:S(2)}, u32[]{:S(2)}) collective-permute-start(bf16[1,2,384,1024]{3,2,1,0:T(8,128)(2,1)} %param.16), channel_id=1, source_target_pairs={{0,8},{8,16},{16,24},{24,0},{1,9},{9,17},{17,25},{25,1},{2,10},{10... | collective-permute-start | bytes 4718600 | tf_op jit(solution)/shard_map/ppermute | solution.py:21
  79.1 128.0 %collective-permute-start.28 = (bf16[1,2,384,1024]{3,2,1,0:T(8,128)(2,1)}, bf16[1,2,384,1024]{3,2,1,0:T(8,128)(2,1)}, u32[]{:S(2)}, u32[]{:S(2)}) collective-permute-start(bf16[1,2,384,1024]{3,2,1,0:T(8,128)(2,1)} %param.16), channel_id=1, source_target_pairs={{0,16},{8,24},{16,0},{24,8},{1,17},{9,25},{17,1},{25,9},{2,18},{10... | collective-permute-start | bytes 4718600 | tf_op jit(solution)/shard_map/ppermute | solution.py:21
  88.6 13.0 %collective-permute-start.18 = (bf16[256,1024]{1,0:T(8,128)(2,1)}, bf16[256,1024]{1,0:T(8,128)(2,1)S(1)}, u32[]{:S(2)}, u32[]{:S(2)}) collective-permute-start(bf16[256,1024]{1,0:T(8,128)(2,1)} %collective-permute-done.16), channel_id=1, source_target_pairs={{0,2},{2,4},{4,6},{6,7},{7,5},{5,3},{3,1},{1,0},{8,10},{10,12},{12... | collective-permute-start | bytes 1572872 | tf_op jit(solution)/shard_map/ppermute | solution.py:50
  89.4 14.0 %collective-permute-start.19 = (bf16[256,1024]{1,0:T(8,128)(2,1)}, bf16[256,1024]{1,0:T(8,128)(2,1)S(1)}, u32[]{:S(2)}, u32[]{:S(2)}) collective-permute-start(bf16[256,1024]{1,0:T(8,128)(2,1)} %collective-permute-done.17), channel_id=1, source_target_pairs={{0,1},{2,0},{4,2},{6,4},{7,6},{5,7},{3,5},{1,3},{8,9},{10,8},{12,1... | collective-permute-start | bytes 1572872 | tf_op jit(solution)/shard_map/ppermute | solution.py:51
  90.6 14.0 %copy-start.4 = (bf16[8,256,1024]{2,1,0:T(8,128)(2,1)S(1)}, bf16[8,256,1024]{2,1,0:T(8,128)(2,1)}, u32[]{:S(2)}) copy-start(bf16[8,256,1024]{2,1,0:T(8,128)(2,1)} %slice.94) | copy-start | bytes 12582916
  103.4 13.5 %collective-permute-start.20 = (bf16[256,1024]{1,0:T(8,128)(2,1)S(1)}, bf16[256,1024]{1,0:T(8,128)(2,1)S(1)}, u32[]{:S(2)}, u32[]{:S(2)}) collective-permute-start(bf16[256,1024]{1,0:T(8,128)(2,1)S(1)} %collective-permute-done.18), channel_id=1, source_target_pairs={{0,2},{2,4},{4,6},{6,7},{7,5},{5,3},{3,1},{1,0},{8,10},{10,12},{12... | collective-permute-start | bytes 1572872 | tf_op jit(solution)/shard_map/ppermute | solution.py:46
  110.0 9.1 %copy-start.13 = (bf16[256,1024]{1,0:T(8,128)(2,1)S(1)}, bf16[256,1024]{1,0:T(8,128)(2,1)}, u32[]{:S(2)}) copy-start(bf16[256,1024]{1,0:T(8,128)(2,1)} %param.11) | copy-start | bytes 1572868
  122.5 14.6 %copy-start.3 = (f32[2048,1024]{1,0:T(8,128)}, f32[2048,1024]{1,0:T(8,128)S(1)}, u32[]{:S(2)}) copy-start(f32[2048,1024]{1,0:T(8,128)S(1)} %convert_element_type.67) | copy-start | bytes 25165828
  145.4 12.3 %copy-start.2 = (f32[2048,1024]{1,0:T(8,128)}, f32[2048,1024]{1,0:T(8,128)S(1)}, u32[]{:S(2)}) copy-start(f32[2048,1024]{1,0:T(8,128)S(1)} %multiply_reduce_fusion) | copy-start | bytes 25165828
  145.4 4.2 %copy-start.7 = (bf16[2,2048,384]{2,1,0:T(8,128)(2,1)S(1)}, bf16[2,2048,384]{2,1,0:T(8,128)(2,1)}, u32[]{:S(2)}) copy-start(bf16[2,2048,384]{2,1,0:T(8,128)(2,1)} %get-tuple-element.127) | copy-start | bytes 9437188
  146.9 29.8 %collective-permute-start.7 = (f32[256,1024]{1,0:T(8,128)}, f32[256,1024]{1,0:T(8,128)S(1)}, u32[]{:S(2)}, u32[]{:S(2)}) collective-permute-start(f32[256,1024]{1,0:T(8,128)} %get-tuple-element.68), channel_id=1, source_target_pairs={{0,2},{2,4},{4,6},{6,7},{7,5},{5,3},{3,1},{1,0},{8,10},{10,12},{12... | collective-permute-start | bytes 3145736 | tf_op jit(solution)/shard_map/ppermute | solution.py:50
  147.7 30.8 %collective-permute-start.8 = (f32[256,1024]{1,0:T(8,128)}, f32[256,1024]{1,0:T(8,128)}, u32[]{:S(2)}, u32[]{:S(2)}) collective-permute-start(f32[256,1024]{1,0:T(8,128)} %get-tuple-element.69), channel_id=1, source_target_pairs={{0,1},{2,0},{4,2},{6,4},{7,6},{5,7},{3,5},{1,3},{8,9},{10,8},{12,1... | collective-permute-start | bytes 3145736 | tf_op jit(solution)/shard_map/ppermute | solution.py:51
  175.8 26.1 %collective-permute-start.21 = (f32[256,1024]{1,0:T(8,128)S(1)}, f32[256,1024]{1,0:T(8,128)S(1)}, u32[]{:S(2)}, u32[]{:S(2)}) collective-permute-start(f32[256,1024]{1,0:T(8,128)S(1)} %get-tuple-element.93), channel_id=1, source_target_pairs={{0,2},{2,4},{4,6},{6,7},{7,5},{5,3},{3,1},{1,0},{8,10},{10,12},{12... | collective-permute-start | bytes 3145736 | tf_op jit(solution)/shard_map/ppermute | solution.py:50
  176.7 1.8 copy-start.11
  176.7 25.2 %collective-permute-start.22 = (f32[256,1024]{1,0:T(8,128)S(1)}, f32[256,1024]{1,0:T(8,128)S(1)}, u32[]{:S(2)}, u32[]{:S(2)}) collective-permute-start(f32[256,1024]{1,0:T(8,128)S(1)} %get-tuple-element.94), channel_id=1, source_target_pairs={{0,1},{2,0},{4,2},{6,4},{7,6},{5,7},{3,5},{1,3},{8,9},{10,8},{12,1... | collective-permute-start | bytes 3145736 | tf_op jit(solution)/shard_map/ppermute | solution.py:51
  181.2 43.2 %collective-permute-start.9 = (f32[256,1024]{1,0:T(8,128)S(1)}, f32[256,1024]{1,0:T(8,128)S(1)}, u32[]{:S(2)}, u32[]{:S(2)}) collective-permute-start(f32[256,1024]{1,0:T(8,128)S(1)} %get-tuple-element.72), channel_id=1, source_target_pairs={{0,2},{2,4},{4,6},{6,7},{7,5},{5,3},{3,1},{1,0},{8,10},{10,12},{12... | collective-permute-start | bytes 3145736 | tf_op jit(solution)/shard_map/ppermute | solution.py:50
  201.9 26.2 %collective-permute-start.10 = (f32[256,1024]{1,0:T(8,128)S(1)}, f32[256,1024]{1,0:T(8,128)}, u32[]{:S(2)}, u32[]{:S(2)}) collective-permute-start(f32[256,1024]{1,0:T(8,128)S(1)} %get-tuple-element.73), channel_id=1, source_target_pairs={{0,1},{2,0},{4,2},{6,4},{7,6},{5,7},{3,5},{1,3},{8,9},{10,8},{12,1... | collective-permute-start | bytes 3145736 | tf_op jit(solution)/shard_map/ppermute | solution.py:51
  204.8 42.0 %collective-permute-start.23 = (f32[256,1024]{1,0:T(8,128)}, f32[256,1024]{1,0:T(8,128)S(1)}, u32[]{:S(2)}, u32[]{:S(2)}) collective-permute-start(f32[256,1024]{1,0:T(8,128)} %get-tuple-element.97), channel_id=1, source_target_pairs={{0,2},{2,4},{4,6},{6,7},{7,5},{5,3},{3,1},{1,0},{8,10},{10,12},{12... | collective-permute-start | bytes 3145736 | tf_op jit(solution)/shard_map/ppermute | solution.py:50
  206.9 43.7 %collective-permute-start.24 = (f32[256,1024]{1,0:T(8,128)S(1)}, f32[256,1024]{1,0:T(8,128)}, u32[]{:S(2)}, u32[]{:S(2)}) collective-permute-start(f32[256,1024]{1,0:T(8,128)S(1)} %get-tuple-element.98), channel_id=1, source_target_pairs={{0,1},{2,0},{4,2},{6,4},{7,6},{5,7},{3,5},{1,3},{8,9},{10,8},{12,1... | collective-permute-start | bytes 3145736 | tf_op jit(solution)/shard_map/ppermute | solution.py:51
  228.1 28.1 %copy-start.8 = (bf16[2,2048,384]{2,1,0:T(8,128)(2,1)S(1)}, bf16[2,2048,384]{2,1,0:T(8,128)(2,1)}, u32[]{:S(2)}) copy-start(bf16[2,2048,384]{2,1,0:T(8,128)(2,1)} %get-tuple-element.127) | copy-start | bytes 9437188
  231.9 24.3 %copy-start.5 = (bf16[8,256,1024]{2,1,0:T(8,128)(2,1)S(1)}, bf16[8,256,1024]{2,1,0:T(8,128)(2,1)}, u32[]{:S(2)}) copy-start(bf16[8,256,1024]{2,1,0:T(8,128)(2,1)} %slice.94) | copy-start | bytes 12582916
  231.9 37.5 %collective-permute-start.11 = (f32[256,1024]{1,0:T(8,128)}, f32[256,1024]{1,0:T(8,128)}, u32[]{:S(2)}, u32[]{:S(2)}) collective-permute-start(f32[256,1024]{1,0:T(8,128)} %get-tuple-element.76), channel_id=1, source_target_pairs={{0,2},{2,4},{4,6},{6,7},{7,5},{5,3},{3,1},{1,0},{8,10},{10,12},{12... | collective-permute-start | bytes 3145736 | tf_op jit(solution)/shard_map/ppermute | solution.py:50
  232.8 40.2 %collective-permute-start.12 = (f32[256,1024]{1,0:T(8,128)}, f32[256,1024]{1,0:T(8,128)S(1)}, u32[]{:S(2)}, u32[]{:S(2)}) collective-permute-start(f32[256,1024]{1,0:T(8,128)} %get-tuple-element.77), channel_id=1, source_target_pairs={{0,1},{2,0},{4,2},{6,4},{7,6},{5,7},{3,5},{1,3},{8,9},{10,8},{12,1... | collective-permute-start | bytes 3145736 | tf_op jit(solution)/shard_map/ppermute | solution.py:51
  254.2 37.7 %collective-permute-start.25 = (f32[256,1024]{1,0:T(8,128)}, f32[256,1024]{1,0:T(8,128)}, u32[]{:S(2)}, u32[]{:S(2)}) collective-permute-start(f32[256,1024]{1,0:T(8,128)} %get-tuple-element.101), channel_id=1, source_target_pairs={{0,2},{2,4},{4,6},{6,7},{7,5},{5,3},{3,1},{1,0},{8,10},{10,12},{12... | collective-permute-start | bytes 3145736 | tf_op jit(solution)/shard_map/ppermute | solution.py:50
  255.1 36.8 %collective-permute-start.26 = (f32[256,1024]{1,0:T(8,128)}, f32[256,1024]{1,0:T(8,128)}, u32[]{:S(2)}, u32[]{:S(2)}) collective-permute-start(f32[256,1024]{1,0:T(8,128)} %get-tuple-element.102), channel_id=1, source_target_pairs={{0,1},{2,0},{4,2},{6,4},{7,6},{5,7},{3,5},{1,3},{8,9},{10,8},{12,1... | collective-permute-start | bytes 3145736 | tf_op jit(solution)/shard_map/ppermute | solution.py:51
  261.4 34.4 %copy-start.6 = (bf16[8,256,1024]{2,1,0:T(8,128)(2,1)S(1)}, bf16[8,256,1024]{2,1,0:T(8,128)(2,1)}, u32[]{:S(2)}) copy-start(bf16[8,256,1024]{2,1,0:T(8,128)(2,1)} %slice.94) | copy-start | bytes 12582916
  273.0 21.7 %copy-start.10 = (f32[256,1024]{1,0:T(8,128)}, f32[256,1024]{1,0:T(8,128)S(1)}, u32[]{:S(2)}) copy-start(f32[256,1024]{1,0:T(8,128)S(1)} %collective-permute-done.12) | copy-start | bytes 3145732
  276.0 38.4 %collective-permute-start.13 = (f32[256,1024]{1,0:T(8,128)}, f32[256,1024]{1,0:T(8,128)}, u32[]{:S(2)}, u32[]{:S(2)}) collective-permute-start(f32[256,1024]{1,0:T(8,128)} %slice_add_fusion.6), channel_id=1, source_target_pairs={{0,2},{2,4},{4,6},{6,7},{7,5},{5,3},{3,1},{1,0},{8,10},{10,12},{12... | collective-permute-start | bytes 3145736 | tf_op jit(solution)/shard_map/ppermute | solution.py:46
  294.6 39.6 %collective-permute-start.27 = (f32[256,1024]{1,0:T(8,128)}, f32[256,1024]{1,0:T(8,128)}, u32[]{:S(2)}, u32[]{:S(2)}) collective-permute-start(f32[256,1024]{1,0:T(8,128)} %slice_add_fusion), channel_id=1, source_target_pairs={{0,2},{2,4},{4,6},{6,7},{7,5},{5,3},{3,1},{1,0},{8,10},{10,12},{12... | collective-permute-start | bytes 3145736 | tf_op jit(solution)/shard_map/ppermute | solution.py:46
  301.2 35.9 %copy-start.1 = (bf16[1,2,1024,384]{3,2,1,0:T(8,128)(2,1)S(1)}, bf16[1,2,1024,384]{3,2,1,0:T(8,128)(2,1)}, u32[]{:S(2)}) copy-start(bf16[1,2,1024,384]{3,2,1,0:T(8,128)(2,1)} %param.14) | copy-start | bytes 4718596

commit v5 on v4

--- a/solution.py
+++ b/solution.py
@@ -73,7 +73,7 @@
     return jnp.concatenate([got[offset] for offset in range(-ahead, behind + 1)])
 
 
-def ring_reduce_scatter(part, axis, ring):
+def ring_reduce_scatter(part, axis, ring, wire_dtype):
     size = len(ring)
     ahead = size // 2
     behind = size - 1 - ahead
@@ -82,9 +82,12 @@
     def block_at(offset):
         return blocks[(offset + ahead) % size]
 
+    def to_wire(value):
+        return value.astype(wire_dtype)
+
     result = block_at(0)
-    ahead_value = block_at(ahead) if ahead else None
-    behind_value = block_at(-behind) if behind else None
+    ahead_value = to_wire(block_at(ahead)) if ahead else None
+    behind_value = to_wire(block_at(-behind)) if behind else None
     for step in range(max(ahead, behind)):
         ahead_value, behind_value = paired_shift(
             ahead_value if step < ahead else None,
@@ -93,13 +96,13 @@
             ring,
         )
         if step < ahead - 1:
-            ahead_value = ahead_value + block_at(ahead - step - 1)
+            ahead_value = to_wire(ahead_value.astype(part.dtype) + block_at(ahead - step - 1))
         elif step == ahead - 1:
-            result = result + ahead_value
+            result = result + ahead_value.astype(part.dtype)
         if step < behind - 1:
-            behind_value = behind_value + block_at(-behind + step + 1)
+            behind_value = to_wire(behind_value.astype(part.dtype) + block_at(-behind + step + 1))
         elif step == behind - 1:
-            result = result + behind_value
+            result = result + behind_value.astype(part.dtype)
     return result
 
 
@@ -138,7 +141,7 @@
 
     def reduce_scatter(value):
         if use_ring:
-            return ring_reduce_scatter(value, "exp", ring)
+            return ring_reduce_scatter(value, "exp", ring, jnp.bfloat16)
         return lax.psum_scatter(value, "exp", scatter_dimension=0, tiled=True)
 
     gathered = gather(packed_tokens[None])

time: 342 us -> 260 us (0.76); the launches traced: 337 us -> 260 us
  waiting for transfers between devices: 170 us -> 96.3 us
  matrix products: 80.8 us -> 77.1 us
    ppermute x12, waiting for transfers between devices: 106 us -> 65.6 us  [paired_shift(): ahead_value = lax.ppermute(ahead_value, axis, ring_pairs(ring, 1))]
    ppermute x4, waiting for transfers between devices: 44.4 us -> 19.2 us  [paired_shift(): return (lax.ppermute(ahead_value, axis, ring_pairs(ring, 1)), None)]
    add x6 -> x0, other arithmetic: 18.7 us -> none  [the longest x4 12.9 us: ring_reduce_scatter(): behind_value = behind_value + block_at(-behind + step + 1)]
    convert_element_type x0 -> x6, other arithmetic: none -> 12.4 us  [to_wire(): return value.astype(wire_dtype)]
    ppermute x12, waiting for transfers between devices: 19.6 us -> 11.5 us  [paired_shift(): behind_value = lax.ppermute(behind_value, axis, ring_pairs(ring, -1))]
    another operation x0 -> x2, other arithmetic: none -> 4.71 us
    unnamed x45 -> x43, local copies, waits for them, and re-layouts: 14.3 us -> 18 us
  transfers between devices with their start and end apart: 30 -> 30, of which waited for: 23 -> 20; matrix products, arithmetic and copies ran while one was open for 36% -> 44% of each run, Pallas kernels for 0% -> 0%
where the time goes in v5:
time: 260 us
  waiting for transfers between devices  96.3 us (37%)
  matrix products  77.1 us (30%)
  starting transfers between devices  32.1 us (12%)
  other arithmetic  26.9 us (10%)
  local copies, waits for them, and re-layouts  25.6 us (10%)
    ppermute x12, waiting for transfers between devices, paired_shift(): ahead_value = lax.ppermute(ahead_value, axis, ring_pairs(ring, 1))  65.6 us
    ppermute x4, waiting for transfers between devices, paired_shift(): return (lax.ppermute(ahead_value, axis, ring_pairs(ring, 1)), None)  19.2 us
    ppermute x12, starting transfers between devices, paired_shift(): ahead_value = lax.ppermute(ahead_value, axis, ring_pairs(ring, 1))  18.6 us
    unnamed x43, local copies, waits for them, and re-layouts  18 us
    dot_general x1, matrix products, chunk_pass(): jnp.einsum('etd,ehd->eth', slot_cot, down_matrix, preferred_element_type=...  14.5 us
    dot_general x1, matrix products, chunk_pass(): jnp.einsum('eth,edh->etd', up_cot, up_matrix, preferred_element_type=jnp....  13.7 us
    dot_general x1, matrix products, chunk_pass(): jnp.einsum('eth,etd->ehd', hidden, slot_cot, preferred_element_type=jnp.f...  13.1 us
    convert_element_type x6, other arithmetic, to_wire(): return value.astype(wire_dtype)  12.4 us
  transfers between devices with their start and end apart: 30, of which 20 were waited for; matrix products, arithmetic and copies ran while one was open for 44% of the time, Pallas kernels for 0%

profile of v5, /device:TPU:0, one launch (start us, length us, event | category | flops | bytes accessed | tf_op | source)
XLA Modules:
  0.0 259.6 jit_solution(13406313099657735480)
XLA Ops:
  2.5 1.1 maximum_bitcast_fusion
  3.6 3.1 %collective-permute-start = (bf16[1,264,1024]{2,1,0:T(8,128)(2,1)S(1)}, bf16[1,264,1024]{2,1,0:T(8,128)(2,1)S(1)}, u32[]{:S(2)}, u32[]{:S(2)}) collective-permute-start(bf16[1,264,1024]{2,1,0:T(8,128)(2,1)S(1)} %maximum_bitcast_fusion), channel_id=1, source_target_pairs={{0,2},{2,4},{4,6},{6,7},{7,5},{5,3},{3,1},{1,0},{8,10},{10,12},{12... | collective-permute-start | bytes 1622024 | tf_op jit(solution)/shard_map/ppermute | solution.py:50
  6.7 12.2 %collective-permute-done = bf16[1,264,1024]{2,1,0:T(8,128)(2,1)S(1)} collective-permute-done((bf16[1,264,1024]{2,1,0:T(8,128)(2,1)S(1)}, bf16[1,264,1024]{2,1,0:T(8,128)(2,1)S(1)}, u32[]{:S(2)}, u32[]{:S(2)}) %collective-permute-start) | collective-permute-done | bytes 540704 | tf_op jit(solution)/shard_map/ppermute | solution.py:50
  18.8 1.5 collective-permute-done.1
  20.4 1.6 collective-permute-start.2
  22.4 10.8 %collective-permute-done.2 = bf16[1,264,1024]{2,1,0:T(8,128)(2,1)S(1)} collective-permute-done((bf16[1,264,1024]{2,1,0:T(8,128)(2,1)S(1)}, bf16[1,264,1024]{2,1,0:T(8,128)(2,1)S(1)}, u32[]{:S(2)}, u32[]{:S(2)}) %collective-permute-start.2) | collective-permute-done | bytes 540704 | tf_op jit(solution)/shard_map/ppermute | solution.py:50
  33.2 1.3 collective-permute-done.3
  34.5 1.6 collective-permute-start.4
  36.5 9.6 %collective-permute-done.4 = bf16[1,264,1024]{2,1,0:T(8,128)(2,1)S(1)} collective-permute-done((bf16[1,264,1024]{2,1,0:T(8,128)(2,1)S(1)}, bf16[1,264,1024]{2,1,0:T(8,128)(2,1)S(1)}, u32[]{:S(2)}, u32[]{:S(2)}) %collective-permute-start.4) | collective-permute-done | bytes 540704 | tf_op jit(solution)/shard_map/ppermute | solution.py:50
  46.1 1.3 collective-permute-done.5
  47.4 1.5 collective-permute-start.6
  48.9 8.9 %collective-permute-done.6 = bf16[1,264,1024]{2,1,0:T(8,128)(2,1)S(1)} collective-permute-done((bf16[1,264,1024]{2,1,0:T(8,128)(2,1)S(1)}, bf16[1,264,1024]{2,1,0:T(8,128)(2,1)S(1)}, u32[]{:S(2)}, u32[]{:S(2)}) %collective-permute-start.6) | collective-permute-done | bytes 540704 | tf_op jit(solution)/shard_map/ppermute | solution.py:46
  64.6 1.5 collective-permute-start.14
  66.6 8.2 %collective-permute-done.14 = bf16[256,1024]{1,0:T(8,128)(2,1)} collective-permute-done((bf16[256,1024]{1,0:T(8,128)(2,1)S(1)}, bf16[256,1024]{1,0:T(8,128)(2,1)}, u32[]{:S(2)}, u32[]{:S(2)}) %collective-permute-start.14) | collective-permute-done | bytes 524320 | tf_op jit(solution)/shard_map/ppermute | solution.py:50
  74.9 1.4 collective-permute-done.15
  76.2 2.9 %collective-permute-start.16 = (bf16[256,1024]{1,0:T(8,128)(2,1)}, bf16[256,1024]{1,0:T(8,128)(2,1)}, u32[]{:S(2)}, u32[]{:S(2)}) collective-permute-start(bf16[256,1024]{1,0:T(8,128)(2,1)} %collective-permute-done.14), channel_id=1, source_target_pairs={{0,2},{2,4},{4,6},{6,7},{7,5},{5,3},{3,1},{1,0},{8,10},{10,12},{12... | collective-permute-start | bytes 1572872 | tf_op jit(solution)/shard_map/ppermute | solution.py:50
  79.1 1.6 collective-permute-start.28
  80.7 4.6 %slice.98 = bf16[8,256,1024]{2,1,0:T(8,128)(2,1)} slice(bf16[8,264,1024]{2,1,0:T(8,128)(2,1)} %constant_dynamic-update-slice_fusion), slice={[0:8], [0:256], [0:1024]} | slice | bytes 8388608 | tf_op jit(solution)/shard_map/slice | solution.py:148
  87.2 1.4 collective-permute-done.17
  89.4 1.2 collective-permute-start.19
  90.6 5.8 %fusion.23 = f32[2048,2,384]{2,0,1:T(8,128)S(1)} fusion(bf16[2048,1024,1]{1,0,2:T(8,128)(2,1)} %bitcast.107, bf16[1,2,1024,384]{3,2,1,0:T(8,128)(2,1)} %param.15), kind=kOutput, calls=%fused_computation.38 | convolution fusion | flops 3221225472 | bytes 12058624 | tf_op jit(solution)/shard_map/td,edh->eth/dot_general | solution.py:169
  96.4 5.2 %collective-permute-done.18 = bf16[256,1024]{1,0:T(8,128)(2,1)S(1)} collective-permute-done((bf16[256,1024]{1,0:T(8,128)(2,1)}, bf16[256,1024]{1,0:T(8,128)(2,1)S(1)}, u32[]{:S(2)}, u32[]{:S(2)}) %collective-permute-start.18) | collective-permute-done | bytes 524320 | tf_op jit(solution)/shard_map/ppermute | solution.py:50
  101.6 1.7 collective-permute-done.19
  104.2 5.3 %fusion.27 = f32[2048,2,384]{2,0,1:T(8,128)} fusion(bf16[2048,1024,1]{1,0,2:T(8,128)(2,1)S(1)} %bitcast.108, bf16[1,2,1024,384]{3,2,1,0:T(8,128)(2,1)S(1)} %copy-done), kind=kOutput, calls=%fused_computation.42 | convolution fusion | flops 3221225472 | bytes 12058624 | tf_op jit(solution)/shard_map/td,edh->eth/dot_general | solution.py:166
  109.5 6.9 %collective-permute-done.20 = bf16[256,1024]{1,0:T(8,128)(2,1)S(1)} collective-permute-done((bf16[256,1024]{1,0:T(8,128)(2,1)S(1)}, bf16[256,1024]{1,0:T(8,128)(2,1)S(1)}, u32[]{:S(2)}, u32[]{:S(2)}) %collective-permute-start.20) | collective-permute-done | bytes 524320 | tf_op jit(solution)/shard_map/ppermute | solution.py:46
  116.5 1.1 constant_dynamic-update-slice_fusion.13
  117.6 1.1 constant_dynamic-update-slice_fusion.12
  118.7 1.1 constant_dynamic-update-slice_fusion.10
  119.8 1.1 constant_dynamic-update-slice_fusion.9
  120.9 1.0 convert_element_type.155
  122.0 14.5 %multiply_convert_fusion.3 = (bf16[2,2048,384]{2,1,0:T(8,128)(2,1)}, bf16[2,2048,384]{2,1,0:T(8,128)(2,1)}, bf16[2,2048,384]{2,1,0:T(8,128)(2,1)}) fusion(f32[2048,2,384]{2,0,1:T(8,128)} %fusion.27, f32[2048,2,384]{2,0,1:T(8,128)S(1)} %fusion.23, bf16[1,2,384,1024]{3,2,1,0:T(8,128)(2,1)} %param.16, f32[2048,1024]{1,0:T(8,128)S(1)} %convert_element_type.155, ...), kind=kOutput, calls=%fused_computation.22 | convolution fusion | flops 3253207040 | bytes 31997952 | tf_op jit(solution)/shard_map/etd,ehd->eth/dot_general | solution.py:180
  136.5 8.4 %multiply_reduce_fusion = f32[2048,1024]{1,0:T(8,128)S(1)} fusion(f32[2,2048]{1,0:T(2,128)S(1)} %copy.33, bf16[2,2048,384]{2,1,0:T(8,128)(2,1)} %get-tuple-element.128, bf16[1,2,384,1024]{3,2,1,0:T(8,128)(2,1)} %param.16), kind=kOutput, calls=%fused_computation.2 | convolution fusion | flops 3231711232 | bytes 13123584 | tf_op jit(solution)/shard_map/eth,ehd->etd/dot_general | solution.py:176
  145.6 3.2 %copy-done.2 = f32[2048,1024]{1,0:T(8,128)} copy-done((f32[2048,1024]{1,0:T(8,128)}, f32[2048,1024]{1,0:T(8,128)S(1)}, u32[]{:S(2)}) %copy-start.2) | copy-done | bytes 8388632
  148.8 1.0 fusion.49
  150.7 1.2 collective-permute-start.8
  151.9 8.2 %fusion.25 = f32[2,2048,1024]{2,1,0:T(8,128)} fusion(bf16[2,2048,384]{2,1,0:T(8,128)(2,1)S(1)} %copy-done.7, bf16[1,2,1024,384]{3,2,1,0:T(8,128)(2,1)S(1)} %copy-done), kind=kOutput, calls=%fused_computation.40 | convolution fusion | flops 3221225472 | bytes 21495808 | tf_op jit(solution)/shard_map/eth,edh->etd/dot_general | solution.py:197
  160.0 13.7 %reduce-precision_reduce_fusion = f32[2048,1024]{1,0:T(8,128)} fusion(f32[2,2048,1024]{2,1,0:T(8,128)} %fusion.25, bf16[2,2048,384]{2,1,0:T(8,128)(2,1)} %get-tuple-element.126, bf16[1,2,1024,384]{3,2,1,0:T(8,128)(2,1)S(1)} %copy-done.10), kind=kOutput, calls=%fused_computation | convolution fusion | flops 3231711232 | bytes 29884416 | tf_op jit(solution)/shard_map/eth,edh->etd/dot_general | solution.py:198
  173.7 4.0 %convert.11 = bf16[2048,1024]{1,0:T(8,128)(2,1)S(1)} convert(f32[2048,1024]{1,0:T(8,128)} %reduce-precision_reduce_fusion) | non-fusion elementwise | flops 2097152 | bytes 12582912 | tf_op jit(solution)/shard_map/convert.3
  177.8 0.9 collective-permute-start.21
  178.8 1.2 collective-permute-start.22
  180.6 2.2 fusion.42
  183.7 9.1 %collective-permute-done.21 = bf16[256,1024]{1,0:T(8,128)(2,1)S(1)} collective-permute-done((bf16[256,1024]{1,0:T(8,128)(2,1)S(1)}, bf16[256,1024]{1,0:T(8,128)(2,1)S(1)}, u32[]{:S(2)}, u32[]{:S(2)}) %collective-permute-start.21) | collective-permute-done | bytes 524320 | tf_op jit(solution)/shard_map/ppermute | solution.py:50
  192.8 1.9 fusion.35
  194.7 2.0 collective-permute-start.23
  196.8 13.1 %fusion.47 = (f32[1,2,384,1024]{3,2,1,0:T(8,128)}, bf16[1,2,384,1024]{3,2,1,0:T(8,128)(2,1)}, f32[1,2,384,1024]{3,2,1,0:T(8,128)}) fusion(f32[1,2,384,1024]{3,2,1,0:T(8,128)} %param.18, f32[1,2,384,1024]{3,2,1,0:T(8,128)} %param.17, bf16[1,2,384,1024]{3,2,1,0:T(8,128)(2,1)} %collective-permute-done.28, ...), kind=kOutput, calls=%fused_computation.75 | convolution fusion | flops 3246129152 | bytes 30425088 | tf_op jit(solution)/shard_map/eth,etd->ehd/dot_general | solution.py:187
  210.0 2.1 fusion.40
  212.1 2.0 collective-permute-start.11
  214.2 1.1 collective-permute-done.23
  216.0 1.9 fusion.33
  218.4 1.6 collective-permute-start.26
  220.0 3.6 %fusion.31 = bf16[1,2,1024,384]{2,3,1,0:T(8,128)(2,1)S(1)} fusion(bf16[2,2048,384]{2,1,0:T(8,128)(2,1)S(1)} %copy-done.6, bf16[2048,1024,1]{1,0,2:T(8,128)(2,1)S(1)} %bitcast.109), kind=kOutput, calls=%fused_computation.46 | convolution fusion | flops 3222011904 | bytes 8912896 | tf_op jit(solution)/shard_map/td,eth->edh/dot_general | solution.py:193
  223.6 3.4 %collective-permute-done.11 = bf16[256,1024]{1,0:T(8,128)(2,1)S(1)} collective-permute-done((bf16[256,1024]{1,0:T(8,128)(2,1)S(1)}, bf16[256,1024]{1,0:T(8,128)(2,1)S(1)}, u32[]{:S(2)}, u32[]{:S(2)}) %collective-permute-start.11) | collective-permute-done | bytes 524320 | tf_op jit(solution)/shard_map/ppermute | solution.py:50
  227.0 2.1 collective-permute-done.12
  229.1 2.2 fusion.39
  231.3 0.9 collective-permute-start.13
  232.2 6.0 %collective-permute-done.25 = bf16[256,1024]{1,0:T(8,128)(2,1)S(1)} collective-permute-done((bf16[256,1024]{1,0:T(8,128)(2,1)S(1)}, bf16[256,1024]{1,0:T(8,128)(2,1)S(1)}, u32[]{:S(2)}, u32[]{:S(2)}) %collective-permute-start.25) | collective-permute-done | bytes 524320 | tf_op jit(solution)/shard_map/ppermute | solution.py:50
  238.2 2.2 fusion.32
  240.4 2.0 collective-permute-start.27
  242.4 4.5 %fusion.30 = bf16[1,2,1024,384]{2,3,1,0:T(8,128)(2,1)} fusion(bf16[2,2048,384]{2,1,0:T(8,128)(2,1)S(1)} %copy-done.8, bf16[2048,1024,1]{1,0,2:T(8,128)(2,1)S(1)} %bitcast.110), kind=kOutput, calls=%fused_computation.45 | convolution fusion | flops 3222011904 | bytes 8912896 | tf_op jit(solution)/shard_map/td,eth->edh/dot_general | solution.py:190
  246.9 2.7 %copy.37 = bf16[1,2,1024,384]{3,2,1,0:T(8,128)(2,1)} copy(bf16[1,2,1024,384]{2,3,1,0:T(8,128)(2,1)} %fusion.30) | data formatting | bytes 3145728
  249.6 1.6 copy.38
  251.2 2.5 fusion.45
  253.7 3.3 %collective-permute-done.27 = bf16[256,1024]{1,0:T(8,128)(2,1)} collective-permute-done((bf16[256,1024]{1,0:T(8,128)(2,1)}, bf16[256,1024]{1,0:T(8,128)(2,1)}, u32[]{:S(2)}, u32[]{:S(2)}) %collective-permute-start.27) | collective-permute-done | bytes 524320 | tf_op jit(solution)/shard_map/ppermute | solution.py:46
  257.1 2.5 fusion.38
  (76 shorter events, 17.5 us)
Async XLA Ops:
  0.6 103.5 %copy-start = (bf16[1,2,1024,384]{3,2,1,0:T(8,128)(2,1)S(1)}, bf16[1,2,1024,384]{3,2,1,0:T(8,128)(2,1)}, u32[]{:S(2)}) copy-start(bf16[1,2,1024,384]{3,2,1,0:T(8,128)(2,1)} %param.14) | copy-start | bytes 4718596
  0.6 60.6 %copy-start.9 = (bf16[256,1024]{1,0:T(8,128)(2,1)S(1)}, bf16[256,1024]{1,0:T(8,128)(2,1)}, u32[]{:S(2)}) copy-start(bf16[256,1024]{1,0:T(8,128)(2,1)} %param.10) | copy-start | bytes 1572868
  3.6 61.0 %copy-start.11 = (bf16[256,1024]{1,0:T(8,128)(2,1)S(1)}, bf16[256,1024]{1,0:T(8,128)(2,1)}, u32[]{:S(2)}) copy-start(bf16[256,1024]{1,0:T(8,128)(2,1)} %param.11) | copy-start | bytes 1572868
  3.6 15.3 %collective-permute-start = (bf16[1,264,1024]{2,1,0:T(8,128)(2,1)S(1)}, bf16[1,264,1024]{2,1,0:T(8,128)(2,1)S(1)}, u32[]{:S(2)}, u32[]{:S(2)}) collective-permute-start(bf16[1,264,1024]{2,1,0:T(8,128)(2,1)S(1)} %maximum_bitcast_fusion), channel_id=1, source_target_pairs={{0,2},{2,4},{4,6},{6,7},{7,5},{5,3},{3,1},{1,0},{8,10},{10,12},{12... | collective-permute-start | bytes 1622024 | tf_op jit(solution)/shard_map/ppermute | solution.py:50
  6.7 13.7 %collective-permute-start.1 = (bf16[1,264,1024]{2,1,0:T(8,128)(2,1)S(1)}, bf16[1,264,1024]{2,1,0:T(8,128)(2,1)S(1)}, u32[]{:S(2)}, u32[]{:S(2)}) collective-permute-start(bf16[1,264,1024]{2,1,0:T(8,128)(2,1)S(1)} %maximum_bitcast_fusion), channel_id=1, source_target_pairs={{0,1},{2,0},{4,2},{6,4},{7,6},{5,7},{3,5},{1,3},{8,9},{10,8},{12,1... | collective-permute-start | bytes 1622024 | tf_op jit(solution)/shard_map/ppermute | solution.py:51
  20.4 12.8 %collective-permute-start.2 = (bf16[1,264,1024]{2,1,0:T(8,128)(2,1)S(1)}, bf16[1,264,1024]{2,1,0:T(8,128)(2,1)S(1)}, u32[]{:S(2)}, u32[]{:S(2)}) collective-permute-start(bf16[1,264,1024]{2,1,0:T(8,128)(2,1)S(1)} %collective-permute-done), channel_id=1, source_target_pairs={{0,2},{2,4},{4,6},{6,7},{7,5},{5,3},{3,1},{1,0},{8,10},{10,12},{12... | collective-permute-start | bytes 1622024 | tf_op jit(solution)/shard_map/ppermute | solution.py:50
  22.0 12.5 %collective-permute-start.3 = (bf16[1,264,1024]{2,1,0:T(8,128)(2,1)S(1)}, bf16[1,264,1024]{2,1,0:T(8,128)(2,1)S(1)}, u32[]{:S(2)}, u32[]{:S(2)}) collective-permute-start(bf16[1,264,1024]{2,1,0:T(8,128)(2,1)S(1)} %collective-permute-done.1), channel_id=1, source_target_pairs={{0,1},{2,0},{4,2},{6,4},{7,6},{5,7},{3,5},{1,3},{8,9},{10,8},{12,1... | collective-permute-start | bytes 1622024 | tf_op jit(solution)/shard_map/ppermute | solution.py:51
  34.5 11.6 %collective-permute-start.4 = (bf16[1,264,1024]{2,1,0:T(8,128)(2,1)S(1)}, bf16[1,264,1024]{2,1,0:T(8,128)(2,1)S(1)}, u32[]{:S(2)}, u32[]{:S(2)}) collective-permute-start(bf16[1,264,1024]{2,1,0:T(8,128)(2,1)S(1)} %collective-permute-done.2), channel_id=1, source_target_pairs={{0,2},{2,4},{4,6},{6,7},{7,5},{5,3},{3,1},{1,0},{8,10},{10,12},{12... | collective-permute-start | bytes 1622024 | tf_op jit(solution)/shard_map/ppermute | solution.py:50
  36.1 11.3 %collective-permute-start.5 = (bf16[1,264,1024]{2,1,0:T(8,128)(2,1)S(1)}, bf16[1,264,1024]{2,1,0:T(8,128)(2,1)S(1)}, u32[]{:S(2)}, u32[]{:S(2)}) collective-permute-start(bf16[1,264,1024]{2,1,0:T(8,128)(2,1)S(1)} %collective-permute-done.3), channel_id=1, source_target_pairs={{0,1},{2,0},{4,2},{6,4},{7,6},{5,7},{3,5},{1,3},{8,9},{10,8},{12,1... | collective-permute-start | bytes 1622024 | tf_op jit(solution)/shard_map/ppermute | solution.py:51
  47.4 10.4 %collective-permute-start.6 = (bf16[1,264,1024]{2,1,0:T(8,128)(2,1)S(1)}, bf16[1,264,1024]{2,1,0:T(8,128)(2,1)S(1)}, u32[]{:S(2)}, u32[]{:S(2)}) collective-permute-start(bf16[1,264,1024]{2,1,0:T(8,128)(2,1)S(1)} %collective-permute-done.4), channel_id=1, source_target_pairs={{0,2},{2,4},{4,6},{6,7},{7,5},{5,3},{3,1},{1,0},{8,10},{10,12},{12... | collective-permute-start | bytes 1622024 | tf_op jit(solution)/shard_map/ppermute | solution.py:46
  64.6 10.3 %collective-permute-start.14 = (bf16[256,1024]{1,0:T(8,128)(2,1)S(1)}, bf16[256,1024]{1,0:T(8,128)(2,1)}, u32[]{:S(2)}, u32[]{:S(2)}) collective-permute-start(bf16[256,1024]{1,0:T(8,128)(2,1)S(1)} %copy-done.11), channel_id=1, source_target_pairs={{0,2},{2,4},{4,6},{6,7},{7,5},{5,3},{3,1},{1,0},{8,10},{10,12},{12... | collective-permute-start | bytes 1572872 | tf_op jit(solution)/shard_map/ppermute | solution.py:50
  66.1 10.1 %collective-permute-start.15 = (bf16[256,1024]{1,0:T(8,128)(2,1)S(1)}, bf16[256,1024]{1,0:T(8,128)(2,1)}, u32[]{:S(2)}, u32[]{:S(2)}) collective-permute-start(bf16[256,1024]{1,0:T(8,128)(2,1)S(1)} %copy-done.11), channel_id=1, source_target_pairs={{0,1},{2,0},{4,2},{6,4},{7,6},{5,7},{3,5},{1,3},{8,9},{10,8},{12,1... | collective-permute-start | bytes 1572872 | tf_op jit(solution)/shard_map/ppermute | solution.py:51
  76.2 11.0 %collective-permute-start.16 = (bf16[256,1024]{1,0:T(8,128)(2,1)}, bf16[256,1024]{1,0:T(8,128)(2,1)}, u32[]{:S(2)}, u32[]{:S(2)}) collective-permute-start(bf16[256,1024]{1,0:T(8,128)(2,1)} %collective-permute-done.14), channel_id=1, source_target_pairs={{0,2},{2,4},{4,6},{6,7},{7,5},{5,3},{3,1},{1,0},{8,10},{10,12},{12... | collective-permute-start | bytes 1572872 | tf_op jit(solution)/shard_map/ppermute | solution.py:50
  79.1 9.5 %collective-permute-start.17 = (bf16[256,1024]{1,0:T(8,128)(2,1)}, bf16[256,1024]{1,0:T(8,128)(2,1)}, u32[]{:S(2)}, u32[]{:S(2)}) collective-permute-start(bf16[256,1024]{1,0:T(8,128)(2,1)} %collective-permute-done.15), channel_id=1, source_target_pairs={{0,1},{2,0},{4,2},{6,4},{7,6},{5,7},{3,5},{1,3},{8,9},{10,8},{12,1... | collective-permute-start | bytes 1572872 | tf_op jit(solution)/shard_map/ppermute | solution.py:51
  79.1 117.7 %collective-permute-start.29 = (bf16[1,2,384,1024]{3,2,1,0:T(8,128)(2,1)}, bf16[1,2,384,1024]{3,2,1,0:T(8,128)(2,1)}, u32[]{:S(2)}, u32[]{:S(2)}) collective-permute-start(bf16[1,2,384,1024]{3,2,1,0:T(8,128)(2,1)} %param.16), channel_id=1, source_target_pairs={{0,8},{8,16},{16,24},{24,0},{1,9},{9,17},{17,25},{25,1},{2,10},{10... | collective-permute-start | bytes 4718600 | tf_op jit(solution)/shard_map/ppermute | solution.py:21
  79.1 117.7 %collective-permute-start.28 = (bf16[1,2,384,1024]{3,2,1,0:T(8,128)(2,1)}, bf16[1,2,384,1024]{3,2,1,0:T(8,128)(2,1)}, u32[]{:S(2)}, u32[]{:S(2)}) collective-permute-start(bf16[1,2,384,1024]{3,2,1,0:T(8,128)(2,1)} %param.16), channel_id=1, source_target_pairs={{0,16},{8,24},{16,0},{24,8},{1,17},{9,25},{17,1},{25,9},{2,18},{10... | collective-permute-start | bytes 4718600 | tf_op jit(solution)/shard_map/ppermute | solution.py:21
  88.6 13.0 %collective-permute-start.18 = (bf16[256,1024]{1,0:T(8,128)(2,1)}, bf16[256,1024]{1,0:T(8,128)(2,1)S(1)}, u32[]{:S(2)}, u32[]{:S(2)}) collective-permute-start(bf16[256,1024]{1,0:T(8,128)(2,1)} %collective-permute-done.16), channel_id=1, source_target_pairs={{0,2},{2,4},{4,6},{6,7},{7,5},{5,3},{3,1},{1,0},{8,10},{10,12},{12... | collective-permute-start | bytes 1572872 | tf_op jit(solution)/shard_map/ppermute | solution.py:50
  89.4 14.0 %collective-permute-start.19 = (bf16[256,1024]{1,0:T(8,128)(2,1)}, bf16[256,1024]{1,0:T(8,128)(2,1)S(1)}, u32[]{:S(2)}, u32[]{:S(2)}) collective-permute-start(bf16[256,1024]{1,0:T(8,128)(2,1)} %collective-permute-done.17), channel_id=1, source_target_pairs={{0,1},{2,0},{4,2},{6,4},{7,6},{5,7},{3,5},{1,3},{8,9},{10,8},{12,1... | collective-permute-start | bytes 1572872 | tf_op jit(solution)/shard_map/ppermute | solution.py:51
  90.6 13.5 %copy-start.4 = (bf16[8,256,1024]{2,1,0:T(8,128)(2,1)S(1)}, bf16[8,256,1024]{2,1,0:T(8,128)(2,1)}, u32[]{:S(2)}) copy-start(bf16[8,256,1024]{2,1,0:T(8,128)(2,1)} %slice.98) | copy-start | bytes 12582916
  103.4 13.0 %collective-permute-start.20 = (bf16[256,1024]{1,0:T(8,128)(2,1)S(1)}, bf16[256,1024]{1,0:T(8,128)(2,1)S(1)}, u32[]{:S(2)}, u32[]{:S(2)}) collective-permute-start(bf16[256,1024]{1,0:T(8,128)(2,1)S(1)} %collective-permute-done.18), channel_id=1, source_target_pairs={{0,2},{2,4},{4,6},{6,7},{7,5},{5,3},{3,1},{1,0},{8,10},{10,12},{12... | collective-permute-start | bytes 1572872 | tf_op jit(solution)/shard_map/ppermute | solution.py:46
  109.5 9.2 %copy-start.12 = (bf16[256,1024]{1,0:T(8,128)(2,1)S(1)}, bf16[256,1024]{1,0:T(8,128)(2,1)}, u32[]{:S(2)}) copy-start(bf16[256,1024]{1,0:T(8,128)(2,1)} %param.11) | copy-start | bytes 1572868
  121.9 14.5 %copy-start.3 = (f32[2048,1024]{1,0:T(8,128)}, f32[2048,1024]{1,0:T(8,128)S(1)}, u32[]{:S(2)}) copy-start(f32[2048,1024]{1,0:T(8,128)S(1)} %convert_element_type.155) | copy-start | bytes 25165828
  144.9 3.9 %copy-start.2 = (f32[2048,1024]{1,0:T(8,128)}, f32[2048,1024]{1,0:T(8,128)S(1)}, u32[]{:S(2)}) copy-start(f32[2048,1024]{1,0:T(8,128)S(1)} %multiply_reduce_fusion) | copy-start | bytes 25165828
  144.9 7.0 %copy-start.7 = (bf16[2,2048,384]{2,1,0:T(8,128)(2,1)S(1)}, bf16[2,2048,384]{2,1,0:T(8,128)(2,1)}, u32[]{:S(2)}) copy-start(bf16[2,2048,384]{2,1,0:T(8,128)(2,1)} %get-tuple-element.127) | copy-start | bytes 9437188
  149.8 29.0 %collective-permute-start.7 = (bf16[256,1024]{1,0:T(8,128)(2,1)}, bf16[256,1024]{1,0:T(8,128)(2,1)}, u32[]{:S(2)}, u32[]{:S(2)}) collective-permute-start(bf16[256,1024]{1,0:T(8,128)(2,1)} %get-tuple-element.68), channel_id=1, source_target_pairs={{0,2},{2,4},{4,6},{6,7},{7,5},{5,3},{3,1},{1,0},{8,10},{10,12},{12... | collective-permute-start | bytes 1572872 | tf_op jit(solution)/shard_map/ppermute | solution.py:50
  150.7 29.9 %collective-permute-start.8 = (bf16[256,1024]{1,0:T(8,128)(2,1)}, bf16[256,1024]{1,0:T(8,128)(2,1)}, u32[]{:S(2)}, u32[]{:S(2)}) collective-permute-start(bf16[256,1024]{1,0:T(8,128)(2,1)} %get-tuple-element.69), channel_id=1, source_target_pairs={{0,1},{2,0},{4,2},{6,4},{7,6},{5,7},{3,5},{1,3},{8,9},{10,8},{12,1... | collective-permute-start | bytes 1572872 | tf_op jit(solution)/shard_map/ppermute | solution.py:51
  151.8 8.2 %copy-start.10 = (bf16[1,2,1024,384]{3,2,1,0:T(8,128)(2,1)S(1)}, bf16[1,2,1024,384]{3,2,1,0:T(8,128)(2,1)}, u32[]{:S(2)}) copy-start(bf16[1,2,1024,384]{3,2,1,0:T(8,128)(2,1)} %param.15) | copy-start | bytes 4718596
  177.8 14.9 %collective-permute-start.21 = (bf16[256,1024]{1,0:T(8,128)(2,1)S(1)}, bf16[256,1024]{1,0:T(8,128)(2,1)S(1)}, u32[]{:S(2)}, u32[]{:S(2)}) collective-permute-start(bf16[256,1024]{1,0:T(8,128)(2,1)S(1)} %get-tuple-element.93), channel_id=1, source_target_pairs={{0,2},{2,4},{4,6},{6,7},{7,5},{5,3},{3,1},{1,0},{8,10},{10,12},{12... | collective-permute-start | bytes 1572872 | tf_op jit(solution)/shard_map/ppermute | solution.py:50
  178.8 14.0 %collective-permute-start.22 = (bf16[256,1024]{1,0:T(8,128)(2,1)S(1)}, bf16[256,1024]{1,0:T(8,128)(2,1)S(1)}, u32[]{:S(2)}, u32[]{:S(2)}) collective-permute-start(bf16[256,1024]{1,0:T(8,128)(2,1)S(1)} %get-tuple-element.94), channel_id=1, source_target_pairs={{0,1},{2,0},{4,2},{6,4},{7,6},{5,7},{3,5},{1,3},{8,9},{10,8},{12,1... | collective-permute-start | bytes 1572872 | tf_op jit(solution)/shard_map/ppermute | solution.py:51
  182.8 27.2 %collective-permute-start.9 = (bf16[256,1024]{1,0:T(8,128)(2,1)S(1)}, bf16[256,1024]{1,0:T(8,128)(2,1)S(1)}, u32[]{:S(2)}, u32[]{:S(2)}) collective-permute-start(bf16[256,1024]{1,0:T(8,128)(2,1)S(1)} %get-tuple-element.72), channel_id=1, source_target_pairs={{0,2},{2,4},{4,6},{6,7},{7,5},{5,3},{3,1},{1,0},{8,10},{10,12},{12... | collective-permute-start | bytes 1572872 | tf_op jit(solution)/shard_map/ppermute | solution.py:50
  192.8 17.2 %collective-permute-start.10 = (bf16[256,1024]{1,0:T(8,128)(2,1)S(1)}, bf16[256,1024]{1,0:T(8,128)(2,1)S(1)}, u32[]{:S(2)}, u32[]{:S(2)}) collective-permute-start(bf16[256,1024]{1,0:T(8,128)(2,1)S(1)} %get-tuple-element.73), channel_id=1, source_target_pairs={{0,1},{2,0},{4,2},{6,4},{7,6},{5,7},{3,5},{1,3},{8,9},{10,8},{12,1... | collective-permute-start | bytes 1572872 | tf_op jit(solution)/shard_map/ppermute | solution.py:51
  194.7 20.5 %collective-permute-start.23 = (bf16[256,1024]{1,0:T(8,128)(2,1)S(1)}, bf16[256,1024]{1,0:T(8,128)(2,1)S(1)}, u32[]{:S(2)}, u32[]{:S(2)}) collective-permute-start(bf16[256,1024]{1,0:T(8,128)(2,1)S(1)} %get-tuple-element.97), channel_id=1, source_target_pairs={{0,2},{2,4},{4,6},{6,7},{7,5},{5,3},{3,1},{1,0},{8,10},{10,12},{12... | collective-permute-start | bytes 1572872 | tf_op jit(solution)/shard_map/ppermute | solution.py:50
  196.8 19.2 %collective-permute-start.24 = (bf16[256,1024]{1,0:T(8,128)(2,1)S(1)}, bf16[256,1024]{1,0:T(8,128)(2,1)S(1)}, u32[]{:S(2)}, u32[]{:S(2)}) collective-permute-start(bf16[256,1024]{1,0:T(8,128)(2,1)S(1)} %get-tuple-element.98), channel_id=1, source_target_pairs={{0,1},{2,0},{4,2},{6,4},{7,6},{5,7},{3,5},{1,3},{8,9},{10,8},{12,1... | collective-permute-start | bytes 1572872 | tf_op jit(solution)/shard_map/ppermute | solution.py:51
  210.0 10.0 %copy-start.5 = (bf16[8,256,1024]{2,1,0:T(8,128)(2,1)S(1)}, bf16[8,256,1024]{2,1,0:T(8,128)(2,1)}, u32[]{:S(2)}) copy-start(bf16[8,256,1024]{2,1,0:T(8,128)(2,1)} %slice.98) | copy-start | bytes 12582916
  210.0 10.0 %copy-start.6 = (bf16[2,2048,384]{2,1,0:T(8,128)(2,1)S(1)}, bf16[2,2048,384]{2,1,0:T(8,128)(2,1)}, u32[]{:S(2)}) copy-start(bf16[2,2048,384]{2,1,0:T(8,128)(2,1)} %get-tuple-element.126) | copy-start | bytes 9437188
  212.1 14.9 %collective-permute-start.11 = (bf16[256,1024]{1,0:T(8,128)(2,1)S(1)}, bf16[256,1024]{1,0:T(8,128)(2,1)S(1)}, u32[]{:S(2)}, u32[]{:S(2)}) collective-permute-start(bf16[256,1024]{1,0:T(8,128)(2,1)S(1)} %get-tuple-element.76), channel_id=1, source_target_pairs={{0,2},{2,4},{4,6},{6,7},{7,5},{5,3},{3,1},{1,0},{8,10},{10,12},{12... | collective-permute-start | bytes 1572872 | tf_op jit(solution)/shard_map/ppermute | solution.py:50
  214.1 15.0 %collective-permute-start.12 = (bf16[256,1024]{1,0:T(8,128)(2,1)S(1)}, bf16[256,1024]{1,0:T(8,128)(2,1)}, u32[]{:S(2)}, u32[]{:S(2)}) collective-permute-start(bf16[256,1024]{1,0:T(8,128)(2,1)S(1)} %get-tuple-element.77), channel_id=1, source_target_pairs={{0,1},{2,0},{4,2},{6,4},{7,6},{5,7},{3,5},{1,3},{8,9},{10,8},{12,1... | collective-permute-start | bytes 1572872 | tf_op jit(solution)/shard_map/ppermute | solution.py:51
  217.9 20.3 %collective-permute-start.25 = (bf16[256,1024]{1,0:T(8,128)(2,1)S(1)}, bf16[256,1024]{1,0:T(8,128)(2,1)S(1)}, u32[]{:S(2)}, u32[]{:S(2)}) collective-permute-start(bf16[256,1024]{1,0:T(8,128)(2,1)S(1)} %get-tuple-element.101), channel_id=1, source_target_pairs={{0,2},{2,4},{4,6},{6,7},{7,5},{5,3},{3,1},{1,0},{8,10},{10,12},{12... | collective-permute-start | bytes 1572872 | tf_op jit(solution)/shard_map/ppermute | solution.py:50
  218.4 19.9 %collective-permute-start.26 = (bf16[256,1024]{1,0:T(8,128)(2,1)S(1)}, bf16[256,1024]{1,0:T(8,128)(2,1)}, u32[]{:S(2)}, u32[]{:S(2)}) collective-permute-start(bf16[256,1024]{1,0:T(8,128)(2,1)S(1)} %get-tuple-element.102), channel_id=1, source_target_pairs={{0,1},{2,0},{4,2},{6,4},{7,6},{5,7},{3,5},{1,3},{8,9},{10,8},{12,1... | collective-permute-start | bytes 1572872 | tf_op jit(solution)/shard_map/ppermute | solution.py:51
  223.6 18.8 %copy-start.8 = (bf16[2,2048,384]{2,1,0:T(8,128)(2,1)S(1)}, bf16[2,2048,384]{2,1,0:T(8,128)(2,1)}, u32[]{:S(2)}) copy-start(bf16[2,2048,384]{2,1,0:T(8,128)(2,1)} %get-tuple-element.127) | copy-start | bytes 9437188
  231.3 19.9 %collective-permute-start.13 = (bf16[256,1024]{1,0:T(8,128)(2,1)}, bf16[256,1024]{1,0:T(8,128)(2,1)}, u32[]{:S(2)}, u32[]{:S(2)}) collective-permute-start(bf16[256,1024]{1,0:T(8,128)(2,1)} %fusion.39), channel_id=1, source_target_pairs={{0,2},{2,4},{4,6},{6,7},{7,5},{5,3},{3,1},{1,0},{8,10},{10,12},{12... | collective-permute-start | bytes 1572872 | tf_op jit(solution)/shard_map/ppermute | solution.py:46
  240.4 16.7 %collective-permute-start.27 = (bf16[256,1024]{1,0:T(8,128)(2,1)}, bf16[256,1024]{1,0:T(8,128)(2,1)}, u32[]{:S(2)}, u32[]{:S(2)}) collective-permute-start(bf16[256,1024]{1,0:T(8,128)(2,1)} %fusion.32), channel_id=1, source_target_pairs={{0,2},{2,4},{4,6},{6,7},{7,5},{5,3},{3,1},{1,0},{8,10},{10,12},{12... | collective-permute-start | bytes 1572872 | tf_op jit(solution)/shard_map/ppermute | solution.py:46
  246.9 12.7 %copy-start.1 = (bf16[1,2,1024,384]{3,2,1,0:T(8,128)(2,1)S(1)}, bf16[1,2,1024,384]{3,2,1,0:T(8,128)(2,1)}, u32[]{:S(2)}) copy-start(bf16[1,2,1024,384]{3,2,1,0:T(8,128)(2,1)} %param.14) | copy-start | bytes 4718596

commit v6 on v5

--- a/solution.py
+++ b/solution.py
@@ -176,6 +176,7 @@
             jnp.einsum("eth,ehd->etd", hidden, down_matrix, preferred_element_type=jnp.float32)
         )
         mixed_part = jnp.sum(chunk_weight * expert_out, axis=0)
+        chunk_cot, mixed_part = lax.optimization_barrier((chunk_cot, mixed_part))
         slot_cot = (chunk_weight * chunk_cot.astype(jnp.float32)[None]).astype(jnp.bfloat16)
         hidden_cot = jnp.einsum(
             "etd,ehd->eth", slot_cot, down_matrix, preferred_element_type=jnp.float32

time: 260 us -> 241 us (0.927)
  waiting for transfers between devices: 96.3 us -> 80.4 us
  matrix products: 77.1 us -> 72.6 us
  other arithmetic: 26.9 us -> 29.6 us
    ppermute x4, waiting for transfers between devices: 19.2 us -> 8.94 us  [paired_shift(): return (lax.ppermute(ahead_value, axis, ring_pairs(ring, 1)), None)]
    ppermute x12, waiting for transfers between devices: 65.6 us -> 60.9 us  [paired_shift(): ahead_value = lax.ppermute(ahead_value, axis, ring_pairs(ring, 1))]
    dot_general x1, matrix products: 14.5 us -> 11.1 us  [chunk_pass(): jnp.einsum('etd,ehd->eth', slot_cot, down_matrix, preferred_element_type=...]
    unnamed x43 -> x53, local copies, waits for them, and re-layouts: 18 us -> 14.9 us
  transfers between devices with their start and end apart: 30 -> 30, of which waited for: 20 -> 18; matrix products, arithmetic and copies ran while one was open for 44% -> 47% of each run, Pallas kernels for 0% -> 0%
where the time goes in v6:
time: 241 us
  waiting for transfers between devices  80.4 us (33%)
  matrix products  72.6 us (30%)
  starting transfers between devices  32.9 us (14%)
  other arithmetic  29.6 us (12%)
  local copies, waits for them, and re-layouts  23.5 us (10%)
    ppermute x12, waiting for transfers between devices, paired_shift(): ahead_value = lax.ppermute(ahead_value, axis, ring_pairs(ring, 1))  60.9 us
    ppermute x12, starting transfers between devices, paired_shift(): ahead_value = lax.ppermute(ahead_value, axis, ring_pairs(ring, 1))  19.4 us
    unnamed x53, local copies, waits for them, and re-layouts  14.9 us
    dot_general x1, matrix products, chunk_pass(): jnp.einsum('eth,edh->etd', up_cot, up_matrix, preferred_element_type=jnp....  13.7 us
    dot_general x1, matrix products, chunk_pass(): jnp.einsum('eth,etd->ehd', hidden, slot_cot, preferred_element_type=jnp.f...  13.3 us
    convert_element_type x6, other arithmetic, to_wire(): return value.astype(wire_dtype)  12.5 us
    dot_general x1, matrix products, chunk_pass(): jnp.einsum('etd,ehd->eth', slot_cot, down_matrix, preferred_element_type=...  11.1 us
    ppermute x12, waiting for transfers between devices, paired_shift(): behind_value = lax.ppermute(behind_value, axis, ring_pairs(ring, -1))  10.5 us
  transfers between devices with their start and end apart: 30, of which 18 were waited for; matrix products, arithmetic and copies ran while one was open for 47% of the time, Pallas kernels for 0%

profile of v6, /device:TPU:0, one launch (start us, length us, event | category | flops | bytes accessed | tf_op | source)
XLA Modules:
  0.0 240.6 jit_solution(11411823323708859375)
XLA Ops:
  2.5 1.1 maximum_bitcast_fusion
  3.6 3.1 %collective-permute-start = (bf16[1,264,1024]{2,1,0:T(8,128)(2,1)S(1)}, bf16[1,264,1024]{2,1,0:T(8,128)(2,1)S(1)}, u32[]{:S(2)}, u32[]{:S(2)}) collective-permute-start(bf16[1,264,1024]{2,1,0:T(8,128)(2,1)S(1)} %maximum_bitcast_fusion), channel_id=1, source_target_pairs={{0,2},{2,4},{4,6},{6,7},{7,5},{5,3},{3,1},{1,0},{8,10},{10,12},{12... | collective-permute-start | bytes 1622024 | tf_op jit(solution)/shard_map/ppermute | solution.py:50
  6.7 12.2 %collective-permute-done = bf16[1,264,1024]{2,1,0:T(8,128)(2,1)S(1)} collective-permute-done((bf16[1,264,1024]{2,1,0:T(8,128)(2,1)S(1)}, bf16[1,264,1024]{2,1,0:T(8,128)(2,1)S(1)}, u32[]{:S(2)}, u32[]{:S(2)}) %collective-permute-start) | collective-permute-done | bytes 540704 | tf_op jit(solution)/shard_map/ppermute | solution.py:50
  18.8 1.5 collective-permute-done.1
  20.4 1.6 collective-permute-start.2
  22.4 10.8 %collective-permute-done.2 = bf16[1,264,1024]{2,1,0:T(8,128)(2,1)S(1)} collective-permute-done((bf16[1,264,1024]{2,1,0:T(8,128)(2,1)S(1)}, bf16[1,264,1024]{2,1,0:T(8,128)(2,1)S(1)}, u32[]{:S(2)}, u32[]{:S(2)}) %collective-permute-start.2) | collective-permute-done | bytes 540704 | tf_op jit(solution)/shard_map/ppermute | solution.py:50
  33.2 1.3 collective-permute-done.3
  34.5 1.6 collective-permute-start.4
  36.5 9.6 %collective-permute-done.4 = bf16[1,264,1024]{2,1,0:T(8,128)(2,1)S(1)} collective-permute-done((bf16[1,264,1024]{2,1,0:T(8,128)(2,1)S(1)}, bf16[1,264,1024]{2,1,0:T(8,128)(2,1)S(1)}, u32[]{:S(2)}, u32[]{:S(2)}) %collective-permute-start.4) | collective-permute-done | bytes 540704 | tf_op jit(solution)/shard_map/ppermute | solution.py:50
  46.1 1.3 collective-permute-done.5
  47.4 1.5 collective-permute-start.6
  48.9 8.9 %collective-permute-done.6 = bf16[1,264,1024]{2,1,0:T(8,128)(2,1)S(1)} collective-permute-done((bf16[1,264,1024]{2,1,0:T(8,128)(2,1)S(1)}, bf16[1,264,1024]{2,1,0:T(8,128)(2,1)S(1)}, u32[]{:S(2)}, u32[]{:S(2)}) %collective-permute-start.6) | collective-permute-done | bytes 540704 | tf_op jit(solution)/shard_map/ppermute | solution.py:46
  64.7 1.5 collective-permute-start.7
  66.7 1.6 collective-permute-start.28
  68.3 2.6 %slice.98 = bf16[8,256,1024]{2,1,0:T(8,128)(2,1)S(1)} slice(bf16[8,264,1024]{2,1,0:T(8,128)(2,1)} %constant_dynamic-update-slice_fusion), slice={[0:8], [0:256], [0:1024]} | slice | bytes 8388608 | tf_op jit(solution)/shard_map/slice | solution.py:148
  71.0 2.9 %collective-permute-done.7 = bf16[256,1024]{1,0:T(8,128)(2,1)S(1)} collective-permute-done((bf16[256,1024]{1,0:T(8,128)(2,1)S(1)}, bf16[256,1024]{1,0:T(8,128)(2,1)S(1)}, u32[]{:S(2)}, u32[]{:S(2)}) %collective-permute-start.7) | collective-permute-done | bytes 524320 | tf_op jit(solution)/shard_map/ppermute | solution.py:50
  73.9 1.8 collective-permute-done.8
  75.7 2.0 collective-permute-start.9
  77.8 3.5 %fusion.27 = f32[2048,2,384]{2,0,1:T(8,128)S(1)} fusion(bf16[2048,1024,1]{1,0,2:T(8,128)(2,1)S(1)} %bitcast.109, bf16[1,2,1024,384]{3,2,1,0:T(8,128)(2,1)S(1)} %copy-done), kind=kOutput, calls=%fused_computation.42 | convolution fusion | flops 3221225472 | bytes 12058624 | tf_op jit(solution)/shard_map/td,edh->eth/dot_general | solution.py:166
  81.3 5.0 %collective-permute-done.9 = bf16[256,1024]{1,0:T(8,128)(2,1)} collective-permute-done((bf16[256,1024]{1,0:T(8,128)(2,1)S(1)}, bf16[256,1024]{1,0:T(8,128)(2,1)}, u32[]{:S(2)}, u32[]{:S(2)}) %collective-permute-start.9) | collective-permute-done | bytes 524320 | tf_op jit(solution)/shard_map/ppermute | solution.py:50
  86.3 1.2 collective-permute-done.10
  87.5 2.2 collective-permute-start.11
  89.7 6.4 %fusion.6 = (bf16[2,2048,384]{2,1,0:T(8,128)(2,1)}, f32[2048,2,384]{2,0,1:T(8,128)}) fusion(f32[2048,2,384]{2,0,1:T(8,128)S(1)} %fusion.27, bf16[2048,1024,1]{1,0,2:T(8,128)(2,1)S(1)} %bitcast.110, bf16[1,2,1024,384]{3,2,1,0:T(8,128)(2,1)S(1)} %copy-done.9), kind=kOutput, calls=%fused_computation.11 | convolution fusion | flops 3230662656 | bytes 21495808 | tf_op jit(solution)/shard_map/td,edh->eth/dot_general | solution.py:169
  96.1 0.9 slice_bitcast_fusion
  99.2 2.0 collective-permute-start.13
  101.2 8.4 %multiply_reduce_fusion = f32[2048,1024]{1,0:T(8,128)S(1)} fusion(f32[2,2048]{1,0:T(2,128)S(1)} %copy.33, bf16[2,2048,384]{2,1,0:T(8,128)(2,1)} %get-tuple-element.147, bf16[1,2,384,1024]{3,2,1,0:T(8,128)(2,1)} %param.16), kind=kOutput, calls=%fused_computation.2 | convolution fusion | flops 3231711232 | bytes 13123584 | tf_op jit(solution)/shard_map/eth,ehd->etd/dot_general | solution.py:176
  109.6 1.8 constant_dynamic-update-slice_fusion.14
  111.4 1.5 constant_dynamic-update-slice_fusion.13
  113.1 1.1 constant_dynamic-update-slice_fusion.9
  114.2 1.1 constant_dynamic-update-slice_fusion.8
  115.3 1.0 convert_element_type.151
  116.3 3.2 %convert.10 = bf16[2048,1024]{1,0:T(8,128)(2,1)} convert(f32[2048,1024]{1,0:T(8,128)S(1)} %multiply_reduce_fusion) | non-fusion elementwise | flops 2097152 | bytes 12582912 | tf_op jit(solution)/shard_map/convert.5
  119.5 3.0 %fusion.42 = (bf16[256,1024]{1,0:T(8,128)(2,1)}, bf16[256,1024]{1,0:T(8,128)(2,1)}) fusion(bf16[2048,1024]{1,0:T(8,128)(2,1)} %convert.10), kind=kLoop, calls=%fused_computation.90 | loop fusion | bytes 2097152 | tf_op jit(solution)/shard_map/slice | solution.py:83
  122.5 1.0 collective-permute-start.14
  123.5 1.0 collective-permute-start.15
  124.6 11.1 %multiply_convert_fusion.3 = (bf16[2,2048,384]{2,1,0:T(8,128)(2,1)}, bf16[2,2048,384]{2,1,0:T(8,128)(2,1)S(1)}) fusion(f32[2048,2,384]{2,0,1:T(8,128)} %copy-done.17, f32[2048,2,384]{2,0,1:T(8,128)} %get-tuple-element.148, bf16[1,2,384,1024]{3,2,1,0:T(8,128)(2,1)} %param.16, f32[2048,1024]{1,0:T(8,128)S(1)} %convert_element_type.151, f32[2,2048]{1,0:T(2,128)S(1)} %copy.33), kind=kOutput, calls=%fused_computation.22 | convolution fusion | flops 3250061312 | bytes 28852224 | tf_op jit(solution)/shard_map/etd,ehd->eth/dot_general | solution.py:181
  135.6 8.2 %fusion.25 = f32[2,2048,1024]{2,1,0:T(8,128)} fusion(bf16[2,2048,384]{2,1,0:T(8,128)(2,1)S(1)} %get-tuple-element.131, bf16[1,2,1024,384]{3,2,1,0:T(8,128)(2,1)S(1)} %copy-done), kind=kOutput, calls=%fused_computation.40 | convolution fusion | flops 3221225472 | bytes 21495808 | tf_op jit(solution)/shard_map/eth,edh->etd/dot_general | solution.py:198
  143.8 13.7 %reduce-precision_reduce_fusion = f32[2048,1024]{1,0:T(8,128)} fusion(f32[2,2048,1024]{2,1,0:T(8,128)} %fusion.25, bf16[2,2048,384]{2,1,0:T(8,128)(2,1)} %get-tuple-element.130, bf16[1,2,1024,384]{3,2,1,0:T(8,128)(2,1)S(1)} %copy-done.10), kind=kOutput, calls=%fused_computation | convolution fusion | flops 3231711232 | bytes 29884416 | tf_op jit(solution)/shard_map/eth,edh->etd/dot_general | solution.py:199
  157.5 4.0 %convert.11 = bf16[2048,1024]{1,0:T(8,128)(2,1)S(1)} convert(f32[2048,1024]{1,0:T(8,128)} %reduce-precision_reduce_fusion) | non-fusion elementwise | flops 2097152 | bytes 12582912 | tf_op jit(solution)/shard_map/convert.3
  161.6 1.1 collective-permute-start.21
  162.7 1.0 collective-permute-start.22
  164.4 2.2 add_convert_fusion.4
  166.6 1.1 collective-permute-start.16
  167.7 8.9 %collective-permute-done.21 = bf16[256,1024]{1,0:T(8,128)(2,1)S(1)} collective-permute-done((bf16[256,1024]{1,0:T(8,128)(2,1)S(1)}, bf16[256,1024]{1,0:T(8,128)(2,1)S(1)}, u32[]{:S(2)}, u32[]{:S(2)}) %collective-permute-start.21) | collective-permute-done | bytes 524320 | tf_op jit(solution)/shard_map/ppermute | solution.py:50
  177.5 1.9 fusion.35
  179.5 1.5 collective-permute-start.23
  181.5 13.3 %fusion.40 = (f32[1,2,384,1024]{3,2,1,0:T(8,128)}, bf16[1,2,384,1024]{3,2,1,0:T(8,128)(2,1)}, f32[1,2,384,1024]{3,2,1,0:T(8,128)}) fusion(f32[1,2,384,1024]{3,2,1,0:T(8,128)} %param.18, f32[1,2,384,1024]{3,2,1,0:T(8,128)} %param.17, bf16[1,2,384,1024]{3,2,1,0:T(8,128)(2,1)} %collective-permute-done.28, ...), kind=kOutput, calls=%fused_computation.68 | convolution fusion | flops 3246129152 | bytes 30425088 | tf_op jit(solution)/shard_map/eth,etd->ehd/dot_general | solution.py:188
  194.9 2.1 add_convert_fusion.2
  197.0 1.5 collective-permute-start.18
  199.0 1.9 collective-permute-done.24
  201.0 1.9 fusion.33
  202.9 1.2 collective-permute-start.25
  205.0 3.6 %fusion.31 = bf16[1,2,1024,384]{2,3,1,0:T(8,128)(2,1)S(1)} fusion(bf16[2,2048,384]{2,1,0:T(8,128)(2,1)S(1)} %copy-done.5, bf16[2048,1024,1]{1,0,2:T(8,128)(2,1)S(1)} %bitcast.111), kind=kOutput, calls=%fused_computation.46 | convolution fusion | flops 3222011904 | bytes 8912896 | tf_op jit(solution)/shard_map/td,eth->edh/dot_general | solution.py:194
  208.5 3.3 %collective-permute-done.18 = bf16[256,1024]{1,0:T(8,128)(2,1)S(1)} collective-permute-done((bf16[256,1024]{1,0:T(8,128)(2,1)S(1)}, bf16[256,1024]{1,0:T(8,128)(2,1)S(1)}, u32[]{:S(2)}, u32[]{:S(2)}) %collective-permute-start.18) | collective-permute-done | bytes 524320 | tf_op jit(solution)/shard_map/ppermute | solution.py:50
  211.9 2.2 add_convert_fusion.1
  214.1 1.5 collective-permute-start.20
  215.5 7.6 %collective-permute-done.25 = bf16[256,1024]{1,0:T(8,128)(2,1)S(1)} collective-permute-done((bf16[256,1024]{1,0:T(8,128)(2,1)S(1)}, bf16[256,1024]{1,0:T(8,128)(2,1)S(1)}, u32[]{:S(2)}, u32[]{:S(2)}) %collective-permute-start.25) | collective-permute-done | bytes 524320 | tf_op jit(solution)/shard_map/ppermute | solution.py:50
  223.1 2.2 fusion.32
  225.3 1.5 collective-permute-start.27
  226.8 4.5 %fusion.30 = bf16[1,2,1024,384]{2,3,1,0:T(8,128)(2,1)} fusion(bf16[2,2048,384]{2,1,0:T(8,128)(2,1)S(1)} %copy-done.7, bf16[2048,1024,1]{1,0,2:T(8,128)(2,1)S(1)} %bitcast.112), kind=kOutput, calls=%fused_computation.45 | convolution fusion | flops 3222011904 | bytes 8912896 | tf_op jit(solution)/shard_map/td,eth->edh/dot_general | solution.py:191
  231.3 2.6 %copy.37 = bf16[1,2,1024,384]{3,2,1,0:T(8,128)(2,1)} copy(bf16[1,2,1024,384]{2,3,1,0:T(8,128)(2,1)} %fusion.30) | data formatting | bytes 3145728
  233.9 1.6 copy.38
  235.5 2.6 %add_convert_fusion = bf16[256,1024]{1,0:T(8,128)(2,1)} fusion(bf16[256,1024]{1,0:T(8,128)(2,1)} %collective-permute-done.20, bf16[256,1024]{1,0:T(8,128)(2,1)} %collective-permute-done.19, f32[2048,1024]{1,0:T(8,128)} %copy-done.1), kind=kLoop, calls=%fused_computation.61 | loop fusion | flops 1310720 | bytes 2621440 | tf_op jit(solution)/shard_map/convert_element_type | solution.py:235
  238.0 2.5 %fusion.38 = bf16[256,1024]{1,0:T(8,128)(2,1)} fusion(f32[2048,1024]{1,0:T(8,128)} %reduce-precision_reduce_fusion, bf16[256,1024]{1,0:T(8,128)(2,1)} %collective-permute-done.27, bf16[256,1024]{1,0:T(8,128)(2,1)} %collective-permute-done.26), kind=kLoop, calls=%fused_computation.59 | loop fusion | flops 1310720 | bytes 2621440 | tf_op jit(solution)/shard_map/convert_element_type | solution.py:236
  (86 shorter events, 15.6 us)
Async XLA Ops:
  0.6 77.1 %copy-start = (bf16[1,2,1024,384]{3,2,1,0:T(8,128)(2,1)S(1)}, bf16[1,2,1024,384]{3,2,1,0:T(8,128)(2,1)}, u32[]{:S(2)}) copy-start(bf16[1,2,1024,384]{3,2,1,0:T(8,128)(2,1)} %param.14) | copy-start | bytes 4718596
  0.6 60.7 %copy-start.8 = (bf16[256,1024]{1,0:T(8,128)(2,1)S(1)}, bf16[256,1024]{1,0:T(8,128)(2,1)}, u32[]{:S(2)}) copy-start(bf16[256,1024]{1,0:T(8,128)(2,1)} %param.10) | copy-start | bytes 1572868
  3.6 61.2 %copy-start.11 = (bf16[256,1024]{1,0:T(8,128)(2,1)S(1)}, bf16[256,1024]{1,0:T(8,128)(2,1)}, u32[]{:S(2)}) copy-start(bf16[256,1024]{1,0:T(8,128)(2,1)} %param.11) | copy-start | bytes 1572868
  3.6 15.3 %collective-permute-start = (bf16[1,264,1024]{2,1,0:T(8,128)(2,1)S(1)}, bf16[1,264,1024]{2,1,0:T(8,128)(2,1)S(1)}, u32[]{:S(2)}, u32[]{:S(2)}) collective-permute-start(bf16[1,264,1024]{2,1,0:T(8,128)(2,1)S(1)} %maximum_bitcast_fusion), channel_id=1, source_target_pairs={{0,2},{2,4},{4,6},{6,7},{7,5},{5,3},{3,1},{1,0},{8,10},{10,12},{12... | collective-permute-start | bytes 1622024 | tf_op jit(solution)/shard_map/ppermute | solution.py:50
  6.7 13.7 %collective-permute-start.1 = (bf16[1,264,1024]{2,1,0:T(8,128)(2,1)S(1)}, bf16[1,264,1024]{2,1,0:T(8,128)(2,1)S(1)}, u32[]{:S(2)}, u32[]{:S(2)}) collective-permute-start(bf16[1,264,1024]{2,1,0:T(8,128)(2,1)S(1)} %maximum_bitcast_fusion), channel_id=1, source_target_pairs={{0,1},{2,0},{4,2},{6,4},{7,6},{5,7},{3,5},{1,3},{8,9},{10,8},{12,1... | collective-permute-start | bytes 1622024 | tf_op jit(solution)/shard_map/ppermute | solution.py:51
  20.4 12.8 %collective-permute-start.2 = (bf16[1,264,1024]{2,1,0:T(8,128)(2,1)S(1)}, bf16[1,264,1024]{2,1,0:T(8,128)(2,1)S(1)}, u32[]{:S(2)}, u32[]{:S(2)}) collective-permute-start(bf16[1,264,1024]{2,1,0:T(8,128)(2,1)S(1)} %collective-permute-done), channel_id=1, source_target_pairs={{0,2},{2,4},{4,6},{6,7},{7,5},{5,3},{3,1},{1,0},{8,10},{10,12},{12... | collective-permute-start | bytes 1622024 | tf_op jit(solution)/shard_map/ppermute | solution.py:50
  22.0 12.5 %collective-permute-start.3 = (bf16[1,264,1024]{2,1,0:T(8,128)(2,1)S(1)}, bf16[1,264,1024]{2,1,0:T(8,128)(2,1)S(1)}, u32[]{:S(2)}, u32[]{:S(2)}) collective-permute-start(bf16[1,264,1024]{2,1,0:T(8,128)(2,1)S(1)} %collective-permute-done.1), channel_id=1, source_target_pairs={{0,1},{2,0},{4,2},{6,4},{7,6},{5,7},{3,5},{1,3},{8,9},{10,8},{12,1... | collective-permute-start | bytes 1622024 | tf_op jit(solution)/shard_map/ppermute | solution.py:51
  34.5 11.6 %collective-permute-start.4 = (bf16[1,264,1024]{2,1,0:T(8,128)(2,1)S(1)}, bf16[1,264,1024]{2,1,0:T(8,128)(2,1)S(1)}, u32[]{:S(2)}, u32[]{:S(2)}) collective-permute-start(bf16[1,264,1024]{2,1,0:T(8,128)(2,1)S(1)} %collective-permute-done.2), channel_id=1, source_target_pairs={{0,2},{2,4},{4,6},{6,7},{7,5},{5,3},{3,1},{1,0},{8,10},{10,12},{12... | collective-permute-start | bytes 1622024 | tf_op jit(solution)/shard_map/ppermute | solution.py:50
  36.1 11.3 %collective-permute-start.5 = (bf16[1,264,1024]{2,1,0:T(8,128)(2,1)S(1)}, bf16[1,264,1024]{2,1,0:T(8,128)(2,1)S(1)}, u32[]{:S(2)}, u32[]{:S(2)}) collective-permute-start(bf16[1,264,1024]{2,1,0:T(8,128)(2,1)S(1)} %collective-permute-done.3), channel_id=1, source_target_pairs={{0,1},{2,0},{4,2},{6,4},{7,6},{5,7},{3,5},{1,3},{8,9},{10,8},{12,1... | collective-permute-start | bytes 1622024 | tf_op jit(solution)/shard_map/ppermute | solution.py:51
  47.4 10.4 %collective-permute-start.6 = (bf16[1,264,1024]{2,1,0:T(8,128)(2,1)S(1)}, bf16[1,264,1024]{2,1,0:T(8,128)(2,1)S(1)}, u32[]{:S(2)}, u32[]{:S(2)}) collective-permute-start(bf16[1,264,1024]{2,1,0:T(8,128)(2,1)S(1)} %collective-permute-done.4), channel_id=1, source_target_pairs={{0,2},{2,4},{4,6},{6,7},{7,5},{5,3},{3,1},{1,0},{8,10},{10,12},{12... | collective-permute-start | bytes 1622024 | tf_op jit(solution)/shard_map/ppermute | solution.py:46
  64.7 9.2 %collective-permute-start.7 = (bf16[256,1024]{1,0:T(8,128)(2,1)S(1)}, bf16[256,1024]{1,0:T(8,128)(2,1)S(1)}, u32[]{:S(2)}, u32[]{:S(2)}) collective-permute-start(bf16[256,1024]{1,0:T(8,128)(2,1)S(1)} %copy-done.11), channel_id=1, source_target_pairs={{0,2},{2,4},{4,6},{6,7},{7,5},{5,3},{3,1},{1,0},{8,10},{10,12},{12... | collective-permute-start | bytes 1572872 | tf_op jit(solution)/shard_map/ppermute | solution.py:50
  66.2 9.5 %collective-permute-start.8 = (bf16[256,1024]{1,0:T(8,128)(2,1)S(1)}, bf16[256,1024]{1,0:T(8,128)(2,1)S(1)}, u32[]{:S(2)}, u32[]{:S(2)}) collective-permute-start(bf16[256,1024]{1,0:T(8,128)(2,1)S(1)} %copy-done.11), channel_id=1, source_target_pairs={{0,1},{2,0},{4,2},{6,4},{7,6},{5,7},{3,5},{1,3},{8,9},{10,8},{12,1... | collective-permute-start | bytes 1572872 | tf_op jit(solution)/shard_map/ppermute | solution.py:51
  66.7 114.2 %collective-permute-start.29 = (bf16[1,2,384,1024]{3,2,1,0:T(8,128)(2,1)}, bf16[1,2,384,1024]{3,2,1,0:T(8,128)(2,1)}, u32[]{:S(2)}, u32[]{:S(2)}) collective-permute-start(bf16[1,2,384,1024]{3,2,1,0:T(8,128)(2,1)} %param.16), channel_id=1, source_target_pairs={{0,8},{8,16},{16,24},{24,0},{1,9},{9,17},{17,25},{25,1},{2,10},{10... | collective-permute-start | bytes 4718600 | tf_op jit(solution)/shard_map/ppermute | solution.py:21
  66.7 114.8 %collective-permute-start.28 = (bf16[1,2,384,1024]{3,2,1,0:T(8,128)(2,1)}, bf16[1,2,384,1024]{3,2,1,0:T(8,128)(2,1)}, u32[]{:S(2)}, u32[]{:S(2)}) collective-permute-start(bf16[1,2,384,1024]{3,2,1,0:T(8,128)(2,1)} %param.16), channel_id=1, source_target_pairs={{0,16},{8,24},{16,0},{24,8},{1,17},{9,25},{17,1},{25,9},{2,18},{10... | collective-permute-start | bytes 4718600 | tf_op jit(solution)/shard_map/ppermute | solution.py:21
  70.9 18.8 %copy-start.3 = (bf16[8,256,1024]{2,1,0:T(8,128)(2,1)}, bf16[8,256,1024]{2,1,0:T(8,128)(2,1)S(1)}, u32[]{:S(2)}) copy-start(bf16[8,256,1024]{2,1,0:T(8,128)(2,1)S(1)} %slice.98) | copy-start | bytes 12582916
  73.9 7.4 %copy-start.15 = (bf16[256,1024]{1,0:T(8,128)(2,1)}, bf16[256,1024]{1,0:T(8,128)(2,1)S(1)}, u32[]{:S(2)}) copy-start(bf16[256,1024]{1,0:T(8,128)(2,1)S(1)} %collective-permute-done.7) | copy-start | bytes 1572868
  75.7 5.6 %copy-start.13 = (bf16[256,1024]{1,0:T(8,128)(2,1)}, bf16[256,1024]{1,0:T(8,128)(2,1)S(1)}, u32[]{:S(2)}) copy-start(bf16[256,1024]{1,0:T(8,128)(2,1)S(1)} %collective-permute-done.8) | copy-start | bytes 1572868
  75.7 10.6 %collective-permute-start.9 = (bf16[256,1024]{1,0:T(8,128)(2,1)S(1)}, bf16[256,1024]{1,0:T(8,128)(2,1)}, u32[]{:S(2)}, u32[]{:S(2)}) collective-permute-start(bf16[256,1024]{1,0:T(8,128)(2,1)S(1)} %collective-permute-done.7), channel_id=1, source_target_pairs={{0,2},{2,4},{4,6},{6,7},{7,5},{5,3},{3,1},{1,0},{8,10},{10,12},{12... | collective-permute-start | bytes 1572872 | tf_op jit(solution)/shard_map/ppermute | solution.py:50
  77.7 9.7 %collective-permute-start.10 = (bf16[256,1024]{1,0:T(8,128)(2,1)S(1)}, bf16[256,1024]{1,0:T(8,128)(2,1)}, u32[]{:S(2)}, u32[]{:S(2)}) collective-permute-start(bf16[256,1024]{1,0:T(8,128)(2,1)S(1)} %collective-permute-done.8), channel_id=1, source_target_pairs={{0,1},{2,0},{4,2},{6,4},{7,6},{5,7},{3,5},{1,3},{8,9},{10,8},{12,1... | collective-permute-start | bytes 1572872 | tf_op jit(solution)/shard_map/ppermute | solution.py:51
  77.8 12.0 %copy-start.9 = (bf16[1,2,1024,384]{3,2,1,0:T(8,128)(2,1)S(1)}, bf16[1,2,1024,384]{3,2,1,0:T(8,128)(2,1)}, u32[]{:S(2)}) copy-start(bf16[1,2,1024,384]{3,2,1,0:T(8,128)(2,1)} %param.15) | copy-start | bytes 4718596
  81.3 14.8 %copy-start.17 = (f32[2048,2,384]{2,0,1:T(8,128)}, f32[2048,2,384]{2,0,1:T(8,128)S(1)}, u32[]{:S(2)}) copy-start(f32[2048,2,384]{2,0,1:T(8,128)S(1)} %fusion.27) | copy-start | bytes 18874372
  87.5 11.2 %collective-permute-start.11 = (bf16[256,1024]{1,0:T(8,128)(2,1)}, bf16[256,1024]{1,0:T(8,128)(2,1)}, u32[]{:S(2)}, u32[]{:S(2)}) collective-permute-start(bf16[256,1024]{1,0:T(8,128)(2,1)} %collective-permute-done.9), channel_id=1, source_target_pairs={{0,2},{2,4},{4,6},{6,7},{7,5},{5,3},{3,1},{1,0},{8,10},{10,12},{12... | collective-permute-start | bytes 1572872 | tf_op jit(solution)/shard_map/ppermute | solution.py:50
  89.7 9.5 %collective-permute-start.12 = (bf16[256,1024]{1,0:T(8,128)(2,1)}, bf16[256,1024]{1,0:T(8,128)(2,1)}, u32[]{:S(2)}, u32[]{:S(2)}) collective-permute-start(bf16[256,1024]{1,0:T(8,128)(2,1)} %collective-permute-done.10), channel_id=1, source_target_pairs={{0,1},{2,0},{4,2},{6,4},{7,6},{5,7},{3,5},{1,3},{8,9},{10,8},{12,1... | collective-permute-start | bytes 1572872 | tf_op jit(solution)/shard_map/ppermute | solution.py:51
  99.2 10.4 %collective-permute-start.13 = (bf16[256,1024]{1,0:T(8,128)(2,1)}, bf16[256,1024]{1,0:T(8,128)(2,1)S(1)}, u32[]{:S(2)}, u32[]{:S(2)}) collective-permute-start(bf16[256,1024]{1,0:T(8,128)(2,1)} %collective-permute-done.11), channel_id=1, source_target_pairs={{0,2},{2,4},{4,6},{6,7},{7,5},{5,3},{3,1},{1,0},{8,10},{10,12},{12... | collective-permute-start | bytes 1572872 | tf_op jit(solution)/shard_map/ppermute | solution.py:46
  101.2 11.7 %copy-start.16 = (bf16[256,1024]{1,0:T(8,128)(2,1)S(1)}, bf16[256,1024]{1,0:T(8,128)(2,1)}, u32[]{:S(2)}) copy-start(bf16[256,1024]{1,0:T(8,128)(2,1)} %copy-done.15) | copy-start | bytes 1572868
  109.5 6.7 %copy-start.1 = (f32[2048,1024]{1,0:T(8,128)}, f32[2048,1024]{1,0:T(8,128)S(1)}, u32[]{:S(2)}) copy-start(f32[2048,1024]{1,0:T(8,128)S(1)} %multiply_reduce_fusion) | copy-start | bytes 25165828
  109.6 3.4 %copy-start.12 = (bf16[256,1024]{1,0:T(8,128)(2,1)S(1)}, bf16[256,1024]{1,0:T(8,128)(2,1)}, u32[]{:S(2)}) copy-start(bf16[256,1024]{1,0:T(8,128)(2,1)} %param.11) | copy-start | bytes 1572868
  109.6 3.4 %copy-start.14 = (bf16[256,1024]{1,0:T(8,128)(2,1)S(1)}, bf16[256,1024]{1,0:T(8,128)(2,1)}, u32[]{:S(2)}) copy-start(bf16[256,1024]{1,0:T(8,128)(2,1)} %copy-done.13) | copy-start | bytes 1572868
  116.3 8.3 %copy-start.2 = (f32[2048,1024]{1,0:T(8,128)}, f32[2048,1024]{1,0:T(8,128)S(1)}, u32[]{:S(2)}) copy-start(f32[2048,1024]{1,0:T(8,128)S(1)} %convert_element_type.151) | copy-start | bytes 25165828
  122.5 40.2 %collective-permute-start.14 = (bf16[256,1024]{1,0:T(8,128)(2,1)}, bf16[256,1024]{1,0:T(8,128)(2,1)}, u32[]{:S(2)}, u32[]{:S(2)}) collective-permute-start(bf16[256,1024]{1,0:T(8,128)(2,1)} %get-tuple-element.84), channel_id=1, source_target_pairs={{0,2},{2,4},{4,6},{6,7},{7,5},{5,3},{3,1},{1,0},{8,10},{10,12},{12... | collective-permute-start | bytes 1572872 | tf_op jit(solution)/shard_map/ppermute | solution.py:50
  123.5 40.8 %collective-permute-start.15 = (bf16[256,1024]{1,0:T(8,128)(2,1)}, bf16[256,1024]{1,0:T(8,128)(2,1)}, u32[]{:S(2)}, u32[]{:S(2)}) collective-permute-start(bf16[256,1024]{1,0:T(8,128)(2,1)} %get-tuple-element.85), channel_id=1, source_target_pairs={{0,1},{2,0},{4,2},{6,4},{7,6},{5,7},{3,5},{1,3},{8,9},{10,8},{12,1... | collective-permute-start | bytes 1572872 | tf_op jit(solution)/shard_map/ppermute | solution.py:51
  135.6 8.2 %copy-start.6 = (bf16[2,2048,384]{2,1,0:T(8,128)(2,1)}, bf16[2,2048,384]{2,1,0:T(8,128)(2,1)S(1)}, u32[]{:S(2)}) copy-start(bf16[2,2048,384]{2,1,0:T(8,128)(2,1)S(1)} %get-tuple-element.131) | copy-start | bytes 9437188
  135.6 8.2 %copy-start.10 = (bf16[1,2,1024,384]{3,2,1,0:T(8,128)(2,1)S(1)}, bf16[1,2,1024,384]{3,2,1,0:T(8,128)(2,1)}, u32[]{:S(2)}) copy-start(bf16[1,2,1024,384]{3,2,1,0:T(8,128)(2,1)} %param.15) | copy-start | bytes 4718596
  161.6 14.9 %collective-permute-start.21 = (bf16[256,1024]{1,0:T(8,128)(2,1)S(1)}, bf16[256,1024]{1,0:T(8,128)(2,1)S(1)}, u32[]{:S(2)}, u32[]{:S(2)}) collective-permute-start(bf16[256,1024]{1,0:T(8,128)(2,1)S(1)} %get-tuple-element.97), channel_id=1, source_target_pairs={{0,2},{2,4},{4,6},{6,7},{7,5},{5,3},{3,1},{1,0},{8,10},{10,12},{12... | collective-permute-start | bytes 1572872 | tf_op jit(solution)/shard_map/ppermute | solution.py:50
  162.7 14.8 %collective-permute-start.22 = (bf16[256,1024]{1,0:T(8,128)(2,1)S(1)}, bf16[256,1024]{1,0:T(8,128)(2,1)S(1)}, u32[]{:S(2)}, u32[]{:S(2)}) collective-permute-start(bf16[256,1024]{1,0:T(8,128)(2,1)S(1)} %get-tuple-element.98), channel_id=1, source_target_pairs={{0,1},{2,0},{4,2},{6,4},{7,6},{5,7},{3,5},{1,3},{8,9},{10,8},{12,1... | collective-permute-start | bytes 1572872 | tf_op jit(solution)/shard_map/ppermute | solution.py:51
  166.6 28.3 %collective-permute-start.16 = (bf16[256,1024]{1,0:T(8,128)(2,1)S(1)}, bf16[256,1024]{1,0:T(8,128)(2,1)S(1)}, u32[]{:S(2)}, u32[]{:S(2)}) collective-permute-start(bf16[256,1024]{1,0:T(8,128)(2,1)S(1)} %get-tuple-element.88), channel_id=1, source_target_pairs={{0,2},{2,4},{4,6},{6,7},{7,5},{5,3},{3,1},{1,0},{8,10},{10,12},{12... | collective-permute-start | bytes 1572872 | tf_op jit(solution)/shard_map/ppermute | solution.py:50
  176.6 18.3 %collective-permute-start.17 = (bf16[256,1024]{1,0:T(8,128)(2,1)S(1)}, bf16[256,1024]{1,0:T(8,128)(2,1)S(1)}, u32[]{:S(2)}, u32[]{:S(2)}) collective-permute-start(bf16[256,1024]{1,0:T(8,128)(2,1)S(1)} %get-tuple-element.89), channel_id=1, source_target_pairs={{0,1},{2,0},{4,2},{6,4},{7,6},{5,7},{3,5},{1,3},{8,9},{10,8},{12,1... | collective-permute-start | bytes 1572872 | tf_op jit(solution)/shard_map/ppermute | solution.py:51
  179.5 19.6 %collective-permute-start.23 = (bf16[256,1024]{1,0:T(8,128)(2,1)S(1)}, bf16[256,1024]{1,0:T(8,128)(2,1)S(1)}, u32[]{:S(2)}, u32[]{:S(2)}) collective-permute-start(bf16[256,1024]{1,0:T(8,128)(2,1)S(1)} %get-tuple-element.101), channel_id=1, source_target_pairs={{0,2},{2,4},{4,6},{6,7},{7,5},{5,3},{3,1},{1,0},{8,10},{10,12},{12... | collective-permute-start | bytes 1572872 | tf_op jit(solution)/shard_map/ppermute | solution.py:50
  181.0 20.0 %collective-permute-start.24 = (bf16[256,1024]{1,0:T(8,128)(2,1)S(1)}, bf16[256,1024]{1,0:T(8,128)(2,1)S(1)}, u32[]{:S(2)}, u32[]{:S(2)}) collective-permute-start(bf16[256,1024]{1,0:T(8,128)(2,1)S(1)} %get-tuple-element.102), channel_id=1, source_target_pairs={{0,1},{2,0},{4,2},{6,4},{7,6},{5,7},{3,5},{1,3},{8,9},{10,8},{12,1... | collective-permute-start | bytes 1572872 | tf_op jit(solution)/shard_map/ppermute | solution.py:51
  194.8 10.1 %copy-start.4 = (bf16[8,256,1024]{2,1,0:T(8,128)(2,1)S(1)}, bf16[8,256,1024]{2,1,0:T(8,128)(2,1)}, u32[]{:S(2)}) copy-start(bf16[8,256,1024]{2,1,0:T(8,128)(2,1)} %copy-done.3) | copy-start | bytes 12582916
  194.8 10.1 %copy-start.5 = (bf16[2,2048,384]{2,1,0:T(8,128)(2,1)S(1)}, bf16[2,2048,384]{2,1,0:T(8,128)(2,1)}, u32[]{:S(2)}) copy-start(bf16[2,2048,384]{2,1,0:T(8,128)(2,1)} %get-tuple-element.130) | copy-start | bytes 9437188
  197.0 14.9 %collective-permute-start.18 = (bf16[256,1024]{1,0:T(8,128)(2,1)S(1)}, bf16[256,1024]{1,0:T(8,128)(2,1)S(1)}, u32[]{:S(2)}, u32[]{:S(2)}) collective-permute-start(bf16[256,1024]{1,0:T(8,128)(2,1)S(1)} %get-tuple-element.92), channel_id=1, source_target_pairs={{0,2},{2,4},{4,6},{6,7},{7,5},{5,3},{3,1},{1,0},{8,10},{10,12},{12... | collective-permute-start | bytes 1572872 | tf_op jit(solution)/shard_map/ppermute | solution.py:50
  198.5 13.4 %collective-permute-start.19 = (bf16[256,1024]{1,0:T(8,128)(2,1)S(1)}, bf16[256,1024]{1,0:T(8,128)(2,1)}, u32[]{:S(2)}, u32[]{:S(2)}) collective-permute-start(bf16[256,1024]{1,0:T(8,128)(2,1)S(1)} %get-tuple-element.93), channel_id=1, source_target_pairs={{0,1},{2,0},{4,2},{6,4},{7,6},{5,7},{3,5},{1,3},{8,9},{10,8},{12,1... | collective-permute-start | bytes 1572872 | tf_op jit(solution)/shard_map/ppermute | solution.py:51
  202.9 20.2 %collective-permute-start.25 = (bf16[256,1024]{1,0:T(8,128)(2,1)S(1)}, bf16[256,1024]{1,0:T(8,128)(2,1)S(1)}, u32[]{:S(2)}, u32[]{:S(2)}) collective-permute-start(bf16[256,1024]{1,0:T(8,128)(2,1)S(1)} %get-tuple-element.105), channel_id=1, source_target_pairs={{0,2},{2,4},{4,6},{6,7},{7,5},{5,3},{3,1},{1,0},{8,10},{10,12},{12... | collective-permute-start | bytes 1572872 | tf_op jit(solution)/shard_map/ppermute | solution.py:50
  204.1 19.0 %collective-permute-start.26 = (bf16[256,1024]{1,0:T(8,128)(2,1)S(1)}, bf16[256,1024]{1,0:T(8,128)(2,1)}, u32[]{:S(2)}, u32[]{:S(2)}) collective-permute-start(bf16[256,1024]{1,0:T(8,128)(2,1)S(1)} %get-tuple-element.106), channel_id=1, source_target_pairs={{0,1},{2,0},{4,2},{6,4},{7,6},{5,7},{3,5},{1,3},{8,9},{10,8},{12,1... | collective-permute-start | bytes 1572872 | tf_op jit(solution)/shard_map/ppermute | solution.py:51
  208.5 18.3 %copy-start.7 = (bf16[2,2048,384]{2,1,0:T(8,128)(2,1)S(1)}, bf16[2,2048,384]{2,1,0:T(8,128)(2,1)}, u32[]{:S(2)}) copy-start(bf16[2,2048,384]{2,1,0:T(8,128)(2,1)} %copy-done.6) | copy-start | bytes 9437188
  214.1 21.4 %collective-permute-start.20 = (bf16[256,1024]{1,0:T(8,128)(2,1)}, bf16[256,1024]{1,0:T(8,128)(2,1)}, u32[]{:S(2)}, u32[]{:S(2)}) collective-permute-start(bf16[256,1024]{1,0:T(8,128)(2,1)} %add_convert_fusion.1), channel_id=1, source_target_pairs={{0,2},{2,4},{4,6},{6,7},{7,5},{5,3},{3,1},{1,0},{8,10},{10,12},{12... | collective-permute-start | bytes 1572872 | tf_op jit(solution)/shard_map/ppermute | solution.py:46
  225.3 12.7 %collective-permute-start.27 = (bf16[256,1024]{1,0:T(8,128)(2,1)}, bf16[256,1024]{1,0:T(8,128)(2,1)}, u32[]{:S(2)}, u32[]{:S(2)}) collective-permute-start(bf16[256,1024]{1,0:T(8,128)(2,1)} %fusion.32), channel_id=1, source_target_pairs={{0,2},{2,4},{4,6},{6,7},{7,5},{5,3},{3,1},{1,0},{8,10},{10,12},{12... | collective-permute-start | bytes 1572872 | tf_op jit(solution)/shard_map/ppermute | solution.py:46

commit v7 on v5

--- a/solution.py
+++ b/solution.py
@@ -6,6 +6,7 @@
 ROUNDS = 2
 CHUNK_ROWS = 2048
 RING_MAX = 8
+SLICES = 2
 
 
 beta_one = 0.9
@@ -123,14 +124,6 @@
     experts = local_experts * devices_exp
     my_exp = lax.axis_index("exp")
 
-    token_count, model_width = tokens.shape
-    weight_table = dense_weights(expert_ids, combine, experts)
-    weight_rows = -(-(token_count * experts) // model_width)
-    weight_rows = -(-weight_rows // 8) * 8
-    weight_flat = jnp.pad(
-        weight_table.reshape(-1), (0, weight_rows * model_width - token_count * experts)
-    )
-    packed_tokens = jnp.concatenate([tokens, weight_flat.reshape(weight_rows, model_width)])
     ring = ring_order(devices_exp)
     use_ring = devices_exp <= RING_MAX
 
@@ -144,95 +137,123 @@
             return ring_reduce_scatter(value, "exp", ring, jnp.bfloat16)
         return lax.psum_scatter(value, "exp", scatter_dimension=0, tiled=True)
 
-    gathered = gather(packed_tokens[None])
-    group_tokens = gathered[:, :token_count].reshape(devices_exp * token_count, model_width)
-    group_weight = (
-        gathered[:, token_count:]
-        .reshape(devices_exp, -1)[:, : token_count * experts]
-        .reshape(devices_exp * token_count, experts)
-    )
-    _, cotangent = lax.optimization_barrier((gathered, cotangent))
-    group_cot = gather(cotangent)
-    local_weight = lax.dynamic_slice_in_dim(
-        group_weight, my_exp * local_experts, local_experts, axis=1
-    ).astype(jnp.float32)
-    local_weight = jnp.transpose(local_weight)[:, :, None]
-
     gate_matrix = gate_weight[0]
     up_matrix = up_weight[0]
     down_matrix = down_weight[0]
 
-    def chunk_pass(chunk_tokens, chunk_cot, chunk_weight):
-        gate_value = jnp.einsum(
-            "td,edh->eth", chunk_tokens, gate_matrix, preferred_element_type=jnp.float32
-        )
-        up_value = jnp.einsum(
-            "td,edh->eth", chunk_tokens, up_matrix, preferred_element_type=jnp.float32
-        )
-        sigmoid_gate = jax.nn.sigmoid(gate_value)
-        active = gate_value * sigmoid_gate
-        hidden = (active * up_value).astype(jnp.bfloat16)
-        expert_out = as_bf16(
-            jnp.einsum("eth,ehd->etd", hidden, down_matrix, preferred_element_type=jnp.float32)
-        )
-        mixed_part = jnp.sum(chunk_weight * expert_out, axis=0)
-        slot_cot = (chunk_weight * chunk_cot.astype(jnp.float32)[None]).astype(jnp.bfloat16)
-        hidden_cot = jnp.einsum(
-            "etd,ehd->eth", slot_cot, down_matrix, preferred_element_type=jnp.float32
-        )
-        gate_cot = (
-            hidden_cot * up_value * sigmoid_gate * (1.0 + gate_value * (1.0 - sigmoid_gate))
-        ).astype(jnp.bfloat16)
-        up_cot = (hidden_cot * active).astype(jnp.bfloat16)
-        down_grad = jnp.einsum(
-            "eth,etd->ehd", hidden, slot_cot, preferred_element_type=jnp.float32
-        )
-        gate_grad = jnp.einsum(
-            "td,eth->edh", chunk_tokens, gate_cot, preferred_element_type=jnp.float32
-        )
-        up_grad = jnp.einsum(
-            "td,eth->edh", chunk_tokens, up_cot, preferred_element_type=jnp.float32
-        )
-        input_cot = as_bf16(
-            jnp.einsum("eth,edh->etd", gate_cot, gate_matrix, preferred_element_type=jnp.float32)
-            + jnp.einsum("eth,edh->etd", up_cot, up_matrix, preferred_element_type=jnp.float32)
-        )
-        input_part = jnp.sum(input_cot, axis=0)
-        return mixed_part, input_part, gate_grad, up_grad, down_grad
-
-    group_count = group_tokens.shape[0]
-    chunk = min(group_count, CHUNK_ROWS)
-    chunks = group_count // chunk
-    if chunks == 1:
-        mixed_part, input_part, gate_grad, up_grad, down_grad = chunk_pass(
-            group_tokens, group_cot, local_weight
-        )
-    else:
-
-        def step(carry, packed):
-            parts = chunk_pass(*packed)
-            grads = tuple(acc + part for acc, part in zip(carry, parts[2:]))
-            return grads, parts[:2]
-
-        zeros = (
-            jnp.zeros(gate_matrix.shape, jnp.float32),
-            jnp.zeros(up_matrix.shape, jnp.float32),
-            jnp.zeros(down_matrix.shape, jnp.float32),
-        )
-        packed = (
-            group_tokens.reshape(chunks, chunk, -1),
-            group_cot.reshape(chunks, chunk, -1),
-            jnp.transpose(local_weight.reshape(local_experts, chunks, chunk, 1), (1, 0, 2, 3)),
-        )
-        (gate_grad, up_grad, down_grad), (mixed_parts, input_parts) = lax.scan(
-            step, zeros, packed
-        )
-        mixed_part = mixed_parts.reshape(group_count, -1)
-        input_part = input_parts.reshape(group_count, -1)
+    def token_slice(tokens, cotangent, expert_ids, combine):
+        token_count, model_width = tokens.shape
+        weight_table = dense_weights(expert_ids, combine, experts)
+        weight_rows = -(-(token_count * experts) // model_width)
+        weight_rows = -(-weight_rows // 8) * 8
+        weight_flat = jnp.pad(
+            weight_table.reshape(-1), (0, weight_rows * model_width - token_count * experts)
+        )
+        packed_tokens = jnp.concatenate([tokens, weight_flat.reshape(weight_rows, model_width)])
+        gathered = gather(packed_tokens[None])
+        group_tokens = gathered[:, :token_count].reshape(devices_exp * token_count, model_width)
+        group_weight = (
+            gathered[:, token_count:]
+            .reshape(devices_exp, -1)[:, : token_count * experts]
+            .reshape(devices_exp * token_count, experts)
+        )
+        _, cotangent = lax.optimization_barrier((gathered, cotangent))
+        group_cot = gather(cotangent)
+        local_weight = lax.dynamic_slice_in_dim(
+            group_weight, my_exp * local_experts, local_experts, axis=1
+        ).astype(jnp.float32)
+        local_weight = jnp.transpose(local_weight)[:, :, None]
+
+        def chunk_pass(chunk_tokens, chunk_cot, chunk_weight):
+            gate_value = jnp.einsum(
+                "td,edh->eth", chunk_tokens, gate_matrix, preferred_element_type=jnp.float32
+            )
+            up_value = jnp.einsum(
+                "td,edh->eth", chunk_tokens, up_matrix, preferred_element_type=jnp.float32
+            )
+            sigmoid_gate = jax.nn.sigmoid(gate_value)
+            active = gate_value * sigmoid_gate
+            hidden = (active * up_value).astype(jnp.bfloat16)
+            expert_out = as_bf16(
+                jnp.einsum("eth,ehd->etd", hidden, down_matrix, preferred_element_type=jnp.float32)
+            )
+            mixed_part = jnp.sum(chunk_weight * expert_out, axis=0)
+            chunk_cot, mixed_part = lax.optimization_barrier((chunk_cot, mixed_part))
+            slot_cot = (chunk_weight * chunk_cot.astype(jnp.float32)[None]).astype(jnp.bfloat16)
+            hidden_cot = jnp.einsum(
+                "etd,ehd->eth", slot_cot, down_matrix, preferred_element_type=jnp.float32
+            )
+            gate_cot = (
+                hidden_cot * up_value * sigmoid_gate * (1.0 + gate_value * (1.0 - sigmoid_gate))
+            ).astype(jnp.bfloat16)
+            up_cot = (hidden_cot * active).astype(jnp.bfloat16)
+            down_grad = jnp.einsum(
+                "eth,etd->ehd", hidden, slot_cot, preferred_element_type=jnp.float32
+            )
+            gate_grad = jnp.einsum(
+                "td,eth->edh", chunk_tokens, gate_cot, preferred_element_type=jnp.float32
+            )
+            up_grad = jnp.einsum(
+                "td,eth->edh", chunk_tokens, up_cot, preferred_element_type=jnp.float32
+            )
+            input_cot = as_bf16(
+                jnp.einsum("eth,edh->etd", gate_cot, gate_matrix, preferred_element_type=jnp.float32)
+                + jnp.einsum("eth,edh->etd", up_cot, up_matrix, preferred_element_type=jnp.float32)
+            )
+            input_part = jnp.sum(input_cot, axis=0)
+            return mixed_part, input_part, gate_grad, up_grad, down_grad
+
+        group_count = group_tokens.shape[0]
+        chunk = min(group_count, CHUNK_ROWS)
+        chunks = group_count // chunk
+        if chunks == 1:
+            mixed_part, input_part, gate_grad, up_grad, down_grad = chunk_pass(
+                group_tokens, group_cot, local_weight
+            )
+        else:
+
+            def step(carry, packed):
+                parts = chunk_pass(*packed)
+                grads = tuple(acc + part for acc, part in zip(carry, parts[2:]))
+                return grads, parts[:2]
+
+            zeros = (
+                jnp.zeros(gate_matrix.shape, jnp.float32),
+                jnp.zeros(up_matrix.shape, jnp.float32),
+                jnp.zeros(down_matrix.shape, jnp.float32),
+            )
+            packed = (
+                group_tokens.reshape(chunks, chunk, -1),
+                group_cot.reshape(chunks, chunk, -1),
+                jnp.transpose(local_weight.reshape(local_experts, chunks, chunk, 1), (1, 0, 2, 3)),
+            )
+            (gate_grad, up_grad, down_grad), (mixed_parts, input_parts) = lax.scan(
+                step, zeros, packed
+            )
+            mixed_part = mixed_parts.reshape(group_count, -1)
+            input_part = input_parts.reshape(group_count, -1)
+        mixed = reduce_scatter(mixed_part).astype(jnp.bfloat16)
+        input_grad = reduce_scatter(input_part).astype(jnp.bfloat16)
+        return mixed, input_grad, gate_grad, up_grad, down_grad
+
+    slices = SLICES if use_ring else 1
+    rows = tokens.shape[0] // slices
+    results = [
+        token_slice(
+            tokens[s * rows : (s + 1) * rows],
+            cotangent[s * rows : (s + 1) * rows],
+            expert_ids[s * rows : (s + 1) * rows],
+            combine[s * rows : (s + 1) * rows],
+        )
+        for s in range(slices)
+    ]
+    mixed = jnp.concatenate([r[0] for r in results])
+    input_grad = jnp.concatenate([r[1] for r in results])
+    gate_grad, up_grad, down_grad = results[0][2:]
+    for r in results[1:]:
+        gate_grad, up_grad, down_grad = gate_grad + r[2], up_grad + r[3], down_grad + r[4]
     gate_grad = gate_grad.astype(jnp.bfloat16)
     up_grad = up_grad.astype(jnp.bfloat16)
-    mixed = reduce_scatter(mixed_part).astype(jnp.bfloat16)
-    input_grad = reduce_scatter(input_part).astype(jnp.bfloat16)
 
     peers = [shifted(down_weight, "rep", 1 << bit_index) for bit_index in range(ROUNDS)]
     peer_down = peers[0]

time: 260 us -> 277 us (1.065); the launches traced: 260 us -> 272 us
  starting transfers between devices: 32.1 us -> 73.5 us
  waiting for transfers between devices: 96.3 us -> 77.4 us
  other arithmetic: 26.9 us -> 15.6 us
  matrix products: 77.1 us -> 74.3 us
    ppermute x12 -> x24, waiting for transfers between devices: 65.6 us -> 17.3 us  [paired_shift(): ahead_value = lax.ppermute(ahead_value, axis, ring_pairs(ring, 1))]
    ppermute x12 -> x24, starting transfers between devices: 18.6 us -> 50.3 us  [paired_shift(): ahead_value = lax.ppermute(ahead_value, axis, ring_pairs(ring, 1))]
    ppermute x12 -> x24, waiting for transfers between devices: 11.5 us -> 40.9 us  [paired_shift(): behind_value = lax.ppermute(behind_value, axis, ring_pairs(ring, -1))]
    ppermute x4 -> x8, starting transfers between devices: 5.2 us -> 12.7 us  [paired_shift(): return (lax.ppermute(ahead_value, axis, ring_pairs(ring, 1)), None)]
    dot_general x1 -> x2, matrix products: 13.7 us -> 7.86 us  [chunk_pass(): jnp.einsum('eth,edh->etd', up_cot, up_matrix, preferred_element_type=jnp....]
    convert_element_type x6 -> x12, other arithmetic: 12.4 us -> 8.43 us  [to_wire(): return value.astype(wire_dtype)]
    convert_element_type x2 -> x4, other arithmetic: 5.1 us -> 1.43 us  [the longest x2 1.24 us: token_slice(): mixed = reduce_scatter(mixed_part).astype(jnp.bfloat16)]
    another operation x2 -> x4, other arithmetic: 4.71 us -> 1.29 us
  transfers between devices with their start and end apart: 30 -> 58, of which waited for: 20 -> 31; matrix products, arithmetic and copies ran while one was open for 44% -> 40% of each run, Pallas kernels for 0% -> 0%
where the time goes in v7:
time: 277 us; the launch traced here: 272 us
  waiting for transfers between devices  77.4 us (28%)
  matrix products  74.3 us (27%)
  starting transfers between devices  73.5 us (27%)
  local copies, waits for them, and re-layouts  28.1 us (10%)
  other arithmetic  15.6 us (6%)
    ppermute x24, starting transfers between devices, paired_shift(): ahead_value = lax.ppermute(ahead_value, axis, ring_pairs(ring, 1))  50.3 us
    ppermute x24, waiting for transfers between devices, paired_shift(): behind_value = lax.ppermute(behind_value, axis, ring_pairs(ring, -1))  40.9 us
    unnamed x124, local copies, waits for them, and re-layouts  20.1 us
    ppermute x8, waiting for transfers between devices, paired_shift(): return (lax.ppermute(ahead_value, axis, ring_pairs(ring, 1)), None)  19.2 us
    ppermute x24, waiting for transfers between devices, paired_shift(): ahead_value = lax.ppermute(ahead_value, axis, ring_pairs(ring, 1))  17.3 us
    dot_general x2, matrix products, chunk_pass(): jnp.einsum('eth,etd->ehd', hidden, slot_cot, preferred_element_type=jnp.f...  14.4 us
    dot_general x2, matrix products, chunk_pass(): jnp.einsum('etd,ehd->eth', slot_cot, down_matrix, preferred_element_type=...  12.9 us
    ppermute x8, starting transfers between devices, paired_shift(): return (lax.ppermute(ahead_value, axis, ring_pairs(ring, 1)), None)  12.7 us
  transfers between devices with their start and end apart: 58, of which 31 were waited for; matrix products, arithmetic and copies ran while one was open for 40% of the time, Pallas kernels for 0%

profile of v7, /device:TPU:0, one launch (start us, length us, event | category | flops | bytes accessed | tf_op | source)
XLA Modules:
  0.0 271.5 jit_solution(11836350631601412979)
XLA Ops:
  4.3 3.0 %collective-permute-start.21 = (bf16[1,136,1024]{2,1,0:T(8,128)(2,1)}, bf16[1,136,1024]{2,1,0:T(8,128)(2,1)}, u32[]{:S(2)}, u32[]{:S(2)}) collective-permute-start(bf16[1,136,1024]{2,1,0:T(8,128)(2,1)} %maximum_bitcast_fusion.1), channel_id=1, source_target_pairs={{0,2},{2,4},{4,6},{6,7},{7,5},{5,3},{3,1},{1,0},{8,10},{10,12},{12... | collective-permute-start | bytes 835592 | tf_op jit(solution)/shard_map/ppermute | solution.py:51
  7.6 2.1 collective-permute-start
  9.7 5.3 %collective-permute-done.21 = bf16[1,136,1024]{2,1,0:T(8,128)(2,1)} collective-permute-done((bf16[1,136,1024]{2,1,0:T(8,128)(2,1)}, bf16[1,136,1024]{2,1,0:T(8,128)(2,1)}, u32[]{:S(2)}, u32[]{:S(2)}) %collective-permute-start.21) | collective-permute-done | bytes 278560 | tf_op jit(solution)/shard_map/ppermute | solution.py:51
  15.0 2.2 collective-permute-done.22
  19.2 1.7 collective-permute-done
  20.9 2.2 collective-permute-done.1
  25.1 1.9 collective-permute-done.23
  27.0 2.0 collective-permute-done.24
  31.1 2.0 collective-permute-done.2
  33.1 2.0 collective-permute-done.3
  37.1 1.9 collective-permute-done.25
  39.1 1.9 collective-permute-done.26
  47.2 3.8 %collective-permute-done.27 = bf16[1,136,1024]{2,1,0:T(8,128)(2,1)} collective-permute-done((bf16[1,136,1024]{2,1,0:T(8,128)(2,1)}, bf16[1,136,1024]{2,1,0:T(8,128)(2,1)}, u32[]{:S(2)}, u32[]{:S(2)}) %collective-permute-start.27) | collective-permute-done | bytes 278560 | tf_op jit(solution)/shard_map/ppermute | solution.py:47
  55.3 2.0 collective-permute-start.28
  61.7 2.0 collective-permute-start.7
  63.8 1.8 fusion.49
  65.6 1.8 fusion.51
  68.2 4.2 %fusion.18 = (bf16[2,1024,384]{2,1,0:T(8,128)(2,1)}, f32[1024,2,384]{2,0,1:T(8,128)}) fusion(f32[1024,2,384]{2,0,1:T(8,128)S(1)} %fusion.49, bf16[1024,1024,1]{1,0,2:T(8,128)(2,1)S(1)} %bitcast.185, bf16[1,2,1024,384]{3,2,1,0:T(8,128)(2,1)S(1)} %copy-done.12), kind=kOutput, calls=%fused_computation.30 | convolution fusion | flops 1615331328 | bytes 11534336 | tf_op jit(solution)/shard_map/td,edh->eth/dot_general | solution.py:171
  72.3 4.2 %fusion.26 = (bf16[2,1024,384]{2,1,0:T(8,128)(2,1)}, f32[1024,2,384]{2,0,1:T(8,128)}) fusion(f32[1024,2,384]{2,0,1:T(8,128)S(1)} %fusion.51, bf16[1024,1024,1]{1,0,2:T(8,128)(2,1)S(1)} %bitcast.181, bf16[1,2,1024,384]{3,2,1,0:T(8,128)(2,1)S(1)} %copy-done.12), kind=kOutput, calls=%fused_computation.43 | convolution fusion | flops 1615331328 | bytes 11534336 | tf_op jit(solution)/shard_map/td,edh->eth/dot_general | solution.py:171
  77.2 2.0 collective-permute-start.9
  80.8 2.0 collective-permute-start.30
  82.9 3.5 %collective-permute-done.9 = bf16[128,1024]{1,0:T(8,128)(2,1)} collective-permute-done((bf16[128,1024]{1,0:T(8,128)(2,1)S(1)}, bf16[128,1024]{1,0:T(8,128)(2,1)}, u32[]{:S(2)}, u32[]{:S(2)}) %collective-permute-start.9) | collective-permute-done | bytes 262176 | tf_op jit(solution)/shard_map/ppermute | solution.py:51
  86.5 2.1 collective-permute-done.10
  90.8 4.9 %multiply_reduce_fusion = f32[1024,1024]{1,0:T(8,128)S(1)} fusion(f32[2,1024]{1,0:T(2,128)S(1)} %copy.46, bf16[2,1024,384]{2,1,0:T(8,128)(2,1)} %get-tuple-element.271, bf16[1,2,384,1024]{3,2,1,0:T(8,128)(2,1)} %param.16), kind=kOutput, calls=%fused_computation.4 | convolution fusion | flops 1615855616 | bytes 7348224 | tf_op jit(solution)/shard_map/eth,ehd->etd/dot_general | solution.py:178
  95.8 1.6 collective-permute-start.32
  99.5 4.3 %multiply_reduce_fusion.1 = f32[1024,1024]{1,0:T(8,128)S(1)} fusion(f32[2,1024]{1,0:T(2,128)S(1)} %copy.44, bf16[2,1024,384]{2,1,0:T(8,128)(2,1)S(1)} %copy-done.39, bf16[1,2,384,1024]{3,2,1,0:T(8,128)(2,1)} %param.16), kind=kOutput, calls=%fused_computation.5 | convolution fusion | flops 1615855616 | bytes 7348224 | tf_op jit(solution)/shard_map/eth,ehd->etd/dot_general | solution.py:178
  104.5 1.8 collective-permute-done.33
  107.9 2.2 collective-permute-done.13
  112.7 3.7 %fusion = f32[2,384,1024]{2,1,0:T(8,128)} fusion(bf16[2,1024,384]{2,1,0:T(8,128)(2,1)S(1)} %copy-done.39, f32[1024,1024]{1,0:T(8,128)S(1)} %convert_element_type.277, f32[2,1024]{1,0:T(2,128)S(1)} %copy.44), kind=kOutput, calls=%fused_computation.6 | convolution fusion | flops 1614807040 | bytes 8921088 | tf_op jit(solution)/shard_map/eth,etd->ehd/dot_general | solution.py:190
  116.4 5.8 %multiply_convert_fusion.7 = (bf16[2,1024,384]{2,1,0:T(8,128)(2,1)}, bf16[2,1024,384]{2,1,0:T(8,128)(2,1)S(1)}) fusion(f32[1024,2,384]{2,0,1:T(8,128)S(1)} %copy-done.43, f32[1024,2,384]{2,0,1:T(8,128)S(1)} %copy-done.45, bf16[1,2,384,1024]{3,2,1,0:T(8,128)(2,1)} %param.16, f32[1024,1024]{1,0:T(8,128)S(1)} %convert_element_type.277, f32[2,1024]{1,0:T(2,128)S(1)} %copy.44), kind=kOutput, calls=%fused_computation.57 | convolution fusion | flops 1625030656 | bytes 15212544 | tf_op jit(solution)/shard_map/etd,ehd->eth/dot_general | solution.py:183
  122.2 2.4 fusion.47
  124.6 3.5 %fusion.79 = f32[2,384,1024]{2,1,0:T(8,128)} fusion(bf16[2,1024,384]{2,1,0:T(8,128)(2,1)S(1)} %get-tuple-element.236, bf16[1024,1024,1]{1,0,2:T(8,128)(2,1)S(1)} %bitcast.182), kind=kOutput, calls=%fused_computation.173 | convolution fusion | flops 1610612736 | bytes 6815744 | tf_op jit(solution)/shard_map/td,eth->edh/dot_general | solution.py:193
  134.6 9.8 %collective-permute-start.14 = (bf16[128,1024]{1,0:T(8,128)(2,1)}, bf16[128,1024]{1,0:T(8,128)(2,1)}, u32[]{:S(2)}, u32[]{:S(2)}) collective-permute-start(bf16[128,1024]{1,0:T(8,128)(2,1)} %get-tuple-element.135), channel_id=1, source_target_pairs={{0,2},{2,4},{4,6},{6,7},{7,5},{5,3},{3,1},{1,0},{8,10},{10,12},{12... | collective-permute-start | bytes 786440 | tf_op jit(solution)/shard_map/ppermute | solution.py:51
  144.9 7.0 %multiply_convert_fusion.6 = (bf16[2,1024,384]{2,1,0:T(8,128)(2,1)}, bf16[2,1024,384]{2,1,0:T(8,128)(2,1)S(1)}) fusion(f32[1024,2,384]{2,0,1:T(8,128)S(1)} %copy-done.41, f32[1024,2,384]{2,0,1:T(8,128)S(1)} %copy-done.44, bf16[1,2,384,1024]{3,2,1,0:T(8,128)(2,1)} %param.16, f32[1024,1024]{1,0:T(8,128)S(1)} %convert_element_type.294, f32[2,1024]{1,0:T(2,128)S(1)} %copy.46), kind=kOutput, calls=%fused_computation.56 | convolution fusion | flops 1625030656 | bytes 15212544 | tf_op jit(solution)/shard_map/etd,ehd->eth/dot_general | solution.py:183
  152.0 2.4 fusion.45
  154.4 5.1 %reduce-precision_reduce_fusion = f32[1024,1024]{1,0:T(8,128)S(1)} fusion(f32[2,1024,1024]{2,1,0:T(8,128)S(1)} %fusion.45, bf16[2,1024,384]{2,1,0:T(8,128)(2,1)} %get-tuple-element.237, bf16[1,2,1024,384]{3,2,1,0:T(8,128)(2,1)} %param.15), kind=kOutput, calls=%fused_computation | convolution fusion | flops 1615855616 | bytes 15728640 | tf_op jit(solution)/shard_map/eth,edh->etd/dot_general | solution.py:201
  159.9 1.8 copy-done.1
  163.3 3.5 %fusion.80 = f32[2,384,1024]{2,1,0:T(8,128)} fusion(bf16[2,1024,384]{2,1,0:T(8,128)(2,1)S(1)} %copy-done.11, bf16[1024,1024,1]{1,0,2:T(8,128)(2,1)S(1)} %bitcast.183), kind=kOutput, calls=%fused_computation.174 | convolution fusion | flops 1610612736 | bytes 6815744 | tf_op jit(solution)/shard_map/td,eth->edh/dot_general | solution.py:196
  166.8 3.1 %fusion.54 = bf16[1,2,1024,384]{2,3,1,0:T(8,128)(2,1)} fusion(f32[2,384,1024]{2,1,0:T(8,128)S(1)} %copy-done.16, bf16[2,1024,384]{2,1,0:T(8,128)(2,1)S(1)} %copy-done.24, bf16[1024,1024,1]{1,0,2:T(8,128)(2,1)S(1)} %bitcast.186), kind=kOutput, calls=%fused_computation.78 | convolution fusion | flops 1612185600 | bytes 8388608 | tf_op jit(solution)/shard_map/td,eth->edh/dot_general | solution.py:193
  169.9 2.8 %reduce-precision_reduce_fusion.1 = f32[1024,1024]{1,0:T(8,128)S(1)} fusion(f32[2,1024,1024]{2,1,0:T(8,128)S(1)} %fusion.47, bf16[2,1024,384]{2,1,0:T(8,128)(2,1)S(1)} %copy-done.11, bf16[1,2,1024,384]{3,2,1,0:T(8,128)(2,1)S(1)} %copy-done.13), kind=kOutput, calls=%fused_computation.2 | convolution fusion | flops 1615855616 | bytes 15728640 | tf_op jit(solution)/shard_map/eth,edh->etd/dot_general | solution.py:201
  173.2 1.8 collective-permute-start.49
  175.0 10.7 %fusion.57 = (f32[1,2,384,1024]{3,2,1,0:T(8,128)}, bf16[1,2,384,1024]{3,2,1,0:T(8,128)(2,1)}, f32[1,2,384,1024]{3,2,1,0:T(8,128)}) fusion(f32[1,2,384,1024]{3,2,1,0:T(8,128)} %param.18, f32[1,2,384,1024]{3,2,1,0:T(8,128)} %param.17, bf16[1,2,384,1024]{3,2,1,0:T(8,128)(2,1)} %collective-permute-done.56, ...), kind=kOutput, calls=%fused_computation.81 | convolution fusion | flops 1632108544 | bytes 27795456 | tf_op jit(solution)/shard_map/eth,etd->ehd/dot_general | solution.py:190
  185.7 3.1 %fusion.55 = bf16[1,2,1024,384]{2,3,1,0:T(8,128)(2,1)} fusion(f32[2,384,1024]{2,1,0:T(8,128)S(1)} %copy-done.17, bf16[2,1024,384]{2,1,0:T(8,128)(2,1)S(1)} %copy-done.25, bf16[1024,1024,1]{1,0,2:T(8,128)(2,1)S(1)} %bitcast.187), kind=kOutput, calls=%fused_computation.79 | convolution fusion | flops 1612185600 | bytes 8388608 | tf_op jit(solution)/shard_map/td,eth->edh/dot_general | solution.py:196
  192.0 2.6 copy.54
  195.1 1.6 collective-permute-start.42
  198.7 1.6 collective-permute-start.37
  207.0 2.4 collective-permute-done.43
  209.5 1.6 collective-permute-start.51
  212.9 2.2 collective-permute-done.38
  215.1 1.6 collective-permute-start.44
  217.3 3.4 %collective-permute-done.17 = bf16[128,1024]{1,0:T(8,128)(2,1)S(1)} collective-permute-done((bf16[128,1024]{1,0:T(8,128)(2,1)S(1)}, bf16[128,1024]{1,0:T(8,128)(2,1)S(1)}, u32[]{:S(2)}, u32[]{:S(2)}) %collective-permute-start.17) | collective-permute-done | bytes 262176 | tf_op jit(solution)/shard_map/ppermute | solution.py:52
  224.1 2.2 collective-permute-done.52
  226.3 1.6 collective-permute-start.18
  228.6 3.4 %collective-permute-done.45 = bf16[128,1024]{1,0:T(8,128)(2,1)S(1)} collective-permute-done((bf16[128,1024]{1,0:T(8,128)(2,1)S(1)}, bf16[128,1024]{1,0:T(8,128)(2,1)S(1)}, u32[]{:S(2)}, u32[]{:S(2)}) %collective-permute-start.45) | collective-permute-done | bytes 262176 | tf_op jit(solution)/shard_map/ppermute | solution.py:52
  234.2 3.4 %collective-permute-done.40 = bf16[128,1024]{1,0:T(8,128)(2,1)S(1)} collective-permute-done((bf16[128,1024]{1,0:T(8,128)(2,1)S(1)}, bf16[128,1024]{1,0:T(8,128)(2,1)S(1)}, u32[]{:S(2)}, u32[]{:S(2)}) %collective-permute-start.40) | collective-permute-done | bytes 262176 | tf_op jit(solution)/shard_map/ppermute | solution.py:52
  237.6 1.6 collective-permute-start.46
  239.7 3.5 %collective-permute-done.19 = bf16[128,1024]{1,0:T(8,128)(2,1)S(1)} collective-permute-done((bf16[128,1024]{1,0:T(8,128)(2,1)S(1)}, bf16[128,1024]{1,0:T(8,128)(2,1)S(1)}, u32[]{:S(2)}, u32[]{:S(2)}) %collective-permute-start.19) | collective-permute-done | bytes 262176 | tf_op jit(solution)/shard_map/ppermute | solution.py:52
  243.2 1.6 collective-permute-start.41
  248.9 1.6 collective-permute-start.55
  250.5 2.8 %collective-permute-done.47 = bf16[128,1024]{1,0:T(8,128)(2,1)S(1)} collective-permute-done((bf16[128,1024]{1,0:T(8,128)(2,1)S(1)}, bf16[128,1024]{1,0:T(8,128)(2,1)S(1)}, u32[]{:S(2)}, u32[]{:S(2)}) %collective-permute-start.47) | collective-permute-done | bytes 262176 | tf_op jit(solution)/shard_map/ppermute | solution.py:52
  253.4 1.6 collective-permute-start.48
  255.1 5.4 %collective-permute-done.20 = bf16[128,1024]{1,0:T(8,128)(2,1)S(1)} collective-permute-done((bf16[128,1024]{1,0:T(8,128)(2,1)S(1)}, bf16[128,1024]{1,0:T(8,128)(2,1)S(1)}, u32[]{:S(2)}, u32[]{:S(2)}) %collective-permute-start.20) | collective-permute-done | bytes 262176 | tf_op jit(solution)/shard_map/ppermute | solution.py:47
  262.5 3.6 %collective-permute-done.55 = bf16[128,1024]{1,0:T(8,128)(2,1)S(1)} collective-permute-done((bf16[128,1024]{1,0:T(8,128)(2,1)S(1)}, bf16[128,1024]{1,0:T(8,128)(2,1)S(1)}, u32[]{:S(2)}, u32[]{:S(2)}) %collective-permute-start.55) | collective-permute-done | bytes 262176 | tf_op jit(solution)/shard_map/ppermute | solution.py:47
  266.2 4.1 %collective-permute-done.48 = bf16[128,1024]{1,0:T(8,128)(2,1)S(1)} collective-permute-done((bf16[128,1024]{1,0:T(8,128)(2,1)S(1)}, bf16[128,1024]{1,0:T(8,128)(2,1)S(1)}, u32[]{:S(2)}, u32[]{:S(2)}) %collective-permute-start.48) | collective-permute-done | bytes 262176 | tf_op jit(solution)/shard_map/ppermute | solution.py:47
  (253 shorter events, 76.3 us)
Async XLA Ops:
  0.6 63.1 %copy-start = (bf16[1,2,1024,384]{3,2,1,0:T(8,128)(2,1)S(1)}, bf16[1,2,1024,384]{3,2,1,0:T(8,128)(2,1)}, u32[]{:S(2)}) copy-start(bf16[1,2,1024,384]{3,2,1,0:T(8,128)(2,1)} %param.14) | copy-start | bytes 4718596
  0.6 44.1 %copy-start.26 = (bf16[256,1024]{1,0:T(8,128)(2,1)S(1)}, bf16[256,1024]{1,0:T(8,128)(2,1)}, u32[]{:S(2)}) copy-start(bf16[256,1024]{1,0:T(8,128)(2,1)} %param.11) | copy-start | bytes 1572868
  4.3 10.7 %collective-permute-start.21 = (bf16[1,136,1024]{2,1,0:T(8,128)(2,1)}, bf16[1,136,1024]{2,1,0:T(8,128)(2,1)}, u32[]{:S(2)}, u32[]{:S(2)}) collective-permute-start(bf16[1,136,1024]{2,1,0:T(8,128)(2,1)} %maximum_bitcast_fusion.1), channel_id=1, source_target_pairs={{0,2},{2,4},{4,6},{6,7},{7,5},{5,3},{3,1},{1,0},{8,10},{10,12},{12... | collective-permute-start | bytes 835592 | tf_op jit(solution)/shard_map/ppermute | solution.py:51
  7.3 9.9 %collective-permute-start.22 = (bf16[1,136,1024]{2,1,0:T(8,128)(2,1)}, bf16[1,136,1024]{2,1,0:T(8,128)(2,1)}, u32[]{:S(2)}, u32[]{:S(2)}) collective-permute-start(bf16[1,136,1024]{2,1,0:T(8,128)(2,1)} %maximum_bitcast_fusion.1), channel_id=1, source_target_pairs={{0,1},{2,0},{4,2},{6,4},{7,6},{5,7},{3,5},{1,3},{8,9},{10,8},{12,1... | collective-permute-start | bytes 835592 | tf_op jit(solution)/shard_map/ppermute | solution.py:52
  7.6 13.3 %collective-permute-start = (bf16[1,136,1024]{2,1,0:T(8,128)(2,1)S(1)}, bf16[1,136,1024]{2,1,0:T(8,128)(2,1)S(1)}, u32[]{:S(2)}, u32[]{:S(2)}) collective-permute-start(bf16[1,136,1024]{2,1,0:T(8,128)(2,1)S(1)} %maximum_bitcast_fusion), channel_id=1, source_target_pairs={{0,2},{2,4},{4,6},{6,7},{7,5},{5,3},{3,1},{1,0},{8,10},{10,12},{12... | collective-permute-start | bytes 835592 | tf_op jit(solution)/shard_map/ppermute | solution.py:51
  9.7 13.4 %collective-permute-start.1 = (bf16[1,136,1024]{2,1,0:T(8,128)(2,1)S(1)}, bf16[1,136,1024]{2,1,0:T(8,128)(2,1)S(1)}, u32[]{:S(2)}, u32[]{:S(2)}) collective-permute-start(bf16[1,136,1024]{2,1,0:T(8,128)(2,1)S(1)} %maximum_bitcast_fusion), channel_id=1, source_target_pairs={{0,1},{2,0},{4,2},{6,4},{7,6},{5,7},{3,5},{1,3},{8,9},{10,8},{12,1... | collective-permute-start | bytes 835592 | tf_op jit(solution)/shard_map/ppermute | solution.py:52
  17.2 9.8 %collective-permute-start.23 = (bf16[1,136,1024]{2,1,0:T(8,128)(2,1)}, bf16[1,136,1024]{2,1,0:T(8,128)(2,1)S(1)}, u32[]{:S(2)}, u32[]{:S(2)}) collective-permute-start(bf16[1,136,1024]{2,1,0:T(8,128)(2,1)} %collective-permute-done.21), channel_id=1, source_target_pairs={{0,2},{2,4},{4,6},{6,7},{7,5},{5,3},{3,1},{1,0},{8,10},{10,12},{12... | collective-permute-start | bytes 835592 | tf_op jit(solution)/shard_map/ppermute | solution.py:51
  18.8 10.3 %collective-permute-start.24 = (bf16[1,136,1024]{2,1,0:T(8,128)(2,1)}, bf16[1,136,1024]{2,1,0:T(8,128)(2,1)S(1)}, u32[]{:S(2)}, u32[]{:S(2)}) collective-permute-start(bf16[1,136,1024]{2,1,0:T(8,128)(2,1)} %collective-permute-done.22), channel_id=1, source_target_pairs={{0,1},{2,0},{4,2},{6,4},{7,6},{5,7},{3,5},{1,3},{8,9},{10,8},{12,1... | collective-permute-start | bytes 835592 | tf_op jit(solution)/shard_map/ppermute | solution.py:52
  20.9 23.8 %copy-start.27 = (bf16[1,136,1024]{2,1,0:T(8,128)(2,1)}, bf16[1,136,1024]{2,1,0:T(8,128)(2,1)S(1)}, u32[]{:S(2)}) copy-start(bf16[1,136,1024]{2,1,0:T(8,128)(2,1)S(1)} %collective-permute-done) | copy-start | bytes 835588
  23.1 10.0 %collective-permute-start.2 = (bf16[1,136,1024]{2,1,0:T(8,128)(2,1)S(1)}, bf16[1,136,1024]{2,1,0:T(8,128)(2,1)}, u32[]{:S(2)}, u32[]{:S(2)}) collective-permute-start(bf16[1,136,1024]{2,1,0:T(8,128)(2,1)S(1)} %collective-permute-done), channel_id=1, source_target_pairs={{0,2},{2,4},{4,6},{6,7},{7,5},{5,3},{3,1},{1,0},{8,10},{10,12},{12... | collective-permute-start | bytes 835592 | tf_op jit(solution)/shard_map/ppermute | solution.py:51
  24.6 10.5 %collective-permute-start.3 = (bf16[1,136,1024]{2,1,0:T(8,128)(2,1)S(1)}, bf16[1,136,1024]{2,1,0:T(8,128)(2,1)}, u32[]{:S(2)}, u32[]{:S(2)}) collective-permute-start(bf16[1,136,1024]{2,1,0:T(8,128)(2,1)S(1)} %collective-permute-done.1), channel_id=1, source_target_pairs={{0,1},{2,0},{4,2},{6,4},{7,6},{5,7},{3,5},{1,3},{8,9},{10,8},{12,1... | collective-permute-start | bytes 835592 | tf_op jit(solution)/shard_map/ppermute | solution.py:52
  29.0 10.0 %collective-permute-start.25 = (bf16[1,136,1024]{2,1,0:T(8,128)(2,1)S(1)}, bf16[1,136,1024]{2,1,0:T(8,128)(2,1)}, u32[]{:S(2)}, u32[]{:S(2)}) collective-permute-start(bf16[1,136,1024]{2,1,0:T(8,128)(2,1)S(1)} %collective-permute-done.23), channel_id=1, source_target_pairs={{0,2},{2,4},{4,6},{6,7},{7,5},{5,3},{3,1},{1,0},{8,10},{10,12},{12... | collective-permute-start | bytes 835592 | tf_op jit(solution)/shard_map/ppermute | solution.py:51
  30.6 10.4 %collective-permute-start.26 = (bf16[1,136,1024]{2,1,0:T(8,128)(2,1)S(1)}, bf16[1,136,1024]{2,1,0:T(8,128)(2,1)S(1)}, u32[]{:S(2)}, u32[]{:S(2)}) collective-permute-start(bf16[1,136,1024]{2,1,0:T(8,128)(2,1)S(1)} %collective-permute-done.24), channel_id=1, source_target_pairs={{0,1},{2,0},{4,2},{6,4},{7,6},{5,7},{3,5},{1,3},{8,9},{10,8},{12,1... | collective-permute-start | bytes 835592 | tf_op jit(solution)/shard_map/ppermute | solution.py:52
  35.1 9.9 %collective-permute-start.4 = (bf16[1,136,1024]{2,1,0:T(8,128)(2,1)}, bf16[1,136,1024]{2,1,0:T(8,128)(2,1)}, u32[]{:S(2)}, u32[]{:S(2)}) collective-permute-start(bf16[1,136,1024]{2,1,0:T(8,128)(2,1)} %collective-permute-done.2), channel_id=1, source_target_pairs={{0,2},{2,4},{4,6},{6,7},{7,5},{5,3},{3,1},{1,0},{8,10},{10,12},{12... | collective-permute-start | bytes 835592 | tf_op jit(solution)/shard_map/ppermute | solution.py:51
  36.7 8.9 %collective-permute-start.5 = (bf16[1,136,1024]{2,1,0:T(8,128)(2,1)}, bf16[1,136,1024]{2,1,0:T(8,128)(2,1)}, u32[]{:S(2)}, u32[]{:S(2)}) collective-permute-start(bf16[1,136,1024]{2,1,0:T(8,128)(2,1)} %collective-permute-done.3), channel_id=1, source_target_pairs={{0,1},{2,0},{4,2},{6,4},{7,6},{5,7},{3,5},{1,3},{8,9},{10,8},{12,1... | collective-permute-start | bytes 835592 | tf_op jit(solution)/shard_map/ppermute | solution.py:52
  41.0 10.0 %collective-permute-start.27 = (bf16[1,136,1024]{2,1,0:T(8,128)(2,1)}, bf16[1,136,1024]{2,1,0:T(8,128)(2,1)}, u32[]{:S(2)}, u32[]{:S(2)}) collective-permute-start(bf16[1,136,1024]{2,1,0:T(8,128)(2,1)} %collective-permute-done.25), channel_id=1, source_target_pairs={{0,2},{2,4},{4,6},{6,7},{7,5},{5,3},{3,1},{1,0},{8,10},{10,12},{12... | collective-permute-start | bytes 835592 | tf_op jit(solution)/shard_map/ppermute | solution.py:47
  42.6 130.1 %collective-permute-start.56 = (bf16[1,2,384,1024]{3,2,1,0:T(8,128)(2,1)}, bf16[1,2,384,1024]{3,2,1,0:T(8,128)(2,1)}, u32[]{:S(2)}, u32[]{:S(2)}) collective-permute-start(bf16[1,2,384,1024]{3,2,1,0:T(8,128)(2,1)} %param.16), channel_id=1, source_target_pairs={{0,16},{8,24},{16,0},{24,8},{1,17},{9,25},{17,1},{25,9},{2,18},{10... | collective-permute-start | bytes 4718600 | tf_op jit(solution)/shard_map/ppermute | solution.py:22
  45.6 11.8 %collective-permute-start.6 = (bf16[1,136,1024]{2,1,0:T(8,128)(2,1)}, bf16[1,136,1024]{2,1,0:T(8,128)(2,1)S(1)}, u32[]{:S(2)}, u32[]{:S(2)}) collective-permute-start(bf16[1,136,1024]{2,1,0:T(8,128)(2,1)} %collective-permute-done.4), channel_id=1, source_target_pairs={{0,2},{2,4},{4,6},{6,7},{7,5},{5,3},{3,1},{1,0},{8,10},{10,12},{12... | collective-permute-start | bytes 835592 | tf_op jit(solution)/shard_map/ppermute | solution.py:47
  55.3 25.5 %collective-permute-start.28 = (bf16[128,1024]{1,0:T(8,128)(2,1)S(1)}, bf16[128,1024]{1,0:T(8,128)(2,1)}, u32[]{:S(2)}, u32[]{:S(2)}) collective-permute-start(bf16[128,1024]{1,0:T(8,128)(2,1)S(1)} %get-tuple-element.161), channel_id=1, source_target_pairs={{0,2},{2,4},{4,6},{6,7},{7,5},{5,3},{3,1},{1,0},{8,10},{10,12},{12... | collective-permute-start | bytes 786440 | tf_op jit(solution)/shard_map/ppermute | solution.py:51
  57.4 23.5 %collective-permute-start.29 = (bf16[128,1024]{1,0:T(8,128)(2,1)S(1)}, bf16[128,1024]{1,0:T(8,128)(2,1)}, u32[]{:S(2)}, u32[]{:S(2)}) collective-permute-start(bf16[128,1024]{1,0:T(8,128)(2,1)S(1)} %get-tuple-element.161), channel_id=1, source_target_pairs={{0,1},{2,0},{4,2},{6,4},{7,6},{5,7},{3,5},{1,3},{8,9},{10,8},{12,1... | collective-permute-start | bytes 786440 | tf_op jit(solution)/shard_map/ppermute | solution.py:52
  61.7 15.5 %collective-permute-start.7 = (bf16[128,1024]{1,0:T(8,128)(2,1)S(1)}, bf16[128,1024]{1,0:T(8,128)(2,1)S(1)}, u32[]{:S(2)}, u32[]{:S(2)}) collective-permute-start(bf16[128,1024]{1,0:T(8,128)(2,1)S(1)} %get-tuple-element.123), channel_id=1, source_target_pairs={{0,2},{2,4},{4,6},{6,7},{7,5},{5,3},{3,1},{1,0},{8,10},{10,12},{12... | collective-permute-start | bytes 786440 | tf_op jit(solution)/shard_map/ppermute | solution.py:51
  63.7 13.4 %collective-permute-start.8 = (bf16[128,1024]{1,0:T(8,128)(2,1)S(1)}, bf16[128,1024]{1,0:T(8,128)(2,1)S(1)}, u32[]{:S(2)}, u32[]{:S(2)}) collective-permute-start(bf16[128,1024]{1,0:T(8,128)(2,1)S(1)} %get-tuple-element.123), channel_id=1, source_target_pairs={{0,1},{2,0},{4,2},{6,4},{7,6},{5,7},{3,5},{1,3},{8,9},{10,8},{12,1... | collective-permute-start | bytes 786440 | tf_op jit(solution)/shard_map/ppermute | solution.py:52
  77.2 9.3 %collective-permute-start.9 = (bf16[128,1024]{1,0:T(8,128)(2,1)S(1)}, bf16[128,1024]{1,0:T(8,128)(2,1)}, u32[]{:S(2)}, u32[]{:S(2)}) collective-permute-start(bf16[128,1024]{1,0:T(8,128)(2,1)S(1)} %collective-permute-done.7), channel_id=1, source_target_pairs={{0,2},{2,4},{4,6},{6,7},{7,5},{5,3},{3,1},{1,0},{8,10},{10,12},{12... | collective-permute-start | bytes 786440 | tf_op jit(solution)/shard_map/ppermute | solution.py:51
  79.2 9.3 %collective-permute-start.10 = (bf16[128,1024]{1,0:T(8,128)(2,1)S(1)}, bf16[128,1024]{1,0:T(8,128)(2,1)}, u32[]{:S(2)}, u32[]{:S(2)}) collective-permute-start(bf16[128,1024]{1,0:T(8,128)(2,1)S(1)} %collective-permute-done.8), channel_id=1, source_target_pairs={{0,1},{2,0},{4,2},{6,4},{7,6},{5,7},{3,5},{1,3},{8,9},{10,8},{12,1... | collective-permute-start | bytes 786440 | tf_op jit(solution)/shard_map/ppermute | solution.py:52
  80.8 14.9 %collective-permute-start.30 = (bf16[128,1024]{1,0:T(8,128)(2,1)}, bf16[128,1024]{1,0:T(8,128)(2,1)S(1)}, u32[]{:S(2)}, u32[]{:S(2)}) collective-permute-start(bf16[128,1024]{1,0:T(8,128)(2,1)} %collective-permute-done.28), channel_id=1, source_target_pairs={{0,2},{2,4},{4,6},{6,7},{7,5},{5,3},{3,1},{1,0},{8,10},{10,12},{12... | collective-permute-start | bytes 786440 | tf_op jit(solution)/shard_map/ppermute | solution.py:51
  82.9 12.9 %collective-permute-start.31 = (bf16[128,1024]{1,0:T(8,128)(2,1)}, bf16[128,1024]{1,0:T(8,128)(2,1)S(1)}, u32[]{:S(2)}, u32[]{:S(2)}) collective-permute-start(bf16[128,1024]{1,0:T(8,128)(2,1)} %collective-permute-done.29), channel_id=1, source_target_pairs={{0,1},{2,0},{4,2},{6,4},{7,6},{5,7},{3,5},{1,3},{8,9},{10,8},{12,1... | collective-permute-start | bytes 786440 | tf_op jit(solution)/shard_map/ppermute | solution.py:52
  88.5 8.9 %collective-permute-start.11 = (bf16[128,1024]{1,0:T(8,128)(2,1)}, bf16[128,1024]{1,0:T(8,128)(2,1)S(1)}, u32[]{:S(2)}, u32[]{:S(2)}) collective-permute-start(bf16[128,1024]{1,0:T(8,128)(2,1)} %collective-permute-done.9), channel_id=1, source_target_pairs={{0,2},{2,4},{4,6},{6,7},{7,5},{5,3},{3,1},{1,0},{8,10},{10,12},{12... | collective-permute-start | bytes 786440 | tf_op jit(solution)/shard_map/ppermute | solution.py:51
  90.1 7.8 %collective-permute-start.12 = (bf16[128,1024]{1,0:T(8,128)(2,1)}, bf16[128,1024]{1,0:T(8,128)(2,1)S(1)}, u32[]{:S(2)}, u32[]{:S(2)}) collective-permute-start(bf16[128,1024]{1,0:T(8,128)(2,1)} %collective-permute-done.10), channel_id=1, source_target_pairs={{0,1},{2,0},{4,2},{6,4},{7,6},{5,7},{3,5},{1,3},{8,9},{10,8},{12,1... | collective-permute-start | bytes 786440 | tf_op jit(solution)/shard_map/ppermute | solution.py:52
  95.7 34.5 %copy-start.8 = (f32[1024,1024]{1,0:T(8,128)}, f32[1024,1024]{1,0:T(8,128)S(1)}, u32[]{:S(2)}) copy-start(f32[1024,1024]{1,0:T(8,128)S(1)} %multiply_reduce_fusion) | copy-start | bytes 12582916
  95.7 77.5 %collective-permute-start.57 = (bf16[1,2,384,1024]{3,2,1,0:T(8,128)(2,1)}, bf16[1,2,384,1024]{3,2,1,0:T(8,128)(2,1)}, u32[]{:S(2)}, u32[]{:S(2)}) collective-permute-start(bf16[1,2,384,1024]{3,2,1,0:T(8,128)(2,1)} %param.16), channel_id=1, source_target_pairs={{0,8},{8,16},{16,24},{24,0},{1,9},{9,17},{17,25},{25,1},{2,10},{10... | collective-permute-start | bytes 4718600 | tf_op jit(solution)/shard_map/ppermute | solution.py:22
  95.8 8.7 %collective-permute-start.32 = (bf16[128,1024]{1,0:T(8,128)(2,1)S(1)}, bf16[128,1024]{1,0:T(8,128)(2,1)S(1)}, u32[]{:S(2)}, u32[]{:S(2)}) collective-permute-start(bf16[128,1024]{1,0:T(8,128)(2,1)S(1)} %collective-permute-done.30), channel_id=1, source_target_pairs={{0,2},{2,4},{4,6},{6,7},{7,5},{5,3},{3,1},{1,0},{8,10},{10,12},{12... | collective-permute-start | bytes 786440 | tf_op jit(solution)/shard_map/ppermute | solution.py:51
  97.4 8.9 %collective-permute-start.33 = (bf16[128,1024]{1,0:T(8,128)(2,1)S(1)}, bf16[128,1024]{1,0:T(8,128)(2,1)S(1)}, u32[]{:S(2)}, u32[]{:S(2)}) collective-permute-start(bf16[128,1024]{1,0:T(8,128)(2,1)S(1)} %collective-permute-done.31), channel_id=1, source_target_pairs={{0,1},{2,0},{4,2},{6,4},{7,6},{5,7},{3,5},{1,3},{8,9},{10,8},{12,1... | collective-permute-start | bytes 786440 | tf_op jit(solution)/shard_map/ppermute | solution.py:52
  97.9 12.2 %collective-permute-start.13 = (bf16[128,1024]{1,0:T(8,128)(2,1)S(1)}, bf16[128,1024]{1,0:T(8,128)(2,1)S(1)}, u32[]{:S(2)}, u32[]{:S(2)}) collective-permute-start(bf16[128,1024]{1,0:T(8,128)(2,1)S(1)} %collective-permute-done.11), channel_id=1, source_target_pairs={{0,2},{2,4},{4,6},{6,7},{7,5},{5,3},{3,1},{1,0},{8,10},{10,12},{12... | collective-permute-start | bytes 786440 | tf_op jit(solution)/shard_map/ppermute | solution.py:47
  103.8 29.6 %copy-start.10 = (f32[1024,1024]{1,0:T(8,128)}, f32[1024,1024]{1,0:T(8,128)S(1)}, u32[]{:S(2)}) copy-start(f32[1024,1024]{1,0:T(8,128)S(1)} %multiply_reduce_fusion.1) | copy-start | bytes 12582916
  106.3 21.8 %collective-permute-start.34 = (bf16[128,1024]{1,0:T(8,128)(2,1)S(1)}, bf16[128,1024]{1,0:T(8,128)(2,1)S(1)}, u32[]{:S(2)}, u32[]{:S(2)}) collective-permute-start(bf16[128,1024]{1,0:T(8,128)(2,1)S(1)} %collective-permute-done.32), channel_id=1, source_target_pairs={{0,2},{2,4},{4,6},{6,7},{7,5},{5,3},{3,1},{1,0},{8,10},{10,12},{12... | collective-permute-start | bytes 786440 | tf_op jit(solution)/shard_map/ppermute | solution.py:47
  131.4 63.2 %collective-permute-start.35 = (bf16[128,1024]{1,0:T(8,128)(2,1)}, bf16[128,1024]{1,0:T(8,128)(2,1)}, u32[]{:S(2)}, u32[]{:S(2)}) collective-permute-start(bf16[128,1024]{1,0:T(8,128)(2,1)} %get-tuple-element.173), channel_id=1, source_target_pairs={{0,2},{2,4},{4,6},{6,7},{7,5},{5,3},{3,1},{1,0},{8,10},{10,12},{12... | collective-permute-start | bytes 786440 | tf_op jit(solution)/shard_map/ppermute | solution.py:51
  133.0 62.1 %collective-permute-start.36 = (bf16[128,1024]{1,0:T(8,128)(2,1)}, bf16[128,1024]{1,0:T(8,128)(2,1)}, u32[]{:S(2)}, u32[]{:S(2)}) collective-permute-start(bf16[128,1024]{1,0:T(8,128)(2,1)} %get-tuple-element.174), channel_id=1, source_target_pairs={{0,1},{2,0},{4,2},{6,4},{7,6},{5,7},{3,5},{1,3},{8,9},{10,8},{12,1... | collective-permute-start | bytes 786440 | tf_op jit(solution)/shard_map/ppermute | solution.py:52
  134.6 63.6 %collective-permute-start.14 = (bf16[128,1024]{1,0:T(8,128)(2,1)}, bf16[128,1024]{1,0:T(8,128)(2,1)}, u32[]{:S(2)}, u32[]{:S(2)}) collective-permute-start(bf16[128,1024]{1,0:T(8,128)(2,1)} %get-tuple-element.135), channel_id=1, source_target_pairs={{0,2},{2,4},{4,6},{6,7},{7,5},{5,3},{3,1},{1,0},{8,10},{10,12},{12... | collective-permute-start | bytes 786440 | tf_op jit(solution)/shard_map/ppermute | solution.py:51
  172.7 26.0 %collective-permute-start.15 = (bf16[128,1024]{1,0:T(8,128)(2,1)S(1)}, bf16[128,1024]{1,0:T(8,128)(2,1)}, u32[]{:S(2)}, u32[]{:S(2)}) collective-permute-start(bf16[128,1024]{1,0:T(8,128)(2,1)S(1)} %copy-done.35), channel_id=1, source_target_pairs={{0,1},{2,0},{4,2},{6,4},{7,6},{5,7},{3,5},{1,3},{8,9},{10,8},{12,1... | collective-permute-start | bytes 786440 | tf_op jit(solution)/shard_map/ppermute | solution.py:52
  173.2 28.6 %collective-permute-start.49 = (bf16[128,1024]{1,0:T(8,128)(2,1)}, bf16[128,1024]{1,0:T(8,128)(2,1)}, u32[]{:S(2)}, u32[]{:S(2)}) collective-permute-start(bf16[128,1024]{1,0:T(8,128)(2,1)} %get-tuple-element.199), channel_id=1, source_target_pairs={{0,2},{2,4},{4,6},{6,7},{7,5},{5,3},{3,1},{1,0},{8,10},{10,12},{12... | collective-permute-start | bytes 786440 | tf_op jit(solution)/shard_map/ppermute | solution.py:51
  194.6 9.2 %collective-permute-start.50 = (bf16[128,1024]{1,0:T(8,128)(2,1)S(1)}, bf16[128,1024]{1,0:T(8,128)(2,1)S(1)}, u32[]{:S(2)}, u32[]{:S(2)}) collective-permute-start(bf16[128,1024]{1,0:T(8,128)(2,1)S(1)} %copy-done.36), channel_id=1, source_target_pairs={{0,1},{2,0},{4,2},{6,4},{7,6},{5,7},{3,5},{1,3},{8,9},{10,8},{12,1... | collective-permute-start | bytes 786440 | tf_op jit(solution)/shard_map/ppermute | solution.py:52
  195.1 11.4 %collective-permute-start.42 = (bf16[128,1024]{1,0:T(8,128)(2,1)S(1)}, bf16[128,1024]{1,0:T(8,128)(2,1)S(1)}, u32[]{:S(2)}, u32[]{:S(2)}) collective-permute-start(bf16[128,1024]{1,0:T(8,128)(2,1)S(1)} %copy-done.38), channel_id=1, source_target_pairs={{0,2},{2,4},{4,6},{6,7},{7,5},{5,3},{3,1},{1,0},{8,10},{10,12},{12... | collective-permute-start | bytes 786440 | tf_op jit(solution)/shard_map/ppermute | solution.py:51
  198.2 11.3 %collective-permute-start.43 = (bf16[128,1024]{1,0:T(8,128)(2,1)S(1)}, bf16[128,1024]{1,0:T(8,128)(2,1)S(1)}, u32[]{:S(2)}, u32[]{:S(2)}) collective-permute-start(bf16[128,1024]{1,0:T(8,128)(2,1)S(1)} %copy-done.37), channel_id=1, source_target_pairs={{0,1},{2,0},{4,2},{6,4},{7,6},{5,7},{3,5},{1,3},{8,9},{10,8},{12,1... | collective-permute-start | bytes 786440 | tf_op jit(solution)/shard_map/ppermute | solution.py:52
  198.7 13.7 %collective-permute-start.37 = (bf16[128,1024]{1,0:T(8,128)(2,1)S(1)}, bf16[128,1024]{1,0:T(8,128)(2,1)S(1)}, u32[]{:S(2)}, u32[]{:S(2)}) collective-permute-start(bf16[128,1024]{1,0:T(8,128)(2,1)S(1)} %get-tuple-element.177), channel_id=1, source_target_pairs={{0,2},{2,4},{4,6},{6,7},{7,5},{5,3},{3,1},{1,0},{8,10},{10,12},{12... | collective-permute-start | bytes 786440 | tf_op jit(solution)/shard_map/ppermute | solution.py:51
  201.8 13.3 %collective-permute-start.38 = (bf16[128,1024]{1,0:T(8,128)(2,1)S(1)}, bf16[128,1024]{1,0:T(8,128)(2,1)S(1)}, u32[]{:S(2)}, u32[]{:S(2)}) collective-permute-start(bf16[128,1024]{1,0:T(8,128)(2,1)S(1)} %get-tuple-element.178), channel_id=1, source_target_pairs={{0,1},{2,0},{4,2},{6,4},{7,6},{5,7},{3,5},{1,3},{8,9},{10,8},{12,1... | collective-permute-start | bytes 786440 | tf_op jit(solution)/shard_map/ppermute | solution.py:52
  203.9 13.0 %collective-permute-start.16 = (bf16[128,1024]{1,0:T(8,128)(2,1)S(1)}, bf16[128,1024]{1,0:T(8,128)(2,1)S(1)}, u32[]{:S(2)}, u32[]{:S(2)}) collective-permute-start(bf16[128,1024]{1,0:T(8,128)(2,1)S(1)} %get-tuple-element.139), channel_id=1, source_target_pairs={{0,2},{2,4},{4,6},{6,7},{7,5},{5,3},{3,1},{1,0},{8,10},{10,12},{12... | collective-permute-start | bytes 786440 | tf_op jit(solution)/shard_map/ppermute | solution.py:51
  206.6 14.2 %collective-permute-start.17 = (bf16[128,1024]{1,0:T(8,128)(2,1)S(1)}, bf16[128,1024]{1,0:T(8,128)(2,1)S(1)}, u32[]{:S(2)}, u32[]{:S(2)}) collective-permute-start(bf16[128,1024]{1,0:T(8,128)(2,1)S(1)} %get-tuple-element.140), channel_id=1, source_target_pairs={{0,1},{2,0},{4,2},{6,4},{7,6},{5,7},{3,5},{1,3},{8,9},{10,8},{12,1... | collective-permute-start | bytes 786440 | tf_op jit(solution)/shard_map/ppermute | solution.py:52
  209.5 14.2 %collective-permute-start.51 = (bf16[128,1024]{1,0:T(8,128)(2,1)S(1)}, bf16[128,1024]{1,0:T(8,128)(2,1)S(1)}, u32[]{:S(2)}, u32[]{:S(2)}) collective-permute-start(bf16[128,1024]{1,0:T(8,128)(2,1)S(1)} %get-tuple-element.203), channel_id=1, source_target_pairs={{0,2},{2,4},{4,6},{6,7},{7,5},{5,3},{3,1},{1,0},{8,10},{10,12},{12... | collective-permute-start | bytes 786440 | tf_op jit(solution)/shard_map/ppermute | solution.py:51
  212.4 13.9 %collective-permute-start.52 = (bf16[128,1024]{1,0:T(8,128)(2,1)S(1)}, bf16[128,1024]{1,0:T(8,128)(2,1)S(1)}, u32[]{:S(2)}, u32[]{:S(2)}) collective-permute-start(bf16[128,1024]{1,0:T(8,128)(2,1)S(1)} %get-tuple-element.204), channel_id=1, source_target_pairs={{0,1},{2,0},{4,2},{6,4},{7,6},{5,7},{3,5},{1,3},{8,9},{10,8},{12,1... | collective-permute-start | bytes 786440 | tf_op jit(solution)/shard_map/ppermute | solution.py:52
  215.1 13.0 %collective-permute-start.44 = (bf16[128,1024]{1,0:T(8,128)(2,1)S(1)}, bf16[128,1024]{1,0:T(8,128)(2,1)S(1)}, u32[]{:S(2)}, u32[]{:S(2)}) collective-permute-start(bf16[128,1024]{1,0:T(8,128)(2,1)S(1)} %get-tuple-element.190), channel_id=1, source_target_pairs={{0,2},{2,4},{4,6},{6,7},{7,5},{5,3},{3,1},{1,0},{8,10},{10,12},{12... | collective-permute-start | bytes 786440 | tf_op jit(solution)/shard_map/ppermute | solution.py:51
  216.8 16.7 %copy-start.4 = (f32[1024,1024]{1,0:T(8,128)S(1)}, f32[1024,1024]{1,0:T(8,128)}, u32[]{:S(2)}) copy-start(f32[1024,1024]{1,0:T(8,128)} %copy-done.3) | copy-start | bytes 12582916
  216.9 15.1 %collective-permute-start.45 = (bf16[128,1024]{1,0:T(8,128)(2,1)S(1)}, bf16[128,1024]{1,0:T(8,128)(2,1)S(1)}, u32[]{:S(2)}, u32[]{:S(2)}) collective-permute-start(bf16[128,1024]{1,0:T(8,128)(2,1)S(1)} %get-tuple-element.191), channel_id=1, source_target_pairs={{0,1},{2,0},{4,2},{6,4},{7,6},{5,7},{3,5},{1,3},{8,9},{10,8},{12,1... | collective-permute-start | bytes 786440 | tf_op jit(solution)/shard_map/ppermute | solution.py:52
  220.7 13.0 %collective-permute-start.39 = (bf16[128,1024]{1,0:T(8,128)(2,1)S(1)}, bf16[128,1024]{1,0:T(8,128)(2,1)S(1)}, u32[]{:S(2)}, u32[]{:S(2)}) collective-permute-start(bf16[128,1024]{1,0:T(8,128)(2,1)S(1)} %get-tuple-element.181), channel_id=1, source_target_pairs={{0,2},{2,4},{4,6},{6,7},{7,5},{5,3},{3,1},{1,0},{8,10},{10,12},{12... | collective-permute-start | bytes 786440 | tf_op jit(solution)/shard_map/ppermute | solution.py:51
  223.7 13.9 %collective-permute-start.40 = (bf16[128,1024]{1,0:T(8,128)(2,1)S(1)}, bf16[128,1024]{1,0:T(8,128)(2,1)S(1)}, u32[]{:S(2)}, u32[]{:S(2)}) collective-permute-start(bf16[128,1024]{1,0:T(8,128)(2,1)S(1)} %get-tuple-element.182), channel_id=1, source_target_pairs={{0,1},{2,0},{4,2},{6,4},{7,6},{5,7},{3,5},{1,3},{8,9},{10,8},{12,1... | collective-permute-start | bytes 786440 | tf_op jit(solution)/shard_map/ppermute | solution.py:52
  226.3 12.9 %collective-permute-start.18 = (bf16[128,1024]{1,0:T(8,128)(2,1)S(1)}, bf16[128,1024]{1,0:T(8,128)(2,1)S(1)}, u32[]{:S(2)}, u32[]{:S(2)}) collective-permute-start(bf16[128,1024]{1,0:T(8,128)(2,1)S(1)} %get-tuple-element.143), channel_id=1, source_target_pairs={{0,2},{2,4},{4,6},{6,7},{7,5},{5,3},{3,1},{1,0},{8,10},{10,12},{12... | collective-permute-start | bytes 786440 | tf_op jit(solution)/shard_map/ppermute | solution.py:51
  228.1 15.1 %collective-permute-start.19 = (bf16[128,1024]{1,0:T(8,128)(2,1)S(1)}, bf16[128,1024]{1,0:T(8,128)(2,1)S(1)}, u32[]{:S(2)}, u32[]{:S(2)}) collective-permute-start(bf16[128,1024]{1,0:T(8,128)(2,1)S(1)} %get-tuple-element.144), channel_id=1, source_target_pairs={{0,1},{2,0},{4,2},{6,4},{7,6},{5,7},{3,5},{1,3},{8,9},{10,8},{12,1... | collective-permute-start | bytes 786440 | tf_op jit(solution)/shard_map/ppermute | solution.py:52
  231.9 13.9 %collective-permute-start.53 = (bf16[128,1024]{1,0:T(8,128)(2,1)S(1)}, bf16[128,1024]{1,0:T(8,128)(2,1)S(1)}, u32[]{:S(2)}, u32[]{:S(2)}) collective-permute-start(bf16[128,1024]{1,0:T(8,128)(2,1)S(1)} %get-tuple-element.207), channel_id=1, source_target_pairs={{0,2},{2,4},{4,6},{6,7},{7,5},{5,3},{3,1},{1,0},{8,10},{10,12},{12... | collective-permute-start | bytes 786440 | tf_op jit(solution)/shard_map/ppermute | solution.py:51
  233.7 15.1 %collective-permute-start.54 = (bf16[128,1024]{1,0:T(8,128)(2,1)S(1)}, bf16[128,1024]{1,0:T(8,128)(2,1)S(1)}, u32[]{:S(2)}, u32[]{:S(2)}) collective-permute-start(bf16[128,1024]{1,0:T(8,128)(2,1)S(1)} %get-tuple-element.208), channel_id=1, source_target_pairs={{0,1},{2,0},{4,2},{6,4},{7,6},{5,7},{3,5},{1,3},{8,9},{10,8},{12,1... | collective-permute-start | bytes 786440 | tf_op jit(solution)/shard_map/ppermute | solution.py:52
  237.6 12.9 %collective-permute-start.46 = (bf16[128,1024]{1,0:T(8,128)(2,1)S(1)}, bf16[128,1024]{1,0:T(8,128)(2,1)S(1)}, u32[]{:S(2)}, u32[]{:S(2)}) collective-permute-start(bf16[128,1024]{1,0:T(8,128)(2,1)S(1)} %get-tuple-element.194), channel_id=1, source_target_pairs={{0,2},{2,4},{4,6},{6,7},{7,5},{5,3},{3,1},{1,0},{8,10},{10,12},{12... | collective-permute-start | bytes 786440 | tf_op jit(solution)/shard_map/ppermute | solution.py:51
  239.2 14.1 %collective-permute-start.47 = (bf16[128,1024]{1,0:T(8,128)(2,1)S(1)}, bf16[128,1024]{1,0:T(8,128)(2,1)S(1)}, u32[]{:S(2)}, u32[]{:S(2)}) collective-permute-start(bf16[128,1024]{1,0:T(8,128)(2,1)S(1)} %get-tuple-element.195), channel_id=1, source_target_pairs={{0,1},{2,0},{4,2},{6,4},{7,6},{5,7},{3,5},{1,3},{8,9},{10,8},{12,1... | collective-permute-start | bytes 786440 | tf_op jit(solution)/shard_map/ppermute | solution.py:52
  243.2 11.9 %collective-permute-start.41 = (bf16[128,1024]{1,0:T(8,128)(2,1)S(1)}, bf16[128,1024]{1,0:T(8,128)(2,1)S(1)}, u32[]{:S(2)}, u32[]{:S(2)}) collective-permute-start(bf16[128,1024]{1,0:T(8,128)(2,1)S(1)} %add_convert_fusion.3), channel_id=1, source_target_pairs={{0,2},{2,4},{4,6},{6,7},{7,5},{5,3},{3,1},{1,0},{8,10},{10,12},{12... | collective-permute-start | bytes 786440 | tf_op jit(solution)/shard_map/ppermute | solution.py:47
  245.9 14.6 %collective-permute-start.20 = (bf16[128,1024]{1,0:T(8,128)(2,1)S(1)}, bf16[128,1024]{1,0:T(8,128)(2,1)S(1)}, u32[]{:S(2)}, u32[]{:S(2)}) collective-permute-start(bf16[128,1024]{1,0:T(8,128)(2,1)S(1)} %add_convert_fusion.9), channel_id=1, source_target_pairs={{0,2},{2,4},{4,6},{6,7},{7,5},{5,3},{3,1},{1,0},{8,10},{10,12},{12... | collective-permute-start | bytes 786440 | tf_op jit(solution)/shard_map/ppermute | solution.py:47
  248.9 17.3 %collective-permute-start.55 = (bf16[128,1024]{1,0:T(8,128)(2,1)S(1)}, bf16[128,1024]{1,0:T(8,128)(2,1)S(1)}, u32[]{:S(2)}, u32[]{:S(2)}) collective-permute-start(bf16[128,1024]{1,0:T(8,128)(2,1)S(1)} %fusion.58), channel_id=1, source_target_pairs={{0,2},{2,4},{4,6},{6,7},{7,5},{5,3},{3,1},{1,0},{8,10},{10,12},{12... | collective-permute-start | bytes 786440 | tf_op jit(solution)/shard_map/ppermute | solution.py:47
  253.4 17.0 %collective-permute-start.48 = (bf16[128,1024]{1,0:T(8,128)(2,1)S(1)}, bf16[128,1024]{1,0:T(8,128)(2,1)S(1)}, u32[]{:S(2)}, u32[]{:S(2)}) collective-permute-start(bf16[128,1024]{1,0:T(8,128)(2,1)S(1)} %fusion.65), channel_id=1, source_target_pairs={{0,2},{2,4},{4,6},{6,7},{7,5},{5,3},{3,1},{1,0},{8,10},{10,12},{12... | collective-permute-start | bytes 786440 | tf_op jit(solution)/shard_map/ppermute | solution.py:47
  (40 other events, 256.8 us)

commit v8 on v6

--- a/solution.py
+++ b/solution.py
@@ -162,6 +162,9 @@
     up_matrix = up_weight[0]
     down_matrix = down_weight[0]
 
+    hidden_width = gate_matrix.shape[2]
+    joint_matrix = jnp.concatenate([gate_matrix, up_matrix], axis=2)
+
     def chunk_pass(chunk_tokens, chunk_cot, chunk_weight):
         gate_value = jnp.einsum(
             "td,edh->eth", chunk_tokens, gate_matrix, preferred_element_type=jnp.float32
@@ -188,15 +191,14 @@
         down_grad = jnp.einsum(
             "eth,etd->ehd", hidden, slot_cot, preferred_element_type=jnp.float32
         )
-        gate_grad = jnp.einsum(
-            "td,eth->edh", chunk_tokens, gate_cot, preferred_element_type=jnp.float32
-        )
-        up_grad = jnp.einsum(
-            "td,eth->edh", chunk_tokens, up_cot, preferred_element_type=jnp.float32
-        )
+        joint_cot = jnp.concatenate([gate_cot, up_cot], axis=2)
+        joint_grad = jnp.einsum(
+            "td,eth->edh", chunk_tokens, joint_cot, preferred_element_type=jnp.float32
+        )
+        gate_grad = joint_grad[..., :hidden_width]
+        up_grad = joint_grad[..., hidden_width:]
         input_cot = as_bf16(
-            jnp.einsum("eth,edh->etd", gate_cot, gate_matrix, preferred_element_type=jnp.float32)
-            + jnp.einsum("eth,edh->etd", up_cot, up_matrix, preferred_element_type=jnp.float32)
+            jnp.einsum("eth,edh->etd", joint_cot, joint_matrix, preferred_element_type=jnp.float32)
         )
         input_part = jnp.sum(input_cot, axis=0)
         return mixed_part, input_part, gate_grad, up_grad, down_grad

time: 241 us -> 235 us (0.975)
  local copies, waits for them, and re-layouts: 23.5 us -> 18.8 us
    dot_general x4 -> x2, matrix products: 30 us -> 21.9 us  [the longest x1 14.7 us: chunk_pass(): jnp.einsum('eth,edh->etd', joint_cot, joint_matrix, preferred_element_typ...]
    ppermute x4, waiting for transfers between devices: 8.94 us -> 15.5 us  [paired_shift(): return (lax.ppermute(ahead_value, axis, ring_pairs(ring, 1)), None)]
    ppermute x12, waiting for transfers between devices: 60.9 us -> 56.1 us  [paired_shift(): ahead_value = lax.ppermute(ahead_value, axis, ring_pairs(ring, 1))]
    dot_general x1, matrix products: 8.37 us -> 11.5 us  [chunk_pass(): jnp.einsum('eth,ehd->etd', hidden, down_matrix, preferred_element_type=jn...]
    slice x2, local copies, waits for them, and re-layouts: 3.1 us -> 0.14 us  [block_at(): return blocks[(offset + ahead) % size]]
    dot_general x1, matrix products: 11.1 us -> 14 us  [chunk_pass(): jnp.einsum('etd,ehd->eth', slot_cot, down_matrix, preferred_element_type=...]
    unnamed x53 -> x43, local copies, waits for them, and re-layouts: 14.9 us -> 12.7 us
  transfers between devices with their start and end apart: 30 -> 30, of which waited for: 18 -> 19; matrix products, arithmetic and copies ran while one was open for 47% -> 45% of each run, Pallas kernels for 0% -> 0%
where the time goes in v8:
time: 235 us; the launch traced here: 234 us
  waiting for transfers between devices  82.4 us (35%)
  matrix products  71 us (30%)
  starting transfers between devices  32 us (14%)
  other arithmetic  28.2 us (12%)
  local copies, waits for them, and re-layouts  18.8 us (8%)
    ppermute x12, waiting for transfers between devices, paired_shift(): ahead_value = lax.ppermute(ahead_value, axis, ring_pairs(ring, 1))  56.1 us
    ppermute x12, starting transfers between devices, paired_shift(): ahead_value = lax.ppermute(ahead_value, axis, ring_pairs(ring, 1))  18.3 us
    ppermute x4, waiting for transfers between devices, paired_shift(): return (lax.ppermute(ahead_value, axis, ring_pairs(ring, 1)), None)  15.5 us
    dot_general x1, matrix products, chunk_pass(): jnp.einsum('eth,edh->etd', joint_cot, joint_matrix, preferred_element_typ...  14.7 us
    dot_general x1, matrix products, chunk_pass(): jnp.einsum('etd,ehd->eth', slot_cot, down_matrix, preferred_element_type=...  14 us
    dot_general x1, matrix products, chunk_pass(): jnp.einsum('eth,etd->ehd', hidden, slot_cot, preferred_element_type=jnp.f...  12.9 us
    unnamed x43, local copies, waits for them, and re-layouts  12.7 us
    dot_general x1, matrix products, chunk_pass(): jnp.einsum('eth,ehd->etd', hidden, down_matrix, preferred_element_type=jn...  11.5 us
  transfers between devices with their start and end apart: 30, of which 19 were waited for; matrix products, arithmetic and copies ran while one was open for 45% of the time, Pallas kernels for 0%

profile of v8, /device:TPU:0, one launch (start us, length us, event | category | flops | bytes accessed | tf_op | source)
XLA Modules:
  0.0 234.0 jit_solution(14053478456259132097)
XLA Ops:
  2.4 1.1 maximum_bitcast_fusion
  3.5 3.1 %collective-permute-start = (bf16[1,264,1024]{2,1,0:T(8,128)(2,1)S(1)}, bf16[1,264,1024]{2,1,0:T(8,128)(2,1)S(1)}, u32[]{:S(2)}, u32[]{:S(2)}) collective-permute-start(bf16[1,264,1024]{2,1,0:T(8,128)(2,1)S(1)} %maximum_bitcast_fusion), channel_id=1, source_target_pairs={{0,2},{2,4},{4,6},{6,7},{7,5},{5,3},{3,1},{1,0},{8,10},{10,12},{12... | collective-permute-start | bytes 1622024 | tf_op jit(solution)/shard_map/ppermute | solution.py:50
  6.5 12.2 %collective-permute-done = bf16[1,264,1024]{2,1,0:T(8,128)(2,1)S(1)} collective-permute-done((bf16[1,264,1024]{2,1,0:T(8,128)(2,1)S(1)}, bf16[1,264,1024]{2,1,0:T(8,128)(2,1)S(1)}, u32[]{:S(2)}, u32[]{:S(2)}) %collective-permute-start) | collective-permute-done | bytes 540704 | tf_op jit(solution)/shard_map/ppermute | solution.py:50
  18.7 1.5 collective-permute-done.1
  20.3 1.6 collective-permute-start.2
  22.3 10.8 %collective-permute-done.2 = bf16[1,264,1024]{2,1,0:T(8,128)(2,1)S(1)} collective-permute-done((bf16[1,264,1024]{2,1,0:T(8,128)(2,1)S(1)}, bf16[1,264,1024]{2,1,0:T(8,128)(2,1)S(1)}, u32[]{:S(2)}, u32[]{:S(2)}) %collective-permute-start.2) | collective-permute-done | bytes 540704 | tf_op jit(solution)/shard_map/ppermute | solution.py:50
  33.1 1.3 collective-permute-done.3
  34.4 1.6 collective-permute-start.4
  36.4 9.6 %collective-permute-done.4 = bf16[1,264,1024]{2,1,0:T(8,128)(2,1)S(1)} collective-permute-done((bf16[1,264,1024]{2,1,0:T(8,128)(2,1)S(1)}, bf16[1,264,1024]{2,1,0:T(8,128)(2,1)S(1)}, u32[]{:S(2)}, u32[]{:S(2)}) %collective-permute-start.4) | collective-permute-done | bytes 540704 | tf_op jit(solution)/shard_map/ppermute | solution.py:50
  46.0 1.3 collective-permute-done.5
  47.3 1.5 collective-permute-start.6
  48.8 8.9 %collective-permute-done.6 = bf16[1,264,1024]{2,1,0:T(8,128)(2,1)S(1)} collective-permute-done((bf16[1,264,1024]{2,1,0:T(8,128)(2,1)S(1)}, bf16[1,264,1024]{2,1,0:T(8,128)(2,1)S(1)}, u32[]{:S(2)}, u32[]{:S(2)}) %collective-permute-start.6) | collective-permute-done | bytes 540704 | tf_op jit(solution)/shard_map/ppermute | solution.py:46
  58.6 0.9 constant_dynamic-update-slice_fusion.6
  64.5 1.5 collective-permute-start.7
  66.6 1.5 collective-permute-start.28
  68.1 2.8 %slice.108 = bf16[8,256,1024]{2,1,0:T(8,128)(2,1)S(1)} slice(bf16[8,264,1024]{2,1,0:T(8,128)(2,1)} %constant_dynamic-update-slice_fusion), slice={[0:8], [0:256], [0:1024]} | slice | bytes 8388608 | tf_op jit(solution)/shard_map/slice | solution.py:148
  70.9 2.8 %collective-permute-done.7 = bf16[256,1024]{1,0:T(8,128)(2,1)S(1)} collective-permute-done((bf16[256,1024]{1,0:T(8,128)(2,1)S(1)}, bf16[256,1024]{1,0:T(8,128)(2,1)S(1)}, u32[]{:S(2)}, u32[]{:S(2)}) %collective-permute-start.7) | collective-permute-done | bytes 524320 | tf_op jit(solution)/shard_map/ppermute | solution.py:50
  73.7 1.6 collective-permute-done.8
  75.3 1.9 collective-permute-start.9
  77.3 3.7 %fusion.40 = f32[2048,2,384]{0,2,1:T(8,128)S(1)} fusion(bf16[2048,1024,1]{1,0,2:T(8,128)(2,1)S(1)} %bitcast.98, bf16[1,2,1024,384]{3,2,1,0:T(8,128)(2,1)S(1)} %copy-done.9), kind=kOutput, calls=%fused_computation.90 | convolution fusion | flops 3221225472 | bytes 12058624 | tf_op jit(solution)/shard_map/td,edh->eth/dot_general | solution.py:169
  81.0 5.6 %collective-permute-done.9 = bf16[256,1024]{1,0:T(8,128)(2,1)} collective-permute-done((bf16[256,1024]{1,0:T(8,128)(2,1)S(1)}, bf16[256,1024]{1,0:T(8,128)(2,1)}, u32[]{:S(2)}, u32[]{:S(2)}) %collective-permute-start.9) | collective-permute-done | bytes 524320 | tf_op jit(solution)/shard_map/ppermute | solution.py:50
  86.7 2.4 %collective-permute-start.11 = (bf16[256,1024]{1,0:T(8,128)(2,1)}, bf16[256,1024]{1,0:T(8,128)(2,1)}, u32[]{:S(2)}, u32[]{:S(2)}) collective-permute-start(bf16[256,1024]{1,0:T(8,128)(2,1)} %collective-permute-done.9), channel_id=1, source_target_pairs={{0,2},{2,4},{4,6},{6,7},{7,5},{5,3},{3,1},{1,0},{8,10},{10,12},{12... | collective-permute-start | bytes 1572872 | tf_op jit(solution)/shard_map/ppermute | solution.py:50
  89.1 7.0 %fusion.6 = (bf16[2,2048,384]{1,2,0:T(8,128)(2,1)}, f32[2048,2,384]{0,2,1:T(8,128)}) fusion(f32[2048,2,384]{0,2,1:T(8,128)S(1)} %fusion.40, bf16[2048,1024,1]{1,0,2:T(8,128)(2,1)S(1)} %bitcast.99, bf16[1,2,1024,384]{3,2,1,0:T(8,128)(2,1)S(1)} %copy-done.10), kind=kOutput, calls=%fused_computation.12 | convolution fusion | flops 3230662656 | bytes 21495808 | tf_op jit(solution)/shard_map/td,edh->eth/dot_general | solution.py:172
  96.1 0.9 slice_bitcast_fusion.2
  98.6 1.7 collective-permute-start.13
  100.3 11.5 %multiply_reduce_fusion = f32[2048,1024]{1,0:T(8,128)} fusion(f32[2,2048]{1,0:T(2,128)S(1)} %copy.35, bf16[2,2048,384]{1,2,0:T(8,128)(2,1)} %get-tuple-element.149, bf16[1,2,384,1024]{3,2,1,0:T(8,128)(2,1)} %param.16), kind=kOutput, calls=%fused_computation.2 | convolution fusion | flops 3231711232 | bytes 13123584 | tf_op jit(solution)/shard_map/eth,ehd->etd/dot_general | solution.py:179
  111.9 1.1 constant_dynamic-update-slice_fusion.14
  113.0 1.1 constant_dynamic-update-slice_fusion.13
  114.2 1.1 constant_dynamic-update-slice_fusion.9
  115.2 1.1 constant_dynamic-update-slice_fusion.8
  116.3 4.0 %convert.14 = bf16[2048,1024]{1,0:T(8,128)(2,1)S(1)} convert(f32[2048,1024]{1,0:T(8,128)} %multiply_reduce_fusion) | non-fusion elementwise | flops 2097152 | bytes 12582912 | tf_op jit(solution)/shard_map/convert.7
  120.5 1.0 collective-permute-start.14
  121.4 1.1 collective-permute-start.15
  122.5 1.1 convert_element_type.141
  123.6 14.0 %fusion.9 = (bf16[2,2048,384]{1,2,0:T(8,128)(2,1)}, bf16[2,2048,384]{1,2,0:T(8,128)(2,1)}) fusion(f32[2048,2,384]{0,2,1:T(8,128)} %get-tuple-element.150, f32[2048,2,384]{0,2,1:T(8,128)} %copy-done.11, bf16[1,2,384,1024]{3,2,1,0:T(8,128)(2,1)} %param.16, f32[2048,1024]{1,0:T(8,128)S(1)} %convert_element_type.141, f32[2,2048]{1,0:T(2,128)S(1)} %copy.35), kind=kOutput, calls=%fused_computation.15 | convolution fusion | flops 3250061312 | bytes 28852224 | tf_op jit(solution)/shard_map/etd,ehd->eth/dot_general | solution.py:184
  137.6 14.7 %reduce-precision_reduce_fusion = f32[2048,1024]{1,0:T(8,128)} fusion(bf16[2,2048,384]{1,2,0:T(8,128)(2,1)} %get-tuple-element.131, bf16[2,2048,384]{1,2,0:T(8,128)(2,1)} %get-tuple-element.130, bf16[2,1024,384]{2,1,0:T(8,128)(2,1)} %bitcast.103, bf16[2,1024,384]{2,1,0:T(8,128)(2,1)} %bitcast.102), kind=kOutput, calls=%fused_computation | convolution fusion | flops 6467616768 | bytes 17825792 | tf_op jit(solution)/shard_map/eth,edh->etd/dot_general | solution.py:201
  152.3 4.2 %convert.15 = bf16[2048,1024]{1,0:T(8,128)(2,1)S(1)} convert(f32[2048,1024]{1,0:T(8,128)} %reduce-precision_reduce_fusion) | non-fusion elementwise | flops 2097152 | bytes 12582912 | tf_op jit(solution)/shard_map/convert.5
  156.6 1.0 collective-permute-start.21
  157.5 1.1 collective-permute-start.22
  159.3 2.2 add_convert_fusion.4
  161.5 1.0 collective-permute-start.16
  162.5 9.0 %collective-permute-done.21 = bf16[256,1024]{1,0:T(8,128)(2,1)S(1)} collective-permute-done((bf16[256,1024]{1,0:T(8,128)(2,1)S(1)}, bf16[256,1024]{1,0:T(8,128)(2,1)S(1)}, u32[]{:S(2)}, u32[]{:S(2)}) %collective-permute-start.21) | collective-permute-done | bytes 524320 | tf_op jit(solution)/shard_map/ppermute | solution.py:50
  172.3 1.2 fusion.30
  173.5 1.2 collective-permute-start.23
  175.5 12.9 %fusion.35 = (f32[1,2,384,1024]{3,2,1,0:T(8,128)}, bf16[1,2,384,1024]{3,2,1,0:T(8,128)(2,1)}, f32[1,2,384,1024]{3,2,1,0:T(8,128)}) fusion(f32[1,2,384,1024]{3,2,1,0:T(8,128)} %param.18, f32[1,2,384,1024]{3,2,1,0:T(8,128)} %param.17, bf16[1,2,384,1024]{3,2,1,0:T(8,128)(2,1)} %collective-permute-done.28, ...), kind=kOutput, calls=%fused_computation.65 | convolution fusion | flops 3246129152 | bytes 30425088 | tf_op jit(solution)/shard_map/eth,etd->ehd/dot_general | solution.py:191
  188.5 2.2 add_convert_fusion.2
  190.6 1.2 collective-permute-start.18
  192.7 1.1 collective-permute-done.23
  193.8 3.9 %collective-permute-done.24 = bf16[256,1024]{1,0:T(8,128)(2,1)} collective-permute-done((bf16[256,1024]{1,0:T(8,128)(2,1)S(1)}, bf16[256,1024]{1,0:T(8,128)(2,1)}, u32[]{:S(2)}, u32[]{:S(2)}) %collective-permute-start.24) | collective-permute-done | bytes 524320 | tf_op jit(solution)/shard_map/ppermute | solution.py:51
  197.7 1.4 fusion.28
  199.1 1.0 collective-permute-start.25
  200.1 1.1 collective-permute-start.26
  201.2 7.2 %convert_bitcast_fusion = bf16[2,1024,768]{1,2,0:T(8,128)(2,1)S(1)} fusion(bf16[2048,1024,1]{1,0,2:T(8,128)(2,1)S(1)} %bitcast.100, bf16[2,2048,384]{1,2,0:T(8,128)(2,1)} %get-tuple-element.131, bf16[2,2048,384]{1,2,0:T(8,128)(2,1)S(1)} %copy-done.12), kind=kOutput, calls=%fused_computation.38 | convolution fusion | flops 6456606720 | bytes 13631488 | tf_op jit(solution)/shard_map/td,eth->edh/dot_general | solution.py:195
  208.5 2.4 %add_convert_fusion.1 = bf16[256,1024]{1,0:T(8,128)(2,1)} fusion(f32[2048,1024]{1,0:T(8,128)} %multiply_reduce_fusion, bf16[256,1024]{1,0:T(8,128)(2,1)S(1)} %collective-permute-done.18), kind=kLoop, calls=%fused_computation.59 | loop fusion | flops 786432 | bytes 2097152 | tf_op jit(solution)/shard_map/convert_element_type | solution.py:86
  210.8 0.9 collective-permute-start.20
  211.7 5.0 %collective-permute-done.25 = bf16[256,1024]{1,0:T(8,128)(2,1)S(1)} collective-permute-done((bf16[256,1024]{1,0:T(8,128)(2,1)S(1)}, bf16[256,1024]{1,0:T(8,128)(2,1)S(1)}, u32[]{:S(2)}, u32[]{:S(2)}) %collective-permute-start.25) | collective-permute-done | bytes 524320 | tf_op jit(solution)/shard_map/ppermute | solution.py:50
  216.8 1.0 fusion.27
  217.8 1.2 collective-permute-start.27
  219.3 1.6 copy.40
  220.9 1.6 copy.41
  222.4 3.5 %collective-permute-done.20 = bf16[256,1024]{1,0:T(8,128)(2,1)} collective-permute-done((bf16[256,1024]{1,0:T(8,128)(2,1)}, bf16[256,1024]{1,0:T(8,128)(2,1)}, u32[]{:S(2)}, u32[]{:S(2)}) %collective-permute-start.20) | collective-permute-done | bytes 524320 | tf_op jit(solution)/shard_map/ppermute | solution.py:46
  225.9 2.6 %add_convert_fusion = bf16[256,1024]{1,0:T(8,128)(2,1)} fusion(bf16[256,1024]{1,0:T(8,128)(2,1)} %collective-permute-done.20, bf16[256,1024]{1,0:T(8,128)(2,1)} %copy-done.5, f32[2048,1024]{1,0:T(8,128)} %multiply_reduce_fusion), kind=kLoop, calls=%fused_computation.58 | loop fusion | flops 1310720 | bytes 2621440 | tf_op jit(solution)/shard_map/convert_element_type | solution.py:237
  228.5 3.0 %collective-permute-done.27 = bf16[256,1024]{1,0:T(8,128)(2,1)} collective-permute-done((bf16[256,1024]{1,0:T(8,128)(2,1)}, bf16[256,1024]{1,0:T(8,128)(2,1)}, u32[]{:S(2)}, u32[]{:S(2)}) %collective-permute-start.27) | collective-permute-done | bytes 524320 | tf_op jit(solution)/shard_map/ppermute | solution.py:46
  231.6 2.4 %fusion.33 = bf16[256,1024]{1,0:T(8,128)(2,1)} fusion(f32[2048,1024]{1,0:T(8,128)} %reduce-precision_reduce_fusion, bf16[256,1024]{1,0:T(8,128)(2,1)} %collective-permute-done.27, bf16[256,1024]{1,0:T(8,128)(2,1)S(1)} %copy-done.7), kind=kLoop, calls=%fused_computation.56 | loop fusion | flops 1310720 | bytes 2621440 | tf_op jit(solution)/shard_map/convert_element_type | solution.py:238
  (75 shorter events, 14.1 us)
Async XLA Ops:
  0.6 60.5 %copy-start.4 = (bf16[256,1024]{1,0:T(8,128)(2,1)S(1)}, bf16[256,1024]{1,0:T(8,128)(2,1)}, u32[]{:S(2)}) copy-start(bf16[256,1024]{1,0:T(8,128)(2,1)} %param.10) | copy-start | bytes 1572868
  3.5 61.1 %copy-start.8 = (bf16[256,1024]{1,0:T(8,128)(2,1)S(1)}, bf16[256,1024]{1,0:T(8,128)(2,1)}, u32[]{:S(2)}) copy-start(bf16[256,1024]{1,0:T(8,128)(2,1)} %param.11) | copy-start | bytes 1572868
  3.5 15.3 %collective-permute-start = (bf16[1,264,1024]{2,1,0:T(8,128)(2,1)S(1)}, bf16[1,264,1024]{2,1,0:T(8,128)(2,1)S(1)}, u32[]{:S(2)}, u32[]{:S(2)}) collective-permute-start(bf16[1,264,1024]{2,1,0:T(8,128)(2,1)S(1)} %maximum_bitcast_fusion), channel_id=1, source_target_pairs={{0,2},{2,4},{4,6},{6,7},{7,5},{5,3},{3,1},{1,0},{8,10},{10,12},{12... | collective-permute-start | bytes 1622024 | tf_op jit(solution)/shard_map/ppermute | solution.py:50
  6.5 13.7 %collective-permute-start.1 = (bf16[1,264,1024]{2,1,0:T(8,128)(2,1)S(1)}, bf16[1,264,1024]{2,1,0:T(8,128)(2,1)S(1)}, u32[]{:S(2)}, u32[]{:S(2)}) collective-permute-start(bf16[1,264,1024]{2,1,0:T(8,128)(2,1)S(1)} %maximum_bitcast_fusion), channel_id=1, source_target_pairs={{0,1},{2,0},{4,2},{6,4},{7,6},{5,7},{3,5},{1,3},{8,9},{10,8},{12,1... | collective-permute-start | bytes 1622024 | tf_op jit(solution)/shard_map/ppermute | solution.py:51
  20.3 12.8 %collective-permute-start.2 = (bf16[1,264,1024]{2,1,0:T(8,128)(2,1)S(1)}, bf16[1,264,1024]{2,1,0:T(8,128)(2,1)S(1)}, u32[]{:S(2)}, u32[]{:S(2)}) collective-permute-start(bf16[1,264,1024]{2,1,0:T(8,128)(2,1)S(1)} %collective-permute-done), channel_id=1, source_target_pairs={{0,2},{2,4},{4,6},{6,7},{7,5},{5,3},{3,1},{1,0},{8,10},{10,12},{12... | collective-permute-start | bytes 1622024 | tf_op jit(solution)/shard_map/ppermute | solution.py:50
  21.9 12.5 %collective-permute-start.3 = (bf16[1,264,1024]{2,1,0:T(8,128)(2,1)S(1)}, bf16[1,264,1024]{2,1,0:T(8,128)(2,1)S(1)}, u32[]{:S(2)}, u32[]{:S(2)}) collective-permute-start(bf16[1,264,1024]{2,1,0:T(8,128)(2,1)S(1)} %collective-permute-done.1), channel_id=1, source_target_pairs={{0,1},{2,0},{4,2},{6,4},{7,6},{5,7},{3,5},{1,3},{8,9},{10,8},{12,1... | collective-permute-start | bytes 1622024 | tf_op jit(solution)/shard_map/ppermute | solution.py:51
  34.4 11.6 %collective-permute-start.4 = (bf16[1,264,1024]{2,1,0:T(8,128)(2,1)S(1)}, bf16[1,264,1024]{2,1,0:T(8,128)(2,1)S(1)}, u32[]{:S(2)}, u32[]{:S(2)}) collective-permute-start(bf16[1,264,1024]{2,1,0:T(8,128)(2,1)S(1)} %collective-permute-done.2), channel_id=1, source_target_pairs={{0,2},{2,4},{4,6},{6,7},{7,5},{5,3},{3,1},{1,0},{8,10},{10,12},{12... | collective-permute-start | bytes 1622024 | tf_op jit(solution)/shard_map/ppermute | solution.py:50
  36.0 11.3 %collective-permute-start.5 = (bf16[1,264,1024]{2,1,0:T(8,128)(2,1)S(1)}, bf16[1,264,1024]{2,1,0:T(8,128)(2,1)S(1)}, u32[]{:S(2)}, u32[]{:S(2)}) collective-permute-start(bf16[1,264,1024]{2,1,0:T(8,128)(2,1)S(1)} %collective-permute-done.3), channel_id=1, source_target_pairs={{0,1},{2,0},{4,2},{6,4},{7,6},{5,7},{3,5},{1,3},{8,9},{10,8},{12,1... | collective-permute-start | bytes 1622024 | tf_op jit(solution)/shard_map/ppermute | solution.py:51
  47.3 10.4 %collective-permute-start.6 = (bf16[1,264,1024]{2,1,0:T(8,128)(2,1)S(1)}, bf16[1,264,1024]{2,1,0:T(8,128)(2,1)S(1)}, u32[]{:S(2)}, u32[]{:S(2)}) collective-permute-start(bf16[1,264,1024]{2,1,0:T(8,128)(2,1)S(1)} %collective-permute-done.4), channel_id=1, source_target_pairs={{0,2},{2,4},{4,6},{6,7},{7,5},{5,3},{3,1},{1,0},{8,10},{10,12},{12... | collective-permute-start | bytes 1622024 | tf_op jit(solution)/shard_map/ppermute | solution.py:46
  64.5 9.2 %collective-permute-start.7 = (bf16[256,1024]{1,0:T(8,128)(2,1)S(1)}, bf16[256,1024]{1,0:T(8,128)(2,1)S(1)}, u32[]{:S(2)}, u32[]{:S(2)}) collective-permute-start(bf16[256,1024]{1,0:T(8,128)(2,1)S(1)} %copy-done.8), channel_id=1, source_target_pairs={{0,2},{2,4},{4,6},{6,7},{7,5},{5,3},{3,1},{1,0},{8,10},{10,12},{12... | collective-permute-start | bytes 1572872 | tf_op jit(solution)/shard_map/ppermute | solution.py:50
  66.0 9.2 %collective-permute-start.8 = (bf16[256,1024]{1,0:T(8,128)(2,1)S(1)}, bf16[256,1024]{1,0:T(8,128)(2,1)S(1)}, u32[]{:S(2)}, u32[]{:S(2)}) collective-permute-start(bf16[256,1024]{1,0:T(8,128)(2,1)S(1)} %copy-done.8), channel_id=1, source_target_pairs={{0,1},{2,0},{4,2},{6,4},{7,6},{5,7},{3,5},{1,3},{8,9},{10,8},{12,1... | collective-permute-start | bytes 1572872 | tf_op jit(solution)/shard_map/ppermute | solution.py:51
  66.6 108.1 %collective-permute-start.28 = (bf16[1,2,384,1024]{3,2,1,0:T(8,128)(2,1)}, bf16[1,2,384,1024]{3,2,1,0:T(8,128)(2,1)}, u32[]{:S(2)}, u32[]{:S(2)}) collective-permute-start(bf16[1,2,384,1024]{3,2,1,0:T(8,128)(2,1)} %param.16), channel_id=1, source_target_pairs={{0,16},{8,24},{16,0},{24,8},{1,17},{9,25},{17,1},{25,9},{2,18},{10... | collective-permute-start | bytes 4718600 | tf_op jit(solution)/shard_map/ppermute | solution.py:21
  68.1 107.4 %collective-permute-start.29 = (bf16[1,2,384,1024]{3,2,1,0:T(8,128)(2,1)}, bf16[1,2,384,1024]{3,2,1,0:T(8,128)(2,1)}, u32[]{:S(2)}, u32[]{:S(2)}) collective-permute-start(bf16[1,2,384,1024]{3,2,1,0:T(8,128)(2,1)} %param.16), channel_id=1, source_target_pairs={{0,8},{8,16},{16,24},{24,0},{1,9},{9,17},{17,25},{25,1},{2,10},{10... | collective-permute-start | bytes 4718600 | tf_op jit(solution)/shard_map/ppermute | solution.py:21
  68.1 9.2 %copy-start.9 = (bf16[1,2,1024,384]{3,2,1,0:T(8,128)(2,1)S(1)}, bf16[1,2,1024,384]{3,2,1,0:T(8,128)(2,1)}, u32[]{:S(2)}) copy-start(bf16[1,2,1024,384]{3,2,1,0:T(8,128)(2,1)} %param.14) | copy-start | bytes 4718596
  70.9 18.2 %copy-start.2 = (bf16[8,256,1024]{2,1,0:T(8,128)(2,1)}, bf16[8,256,1024]{2,1,0:T(8,128)(2,1)S(1)}, u32[]{:S(2)}) copy-start(bf16[8,256,1024]{2,1,0:T(8,128)(2,1)S(1)} %slice.108) | copy-start | bytes 12582916
  75.3 11.3 %collective-permute-start.9 = (bf16[256,1024]{1,0:T(8,128)(2,1)S(1)}, bf16[256,1024]{1,0:T(8,128)(2,1)}, u32[]{:S(2)}, u32[]{:S(2)}) collective-permute-start(bf16[256,1024]{1,0:T(8,128)(2,1)S(1)} %collective-permute-done.7), channel_id=1, source_target_pairs={{0,2},{2,4},{4,6},{6,7},{7,5},{5,3},{3,1},{1,0},{8,10},{10,12},{12... | collective-permute-start | bytes 1572872 | tf_op jit(solution)/shard_map/ppermute | solution.py:50
  77.1 9.6 %collective-permute-start.10 = (bf16[256,1024]{1,0:T(8,128)(2,1)S(1)}, bf16[256,1024]{1,0:T(8,128)(2,1)}, u32[]{:S(2)}, u32[]{:S(2)}) collective-permute-start(bf16[256,1024]{1,0:T(8,128)(2,1)S(1)} %collective-permute-done.8), channel_id=1, source_target_pairs={{0,1},{2,0},{4,2},{6,4},{7,6},{5,7},{3,5},{1,3},{8,9},{10,8},{12,1... | collective-permute-start | bytes 1572872 | tf_op jit(solution)/shard_map/ppermute | solution.py:51
  77.3 11.8 %copy-start.10 = (bf16[1,2,1024,384]{3,2,1,0:T(8,128)(2,1)S(1)}, bf16[1,2,1024,384]{3,2,1,0:T(8,128)(2,1)}, u32[]{:S(2)}) copy-start(bf16[1,2,1024,384]{3,2,1,0:T(8,128)(2,1)} %param.15) | copy-start | bytes 4718596
  81.0 15.1 %copy-start.11 = (f32[2048,2,384]{0,2,1:T(8,128)}, f32[2048,2,384]{0,2,1:T(8,128)S(1)}, u32[]{:S(2)}) copy-start(f32[2048,2,384]{0,2,1:T(8,128)S(1)} %fusion.40) | copy-start | bytes 18874372
  86.7 11.4 %collective-permute-start.11 = (bf16[256,1024]{1,0:T(8,128)(2,1)}, bf16[256,1024]{1,0:T(8,128)(2,1)}, u32[]{:S(2)}, u32[]{:S(2)}) collective-permute-start(bf16[256,1024]{1,0:T(8,128)(2,1)} %collective-permute-done.9), channel_id=1, source_target_pairs={{0,2},{2,4},{4,6},{6,7},{7,5},{5,3},{3,1},{1,0},{8,10},{10,12},{12... | collective-permute-start | bytes 1572872 | tf_op jit(solution)/shard_map/ppermute | solution.py:50
  89.1 9.5 %collective-permute-start.12 = (bf16[256,1024]{1,0:T(8,128)(2,1)}, bf16[256,1024]{1,0:T(8,128)(2,1)}, u32[]{:S(2)}, u32[]{:S(2)}) collective-permute-start(bf16[256,1024]{1,0:T(8,128)(2,1)} %collective-permute-done.10), channel_id=1, source_target_pairs={{0,1},{2,0},{4,2},{6,4},{7,6},{5,7},{3,5},{1,3},{8,9},{10,8},{12,1... | collective-permute-start | bytes 1572872 | tf_op jit(solution)/shard_map/ppermute | solution.py:51
  98.6 13.2 %collective-permute-start.13 = (bf16[256,1024]{1,0:T(8,128)(2,1)}, bf16[256,1024]{1,0:T(8,128)(2,1)S(1)}, u32[]{:S(2)}, u32[]{:S(2)}) collective-permute-start(bf16[256,1024]{1,0:T(8,128)(2,1)} %collective-permute-done.11), channel_id=1, source_target_pairs={{0,2},{2,4},{4,6},{6,7},{7,5},{5,3},{3,1},{1,0},{8,10},{10,12},{12... | collective-permute-start | bytes 1572872 | tf_op jit(solution)/shard_map/ppermute | solution.py:46
  120.5 37.1 %collective-permute-start.14 = (bf16[256,1024]{1,0:T(8,128)(2,1)S(1)}, bf16[256,1024]{1,0:T(8,128)(2,1)}, u32[]{:S(2)}, u32[]{:S(2)}) collective-permute-start(bf16[256,1024]{1,0:T(8,128)(2,1)S(1)} %get-tuple-element.84), channel_id=1, source_target_pairs={{0,2},{2,4},{4,6},{6,7},{7,5},{5,3},{3,1},{1,0},{8,10},{10,12},{12... | collective-permute-start | bytes 1572872 | tf_op jit(solution)/shard_map/ppermute | solution.py:50
  121.4 37.9 %collective-permute-start.15 = (bf16[256,1024]{1,0:T(8,128)(2,1)S(1)}, bf16[256,1024]{1,0:T(8,128)(2,1)}, u32[]{:S(2)}, u32[]{:S(2)}) collective-permute-start(bf16[256,1024]{1,0:T(8,128)(2,1)S(1)} %get-tuple-element.85), channel_id=1, source_target_pairs={{0,1},{2,0},{4,2},{6,4},{7,6},{5,7},{3,5},{1,3},{8,9},{10,8},{12,1... | collective-permute-start | bytes 1572872 | tf_op jit(solution)/shard_map/ppermute | solution.py:51
  123.6 14.0 %copy-start.1 = (f32[2048,1024]{1,0:T(8,128)}, f32[2048,1024]{1,0:T(8,128)S(1)}, u32[]{:S(2)}) copy-start(f32[2048,1024]{1,0:T(8,128)S(1)} %convert_element_type.141) | copy-start | bytes 25165828
  152.3 20.1 %copy-start = (f32[2048,1024]{1,0:T(8,128)S(1)}, f32[2048,1024]{1,0:T(8,128)}, u32[]{:S(2)}) copy-start(f32[2048,1024]{1,0:T(8,128)} %reduce-precision_reduce_fusion) | copy-start | bytes 25165828
  156.6 14.9 %collective-permute-start.21 = (bf16[256,1024]{1,0:T(8,128)(2,1)S(1)}, bf16[256,1024]{1,0:T(8,128)(2,1)S(1)}, u32[]{:S(2)}, u32[]{:S(2)}) collective-permute-start(bf16[256,1024]{1,0:T(8,128)(2,1)S(1)} %get-tuple-element.97), channel_id=1, source_target_pairs={{0,2},{2,4},{4,6},{6,7},{7,5},{5,3},{3,1},{1,0},{8,10},{10,12},{12... | collective-permute-start | bytes 1572872 | tf_op jit(solution)/shard_map/ppermute | solution.py:50
  157.5 14.8 %collective-permute-start.22 = (bf16[256,1024]{1,0:T(8,128)(2,1)S(1)}, bf16[256,1024]{1,0:T(8,128)(2,1)S(1)}, u32[]{:S(2)}, u32[]{:S(2)}) collective-permute-start(bf16[256,1024]{1,0:T(8,128)(2,1)S(1)} %get-tuple-element.98), channel_id=1, source_target_pairs={{0,1},{2,0},{4,2},{6,4},{7,6},{5,7},{3,5},{1,3},{8,9},{10,8},{12,1... | collective-permute-start | bytes 1572872 | tf_op jit(solution)/shard_map/ppermute | solution.py:51
  161.5 26.9 %collective-permute-start.16 = (bf16[256,1024]{1,0:T(8,128)(2,1)S(1)}, bf16[256,1024]{1,0:T(8,128)(2,1)S(1)}, u32[]{:S(2)}, u32[]{:S(2)}) collective-permute-start(bf16[256,1024]{1,0:T(8,128)(2,1)S(1)} %get-tuple-element.88), channel_id=1, source_target_pairs={{0,2},{2,4},{4,6},{6,7},{7,5},{5,3},{3,1},{1,0},{8,10},{10,12},{12... | collective-permute-start | bytes 1572872 | tf_op jit(solution)/shard_map/ppermute | solution.py:50
  171.5 17.0 %collective-permute-start.17 = (bf16[256,1024]{1,0:T(8,128)(2,1)S(1)}, bf16[256,1024]{1,0:T(8,128)(2,1)}, u32[]{:S(2)}, u32[]{:S(2)}) collective-permute-start(bf16[256,1024]{1,0:T(8,128)(2,1)S(1)} %get-tuple-element.89), channel_id=1, source_target_pairs={{0,1},{2,0},{4,2},{6,4},{7,6},{5,7},{3,5},{1,3},{8,9},{10,8},{12,1... | collective-permute-start | bytes 1572872 | tf_op jit(solution)/shard_map/ppermute | solution.py:51
  173.5 20.3 %collective-permute-start.23 = (bf16[256,1024]{1,0:T(8,128)(2,1)}, bf16[256,1024]{1,0:T(8,128)(2,1)S(1)}, u32[]{:S(2)}, u32[]{:S(2)}) collective-permute-start(bf16[256,1024]{1,0:T(8,128)(2,1)} %get-tuple-element.101), channel_id=1, source_target_pairs={{0,2},{2,4},{4,6},{6,7},{7,5},{5,3},{3,1},{1,0},{8,10},{10,12},{12... | collective-permute-start | bytes 1572872 | tf_op jit(solution)/shard_map/ppermute | solution.py:50
  174.7 23.0 %collective-permute-start.24 = (bf16[256,1024]{1,0:T(8,128)(2,1)S(1)}, bf16[256,1024]{1,0:T(8,128)(2,1)}, u32[]{:S(2)}, u32[]{:S(2)}) collective-permute-start(bf16[256,1024]{1,0:T(8,128)(2,1)S(1)} %get-tuple-element.102), channel_id=1, source_target_pairs={{0,1},{2,0},{4,2},{6,4},{7,6},{5,7},{3,5},{1,3},{8,9},{10,8},{12,1... | collective-permute-start | bytes 1572872 | tf_op jit(solution)/shard_map/ppermute | solution.py:51
  188.4 12.8 %copy-start.3 = (bf16[8,256,1024]{2,1,0:T(8,128)(2,1)S(1)}, bf16[8,256,1024]{2,1,0:T(8,128)(2,1)}, u32[]{:S(2)}) copy-start(bf16[8,256,1024]{2,1,0:T(8,128)(2,1)} %copy-done.2) | copy-start | bytes 12582916
  188.4 12.8 %copy-start.12 = (bf16[2,2048,384]{1,2,0:T(8,128)(2,1)S(1)}, bf16[2,2048,384]{1,2,0:T(8,128)(2,1)}, u32[]{:S(2)}) copy-start(bf16[2,2048,384]{1,2,0:T(8,128)(2,1)} %get-tuple-element.130) | copy-start | bytes 9437188
  190.6 17.8 %collective-permute-start.18 = (bf16[256,1024]{1,0:T(8,128)(2,1)S(1)}, bf16[256,1024]{1,0:T(8,128)(2,1)S(1)}, u32[]{:S(2)}, u32[]{:S(2)}) collective-permute-start(bf16[256,1024]{1,0:T(8,128)(2,1)S(1)} %get-tuple-element.92), channel_id=1, source_target_pairs={{0,2},{2,4},{4,6},{6,7},{7,5},{5,3},{3,1},{1,0},{8,10},{10,12},{12... | collective-permute-start | bytes 1572872 | tf_op jit(solution)/shard_map/ppermute | solution.py:50
  191.9 16.6 %collective-permute-start.19 = (bf16[256,1024]{1,0:T(8,128)(2,1)S(1)}, bf16[256,1024]{1,0:T(8,128)(2,1)S(1)}, u32[]{:S(2)}, u32[]{:S(2)}) collective-permute-start(bf16[256,1024]{1,0:T(8,128)(2,1)S(1)} %get-tuple-element.93), channel_id=1, source_target_pairs={{0,1},{2,0},{4,2},{6,4},{7,6},{5,7},{3,5},{1,3},{8,9},{10,8},{12,1... | collective-permute-start | bytes 1572872 | tf_op jit(solution)/shard_map/ppermute | solution.py:51
  199.1 17.7 %collective-permute-start.25 = (bf16[256,1024]{1,0:T(8,128)(2,1)S(1)}, bf16[256,1024]{1,0:T(8,128)(2,1)S(1)}, u32[]{:S(2)}, u32[]{:S(2)}) collective-permute-start(bf16[256,1024]{1,0:T(8,128)(2,1)S(1)} %get-tuple-element.105), channel_id=1, source_target_pairs={{0,2},{2,4},{4,6},{6,7},{7,5},{5,3},{3,1},{1,0},{8,10},{10,12},{12... | collective-permute-start | bytes 1572872 | tf_op jit(solution)/shard_map/ppermute | solution.py:50
  200.1 16.7 %collective-permute-start.26 = (bf16[256,1024]{1,0:T(8,128)(2,1)S(1)}, bf16[256,1024]{1,0:T(8,128)(2,1)S(1)}, u32[]{:S(2)}, u32[]{:S(2)}) collective-permute-start(bf16[256,1024]{1,0:T(8,128)(2,1)S(1)} %get-tuple-element.106), channel_id=1, source_target_pairs={{0,1},{2,0},{4,2},{6,4},{7,6},{5,7},{3,5},{1,3},{8,9},{10,8},{12,1... | collective-permute-start | bytes 1572872 | tf_op jit(solution)/shard_map/ppermute | solution.py:51
  208.4 10.8 %copy-start.5 = (bf16[256,1024]{1,0:T(8,128)(2,1)}, bf16[256,1024]{1,0:T(8,128)(2,1)S(1)}, u32[]{:S(2)}) copy-start(bf16[256,1024]{1,0:T(8,128)(2,1)S(1)} %collective-permute-done.19) | copy-start | bytes 1572868
  210.8 15.1 %collective-permute-start.20 = (bf16[256,1024]{1,0:T(8,128)(2,1)}, bf16[256,1024]{1,0:T(8,128)(2,1)}, u32[]{:S(2)}, u32[]{:S(2)}) collective-permute-start(bf16[256,1024]{1,0:T(8,128)(2,1)} %add_convert_fusion.1), channel_id=1, source_target_pairs={{0,2},{2,4},{4,6},{6,7},{7,5},{5,3},{3,1},{1,0},{8,10},{10,12},{12... | collective-permute-start | bytes 1572872 | tf_op jit(solution)/shard_map/ppermute | solution.py:46
  216.8 2.5 %copy-start.6 = (bf16[256,1024]{1,0:T(8,128)(2,1)}, bf16[256,1024]{1,0:T(8,128)(2,1)S(1)}, u32[]{:S(2)}) copy-start(bf16[256,1024]{1,0:T(8,128)(2,1)S(1)} %collective-permute-done.26) | copy-start | bytes 1572868
  217.8 13.8 %collective-permute-start.27 = (bf16[256,1024]{1,0:T(8,128)(2,1)}, bf16[256,1024]{1,0:T(8,128)(2,1)}, u32[]{:S(2)}, u32[]{:S(2)}) collective-permute-start(bf16[256,1024]{1,0:T(8,128)(2,1)} %fusion.27), channel_id=1, source_target_pairs={{0,2},{2,4},{4,6},{6,7},{7,5},{5,3},{3,1},{1,0},{8,10},{10,12},{12... | collective-permute-start | bytes 1572872 | tf_op jit(solution)/shard_map/ppermute | solution.py:46
  220.9 10.7 %copy-start.7 = (bf16[256,1024]{1,0:T(8,128)(2,1)S(1)}, bf16[256,1024]{1,0:T(8,128)(2,1)}, u32[]{:S(2)}) copy-start(bf16[256,1024]{1,0:T(8,128)(2,1)} %copy-done.6) | copy-start | bytes 1572868

commit v9 on v8

--- a/solution.py
+++ b/solution.py
@@ -166,12 +166,11 @@
     joint_matrix = jnp.concatenate([gate_matrix, up_matrix], axis=2)
 
     def chunk_pass(chunk_tokens, chunk_cot, chunk_weight):
-        gate_value = jnp.einsum(
-            "td,edh->eth", chunk_tokens, gate_matrix, preferred_element_type=jnp.float32
-        )
-        up_value = jnp.einsum(
-            "td,edh->eth", chunk_tokens, up_matrix, preferred_element_type=jnp.float32
-        )
+        joint_value = jnp.einsum(
+            "td,edh->eth", chunk_tokens, joint_matrix, preferred_element_type=jnp.float32
+        )
+        gate_value = joint_value[..., :hidden_width]
+        up_value = joint_value[..., hidden_width:]
         sigmoid_gate = jax.nn.sigmoid(gate_value)
         active = gate_value * sigmoid_gate
         hidden = (active * up_value).astype(jnp.bfloat16)

time: 235 us -> 245 us (1.043)
  other arithmetic: 28.2 us -> 38 us
  matrix products: 71 us -> 64.7 us
  local copies, waits for them, and re-layouts: 18.8 us -> 24.6 us
    unnamed x43 -> x51, local copies, waits for them, and re-layouts: 12.7 us -> 19.1 us
    convert_element_type x0 -> x1, other arithmetic: none -> 5.62 us  [chunk_pass(): hidden = (active * up_value).astype(jnp.bfloat16)]
    dot_general x1, matrix products: 14 us -> 10.7 us  [chunk_pass(): jnp.einsum('etd,ehd->eth', slot_cot, down_matrix, preferred_element_type=...]
    convert_element_type x1, other arithmetic: 1.06 us -> 4.34 us  [chunk_pass(): chunk_cot.astype(jnp.float32)[None]]
    dot_general x2 -> x1, matrix products: 10.7 us -> 9.68 us  [chunk_pass(): jnp.einsum('td,edh->eth', chunk_tokens, joint_matrix, preferred_element_t...]
  transfers between devices with their start and end apart: 30 -> 30, of which waited for: 19 -> 21; matrix products, arithmetic and copies ran while one was open for 45% -> 47% of each run, Pallas kernels for 0% -> 0%
where the time goes in v9:
time: 245 us; the launch traced here: 244 us
  waiting for transfers between devices  83.1 us (34%)
  matrix products  64.7 us (26%)
  other arithmetic  38 us (16%)
  starting transfers between devices  31.7 us (13%)
  local copies, waits for them, and re-layouts  24.6 us (10%)
    ppermute x12, waiting for transfers between devices, paired_shift(): ahead_value = lax.ppermute(ahead_value, axis, ring_pairs(ring, 1))  56 us
    unnamed x51, local copies, waits for them, and re-layouts  19.1 us
    ppermute x12, starting transfers between devices, paired_shift(): ahead_value = lax.ppermute(ahead_value, axis, ring_pairs(ring, 1))  18.3 us
    ppermute x4, waiting for transfers between devices, paired_shift(): return (lax.ppermute(ahead_value, axis, ring_pairs(ring, 1)), None)  16.9 us
    dot_general x1, matrix products, chunk_pass(): jnp.einsum('eth,edh->etd', joint_cot, joint_matrix, preferred_element_typ...  13.7 us
    dot_general x1, matrix products, chunk_pass(): jnp.einsum('eth,etd->ehd', hidden, slot_cot, preferred_element_type=jnp.f...  12.8 us
    convert_element_type x6, other arithmetic, to_wire(): return value.astype(wire_dtype)  11.2 us
    dot_general x1, matrix products, chunk_pass(): jnp.einsum('etd,ehd->eth', slot_cot, down_matrix, preferred_element_type=...  10.7 us
  transfers between devices with their start and end apart: 30, of which 21 were waited for; matrix products, arithmetic and copies ran while one was open for 47% of the time, Pallas kernels for 0%

profile of v9, /device:TPU:0, one launch (start us, length us, event | category | flops | bytes accessed | tf_op | source)
XLA Modules:
  0.0 243.7 jit_solution(12890080482049221399)
XLA Ops:
  2.4 1.1 maximum_bitcast_fusion
  3.5 3.1 %collective-permute-start = (bf16[1,264,1024]{2,1,0:T(8,128)(2,1)S(1)}, bf16[1,264,1024]{2,1,0:T(8,128)(2,1)S(1)}, u32[]{:S(2)}, u32[]{:S(2)}) collective-permute-start(bf16[1,264,1024]{2,1,0:T(8,128)(2,1)S(1)} %maximum_bitcast_fusion), channel_id=1, source_target_pairs={{0,2},{2,4},{4,6},{6,7},{7,5},{5,3},{3,1},{1,0},{8,10},{10,12},{12... | collective-permute-start | bytes 1622024 | tf_op jit(solution)/shard_map/ppermute | solution.py:50
  6.5 12.2 %collective-permute-done = bf16[1,264,1024]{2,1,0:T(8,128)(2,1)S(1)} collective-permute-done((bf16[1,264,1024]{2,1,0:T(8,128)(2,1)S(1)}, bf16[1,264,1024]{2,1,0:T(8,128)(2,1)S(1)}, u32[]{:S(2)}, u32[]{:S(2)}) %collective-permute-start) | collective-permute-done | bytes 540704 | tf_op jit(solution)/shard_map/ppermute | solution.py:50
  18.7 1.5 collective-permute-done.1
  20.3 1.6 collective-permute-start.2
  22.3 10.8 %collective-permute-done.2 = bf16[1,264,1024]{2,1,0:T(8,128)(2,1)S(1)} collective-permute-done((bf16[1,264,1024]{2,1,0:T(8,128)(2,1)S(1)}, bf16[1,264,1024]{2,1,0:T(8,128)(2,1)S(1)}, u32[]{:S(2)}, u32[]{:S(2)}) %collective-permute-start.2) | collective-permute-done | bytes 540704 | tf_op jit(solution)/shard_map/ppermute | solution.py:50
  33.1 1.3 collective-permute-done.3
  34.4 1.6 collective-permute-start.4
  36.4 9.6 %collective-permute-done.4 = bf16[1,264,1024]{2,1,0:T(8,128)(2,1)S(1)} collective-permute-done((bf16[1,264,1024]{2,1,0:T(8,128)(2,1)S(1)}, bf16[1,264,1024]{2,1,0:T(8,128)(2,1)S(1)}, u32[]{:S(2)}, u32[]{:S(2)}) %collective-permute-start.4) | collective-permute-done | bytes 540704 | tf_op jit(solution)/shard_map/ppermute | solution.py:50
  46.0 1.3 collective-permute-done.5
  47.3 1.5 collective-permute-start.6
  48.8 8.9 %collective-permute-done.6 = bf16[1,264,1024]{2,1,0:T(8,128)(2,1)S(1)} collective-permute-done((bf16[1,264,1024]{2,1,0:T(8,128)(2,1)S(1)}, bf16[1,264,1024]{2,1,0:T(8,128)(2,1)S(1)}, u32[]{:S(2)}, u32[]{:S(2)}) %collective-permute-start.6) | collective-permute-done | bytes 540704 | tf_op jit(solution)/shard_map/ppermute | solution.py:46
  64.5 1.5 collective-permute-start.7
  66.6 1.5 collective-permute-start.28
  68.1 1.6 copy.39
  69.7 1.7 copy.38
  71.4 3.2 %slice.116 = bf16[8,256,1024]{2,1,0:T(8,128)(2,1)S(1)} slice(bf16[8,264,1024]{2,1,0:T(8,128)(2,1)} %constant_dynamic-update-slice_fusion), slice={[0:8], [0:256], [0:1024]} | slice | bytes 8388608 | tf_op jit(solution)/shard_map/slice | solution.py:148
  74.7 0.9 collective-permute-done.8
  75.6 1.7 collective-permute-start.9
  77.6 9.7 %convolution_bitcast_fusion = f32[2,2048,768]{1,2,0:T(8,128)} fusion(bf16[2048,1024,1]{1,0,2:T(8,128)(2,1)S(1)} %bitcast.64, bf16[2,1024,384]{1,2,0:T(8,128)(2,1)S(1)} %bitcast.66, bf16[2,1024,384]{1,2,0:T(8,128)(2,1)S(1)} %bitcast.68), kind=kOutput, calls=%fused_computation.15 | convolution fusion | flops 6448742400 | bytes 19922944 | tf_op jit(solution)/shard_map/td,edh->eth/dot_general | solution.py:169
  87.3 0.9 slice_bitcast_fusion.2
  89.5 1.2 collective-permute-done.10
  90.7 1.4 collective-permute-start.11
  92.7 5.6 %multiply_convert_fusion.5 = bf16[2,2048,384]{1,2,0:T(8,128)(2,1)S(1)} fusion(f32[2,2048,768]{1,2,0:T(8,128)} %convolution_bitcast_fusion), kind=kLoop, calls=%fused_computation.12 | loop fusion | flops 9437184 | bytes 15728640 | tf_op jit(solution)/shard_map/convert_element_type | solution.py:176
  98.4 4.7 %collective-permute-done.11 = bf16[256,1024]{1,0:T(8,128)(2,1)S(1)} collective-permute-done((bf16[256,1024]{1,0:T(8,128)(2,1)}, bf16[256,1024]{1,0:T(8,128)(2,1)S(1)}, u32[]{:S(2)}, u32[]{:S(2)}) %collective-permute-start.11) | collective-permute-done | bytes 524320 | tf_op jit(solution)/shard_map/ppermute | solution.py:50
  103.1 2.0 collective-permute-done.12
  105.1 1.0 collective-permute-start.13
  106.1 10.6 %multiply_reduce_fusion = f32[2048,1024]{1,0:T(8,128)} fusion(f32[2,2048]{1,0:T(2,128)S(1)} %copy.37, bf16[2,2048,384]{1,2,0:T(8,128)(2,1)S(1)} %multiply_convert_fusion.5, bf16[1,2,384,1024]{3,2,1,0:T(8,128)(2,1)} %param.16), kind=kOutput, calls=%fused_computation.2 | convolution fusion | flops 3231711232 | bytes 13123584 | tf_op jit(solution)/shard_map/eth,ehd->etd/dot_general | solution.py:178
  117.1 1.1 constant_dynamic-update-slice_fusion.15
  118.2 1.1 constant_dynamic-update-slice_fusion.13
  119.3 1.1 constant_dynamic-update-slice_fusion.12
  120.4 1.1 constant_dynamic-update-slice_fusion.11
  121.5 1.1 constant_dynamic-update-slice_fusion.10
  122.6 1.1 constant_dynamic-update-slice_fusion.9
  123.7 4.2 %convert.14 = bf16[2048,1024]{1,0:T(8,128)(2,1)S(1)} convert(f32[2048,1024]{1,0:T(8,128)} %multiply_reduce_fusion) | non-fusion elementwise | flops 2097152 | bytes 12582912 | tf_op jit(solution)/shard_map/convert.7
  128.0 1.2 collective-permute-start.14
  129.2 0.9 collective-permute-start.15
  130.1 4.3 %convert_element_type.141 = f32[2048,1024]{1,0:T(8,128)} convert(bf16[2048,1024]{1,0:T(8,128)(2,1)S(1)} %constant_dynamic-update-slice_fusion.8) | non-fusion elementwise | flops 2097152 | bytes 12582912 | tf_op jit(solution)/shard_map/convert_element_type | solution.py:182
  134.4 10.7 %multiply_convert_fusion.4 = (bf16[2,2048,384]{1,2,0:T(8,128)(2,1)}, bf16[2,2048,384]{1,2,0:T(8,128)(2,1)}) fusion(f32[2,2048,768]{1,2,0:T(8,128)S(1)} %bitcast.63, bf16[1,2,384,1024]{3,2,1,0:T(8,128)(2,1)} %param.16, f32[2048,1024]{1,0:T(8,128)} %convert_element_type.141, f32[2,2048]{1,0:T(2,128)S(1)} %copy.37), kind=kOutput, calls=%fused_computation.11 | convolution fusion | flops 3250061312 | bytes 28852224 | tf_op jit(solution)/shard_map/etd,ehd->eth/dot_general | solution.py:183
  145.2 13.7 %reduce-precision_reduce_fusion = f32[2048,1024]{1,0:T(8,128)} fusion(bf16[2,2048,384]{1,2,0:T(8,128)(2,1)} %get-tuple-element.131, bf16[2,2048,384]{1,2,0:T(8,128)(2,1)} %get-tuple-element.130, bf16[2,1024,384]{1,2,0:T(8,128)(2,1)S(1)} %bitcast.67, bf16[2,1024,384]{1,2,0:T(8,128)(2,1)} %bitcast.69), kind=kOutput, calls=%fused_computation | convolution fusion | flops 6467616768 | bytes 17825792 | tf_op jit(solution)/shard_map/eth,edh->etd/dot_general | solution.py:200
  158.8 4.0 %convert.15 = bf16[2048,1024]{1,0:T(8,128)(2,1)S(1)} convert(f32[2048,1024]{1,0:T(8,128)} %reduce-precision_reduce_fusion) | non-fusion elementwise | flops 2097152 | bytes 12582912 | tf_op jit(solution)/shard_map/convert.5
  162.9 1.2 collective-permute-start.21
  165.7 1.6 add_convert_fusion.4
  167.3 1.2 collective-permute-start.16
  168.5 9.3 %collective-permute-done.21 = bf16[256,1024]{1,0:T(8,128)(2,1)S(1)} collective-permute-done((bf16[256,1024]{1,0:T(8,128)(2,1)S(1)}, bf16[256,1024]{1,0:T(8,128)(2,1)S(1)}, u32[]{:S(2)}, u32[]{:S(2)}) %collective-permute-start.21) | collective-permute-done | bytes 524320 | tf_op jit(solution)/shard_map/ppermute | solution.py:50
  178.5 2.7 %fusion.20 = (bf16[256,1024]{1,0:T(8,128)(2,1)S(1)}, bf16[256,1024]{1,0:T(8,128)(2,1)}) fusion(f32[2048,1024]{1,0:T(8,128)} %reduce-precision_reduce_fusion, bf16[256,1024]{1,0:T(8,128)(2,1)S(1)} %collective-permute-done.22, bf16[256,1024]{1,0:T(8,128)(2,1)S(1)} %collective-permute-done.21), kind=kLoop, calls=%fused_computation.41 | loop fusion | flops 1572864 | bytes 4194304 | tf_op jit(solution)/shard_map/convert_element_type | solution.py:86
  181.2 1.4 collective-permute-start.23
  183.2 12.8 %fusion.25 = (f32[1,2,384,1024]{3,2,1,0:T(8,128)}, bf16[1,2,384,1024]{3,2,1,0:T(8,128)(2,1)}, f32[1,2,384,1024]{3,2,1,0:T(8,128)}) fusion(f32[1,2,384,1024]{3,2,1,0:T(8,128)} %param.18, f32[1,2,384,1024]{3,2,1,0:T(8,128)} %param.17, bf16[1,2,384,1024]{3,2,1,0:T(8,128)(2,1)} %collective-permute-done.28, ...), kind=kOutput, calls=%fused_computation.55 | convolution fusion | flops 3246129152 | bytes 30425088 | tf_op jit(solution)/shard_map/eth,etd->ehd/dot_general | solution.py:190
  196.1 1.6 add_convert_fusion.2
  197.7 1.7 collective-permute-start.18
  201.2 2.0 fusion.18
  203.9 1.4 collective-permute-start.26
  205.3 7.2 %convert_bitcast_fusion = bf16[2,1024,768]{1,2,0:T(8,128)(2,1)S(1)} fusion(bf16[2048,1024,1]{1,0,2:T(8,128)(2,1)S(1)} %bitcast.65, bf16[2,2048,384]{1,2,0:T(8,128)(2,1)} %get-tuple-element.131, bf16[2,2048,384]{1,2,0:T(8,128)(2,1)S(1)} %copy-done.10), kind=kOutput, calls=%fused_computation.28 | convolution fusion | flops 6456606720 | bytes 13631488 | tf_op jit(solution)/shard_map/td,eth->edh/dot_general | solution.py:194
  212.8 1.1 collective-permute-done.19
  213.8 1.0 add_convert_fusion.1
  215.5 8.5 %collective-permute-done.25 = bf16[256,1024]{1,0:T(8,128)(2,1)S(1)} collective-permute-done((bf16[256,1024]{1,0:T(8,128)(2,1)S(1)}, bf16[256,1024]{1,0:T(8,128)(2,1)S(1)}, u32[]{:S(2)}, u32[]{:S(2)}) %collective-permute-start.25) | collective-permute-done | bytes 524320 | tf_op jit(solution)/shard_map/ppermute | solution.py:50
  224.0 2.4 fusion.17
  226.4 1.4 collective-permute-start.27
  228.1 1.6 copy.43
  229.7 1.6 copy.44
  231.3 4.1 %collective-permute-done.20 = bf16[256,1024]{1,0:T(8,128)(2,1)} collective-permute-done((bf16[256,1024]{1,0:T(8,128)(2,1)}, bf16[256,1024]{1,0:T(8,128)(2,1)}, u32[]{:S(2)}, u32[]{:S(2)}) %collective-permute-start.20) | collective-permute-done | bytes 524320 | tf_op jit(solution)/shard_map/ppermute | solution.py:46
  235.4 2.6 %add_convert_fusion = bf16[256,1024]{1,0:T(8,128)(2,1)} fusion(bf16[256,1024]{1,0:T(8,128)(2,1)} %collective-permute-done.20, bf16[256,1024]{1,0:T(8,128)(2,1)} %copy-done.7, f32[2048,1024]{1,0:T(8,128)} %multiply_reduce_fusion), kind=kLoop, calls=%fused_computation.48 | loop fusion | flops 1310720 | bytes 2621440 | tf_op jit(solution)/shard_map/convert_element_type | solution.py:236
  237.9 3.4 %collective-permute-done.27 = bf16[256,1024]{1,0:T(8,128)(2,1)} collective-permute-done((bf16[256,1024]{1,0:T(8,128)(2,1)}, bf16[256,1024]{1,0:T(8,128)(2,1)}, u32[]{:S(2)}, u32[]{:S(2)}) %collective-permute-start.27) | collective-permute-done | bytes 524320 | tf_op jit(solution)/shard_map/ppermute | solution.py:46
  241.3 2.4 fusion.23
  (85 shorter events, 18.7 us)
Async XLA Ops:
  0.6 60.5 %copy-start.3 = (bf16[256,1024]{1,0:T(8,128)(2,1)S(1)}, bf16[256,1024]{1,0:T(8,128)(2,1)}, u32[]{:S(2)}) copy-start(bf16[256,1024]{1,0:T(8,128)(2,1)} %param.10) | copy-start | bytes 1572868
  3.5 64.6 %copy-start.4 = (bf16[1,2,1024,384]{3,2,1,0:T(8,128)(2,1)S(1)}, bf16[1,2,1024,384]{3,2,1,0:T(8,128)(2,1)}, u32[]{:S(2)}) copy-start(bf16[1,2,1024,384]{3,2,1,0:T(8,128)(2,1)} %param.15) | copy-start | bytes 4718596
  3.5 15.3 %collective-permute-start = (bf16[1,264,1024]{2,1,0:T(8,128)(2,1)S(1)}, bf16[1,264,1024]{2,1,0:T(8,128)(2,1)S(1)}, u32[]{:S(2)}, u32[]{:S(2)}) collective-permute-start(bf16[1,264,1024]{2,1,0:T(8,128)(2,1)S(1)} %maximum_bitcast_fusion), channel_id=1, source_target_pairs={{0,2},{2,4},{4,6},{6,7},{7,5},{5,3},{3,1},{1,0},{8,10},{10,12},{12... | collective-permute-start | bytes 1622024 | tf_op jit(solution)/shard_map/ppermute | solution.py:50
  6.5 13.7 %collective-permute-start.1 = (bf16[1,264,1024]{2,1,0:T(8,128)(2,1)S(1)}, bf16[1,264,1024]{2,1,0:T(8,128)(2,1)S(1)}, u32[]{:S(2)}, u32[]{:S(2)}) collective-permute-start(bf16[1,264,1024]{2,1,0:T(8,128)(2,1)S(1)} %maximum_bitcast_fusion), channel_id=1, source_target_pairs={{0,1},{2,0},{4,2},{6,4},{7,6},{5,7},{3,5},{1,3},{8,9},{10,8},{12,1... | collective-permute-start | bytes 1622024 | tf_op jit(solution)/shard_map/ppermute | solution.py:51
  20.3 12.8 %collective-permute-start.2 = (bf16[1,264,1024]{2,1,0:T(8,128)(2,1)S(1)}, bf16[1,264,1024]{2,1,0:T(8,128)(2,1)S(1)}, u32[]{:S(2)}, u32[]{:S(2)}) collective-permute-start(bf16[1,264,1024]{2,1,0:T(8,128)(2,1)S(1)} %collective-permute-done), channel_id=1, source_target_pairs={{0,2},{2,4},{4,6},{6,7},{7,5},{5,3},{3,1},{1,0},{8,10},{10,12},{12... | collective-permute-start | bytes 1622024 | tf_op jit(solution)/shard_map/ppermute | solution.py:50
  21.9 12.5 %collective-permute-start.3 = (bf16[1,264,1024]{2,1,0:T(8,128)(2,1)S(1)}, bf16[1,264,1024]{2,1,0:T(8,128)(2,1)S(1)}, u32[]{:S(2)}, u32[]{:S(2)}) collective-permute-start(bf16[1,264,1024]{2,1,0:T(8,128)(2,1)S(1)} %collective-permute-done.1), channel_id=1, source_target_pairs={{0,1},{2,0},{4,2},{6,4},{7,6},{5,7},{3,5},{1,3},{8,9},{10,8},{12,1... | collective-permute-start | bytes 1622024 | tf_op jit(solution)/shard_map/ppermute | solution.py:51
  34.4 11.6 %collective-permute-start.4 = (bf16[1,264,1024]{2,1,0:T(8,128)(2,1)S(1)}, bf16[1,264,1024]{2,1,0:T(8,128)(2,1)S(1)}, u32[]{:S(2)}, u32[]{:S(2)}) collective-permute-start(bf16[1,264,1024]{2,1,0:T(8,128)(2,1)S(1)} %collective-permute-done.2), channel_id=1, source_target_pairs={{0,2},{2,4},{4,6},{6,7},{7,5},{5,3},{3,1},{1,0},{8,10},{10,12},{12... | collective-permute-start | bytes 1622024 | tf_op jit(solution)/shard_map/ppermute | solution.py:50
  36.0 11.3 %collective-permute-start.5 = (bf16[1,264,1024]{2,1,0:T(8,128)(2,1)S(1)}, bf16[1,264,1024]{2,1,0:T(8,128)(2,1)S(1)}, u32[]{:S(2)}, u32[]{:S(2)}) collective-permute-start(bf16[1,264,1024]{2,1,0:T(8,128)(2,1)S(1)} %collective-permute-done.3), channel_id=1, source_target_pairs={{0,1},{2,0},{4,2},{6,4},{7,6},{5,7},{3,5},{1,3},{8,9},{10,8},{12,1... | collective-permute-start | bytes 1622024 | tf_op jit(solution)/shard_map/ppermute | solution.py:51
  47.3 10.4 %collective-permute-start.6 = (bf16[1,264,1024]{2,1,0:T(8,128)(2,1)S(1)}, bf16[1,264,1024]{2,1,0:T(8,128)(2,1)S(1)}, u32[]{:S(2)}, u32[]{:S(2)}) collective-permute-start(bf16[1,264,1024]{2,1,0:T(8,128)(2,1)S(1)} %collective-permute-done.4), channel_id=1, source_target_pairs={{0,2},{2,4},{4,6},{6,7},{7,5},{5,3},{3,1},{1,0},{8,10},{10,12},{12... | collective-permute-start | bytes 1622024 | tf_op jit(solution)/shard_map/ppermute | solution.py:46
  64.5 10.2 %collective-permute-start.7 = (bf16[256,1024]{1,0:T(8,128)(2,1)}, bf16[256,1024]{1,0:T(8,128)(2,1)}, u32[]{:S(2)}, u32[]{:S(2)}) collective-permute-start(bf16[256,1024]{1,0:T(8,128)(2,1)} %param.11), channel_id=1, source_target_pairs={{0,2},{2,4},{4,6},{6,7},{7,5},{5,3},{3,1},{1,0},{8,10},{10,12},{12... | collective-permute-start | bytes 1572872 | tf_op jit(solution)/shard_map/ppermute | solution.py:50
  66.0 9.6 %collective-permute-start.8 = (bf16[256,1024]{1,0:T(8,128)(2,1)}, bf16[256,1024]{1,0:T(8,128)(2,1)}, u32[]{:S(2)}, u32[]{:S(2)}) collective-permute-start(bf16[256,1024]{1,0:T(8,128)(2,1)} %param.11), channel_id=1, source_target_pairs={{0,1},{2,0},{4,2},{6,4},{7,6},{5,7},{3,5},{1,3},{8,9},{10,8},{12,1... | collective-permute-start | bytes 1572872 | tf_op jit(solution)/shard_map/ppermute | solution.py:51
  66.6 116.0 %collective-permute-start.28 = (bf16[1,2,384,1024]{3,2,1,0:T(8,128)(2,1)}, bf16[1,2,384,1024]{3,2,1,0:T(8,128)(2,1)}, u32[]{:S(2)}, u32[]{:S(2)}) collective-permute-start(bf16[1,2,384,1024]{3,2,1,0:T(8,128)(2,1)} %param.16), channel_id=1, source_target_pairs={{0,16},{8,24},{16,0},{24,8},{1,17},{9,25},{17,1},{25,9},{2,18},{10... | collective-permute-start | bytes 4718600 | tf_op jit(solution)/shard_map/ppermute | solution.py:21
  68.1 115.1 %collective-permute-start.29 = (bf16[1,2,384,1024]{3,2,1,0:T(8,128)(2,1)}, bf16[1,2,384,1024]{3,2,1,0:T(8,128)(2,1)}, u32[]{:S(2)}, u32[]{:S(2)}) collective-permute-start(bf16[1,2,384,1024]{3,2,1,0:T(8,128)(2,1)} %param.16), channel_id=1, source_target_pairs={{0,8},{8,16},{16,24},{24,0},{1,9},{9,17},{17,25},{25,1},{2,10},{10... | collective-permute-start | bytes 4718600 | tf_op jit(solution)/shard_map/ppermute | solution.py:21
  71.4 6.2 %copy-start.6 = (bf16[1,2,1024,384]{2,3,1,0:T(8,128)(2,1)}, bf16[1,2,1024,384]{2,3,1,0:T(8,128)(2,1)S(1)}, u32[]{:S(2)}) copy-start(bf16[1,2,1024,384]{2,3,1,0:T(8,128)(2,1)S(1)} %copy.38) | copy-start | bytes 4718596
  71.4 6.2 %copy-start.5 = (bf16[1,2,1024,384]{2,3,1,0:T(8,128)(2,1)S(1)}, bf16[1,2,1024,384]{2,3,1,0:T(8,128)(2,1)}, u32[]{:S(2)}) copy-start(bf16[1,2,1024,384]{2,3,1,0:T(8,128)(2,1)} %copy.39) | copy-start | bytes 4718596
  74.7 12.7 %copy-start = (bf16[8,256,1024]{2,1,0:T(8,128)(2,1)}, bf16[8,256,1024]{2,1,0:T(8,128)(2,1)S(1)}, u32[]{:S(2)}) copy-start(bf16[8,256,1024]{2,1,0:T(8,128)(2,1)S(1)} %slice.116) | copy-start | bytes 12582916
  75.6 13.9 %collective-permute-start.9 = (bf16[256,1024]{1,0:T(8,128)(2,1)}, bf16[256,1024]{1,0:T(8,128)(2,1)}, u32[]{:S(2)}, u32[]{:S(2)}) collective-permute-start(bf16[256,1024]{1,0:T(8,128)(2,1)} %collective-permute-done.7), channel_id=1, source_target_pairs={{0,2},{2,4},{4,6},{6,7},{7,5},{5,3},{3,1},{1,0},{8,10},{10,12},{12... | collective-permute-start | bytes 1572872 | tf_op jit(solution)/shard_map/ppermute | solution.py:50
  77.3 13.4 %collective-permute-start.10 = (bf16[256,1024]{1,0:T(8,128)(2,1)}, bf16[256,1024]{1,0:T(8,128)(2,1)}, u32[]{:S(2)}, u32[]{:S(2)}) collective-permute-start(bf16[256,1024]{1,0:T(8,128)(2,1)} %collective-permute-done.8), channel_id=1, source_target_pairs={{0,1},{2,0},{4,2},{6,4},{7,6},{5,7},{3,5},{1,3},{8,9},{10,8},{12,1... | collective-permute-start | bytes 1572872 | tf_op jit(solution)/shard_map/ppermute | solution.py:51
  90.7 12.4 %collective-permute-start.11 = (bf16[256,1024]{1,0:T(8,128)(2,1)}, bf16[256,1024]{1,0:T(8,128)(2,1)S(1)}, u32[]{:S(2)}, u32[]{:S(2)}) collective-permute-start(bf16[256,1024]{1,0:T(8,128)(2,1)} %collective-permute-done.9), channel_id=1, source_target_pairs={{0,2},{2,4},{4,6},{6,7},{7,5},{5,3},{3,1},{1,0},{8,10},{10,12},{12... | collective-permute-start | bytes 1572872 | tf_op jit(solution)/shard_map/ppermute | solution.py:50
  92.2 12.9 %collective-permute-start.12 = (bf16[256,1024]{1,0:T(8,128)(2,1)}, bf16[256,1024]{1,0:T(8,128)(2,1)S(1)}, u32[]{:S(2)}, u32[]{:S(2)}) collective-permute-start(bf16[256,1024]{1,0:T(8,128)(2,1)} %collective-permute-done.10), channel_id=1, source_target_pairs={{0,1},{2,0},{4,2},{6,4},{7,6},{5,7},{3,5},{1,3},{8,9},{10,8},{12,1... | collective-permute-start | bytes 1572872 | tf_op jit(solution)/shard_map/ppermute | solution.py:51
  98.4 18.3 %copy-start.2 = (bf16[2,2048,384]{1,2,0:T(8,128)(2,1)}, bf16[2,2048,384]{1,2,0:T(8,128)(2,1)S(1)}, u32[]{:S(2)}) copy-start(bf16[2,2048,384]{1,2,0:T(8,128)(2,1)S(1)} %multiply_convert_fusion.5) | copy-start | bytes 9437188
  105.1 12.0 %collective-permute-start.13 = (bf16[256,1024]{1,0:T(8,128)(2,1)S(1)}, bf16[256,1024]{1,0:T(8,128)(2,1)}, u32[]{:S(2)}, u32[]{:S(2)}) collective-permute-start(bf16[256,1024]{1,0:T(8,128)(2,1)S(1)} %collective-permute-done.11), channel_id=1, source_target_pairs={{0,2},{2,4},{4,6},{6,7},{7,5},{5,3},{3,1},{1,0},{8,10},{10,12},{12... | collective-permute-start | bytes 1572872 | tf_op jit(solution)/shard_map/ppermute | solution.py:46
  123.7 10.7 %slice-start.2 = ((s8[12582912]{0:T(1024)(128)(4,1)}), s8[4194304]{0:T(1024)(128)(4,1)S(1)}, s32[]{:S(2)}) async-start(s8[12582912]{0:T(1024)(128)(4,1)} %bitcast.62), calls=%async_computation.2 | async-start | bytes 8388608
  123.7 10.7 %slice-start.3 = ((s8[12582912]{0:T(1024)(128)(4,1)}), s8[4194304]{0:T(1024)(128)(4,1)S(1)}, s32[]{:S(2)}) async-start(s8[12582912]{0:T(1024)(128)(4,1)} %bitcast.62), calls=%async_computation.3 | async-start | bytes 8388608
  128.0 6.4 %slice-start.4 = ((s8[12582912]{0:T(1024)(128)(4,1)}), s8[4194304]{0:T(1024)(128)(4,1)S(1)}, s32[]{:S(2)}) async-start(s8[12582912]{0:T(1024)(128)(4,1)} %bitcast.62), calls=%async_computation.4 | async-start | bytes 8388608
  128.0 36.2 %collective-permute-start.14 = (bf16[256,1024]{1,0:T(8,128)(2,1)S(1)}, bf16[256,1024]{1,0:T(8,128)(2,1)}, u32[]{:S(2)}, u32[]{:S(2)}) collective-permute-start(bf16[256,1024]{1,0:T(8,128)(2,1)S(1)} %get-tuple-element.84), channel_id=1, source_target_pairs={{0,2},{2,4},{4,6},{6,7},{7,5},{5,3},{3,1},{1,0},{8,10},{10,12},{12... | collective-permute-start | bytes 1572872 | tf_op jit(solution)/shard_map/ppermute | solution.py:50
  129.2 36.5 %collective-permute-start.15 = (bf16[256,1024]{1,0:T(8,128)(2,1)S(1)}, bf16[256,1024]{1,0:T(8,128)(2,1)}, u32[]{:S(2)}, u32[]{:S(2)}) collective-permute-start(bf16[256,1024]{1,0:T(8,128)(2,1)S(1)} %get-tuple-element.85), channel_id=1, source_target_pairs={{0,1},{2,0},{4,2},{6,4},{7,6},{5,7},{3,5},{1,3},{8,9},{10,8},{12,1... | collective-permute-start | bytes 1572872 | tf_op jit(solution)/shard_map/ppermute | solution.py:51
  130.1 35.6 %slice-start = ((s8[8388608]{0:T(1024)(128)(4,1)}), s8[4194304]{0:T(1024)(128)(4,1)S(1)}, s32[]{:S(2)}) async-start(s8[8388608]{0:T(1024)(128)(4,1)} %bitcast.60), calls=%async_computation | async-start | bytes 8388608
  134.4 31.3 %slice-start.1 = ((s8[8388608]{0:T(1024)(128)(4,1)}), s8[4194304]{0:T(1024)(128)(4,1)S(1)}, s32[]{:S(2)}) async-start(s8[8388608]{0:T(1024)(128)(4,1)} %bitcast.60), calls=%async_computation.1 | async-start | bytes 8388608
  162.9 14.9 %collective-permute-start.21 = (bf16[256,1024]{1,0:T(8,128)(2,1)S(1)}, bf16[256,1024]{1,0:T(8,128)(2,1)S(1)}, u32[]{:S(2)}, u32[]{:S(2)}) collective-permute-start(bf16[256,1024]{1,0:T(8,128)(2,1)S(1)} %get-tuple-element.97), channel_id=1, source_target_pairs={{0,2},{2,4},{4,6},{6,7},{7,5},{5,3},{3,1},{1,0},{8,10},{10,12},{12... | collective-permute-start | bytes 1572872 | tf_op jit(solution)/shard_map/ppermute | solution.py:50
  164.2 14.3 %collective-permute-start.22 = (bf16[256,1024]{1,0:T(8,128)(2,1)S(1)}, bf16[256,1024]{1,0:T(8,128)(2,1)S(1)}, u32[]{:S(2)}, u32[]{:S(2)}) collective-permute-start(bf16[256,1024]{1,0:T(8,128)(2,1)S(1)} %get-tuple-element.98), channel_id=1, source_target_pairs={{0,1},{2,0},{4,2},{6,4},{7,6},{5,7},{3,5},{1,3},{8,9},{10,8},{12,1... | collective-permute-start | bytes 1572872 | tf_op jit(solution)/shard_map/ppermute | solution.py:51
  167.3 28.7 %collective-permute-start.16 = (bf16[256,1024]{1,0:T(8,128)(2,1)S(1)}, bf16[256,1024]{1,0:T(8,128)(2,1)S(1)}, u32[]{:S(2)}, u32[]{:S(2)}) collective-permute-start(bf16[256,1024]{1,0:T(8,128)(2,1)S(1)} %get-tuple-element.88), channel_id=1, source_target_pairs={{0,2},{2,4},{4,6},{6,7},{7,5},{5,3},{3,1},{1,0},{8,10},{10,12},{12... | collective-permute-start | bytes 1572872 | tf_op jit(solution)/shard_map/ppermute | solution.py:50
  177.9 18.2 %collective-permute-start.17 = (bf16[256,1024]{1,0:T(8,128)(2,1)S(1)}, bf16[256,1024]{1,0:T(8,128)(2,1)}, u32[]{:S(2)}, u32[]{:S(2)}) collective-permute-start(bf16[256,1024]{1,0:T(8,128)(2,1)S(1)} %get-tuple-element.89), channel_id=1, source_target_pairs={{0,1},{2,0},{4,2},{6,4},{7,6},{5,7},{3,5},{1,3},{8,9},{10,8},{12,1... | collective-permute-start | bytes 1572872 | tf_op jit(solution)/shard_map/ppermute | solution.py:51
  181.2 19.2 %collective-permute-start.23 = (bf16[256,1024]{1,0:T(8,128)(2,1)}, bf16[256,1024]{1,0:T(8,128)(2,1)S(1)}, u32[]{:S(2)}, u32[]{:S(2)}) collective-permute-start(bf16[256,1024]{1,0:T(8,128)(2,1)} %get-tuple-element.101), channel_id=1, source_target_pairs={{0,2},{2,4},{4,6},{6,7},{7,5},{5,3},{3,1},{1,0},{8,10},{10,12},{12... | collective-permute-start | bytes 1572872 | tf_op jit(solution)/shard_map/ppermute | solution.py:50
  182.6 18.6 %collective-permute-start.24 = (bf16[256,1024]{1,0:T(8,128)(2,1)S(1)}, bf16[256,1024]{1,0:T(8,128)(2,1)}, u32[]{:S(2)}, u32[]{:S(2)}) collective-permute-start(bf16[256,1024]{1,0:T(8,128)(2,1)S(1)} %get-tuple-element.102), channel_id=1, source_target_pairs={{0,1},{2,0},{4,2},{6,4},{7,6},{5,7},{3,5},{1,3},{8,9},{10,8},{12,1... | collective-permute-start | bytes 1572872 | tf_op jit(solution)/shard_map/ppermute | solution.py:51
  196.0 9.2 %copy-start.1 = (bf16[8,256,1024]{2,1,0:T(8,128)(2,1)S(1)}, bf16[8,256,1024]{2,1,0:T(8,128)(2,1)}, u32[]{:S(2)}) copy-start(bf16[8,256,1024]{2,1,0:T(8,128)(2,1)} %copy-done) | copy-start | bytes 12582916
  196.0 9.2 %copy-start.10 = (bf16[2,2048,384]{1,2,0:T(8,128)(2,1)S(1)}, bf16[2,2048,384]{1,2,0:T(8,128)(2,1)}, u32[]{:S(2)}) copy-start(bf16[2,2048,384]{1,2,0:T(8,128)(2,1)} %get-tuple-element.130) | copy-start | bytes 9437188
  197.7 15.1 %collective-permute-start.18 = (bf16[256,1024]{1,0:T(8,128)(2,1)S(1)}, bf16[256,1024]{1,0:T(8,128)(2,1)S(1)}, u32[]{:S(2)}, u32[]{:S(2)}) collective-permute-start(bf16[256,1024]{1,0:T(8,128)(2,1)S(1)} %get-tuple-element.92), channel_id=1, source_target_pairs={{0,2},{2,4},{4,6},{6,7},{7,5},{5,3},{3,1},{1,0},{8,10},{10,12},{12... | collective-permute-start | bytes 1572872 | tf_op jit(solution)/shard_map/ppermute | solution.py:50
  199.3 14.5 %collective-permute-start.19 = (bf16[256,1024]{1,0:T(8,128)(2,1)S(1)}, bf16[256,1024]{1,0:T(8,128)(2,1)S(1)}, u32[]{:S(2)}, u32[]{:S(2)}) collective-permute-start(bf16[256,1024]{1,0:T(8,128)(2,1)S(1)} %get-tuple-element.93), channel_id=1, source_target_pairs={{0,1},{2,0},{4,2},{6,4},{7,6},{5,7},{3,5},{1,3},{8,9},{10,8},{12,1... | collective-permute-start | bytes 1572872 | tf_op jit(solution)/shard_map/ppermute | solution.py:51
  203.2 20.8 %collective-permute-start.25 = (bf16[256,1024]{1,0:T(8,128)(2,1)S(1)}, bf16[256,1024]{1,0:T(8,128)(2,1)S(1)}, u32[]{:S(2)}, u32[]{:S(2)}) collective-permute-start(bf16[256,1024]{1,0:T(8,128)(2,1)S(1)} %get-tuple-element.105), channel_id=1, source_target_pairs={{0,2},{2,4},{4,6},{6,7},{7,5},{5,3},{3,1},{1,0},{8,10},{10,12},{12... | collective-permute-start | bytes 1572872 | tf_op jit(solution)/shard_map/ppermute | solution.py:50
  203.9 20.1 %collective-permute-start.26 = (bf16[256,1024]{1,0:T(8,128)(2,1)S(1)}, bf16[256,1024]{1,0:T(8,128)(2,1)S(1)}, u32[]{:S(2)}, u32[]{:S(2)}) collective-permute-start(bf16[256,1024]{1,0:T(8,128)(2,1)S(1)} %get-tuple-element.106), channel_id=1, source_target_pairs={{0,1},{2,0},{4,2},{6,4},{7,6},{5,7},{3,5},{1,3},{8,9},{10,8},{12,1... | collective-permute-start | bytes 1572872 | tf_op jit(solution)/shard_map/ppermute | solution.py:51
  213.8 14.3 %copy-start.7 = (bf16[256,1024]{1,0:T(8,128)(2,1)}, bf16[256,1024]{1,0:T(8,128)(2,1)S(1)}, u32[]{:S(2)}) copy-start(bf16[256,1024]{1,0:T(8,128)(2,1)S(1)} %collective-permute-done.19) | copy-start | bytes 1572868
  214.8 20.6 %collective-permute-start.20 = (bf16[256,1024]{1,0:T(8,128)(2,1)}, bf16[256,1024]{1,0:T(8,128)(2,1)}, u32[]{:S(2)}, u32[]{:S(2)}) collective-permute-start(bf16[256,1024]{1,0:T(8,128)(2,1)} %add_convert_fusion.1), channel_id=1, source_target_pairs={{0,2},{2,4},{4,6},{6,7},{7,5},{5,3},{3,1},{1,0},{8,10},{10,12},{12... | collective-permute-start | bytes 1572872 | tf_op jit(solution)/shard_map/ppermute | solution.py:46
  224.0 4.1 %copy-start.8 = (bf16[256,1024]{1,0:T(8,128)(2,1)}, bf16[256,1024]{1,0:T(8,128)(2,1)S(1)}, u32[]{:S(2)}) copy-start(bf16[256,1024]{1,0:T(8,128)(2,1)S(1)} %collective-permute-done.26) | copy-start | bytes 1572868
  226.4 14.9 %collective-permute-start.27 = (bf16[256,1024]{1,0:T(8,128)(2,1)}, bf16[256,1024]{1,0:T(8,128)(2,1)}, u32[]{:S(2)}, u32[]{:S(2)}) collective-permute-start(bf16[256,1024]{1,0:T(8,128)(2,1)} %fusion.17), channel_id=1, source_target_pairs={{0,2},{2,4},{4,6},{6,7},{7,5},{5,3},{3,1},{1,0},{8,10},{10,12},{12... | collective-permute-start | bytes 1572872 | tf_op jit(solution)/shard_map/ppermute | solution.py:46
  229.7 11.6 %copy-start.9 = (bf16[256,1024]{1,0:T(8,128)(2,1)S(1)}, bf16[256,1024]{1,0:T(8,128)(2,1)}, u32[]{:S(2)}) copy-start(bf16[256,1024]{1,0:T(8,128)(2,1)} %copy-done.8) | copy-start | bytes 1572868

commit v10 on v8

--- a/solution.py
+++ b/solution.py
@@ -86,8 +86,9 @@
         return value.astype(wire_dtype)
 
     result = block_at(0)
-    ahead_value = to_wire(block_at(ahead)) if ahead else None
-    behind_value = to_wire(block_at(-behind)) if behind else None
+    first_ahead, first_behind = lax.optimization_barrier((block_at(ahead), block_at(-behind)))
+    ahead_value = to_wire(first_ahead) if ahead else None
+    behind_value = to_wire(first_behind) if behind else None
     for step in range(max(ahead, behind)):
         ahead_value, behind_value = paired_shift(
             ahead_value if step < ahead else None,

time: 235 us -> 230 us (0.979)
  other arithmetic: 28.2 us -> 23.6 us
  local copies, waits for them, and re-layouts: 18.8 us -> 22 us
    another operation x2 -> x0, other arithmetic: 8.24 us -> none
    convert_element_type x6, other arithmetic: 10.3 us -> 14 us  [to_wire(): return value.astype(wire_dtype)]
    slice x2, local copies, waits for them, and re-layouts: 0.14 us -> 3.39 us  [block_at(): return blocks[(offset + ahead) % size]]
where the time goes in v10:
time: 230 us; the launch traced here: 229 us
  waiting for transfers between devices  80.3 us (35%)
  matrix products  69.3 us (30%)
  starting transfers between devices  32 us (14%)
  other arithmetic  23.6 us (10%)
  local copies, waits for them, and re-layouts  22 us (10%)
    ppermute x12, waiting for transfers between devices, paired_shift(): ahead_value = lax.ppermute(ahead_value, axis, ring_pairs(ring, 1))  55.4 us
    ppermute x12, starting transfers between devices, paired_shift(): ahead_value = lax.ppermute(ahead_value, axis, ring_pairs(ring, 1))  18.3 us
    dot_general x1, matrix products, chunk_pass(): jnp.einsum('eth,edh->etd', joint_cot, joint_matrix, preferred_element_typ...  14.7 us
    ppermute x4, waiting for transfers between devices, paired_shift(): return (lax.ppermute(ahead_value, axis, ring_pairs(ring, 1)), None)  14.2 us
    convert_element_type x6, other arithmetic, to_wire(): return value.astype(wire_dtype)  14 us
    dot_general x1, matrix products, chunk_pass(): jnp.einsum('etd,ehd->eth', slot_cot, down_matrix, preferred_element_type=...  14 us
    unnamed x43, local copies, waits for them, and re-layouts  12.7 us
    dot_general x1, matrix products, chunk_pass(): jnp.einsum('eth,ehd->etd', hidden, down_matrix, preferred_element_type=jn...  11.5 us
  transfers between devices with their start and end apart: 30, of which 19 were waited for; matrix products, arithmetic and copies ran while one was open for 45% of the time, Pallas kernels for 0%

profile of v10, /device:TPU:0, one launch (start us, length us, event | category | flops | bytes accessed | tf_op | source)
XLA Modules:
  0.0 228.9 jit_solution(9145481034351347399)
XLA Ops:
  2.4 1.1 maximum_bitcast_fusion
  3.5 3.1 %collective-permute-start = (bf16[1,264,1024]{2,1,0:T(8,128)(2,1)S(1)}, bf16[1,264,1024]{2,1,0:T(8,128)(2,1)S(1)}, u32[]{:S(2)}, u32[]{:S(2)}) collective-permute-start(bf16[1,264,1024]{2,1,0:T(8,128)(2,1)S(1)} %maximum_bitcast_fusion), channel_id=1, source_target_pairs={{0,2},{2,4},{4,6},{6,7},{7,5},{5,3},{3,1},{1,0},{8,10},{10,12},{12... | collective-permute-start | bytes 1622024 | tf_op jit(solution)/shard_map/ppermute | solution.py:50
  6.5 12.2 %collective-permute-done = bf16[1,264,1024]{2,1,0:T(8,128)(2,1)S(1)} collective-permute-done((bf16[1,264,1024]{2,1,0:T(8,128)(2,1)S(1)}, bf16[1,264,1024]{2,1,0:T(8,128)(2,1)S(1)}, u32[]{:S(2)}, u32[]{:S(2)}) %collective-permute-start) | collective-permute-done | bytes 540704 | tf_op jit(solution)/shard_map/ppermute | solution.py:50
  18.7 1.5 collective-permute-done.1
  20.3 1.6 collective-permute-start.2
  22.3 10.8 %collective-permute-done.2 = bf16[1,264,1024]{2,1,0:T(8,128)(2,1)S(1)} collective-permute-done((bf16[1,264,1024]{2,1,0:T(8,128)(2,1)S(1)}, bf16[1,264,1024]{2,1,0:T(8,128)(2,1)S(1)}, u32[]{:S(2)}, u32[]{:S(2)}) %collective-permute-start.2) | collective-permute-done | bytes 540704 | tf_op jit(solution)/shard_map/ppermute | solution.py:50
  33.1 1.3 collective-permute-done.3
  34.4 1.6 collective-permute-start.4
  36.4 9.6 %collective-permute-done.4 = bf16[1,264,1024]{2,1,0:T(8,128)(2,1)S(1)} collective-permute-done((bf16[1,264,1024]{2,1,0:T(8,128)(2,1)S(1)}, bf16[1,264,1024]{2,1,0:T(8,128)(2,1)S(1)}, u32[]{:S(2)}, u32[]{:S(2)}) %collective-permute-start.4) | collective-permute-done | bytes 540704 | tf_op jit(solution)/shard_map/ppermute | solution.py:50
  46.0 1.3 collective-permute-done.5
  47.3 1.5 collective-permute-start.6
  48.8 8.9 %collective-permute-done.6 = bf16[1,264,1024]{2,1,0:T(8,128)(2,1)S(1)} collective-permute-done((bf16[1,264,1024]{2,1,0:T(8,128)(2,1)S(1)}, bf16[1,264,1024]{2,1,0:T(8,128)(2,1)S(1)}, u32[]{:S(2)}, u32[]{:S(2)}) %collective-permute-start.6) | collective-permute-done | bytes 540704 | tf_op jit(solution)/shard_map/ppermute | solution.py:46
  58.6 0.9 constant_dynamic-update-slice_fusion.6
  64.5 1.5 collective-permute-start.7
  66.6 1.5 collective-permute-start.28
  68.1 2.8 %slice.104 = bf16[8,256,1024]{2,1,0:T(8,128)(2,1)S(1)} slice(bf16[8,264,1024]{2,1,0:T(8,128)(2,1)} %constant_dynamic-update-slice_fusion), slice={[0:8], [0:256], [0:1024]} | slice | bytes 8388608 | tf_op jit(solution)/shard_map/slice | solution.py:149
  70.9 2.8 %collective-permute-done.7 = bf16[256,1024]{1,0:T(8,128)(2,1)S(1)} collective-permute-done((bf16[256,1024]{1,0:T(8,128)(2,1)S(1)}, bf16[256,1024]{1,0:T(8,128)(2,1)S(1)}, u32[]{:S(2)}, u32[]{:S(2)}) %collective-permute-start.7) | collective-permute-done | bytes 524320 | tf_op jit(solution)/shard_map/ppermute | solution.py:50
  73.7 1.6 collective-permute-done.8
  75.3 1.9 collective-permute-start.9
  77.3 3.7 %fusion.40 = f32[2048,2,384]{0,2,1:T(8,128)S(1)} fusion(bf16[2048,1024,1]{1,0,2:T(8,128)(2,1)S(1)} %bitcast.98, bf16[1,2,1024,384]{3,2,1,0:T(8,128)(2,1)S(1)} %copy-done.9), kind=kOutput, calls=%fused_computation.90 | convolution fusion | flops 3221225472 | bytes 12058624 | tf_op jit(solution)/shard_map/td,edh->eth/dot_general | solution.py:170
  81.0 5.6 %collective-permute-done.9 = bf16[256,1024]{1,0:T(8,128)(2,1)} collective-permute-done((bf16[256,1024]{1,0:T(8,128)(2,1)S(1)}, bf16[256,1024]{1,0:T(8,128)(2,1)}, u32[]{:S(2)}, u32[]{:S(2)}) %collective-permute-start.9) | collective-permute-done | bytes 524320 | tf_op jit(solution)/shard_map/ppermute | solution.py:50
  86.7 2.4 %collective-permute-start.11 = (bf16[256,1024]{1,0:T(8,128)(2,1)}, bf16[256,1024]{1,0:T(8,128)(2,1)}, u32[]{:S(2)}, u32[]{:S(2)}) collective-permute-start(bf16[256,1024]{1,0:T(8,128)(2,1)} %collective-permute-done.9), channel_id=1, source_target_pairs={{0,2},{2,4},{4,6},{6,7},{7,5},{5,3},{3,1},{1,0},{8,10},{10,12},{12... | collective-permute-start | bytes 1572872 | tf_op jit(solution)/shard_map/ppermute | solution.py:50
  89.1 7.0 %fusion.6 = (bf16[2,2048,384]{1,2,0:T(8,128)(2,1)}, f32[2048,2,384]{0,2,1:T(8,128)}) fusion(f32[2048,2,384]{0,2,1:T(8,128)S(1)} %fusion.40, bf16[2048,1024,1]{1,0,2:T(8,128)(2,1)S(1)} %bitcast.99, bf16[1,2,1024,384]{3,2,1,0:T(8,128)(2,1)S(1)} %copy-done.10), kind=kOutput, calls=%fused_computation.12 | convolution fusion | flops 3230662656 | bytes 21495808 | tf_op jit(solution)/shard_map/td,edh->eth/dot_general | solution.py:173
  96.1 0.9 slice_bitcast_fusion.2
  98.6 1.7 collective-permute-start.13
  100.3 11.5 %multiply_reduce_fusion = f32[2048,1024]{1,0:T(8,128)} fusion(f32[2,2048]{1,0:T(2,128)S(1)} %copy.35, bf16[2,2048,384]{1,2,0:T(8,128)(2,1)} %get-tuple-element.157, bf16[1,2,384,1024]{3,2,1,0:T(8,128)(2,1)} %param.16), kind=kOutput, calls=%fused_computation.2 | convolution fusion | flops 3231711232 | bytes 13123584 | tf_op jit(solution)/shard_map/eth,ehd->etd/dot_general | solution.py:180
  111.9 1.1 constant_dynamic-update-slice_fusion.14
  113.0 1.1 constant_dynamic-update-slice_fusion.13
  114.2 1.1 constant_dynamic-update-slice_fusion.9
  115.2 1.1 constant_dynamic-update-slice_fusion.8
  116.3 1.7 fusion.43
  118.0 1.0 collective-permute-start.14
  119.0 1.1 collective-permute-start.15
  120.1 1.0 convert_element_type.151
  121.2 14.0 %fusion.9 = (bf16[2,2048,384]{1,2,0:T(8,128)(2,1)}, bf16[2,2048,384]{1,2,0:T(8,128)(2,1)}) fusion(f32[2048,2,384]{0,2,1:T(8,128)} %get-tuple-element.158, f32[2048,2,384]{0,2,1:T(8,128)} %copy-done.11, bf16[1,2,384,1024]{3,2,1,0:T(8,128)(2,1)} %param.16, f32[2048,1024]{1,0:T(8,128)S(1)} %convert_element_type.151, f32[2,2048]{1,0:T(2,128)S(1)} %copy.35), kind=kOutput, calls=%fused_computation.15 | convolution fusion | flops 3250061312 | bytes 28852224 | tf_op jit(solution)/shard_map/etd,ehd->eth/dot_general | solution.py:185
  135.1 14.7 %reduce-precision_reduce_fusion = f32[2048,1024]{1,0:T(8,128)} fusion(bf16[2,2048,384]{1,2,0:T(8,128)(2,1)} %get-tuple-element.139, bf16[2,2048,384]{1,2,0:T(8,128)(2,1)} %get-tuple-element.138, bf16[2,1024,384]{2,1,0:T(8,128)(2,1)} %bitcast.103, bf16[2,1024,384]{2,1,0:T(8,128)(2,1)} %bitcast.102), kind=kOutput, calls=%fused_computation | convolution fusion | flops 6467616768 | bytes 17825792 | tf_op jit(solution)/shard_map/eth,edh->etd/dot_general | solution.py:202
  149.8 1.7 fusion.42
  151.5 1.0 collective-permute-start.21
  152.5 1.1 collective-permute-start.22
  154.3 2.3 %add_convert_fusion.4 = (bf16[256,1024]{1,0:T(8,128)(2,1)S(1)}, bf16[256,1024]{1,0:T(8,128)(2,1)S(1)}) fusion(f32[2048,1024]{1,0:T(8,128)} %multiply_reduce_fusion, bf16[256,1024]{1,0:T(8,128)(2,1)} %collective-permute-done.15, bf16[256,1024]{1,0:T(8,128)(2,1)} %collective-permute-done.14), kind=kLoop, calls=%fused_computation.62 | loop fusion | flops 1572864 | bytes 4194304 | tf_op jit(solution)/shard_map/convert_element_type | solution.py:86
  156.6 1.0 collective-permute-start.16
  157.6 8.8 %collective-permute-done.21 = bf16[256,1024]{1,0:T(8,128)(2,1)S(1)} collective-permute-done((bf16[256,1024]{1,0:T(8,128)(2,1)S(1)}, bf16[256,1024]{1,0:T(8,128)(2,1)S(1)}, u32[]{:S(2)}, u32[]{:S(2)}) %collective-permute-start.21) | collective-permute-done | bytes 524320 | tf_op jit(solution)/shard_map/ppermute | solution.py:50
  167.3 2.7 %fusion.30 = (bf16[256,1024]{1,0:T(8,128)(2,1)S(1)}, bf16[256,1024]{1,0:T(8,128)(2,1)}) fusion(f32[2048,1024]{1,0:T(8,128)} %reduce-precision_reduce_fusion, bf16[256,1024]{1,0:T(8,128)(2,1)S(1)} %collective-permute-done.22, bf16[256,1024]{1,0:T(8,128)(2,1)S(1)} %collective-permute-done.21), kind=kLoop, calls=%fused_computation.51 | loop fusion | flops 1572864 | bytes 4194304 | tf_op jit(solution)/shard_map/convert_element_type | solution.py:86
  170.0 1.2 collective-permute-start.23
  172.0 11.2 %fusion.35 = (f32[1,2,384,1024]{3,2,1,0:T(8,128)}, bf16[1,2,384,1024]{3,2,1,0:T(8,128)(2,1)}, f32[1,2,384,1024]{3,2,1,0:T(8,128)}) fusion(f32[1,2,384,1024]{3,2,1,0:T(8,128)} %param.18, f32[1,2,384,1024]{3,2,1,0:T(8,128)} %param.17, bf16[1,2,384,1024]{3,2,1,0:T(8,128)(2,1)} %collective-permute-done.28, ...), kind=kOutput, calls=%fused_computation.65 | convolution fusion | flops 3246129152 | bytes 30425088 | tf_op jit(solution)/shard_map/eth,etd->ehd/dot_general | solution.py:192
  183.3 2.2 add_convert_fusion.2
  185.4 1.2 collective-permute-start.18
  187.5 1.4 collective-permute-done.23
  188.9 3.7 %collective-permute-done.24 = bf16[256,1024]{1,0:T(8,128)(2,1)} collective-permute-done((bf16[256,1024]{1,0:T(8,128)(2,1)S(1)}, bf16[256,1024]{1,0:T(8,128)(2,1)}, u32[]{:S(2)}, u32[]{:S(2)}) %collective-permute-start.24) | collective-permute-done | bytes 524320 | tf_op jit(solution)/shard_map/ppermute | solution.py:51
  192.6 2.0 fusion.28
  194.7 1.0 collective-permute-start.25
  195.7 1.1 collective-permute-start.26
  196.8 7.2 %convert_bitcast_fusion = bf16[2,1024,768]{1,2,0:T(8,128)(2,1)S(1)} fusion(bf16[2048,1024,1]{1,0,2:T(8,128)(2,1)S(1)} %bitcast.100, bf16[2,2048,384]{1,2,0:T(8,128)(2,1)} %get-tuple-element.139, bf16[2,2048,384]{1,2,0:T(8,128)(2,1)S(1)} %copy-done.12), kind=kOutput, calls=%fused_computation.38 | convolution fusion | flops 6456606720 | bytes 13631488 | tf_op jit(solution)/shard_map/td,eth->edh/dot_general | solution.py:196
  204.0 2.4 %add_convert_fusion.1 = bf16[256,1024]{1,0:T(8,128)(2,1)} fusion(f32[2048,1024]{1,0:T(8,128)} %multiply_reduce_fusion, bf16[256,1024]{1,0:T(8,128)(2,1)S(1)} %collective-permute-done.18), kind=kLoop, calls=%fused_computation.59 | loop fusion | flops 786432 | bytes 2097152 | tf_op jit(solution)/shard_map/convert_element_type | solution.py:86
  206.4 0.9 collective-permute-start.20
  207.3 4.3 %collective-permute-done.25 = bf16[256,1024]{1,0:T(8,128)(2,1)S(1)} collective-permute-done((bf16[256,1024]{1,0:T(8,128)(2,1)S(1)}, bf16[256,1024]{1,0:T(8,128)(2,1)S(1)}, u32[]{:S(2)}, u32[]{:S(2)}) %collective-permute-start.25) | collective-permute-done | bytes 524320 | tf_op jit(solution)/shard_map/ppermute | solution.py:50
  211.6 2.4 %fusion.27 = bf16[256,1024]{1,0:T(8,128)(2,1)} fusion(f32[2048,1024]{1,0:T(8,128)} %reduce-precision_reduce_fusion, bf16[256,1024]{1,0:T(8,128)(2,1)S(1)} %collective-permute-done.25), kind=kLoop, calls=%fused_computation.45 | loop fusion | flops 786432 | bytes 2097152 | tf_op jit(solution)/shard_map/convert_element_type | solution.py:86
  214.0 1.2 collective-permute-start.27
  215.5 1.6 copy.40
  217.1 1.6 copy.41
  218.6 2.3 collective-permute-done.20
  220.9 2.6 %add_convert_fusion = bf16[256,1024]{1,0:T(8,128)(2,1)} fusion(bf16[256,1024]{1,0:T(8,128)(2,1)} %collective-permute-done.20, bf16[256,1024]{1,0:T(8,128)(2,1)} %copy-done.5, f32[2048,1024]{1,0:T(8,128)} %multiply_reduce_fusion), kind=kLoop, calls=%fused_computation.58 | loop fusion | flops 1310720 | bytes 2621440 | tf_op jit(solution)/shard_map/convert_element_type | solution.py:238
  223.5 3.0 %collective-permute-done.27 = bf16[256,1024]{1,0:T(8,128)(2,1)} collective-permute-done((bf16[256,1024]{1,0:T(8,128)(2,1)}, bf16[256,1024]{1,0:T(8,128)(2,1)}, u32[]{:S(2)}, u32[]{:S(2)}) %collective-permute-start.27) | collective-permute-done | bytes 524320 | tf_op jit(solution)/shard_map/ppermute | solution.py:46
  226.5 2.4 %fusion.33 = bf16[256,1024]{1,0:T(8,128)(2,1)} fusion(f32[2048,1024]{1,0:T(8,128)} %reduce-precision_reduce_fusion, bf16[256,1024]{1,0:T(8,128)(2,1)} %collective-permute-done.27, bf16[256,1024]{1,0:T(8,128)(2,1)S(1)} %copy-done.7), kind=kLoop, calls=%fused_computation.56 | loop fusion | flops 1310720 | bytes 2621440 | tf_op jit(solution)/shard_map/convert_element_type | solution.py:239
  (73 shorter events, 14.0 us)
Async XLA Ops:
  0.6 60.5 %copy-start.4 = (bf16[256,1024]{1,0:T(8,128)(2,1)S(1)}, bf16[256,1024]{1,0:T(8,128)(2,1)}, u32[]{:S(2)}) copy-start(bf16[256,1024]{1,0:T(8,128)(2,1)} %param.10) | copy-start | bytes 1572868
  3.5 61.1 %copy-start.8 = (bf16[256,1024]{1,0:T(8,128)(2,1)S(1)}, bf16[256,1024]{1,0:T(8,128)(2,1)}, u32[]{:S(2)}) copy-start(bf16[256,1024]{1,0:T(8,128)(2,1)} %param.11) | copy-start | bytes 1572868
  3.5 15.3 %collective-permute-start = (bf16[1,264,1024]{2,1,0:T(8,128)(2,1)S(1)}, bf16[1,264,1024]{2,1,0:T(8,128)(2,1)S(1)}, u32[]{:S(2)}, u32[]{:S(2)}) collective-permute-start(bf16[1,264,1024]{2,1,0:T(8,128)(2,1)S(1)} %maximum_bitcast_fusion), channel_id=1, source_target_pairs={{0,2},{2,4},{4,6},{6,7},{7,5},{5,3},{3,1},{1,0},{8,10},{10,12},{12... | collective-permute-start | bytes 1622024 | tf_op jit(solution)/shard_map/ppermute | solution.py:50
  6.5 13.7 %collective-permute-start.1 = (bf16[1,264,1024]{2,1,0:T(8,128)(2,1)S(1)}, bf16[1,264,1024]{2,1,0:T(8,128)(2,1)S(1)}, u32[]{:S(2)}, u32[]{:S(2)}) collective-permute-start(bf16[1,264,1024]{2,1,0:T(8,128)(2,1)S(1)} %maximum_bitcast_fusion), channel_id=1, source_target_pairs={{0,1},{2,0},{4,2},{6,4},{7,6},{5,7},{3,5},{1,3},{8,9},{10,8},{12,1... | collective-permute-start | bytes 1622024 | tf_op jit(solution)/shard_map/ppermute | solution.py:51
  20.3 12.8 %collective-permute-start.2 = (bf16[1,264,1024]{2,1,0:T(8,128)(2,1)S(1)}, bf16[1,264,1024]{2,1,0:T(8,128)(2,1)S(1)}, u32[]{:S(2)}, u32[]{:S(2)}) collective-permute-start(bf16[1,264,1024]{2,1,0:T(8,128)(2,1)S(1)} %collective-permute-done), channel_id=1, source_target_pairs={{0,2},{2,4},{4,6},{6,7},{7,5},{5,3},{3,1},{1,0},{8,10},{10,12},{12... | collective-permute-start | bytes 1622024 | tf_op jit(solution)/shard_map/ppermute | solution.py:50
  21.9 12.5 %collective-permute-start.3 = (bf16[1,264,1024]{2,1,0:T(8,128)(2,1)S(1)}, bf16[1,264,1024]{2,1,0:T(8,128)(2,1)S(1)}, u32[]{:S(2)}, u32[]{:S(2)}) collective-permute-start(bf16[1,264,1024]{2,1,0:T(8,128)(2,1)S(1)} %collective-permute-done.1), channel_id=1, source_target_pairs={{0,1},{2,0},{4,2},{6,4},{7,6},{5,7},{3,5},{1,3},{8,9},{10,8},{12,1... | collective-permute-start | bytes 1622024 | tf_op jit(solution)/shard_map/ppermute | solution.py:51
  34.4 11.6 %collective-permute-start.4 = (bf16[1,264,1024]{2,1,0:T(8,128)(2,1)S(1)}, bf16[1,264,1024]{2,1,0:T(8,128)(2,1)S(1)}, u32[]{:S(2)}, u32[]{:S(2)}) collective-permute-start(bf16[1,264,1024]{2,1,0:T(8,128)(2,1)S(1)} %collective-permute-done.2), channel_id=1, source_target_pairs={{0,2},{2,4},{4,6},{6,7},{7,5},{5,3},{3,1},{1,0},{8,10},{10,12},{12... | collective-permute-start | bytes 1622024 | tf_op jit(solution)/shard_map/ppermute | solution.py:50
  36.0 11.3 %collective-permute-start.5 = (bf16[1,264,1024]{2,1,0:T(8,128)(2,1)S(1)}, bf16[1,264,1024]{2,1,0:T(8,128)(2,1)S(1)}, u32[]{:S(2)}, u32[]{:S(2)}) collective-permute-start(bf16[1,264,1024]{2,1,0:T(8,128)(2,1)S(1)} %collective-permute-done.3), channel_id=1, source_target_pairs={{0,1},{2,0},{4,2},{6,4},{7,6},{5,7},{3,5},{1,3},{8,9},{10,8},{12,1... | collective-permute-start | bytes 1622024 | tf_op jit(solution)/shard_map/ppermute | solution.py:51
  47.3 10.4 %collective-permute-start.6 = (bf16[1,264,1024]{2,1,0:T(8,128)(2,1)S(1)}, bf16[1,264,1024]{2,1,0:T(8,128)(2,1)S(1)}, u32[]{:S(2)}, u32[]{:S(2)}) collective-permute-start(bf16[1,264,1024]{2,1,0:T(8,128)(2,1)S(1)} %collective-permute-done.4), channel_id=1, source_target_pairs={{0,2},{2,4},{4,6},{6,7},{7,5},{5,3},{3,1},{1,0},{8,10},{10,12},{12... | collective-permute-start | bytes 1622024 | tf_op jit(solution)/shard_map/ppermute | solution.py:46
  64.5 9.2 %collective-permute-start.7 = (bf16[256,1024]{1,0:T(8,128)(2,1)S(1)}, bf16[256,1024]{1,0:T(8,128)(2,1)S(1)}, u32[]{:S(2)}, u32[]{:S(2)}) collective-permute-start(bf16[256,1024]{1,0:T(8,128)(2,1)S(1)} %copy-done.8), channel_id=1, source_target_pairs={{0,2},{2,4},{4,6},{6,7},{7,5},{5,3},{3,1},{1,0},{8,10},{10,12},{12... | collective-permute-start | bytes 1572872 | tf_op jit(solution)/shard_map/ppermute | solution.py:50
  66.0 9.2 %collective-permute-start.8 = (bf16[256,1024]{1,0:T(8,128)(2,1)S(1)}, bf16[256,1024]{1,0:T(8,128)(2,1)S(1)}, u32[]{:S(2)}, u32[]{:S(2)}) collective-permute-start(bf16[256,1024]{1,0:T(8,128)(2,1)S(1)} %copy-done.8), channel_id=1, source_target_pairs={{0,1},{2,0},{4,2},{6,4},{7,6},{5,7},{3,5},{1,3},{8,9},{10,8},{12,1... | collective-permute-start | bytes 1572872 | tf_op jit(solution)/shard_map/ppermute | solution.py:51
  66.6 104.6 %collective-permute-start.28 = (bf16[1,2,384,1024]{3,2,1,0:T(8,128)(2,1)}, bf16[1,2,384,1024]{3,2,1,0:T(8,128)(2,1)}, u32[]{:S(2)}, u32[]{:S(2)}) collective-permute-start(bf16[1,2,384,1024]{3,2,1,0:T(8,128)(2,1)} %param.16), channel_id=1, source_target_pairs={{0,16},{8,24},{16,0},{24,8},{1,17},{9,25},{17,1},{25,9},{2,18},{10... | collective-permute-start | bytes 4718600 | tf_op jit(solution)/shard_map/ppermute | solution.py:21
  68.1 103.9 %collective-permute-start.29 = (bf16[1,2,384,1024]{3,2,1,0:T(8,128)(2,1)}, bf16[1,2,384,1024]{3,2,1,0:T(8,128)(2,1)}, u32[]{:S(2)}, u32[]{:S(2)}) collective-permute-start(bf16[1,2,384,1024]{3,2,1,0:T(8,128)(2,1)} %param.16), channel_id=1, source_target_pairs={{0,8},{8,16},{16,24},{24,0},{1,9},{9,17},{17,25},{25,1},{2,10},{10... | collective-permute-start | bytes 4718600 | tf_op jit(solution)/shard_map/ppermute | solution.py:21
  68.1 9.2 %copy-start.9 = (bf16[1,2,1024,384]{3,2,1,0:T(8,128)(2,1)S(1)}, bf16[1,2,1024,384]{3,2,1,0:T(8,128)(2,1)}, u32[]{:S(2)}) copy-start(bf16[1,2,1024,384]{3,2,1,0:T(8,128)(2,1)} %param.14) | copy-start | bytes 4718596
  70.9 18.2 %copy-start.2 = (bf16[8,256,1024]{2,1,0:T(8,128)(2,1)}, bf16[8,256,1024]{2,1,0:T(8,128)(2,1)S(1)}, u32[]{:S(2)}) copy-start(bf16[8,256,1024]{2,1,0:T(8,128)(2,1)S(1)} %slice.104) | copy-start | bytes 12582916
  75.3 11.3 %collective-permute-start.9 = (bf16[256,1024]{1,0:T(8,128)(2,1)S(1)}, bf16[256,1024]{1,0:T(8,128)(2,1)}, u32[]{:S(2)}, u32[]{:S(2)}) collective-permute-start(bf16[256,1024]{1,0:T(8,128)(2,1)S(1)} %collective-permute-done.7), channel_id=1, source_target_pairs={{0,2},{2,4},{4,6},{6,7},{7,5},{5,3},{3,1},{1,0},{8,10},{10,12},{12... | collective-permute-start | bytes 1572872 | tf_op jit(solution)/shard_map/ppermute | solution.py:50
  77.1 9.6 %collective-permute-start.10 = (bf16[256,1024]{1,0:T(8,128)(2,1)S(1)}, bf16[256,1024]{1,0:T(8,128)(2,1)}, u32[]{:S(2)}, u32[]{:S(2)}) collective-permute-start(bf16[256,1024]{1,0:T(8,128)(2,1)S(1)} %collective-permute-done.8), channel_id=1, source_target_pairs={{0,1},{2,0},{4,2},{6,4},{7,6},{5,7},{3,5},{1,3},{8,9},{10,8},{12,1... | collective-permute-start | bytes 1572872 | tf_op jit(solution)/shard_map/ppermute | solution.py:51
  77.3 11.8 %copy-start.10 = (bf16[1,2,1024,384]{3,2,1,0:T(8,128)(2,1)S(1)}, bf16[1,2,1024,384]{3,2,1,0:T(8,128)(2,1)}, u32[]{:S(2)}) copy-start(bf16[1,2,1024,384]{3,2,1,0:T(8,128)(2,1)} %param.15) | copy-start | bytes 4718596
  81.0 15.1 %copy-start.11 = (f32[2048,2,384]{0,2,1:T(8,128)}, f32[2048,2,384]{0,2,1:T(8,128)S(1)}, u32[]{:S(2)}) copy-start(f32[2048,2,384]{0,2,1:T(8,128)S(1)} %fusion.40) | copy-start | bytes 18874372
  86.7 11.4 %collective-permute-start.11 = (bf16[256,1024]{1,0:T(8,128)(2,1)}, bf16[256,1024]{1,0:T(8,128)(2,1)}, u32[]{:S(2)}, u32[]{:S(2)}) collective-permute-start(bf16[256,1024]{1,0:T(8,128)(2,1)} %collective-permute-done.9), channel_id=1, source_target_pairs={{0,2},{2,4},{4,6},{6,7},{7,5},{5,3},{3,1},{1,0},{8,10},{10,12},{12... | collective-permute-start | bytes 1572872 | tf_op jit(solution)/shard_map/ppermute | solution.py:50
  89.1 9.5 %collective-permute-start.12 = (bf16[256,1024]{1,0:T(8,128)(2,1)}, bf16[256,1024]{1,0:T(8,128)(2,1)}, u32[]{:S(2)}, u32[]{:S(2)}) collective-permute-start(bf16[256,1024]{1,0:T(8,128)(2,1)} %collective-permute-done.10), channel_id=1, source_target_pairs={{0,1},{2,0},{4,2},{6,4},{7,6},{5,7},{3,5},{1,3},{8,9},{10,8},{12,1... | collective-permute-start | bytes 1572872 | tf_op jit(solution)/shard_map/ppermute | solution.py:51
  98.6 13.2 %collective-permute-start.13 = (bf16[256,1024]{1,0:T(8,128)(2,1)}, bf16[256,1024]{1,0:T(8,128)(2,1)S(1)}, u32[]{:S(2)}, u32[]{:S(2)}) collective-permute-start(bf16[256,1024]{1,0:T(8,128)(2,1)} %collective-permute-done.11), channel_id=1, source_target_pairs={{0,2},{2,4},{4,6},{6,7},{7,5},{5,3},{3,1},{1,0},{8,10},{10,12},{12... | collective-permute-start | bytes 1572872 | tf_op jit(solution)/shard_map/ppermute | solution.py:46
  118.0 34.5 %collective-permute-start.14 = (bf16[256,1024]{1,0:T(8,128)(2,1)S(1)}, bf16[256,1024]{1,0:T(8,128)(2,1)}, u32[]{:S(2)}, u32[]{:S(2)}) collective-permute-start(bf16[256,1024]{1,0:T(8,128)(2,1)S(1)} %get-tuple-element.90), channel_id=1, source_target_pairs={{0,2},{2,4},{4,6},{6,7},{7,5},{5,3},{3,1},{1,0},{8,10},{10,12},{12... | collective-permute-start | bytes 1572872 | tf_op jit(solution)/shard_map/ppermute | solution.py:50
  119.0 35.3 %collective-permute-start.15 = (bf16[256,1024]{1,0:T(8,128)(2,1)S(1)}, bf16[256,1024]{1,0:T(8,128)(2,1)}, u32[]{:S(2)}, u32[]{:S(2)}) collective-permute-start(bf16[256,1024]{1,0:T(8,128)(2,1)S(1)} %get-tuple-element.91), channel_id=1, source_target_pairs={{0,1},{2,0},{4,2},{6,4},{7,6},{5,7},{3,5},{1,3},{8,9},{10,8},{12,1... | collective-permute-start | bytes 1572872 | tf_op jit(solution)/shard_map/ppermute | solution.py:51
  121.1 14.0 %copy-start = (f32[2048,1024]{1,0:T(8,128)}, f32[2048,1024]{1,0:T(8,128)S(1)}, u32[]{:S(2)}) copy-start(f32[2048,1024]{1,0:T(8,128)S(1)} %convert_element_type.151) | copy-start | bytes 25165828
  151.5 14.9 %collective-permute-start.21 = (bf16[256,1024]{1,0:T(8,128)(2,1)S(1)}, bf16[256,1024]{1,0:T(8,128)(2,1)S(1)}, u32[]{:S(2)}, u32[]{:S(2)}) collective-permute-start(bf16[256,1024]{1,0:T(8,128)(2,1)S(1)} %get-tuple-element.105), channel_id=1, source_target_pairs={{0,2},{2,4},{4,6},{6,7},{7,5},{5,3},{3,1},{1,0},{8,10},{10,12},{12... | collective-permute-start | bytes 1572872 | tf_op jit(solution)/shard_map/ppermute | solution.py:50
  152.5 14.8 %collective-permute-start.22 = (bf16[256,1024]{1,0:T(8,128)(2,1)S(1)}, bf16[256,1024]{1,0:T(8,128)(2,1)S(1)}, u32[]{:S(2)}, u32[]{:S(2)}) collective-permute-start(bf16[256,1024]{1,0:T(8,128)(2,1)S(1)} %get-tuple-element.106), channel_id=1, source_target_pairs={{0,1},{2,0},{4,2},{6,4},{7,6},{5,7},{3,5},{1,3},{8,9},{10,8},{12,1... | collective-permute-start | bytes 1572872 | tf_op jit(solution)/shard_map/ppermute | solution.py:51
  154.2 17.8 %copy-start.1 = (f32[2048,1024]{1,0:T(8,128)S(1)}, f32[2048,1024]{1,0:T(8,128)}, u32[]{:S(2)}) copy-start(f32[2048,1024]{1,0:T(8,128)} %copy-done) | copy-start | bytes 25165828
  156.6 26.6 %collective-permute-start.16 = (bf16[256,1024]{1,0:T(8,128)(2,1)S(1)}, bf16[256,1024]{1,0:T(8,128)(2,1)S(1)}, u32[]{:S(2)}, u32[]{:S(2)}) collective-permute-start(bf16[256,1024]{1,0:T(8,128)(2,1)S(1)} %get-tuple-element.94), channel_id=1, source_target_pairs={{0,2},{2,4},{4,6},{6,7},{7,5},{5,3},{3,1},{1,0},{8,10},{10,12},{12... | collective-permute-start | bytes 1572872 | tf_op jit(solution)/shard_map/ppermute | solution.py:50
  166.4 16.8 %collective-permute-start.17 = (bf16[256,1024]{1,0:T(8,128)(2,1)S(1)}, bf16[256,1024]{1,0:T(8,128)(2,1)}, u32[]{:S(2)}, u32[]{:S(2)}) collective-permute-start(bf16[256,1024]{1,0:T(8,128)(2,1)S(1)} %get-tuple-element.95), channel_id=1, source_target_pairs={{0,1},{2,0},{4,2},{6,4},{7,6},{5,7},{3,5},{1,3},{8,9},{10,8},{12,1... | collective-permute-start | bytes 1572872 | tf_op jit(solution)/shard_map/ppermute | solution.py:51
  170.0 18.9 %collective-permute-start.23 = (bf16[256,1024]{1,0:T(8,128)(2,1)}, bf16[256,1024]{1,0:T(8,128)(2,1)S(1)}, u32[]{:S(2)}, u32[]{:S(2)}) collective-permute-start(bf16[256,1024]{1,0:T(8,128)(2,1)} %get-tuple-element.109), channel_id=1, source_target_pairs={{0,2},{2,4},{4,6},{6,7},{7,5},{5,3},{3,1},{1,0},{8,10},{10,12},{12... | collective-permute-start | bytes 1572872 | tf_op jit(solution)/shard_map/ppermute | solution.py:50
  171.2 21.5 %collective-permute-start.24 = (bf16[256,1024]{1,0:T(8,128)(2,1)S(1)}, bf16[256,1024]{1,0:T(8,128)(2,1)}, u32[]{:S(2)}, u32[]{:S(2)}) collective-permute-start(bf16[256,1024]{1,0:T(8,128)(2,1)S(1)} %get-tuple-element.110), channel_id=1, source_target_pairs={{0,1},{2,0},{4,2},{6,4},{7,6},{5,7},{3,5},{1,3},{8,9},{10,8},{12,1... | collective-permute-start | bytes 1572872 | tf_op jit(solution)/shard_map/ppermute | solution.py:51
  183.2 13.5 %copy-start.3 = (bf16[8,256,1024]{2,1,0:T(8,128)(2,1)S(1)}, bf16[8,256,1024]{2,1,0:T(8,128)(2,1)}, u32[]{:S(2)}) copy-start(bf16[8,256,1024]{2,1,0:T(8,128)(2,1)} %copy-done.2) | copy-start | bytes 12582916
  183.2 13.5 %copy-start.12 = (bf16[2,2048,384]{1,2,0:T(8,128)(2,1)S(1)}, bf16[2,2048,384]{1,2,0:T(8,128)(2,1)}, u32[]{:S(2)}) copy-start(bf16[2,2048,384]{1,2,0:T(8,128)(2,1)} %get-tuple-element.138) | copy-start | bytes 9437188
  185.4 18.5 %collective-permute-start.18 = (bf16[256,1024]{1,0:T(8,128)(2,1)S(1)}, bf16[256,1024]{1,0:T(8,128)(2,1)S(1)}, u32[]{:S(2)}, u32[]{:S(2)}) collective-permute-start(bf16[256,1024]{1,0:T(8,128)(2,1)S(1)} %get-tuple-element.98), channel_id=1, source_target_pairs={{0,2},{2,4},{4,6},{6,7},{7,5},{5,3},{3,1},{1,0},{8,10},{10,12},{12... | collective-permute-start | bytes 1572872 | tf_op jit(solution)/shard_map/ppermute | solution.py:50
  186.7 17.3 %collective-permute-start.19 = (bf16[256,1024]{1,0:T(8,128)(2,1)S(1)}, bf16[256,1024]{1,0:T(8,128)(2,1)S(1)}, u32[]{:S(2)}, u32[]{:S(2)}) collective-permute-start(bf16[256,1024]{1,0:T(8,128)(2,1)S(1)} %get-tuple-element.99), channel_id=1, source_target_pairs={{0,1},{2,0},{4,2},{6,4},{7,6},{5,7},{3,5},{1,3},{8,9},{10,8},{12,1... | collective-permute-start | bytes 1572872 | tf_op jit(solution)/shard_map/ppermute | solution.py:51
  194.7 16.9 %collective-permute-start.25 = (bf16[256,1024]{1,0:T(8,128)(2,1)S(1)}, bf16[256,1024]{1,0:T(8,128)(2,1)S(1)}, u32[]{:S(2)}, u32[]{:S(2)}) collective-permute-start(bf16[256,1024]{1,0:T(8,128)(2,1)S(1)} %get-tuple-element.113), channel_id=1, source_target_pairs={{0,2},{2,4},{4,6},{6,7},{7,5},{5,3},{3,1},{1,0},{8,10},{10,12},{12... | collective-permute-start | bytes 1572872 | tf_op jit(solution)/shard_map/ppermute | solution.py:50
  195.7 15.9 %collective-permute-start.26 = (bf16[256,1024]{1,0:T(8,128)(2,1)S(1)}, bf16[256,1024]{1,0:T(8,128)(2,1)S(1)}, u32[]{:S(2)}, u32[]{:S(2)}) collective-permute-start(bf16[256,1024]{1,0:T(8,128)(2,1)S(1)} %get-tuple-element.114), channel_id=1, source_target_pairs={{0,1},{2,0},{4,2},{6,4},{7,6},{5,7},{3,5},{1,3},{8,9},{10,8},{12,1... | collective-permute-start | bytes 1572872 | tf_op jit(solution)/shard_map/ppermute | solution.py:51
  204.0 11.5 %copy-start.5 = (bf16[256,1024]{1,0:T(8,128)(2,1)}, bf16[256,1024]{1,0:T(8,128)(2,1)S(1)}, u32[]{:S(2)}) copy-start(bf16[256,1024]{1,0:T(8,128)(2,1)S(1)} %collective-permute-done.19) | copy-start | bytes 1572868
  206.4 14.5 %collective-permute-start.20 = (bf16[256,1024]{1,0:T(8,128)(2,1)}, bf16[256,1024]{1,0:T(8,128)(2,1)}, u32[]{:S(2)}, u32[]{:S(2)}) collective-permute-start(bf16[256,1024]{1,0:T(8,128)(2,1)} %add_convert_fusion.1), channel_id=1, source_target_pairs={{0,2},{2,4},{4,6},{6,7},{7,5},{5,3},{3,1},{1,0},{8,10},{10,12},{12... | collective-permute-start | bytes 1572872 | tf_op jit(solution)/shard_map/ppermute | solution.py:46
  211.6 3.9 %copy-start.6 = (bf16[256,1024]{1,0:T(8,128)(2,1)}, bf16[256,1024]{1,0:T(8,128)(2,1)S(1)}, u32[]{:S(2)}) copy-start(bf16[256,1024]{1,0:T(8,128)(2,1)S(1)} %collective-permute-done.26) | copy-start | bytes 1572868
  214.0 12.5 %collective-permute-start.27 = (bf16[256,1024]{1,0:T(8,128)(2,1)}, bf16[256,1024]{1,0:T(8,128)(2,1)}, u32[]{:S(2)}, u32[]{:S(2)}) collective-permute-start(bf16[256,1024]{1,0:T(8,128)(2,1)} %fusion.27), channel_id=1, source_target_pairs={{0,2},{2,4},{4,6},{6,7},{7,5},{5,3},{3,1},{1,0},{8,10},{10,12},{12... | collective-permute-start | bytes 1572872 | tf_op jit(solution)/shard_map/ppermute | solution.py:46
  217.1 9.4 %copy-start.7 = (bf16[256,1024]{1,0:T(8,128)(2,1)S(1)}, bf16[256,1024]{1,0:T(8,128)(2,1)}, u32[]{:S(2)}) copy-start(bf16[256,1024]{1,0:T(8,128)(2,1)} %copy-done.6) | copy-start | bytes 1572868

commit v11 on v10

--- a/solution.py
+++ b/solution.py
@@ -181,7 +181,7 @@
         )
         mixed_part = jnp.sum(chunk_weight * expert_out, axis=0)
         chunk_cot, mixed_part = lax.optimization_barrier((chunk_cot, mixed_part))
-        slot_cot = (chunk_weight * chunk_cot.astype(jnp.float32)[None]).astype(jnp.bfloat16)
+        slot_cot = chunk_weight.astype(jnp.bfloat16) * chunk_cot[None]
         hidden_cot = jnp.einsum(
             "etd,ehd->eth", slot_cot, down_matrix, preferred_element_type=jnp.float32
         )

time: 230 us -> 223 us (0.970)
  waiting for transfers between devices: 80.3 us -> 87.7 us
  local copies, waits for them, and re-layouts: 22 us -> 16.6 us
  matrix products: 69.3 us -> 64.6 us
  other arithmetic: 23.6 us -> 20.3 us
    ppermute x12, waiting for transfers between devices: 55.4 us -> 62.9 us  [paired_shift(): ahead_value = lax.ppermute(ahead_value, axis, ring_pairs(ring, 1))]
    unnamed x43 -> x54, local copies, waits for them, and re-layouts: 12.7 us -> 8.66 us
    dot_general x1, matrix products: 14 us -> 10.2 us  [chunk_pass(): jnp.einsum('etd,ehd->eth', slot_cot, down_matrix, preferred_element_type=...]
    ppermute x12, starting transfers between devices: 18.3 us -> 14.5 us  [paired_shift(): ahead_value = lax.ppermute(ahead_value, axis, ring_pairs(ring, 1))]
    ppermute x12, starting transfers between devices: 6.94 us -> 10.6 us  [paired_shift(): behind_value = lax.ppermute(behind_value, axis, ring_pairs(ring, -1))]
    ppermute x4, waiting for transfers between devices: 14.2 us -> 10.9 us  [paired_shift(): return (lax.ppermute(ahead_value, axis, ring_pairs(ring, 1)), None)]
    ppermute x12, waiting for transfers between devices: 10.6 us -> 13.9 us  [paired_shift(): behind_value = lax.ppermute(behind_value, axis, ring_pairs(ring, -1))]
  transfers between devices with their start and end apart: 30 -> 30, of which waited for: 19 -> 17; matrix products, arithmetic and copies ran while one was open for 45% -> 43% of each run, Pallas kernels for 0% -> 0%
where the time goes in v11:
time: 223 us; the launch traced here: 222 us
  waiting for transfers between devices  87.7 us (39%)
  matrix products  64.6 us (29%)
  starting transfers between devices  31.2 us (14%)
  other arithmetic  20.3 us (9%)
  local copies, waits for them, and re-layouts  16.6 us (7%)
    ppermute x12, waiting for transfers between devices, paired_shift(): ahead_value = lax.ppermute(ahead_value, axis, ring_pairs(ring, 1))  62.9 us
    dot_general x1, matrix products, chunk_pass(): jnp.einsum('eth,edh->etd', joint_cot, joint_matrix, preferred_element_typ...  14.8 us
    ppermute x12, starting transfers between devices, paired_shift(): ahead_value = lax.ppermute(ahead_value, axis, ring_pairs(ring, 1))  14.5 us
    ppermute x12, waiting for transfers between devices, paired_shift(): behind_value = lax.ppermute(behind_value, axis, ring_pairs(ring, -1))  13.9 us
    convert_element_type x6, other arithmetic, to_wire(): return value.astype(wire_dtype)  12.8 us
    dot_general x1, matrix products, chunk_pass(): jnp.einsum('eth,ehd->etd', hidden, down_matrix, preferred_element_type=jn...  11.5 us
    ppermute x4, waiting for transfers between devices, paired_shift(): return (lax.ppermute(ahead_value, axis, ring_pairs(ring, 1)), None)  10.9 us
    ppermute x12, starting transfers between devices, paired_shift(): behind_value = lax.ppermute(behind_value, axis, ring_pairs(ring, -1))  10.6 us
  transfers between devices with their start and end apart: 30, of which 17 were waited for; matrix products, arithmetic and copies ran while one was open for 43% of the time, Pallas kernels for 0%

profile of v11, /device:TPU:0, one launch (start us, length us, event | category | flops | bytes accessed | tf_op | source)
XLA Modules:
  0.0 222.1 jit_solution(1563311724615105602)
XLA Ops:
  0.6 0.7 convert_element_type.128
  1.4 0.7 select_reduce_fusion
  2.4 1.1 maximum_bitcast_fusion
  3.5 3.1 %collective-permute-start = (bf16[1,264,1024]{2,1,0:T(8,128)(2,1)S(1)}, bf16[1,264,1024]{2,1,0:T(8,128)(2,1)S(1)}, u32[]{:S(2)}, u32[]{:S(2)}) collective-permute-start(bf16[1,264,1024]{2,1,0:T(8,128)(2,1)S(1)} %maximum_bitcast_fusion), channel_id=1, source_target_pairs={{0,2},{2,4},{4,6},{6,7},{7,5},{5,3},{3,1},{1,0},{8,10},{10,12},{12... | collective-permute-start | bytes 1622024 | tf_op jit(solution)/shard_map/ppermute | solution.py:50
  6.5 12.2 %collective-permute-done = bf16[1,264,1024]{2,1,0:T(8,128)(2,1)S(1)} collective-permute-done((bf16[1,264,1024]{2,1,0:T(8,128)(2,1)S(1)}, bf16[1,264,1024]{2,1,0:T(8,128)(2,1)S(1)}, u32[]{:S(2)}, u32[]{:S(2)}) %collective-permute-start) | collective-permute-done | bytes 540704 | tf_op jit(solution)/shard_map/ppermute | solution.py:50
  18.7 1.5 collective-permute-done.1
  20.3 1.6 collective-permute-start.2
  22.3 10.8 %collective-permute-done.2 = bf16[1,264,1024]{2,1,0:T(8,128)(2,1)S(1)} collective-permute-done((bf16[1,264,1024]{2,1,0:T(8,128)(2,1)S(1)}, bf16[1,264,1024]{2,1,0:T(8,128)(2,1)S(1)}, u32[]{:S(2)}, u32[]{:S(2)}) %collective-permute-start.2) | collective-permute-done | bytes 540704 | tf_op jit(solution)/shard_map/ppermute | solution.py:50
  33.1 1.3 collective-permute-done.3
  34.4 1.6 collective-permute-start.4
  36.4 9.7 %collective-permute-done.4 = bf16[1,264,1024]{2,1,0:T(8,128)(2,1)} collective-permute-done((bf16[1,264,1024]{2,1,0:T(8,128)(2,1)S(1)}, bf16[1,264,1024]{2,1,0:T(8,128)(2,1)}, u32[]{:S(2)}, u32[]{:S(2)}) %collective-permute-start.4) | collective-permute-done | bytes 540704 | tf_op jit(solution)/shard_map/ppermute | solution.py:50
  46.1 1.2 collective-permute-done.5
  47.3 1.5 collective-permute-start.6
  48.8 1.5 collective-permute-start.28
  50.3 7.8 %collective-permute-done.6 = bf16[1,264,1024]{2,1,0:T(8,128)(2,1)} collective-permute-done((bf16[1,264,1024]{2,1,0:T(8,128)(2,1)}, bf16[1,264,1024]{2,1,0:T(8,128)(2,1)}, u32[]{:S(2)}, u32[]{:S(2)}) %collective-permute-start.6) | collective-permute-done | bytes 540704 | tf_op jit(solution)/shard_map/ppermute | solution.py:46
  58.2 1.1 constant_dynamic-update-slice_fusion.7
  59.2 1.1 constant_dynamic-update-slice_fusion.6
  60.6 0.6 slice.104
  61.7 1.5 collective-permute-start.7
  63.7 3.7 %fusion.42 = f32[2048,2,384]{0,2,1:T(8,128)S(1)} fusion(bf16[2048,1024,1]{1,0,2:T(8,128)(2,1)S(1)} %bitcast.98, bf16[1,2,1024,384]{3,2,1,0:T(8,128)(2,1)S(1)} %copy-done.10), kind=kOutput, calls=%fused_computation.91 | convolution fusion | flops 3221225472 | bytes 12058624 | tf_op jit(solution)/shard_map/td,edh->eth/dot_general | solution.py:170
  67.4 5.0 %collective-permute-done.7 = bf16[256,1024]{1,0:T(8,128)(2,1)S(1)} collective-permute-done((bf16[256,1024]{1,0:T(8,128)(2,1)S(1)}, bf16[256,1024]{1,0:T(8,128)(2,1)S(1)}, u32[]{:S(2)}, u32[]{:S(2)}) %collective-permute-start.7) | collective-permute-done | bytes 524320 | tf_op jit(solution)/shard_map/ppermute | solution.py:50
  72.4 1.5 collective-permute-done.8
  73.9 1.6 collective-permute-start.9
  76.0 6.8 %fusion.4 = (bf16[2,2048,384]{1,2,0:T(8,128)(2,1)}, f32[2048,2,384]{0,2,1:T(8,128)}) fusion(f32[2048,2,384]{0,2,1:T(8,128)S(1)} %fusion.42, bf16[2048,1024,1]{1,0,2:T(8,128)(2,1)S(1)} %bitcast.99, bf16[1,2,1024,384]{3,2,1,0:T(8,128)(2,1)S(1)} %copy-done.12), kind=kOutput, calls=%fused_computation.9 | convolution fusion | flops 3230662656 | bytes 21495808 | tf_op jit(solution)/shard_map/td,edh->eth/dot_general | solution.py:173
  83.3 2.0 collective-permute-done.9
  85.3 2.3 %collective-permute-done.10 = bf16[256,1024]{1,0:T(8,128)(2,1)S(1)} collective-permute-done((bf16[256,1024]{1,0:T(8,128)(2,1)S(1)}, bf16[256,1024]{1,0:T(8,128)(2,1)S(1)}, u32[]{:S(2)}, u32[]{:S(2)}) %collective-permute-start.10) | collective-permute-done | bytes 524320 | tf_op jit(solution)/shard_map/ppermute | solution.py:51
  87.6 1.5 collective-permute-start.11
  90.1 10.6 %collective-permute-done.11 = bf16[256,1024]{1,0:T(8,128)(2,1)} collective-permute-done((bf16[256,1024]{1,0:T(8,128)(2,1)}, bf16[256,1024]{1,0:T(8,128)(2,1)}, u32[]{:S(2)}, u32[]{:S(2)}) %collective-permute-start.11) | collective-permute-done | bytes 524320 | tf_op jit(solution)/shard_map/ppermute | solution.py:50
  100.6 1.8 collective-permute-start.13
  102.5 11.5 %multiply_reduce_fusion = f32[2048,1024]{1,0:T(8,128)} fusion(f32[2,2048]{1,0:T(2,128)S(1)} %bitcast_convert_fusion, bf16[2,2048,384]{1,2,0:T(8,128)(2,1)} %get-tuple-element.164, bf16[1,2,384,1024]{3,2,1,0:T(8,128)(2,1)} %param.16), kind=kOutput, calls=%fused_computation.1 | convolution fusion | flops 3231711232 | bytes 13123584 | tf_op jit(solution)/shard_map/eth,ehd->etd/dot_general | solution.py:180
  114.0 1.1 constant_dynamic-update-slice_fusion.14
  115.1 1.2 constant_dynamic-update-slice_fusion.13
  116.5 1.1 constant_dynamic-update-slice_fusion.8
  117.6 3.2 %fusion.45 = (bf16[256,1024]{1,0:T(8,128)(2,1)S(1)}, bf16[256,1024]{1,0:T(8,128)(2,1)S(1)}) fusion(f32[2048,1024]{1,0:T(8,128)} %multiply_reduce_fusion), kind=kLoop, calls=%fused_computation.95 | loop fusion | bytes 2097152 | tf_op jit(solution)/shard_map/slice | solution.py:83
  121.4 1.5 collective-permute-start.15
  122.9 10.2 %fusion.7 = (bf16[2,2048,384]{1,2,0:T(8,128)(2,1)}, bf16[2,2048,384]{1,2,0:T(8,128)(2,1)}) fusion(f32[2048,2,384]{0,2,1:T(8,128)} %get-tuple-element.165, f32[2048,2,384]{0,2,1:T(8,128)} %copy-done.16, bf16[1,2,384,1024]{3,2,1,0:T(8,128)(2,1)S(1)} %copy-done.14, bf16[2048,1024]{1,0:T(8,128)(2,1)S(1)} %constant_dynamic-update-slice_fusion.8, ...), kind=kOutput, calls=%fused_computation.12 | convolution fusion | flops 3245867008 | bytes 24649728 | tf_op jit(solution)/shard_map/etd,ehd->eth/dot_general | solution.py:185
  133.1 14.8 %reduce-precision_reduce_fusion = f32[2048,1024]{1,0:T(8,128)} fusion(bf16[2,2048,384]{1,2,0:T(8,128)(2,1)} %get-tuple-element.146, bf16[2,2048,384]{1,2,0:T(8,128)(2,1)} %get-tuple-element.145, bf16[2,1024,384]{2,1,0:T(8,128)(2,1)S(1)} %bitcast.105, bf16[2,1024,384]{2,1,0:T(8,128)(2,1)S(1)} %bitcast.104), kind=kOutput, calls=%fused_computation | convolution fusion | flops 6467616768 | bytes 17825792 | tf_op jit(solution)/shard_map/eth,edh->etd/dot_general | solution.py:202
  147.8 1.8 fusion.44
  149.7 0.6 collective-permute-start.21
  150.3 1.5 collective-permute-start.22
  152.4 2.1 add_convert_fusion.4
  154.5 0.6 collective-permute-start.16
  155.1 8.1 %collective-permute-done.21 = bf16[256,1024]{1,0:T(8,128)(2,1)S(1)} collective-permute-done((bf16[256,1024]{1,0:T(8,128)(2,1)S(1)}, bf16[256,1024]{1,0:T(8,128)(2,1)S(1)}, u32[]{:S(2)}, u32[]{:S(2)}) %collective-permute-start.21) | collective-permute-done | bytes 524320 | tf_op jit(solution)/shard_map/ppermute | solution.py:50
  163.2 0.8 collective-permute-start.17
  164.1 1.1 collective-permute-done.22
  165.1 1.9 fusion.32
  167.5 1.6 collective-permute-start.24
  169.2 10.4 %fusion.37 = (f32[1,2,384,1024]{3,2,1,0:T(8,128)}, bf16[1,2,384,1024]{3,2,1,0:T(8,128)(2,1)}, f32[1,2,384,1024]{3,2,1,0:T(8,128)}) fusion(f32[1,2,384,1024]{3,2,1,0:T(8,128)S(1)} %copy-done.9, f32[1,2,384,1024]{3,2,1,0:T(8,128)} %param.17, bf16[1,2,384,1024]{3,2,1,0:T(8,128)(2,1)} %collective-permute-done.28, ...), kind=kOutput, calls=%fused_computation.65 | convolution fusion | flops 3241934848 | bytes 26222592 | tf_op jit(solution)/shard_map/eth,etd->ehd/dot_general | solution.py:192
  179.6 2.1 add_convert_fusion.2
  182.1 1.6 collective-permute-start.19
  183.8 5.0 %collective-permute-done.24 = bf16[256,1024]{1,0:T(8,128)(2,1)S(1)} collective-permute-done((bf16[256,1024]{1,0:T(8,128)(2,1)S(1)}, bf16[256,1024]{1,0:T(8,128)(2,1)S(1)}, u32[]{:S(2)}, u32[]{:S(2)}) %collective-permute-start.24) | collective-permute-done | bytes 524320 | tf_op jit(solution)/shard_map/ppermute | solution.py:51
  188.8 1.9 fusion.30
  190.7 0.9 collective-permute-start.25
  191.7 1.1 collective-permute-start.26
  192.8 7.2 %convert_bitcast_fusion = bf16[2,1024,768]{1,2,0:T(8,128)(2,1)S(1)} fusion(bf16[2048,1024,1]{1,0,2:T(8,128)(2,1)S(1)} %bitcast.100, bf16[2,2048,384]{1,2,0:T(8,128)(2,1)} %get-tuple-element.146, bf16[2,2048,384]{1,2,0:T(8,128)(2,1)S(1)} %copy-done.17), kind=kOutput, calls=%fused_computation.39 | convolution fusion | flops 6456606720 | bytes 13631488 | tf_op jit(solution)/shard_map/td,eth->edh/dot_general | solution.py:196
  200.1 2.4 %add_convert_fusion.1 = bf16[256,1024]{1,0:T(8,128)(2,1)} fusion(f32[2048,1024]{1,0:T(8,128)} %multiply_reduce_fusion, bf16[256,1024]{1,0:T(8,128)(2,1)S(1)} %collective-permute-done.18), kind=kLoop, calls=%fused_computation.59 | loop fusion | flops 786432 | bytes 2097152 | tf_op jit(solution)/shard_map/convert_element_type | solution.py:86
  202.4 0.9 collective-permute-start.20
  203.3 4.5 %collective-permute-done.25 = bf16[256,1024]{1,0:T(8,128)(2,1)S(1)} collective-permute-done((bf16[256,1024]{1,0:T(8,128)(2,1)S(1)}, bf16[256,1024]{1,0:T(8,128)(2,1)S(1)}, u32[]{:S(2)}, u32[]{:S(2)}) %collective-permute-start.25) | collective-permute-done | bytes 524320 | tf_op jit(solution)/shard_map/ppermute | solution.py:50
  207.8 2.4 %fusion.29 = bf16[256,1024]{1,0:T(8,128)(2,1)} fusion(f32[2048,1024]{1,0:T(8,128)} %reduce-precision_reduce_fusion, bf16[256,1024]{1,0:T(8,128)(2,1)S(1)} %collective-permute-done.25), kind=kLoop, calls=%fused_computation.46 | loop fusion | flops 786432 | bytes 2097152 | tf_op jit(solution)/shard_map/convert_element_type | solution.py:86
  211.0 1.6 copy.50
  212.5 1.6 copy.51
  214.1 2.6 %add_convert_fusion = bf16[256,1024]{1,0:T(8,128)(2,1)} fusion(bf16[256,1024]{1,0:T(8,128)(2,1)} %collective-permute-done.20, bf16[256,1024]{1,0:T(8,128)(2,1)} %copy-done.3, f32[2048,1024]{1,0:T(8,128)} %multiply_reduce_fusion), kind=kLoop, calls=%fused_computation.58 | loop fusion | flops 1310720 | bytes 2621440 | tf_op jit(solution)/shard_map/convert_element_type | solution.py:238
  216.7 3.1 %collective-permute-done.27 = bf16[256,1024]{1,0:T(8,128)(2,1)} collective-permute-done((bf16[256,1024]{1,0:T(8,128)(2,1)}, bf16[256,1024]{1,0:T(8,128)(2,1)}, u32[]{:S(2)}, u32[]{:S(2)}) %collective-permute-start.27) | collective-permute-done | bytes 524320 | tf_op jit(solution)/shard_map/ppermute | solution.py:46
  219.7 2.4 %fusion.35 = bf16[256,1024]{1,0:T(8,128)(2,1)} fusion(f32[2048,1024]{1,0:T(8,128)} %reduce-precision_reduce_fusion, bf16[256,1024]{1,0:T(8,128)(2,1)} %collective-permute-done.27, bf16[256,1024]{1,0:T(8,128)(2,1)S(1)} %copy-done.5), kind=kLoop, calls=%fused_computation.57 | loop fusion | flops 1310720 | bytes 2621440 | tf_op jit(solution)/shard_map/convert_element_type | solution.py:239
  (83 shorter events, 6.6 us)
Async XLA Ops:
  0.6 59.8 %copy-start.2 = (bf16[256,1024]{1,0:T(8,128)(2,1)S(1)}, bf16[256,1024]{1,0:T(8,128)(2,1)}, u32[]{:S(2)}) copy-start(bf16[256,1024]{1,0:T(8,128)(2,1)} %param.10) | copy-start | bytes 1572868
  3.5 15.3 %collective-permute-start = (bf16[1,264,1024]{2,1,0:T(8,128)(2,1)S(1)}, bf16[1,264,1024]{2,1,0:T(8,128)(2,1)S(1)}, u32[]{:S(2)}, u32[]{:S(2)}) collective-permute-start(bf16[1,264,1024]{2,1,0:T(8,128)(2,1)S(1)} %maximum_bitcast_fusion), channel_id=1, source_target_pairs={{0,2},{2,4},{4,6},{6,7},{7,5},{5,3},{3,1},{1,0},{8,10},{10,12},{12... | collective-permute-start | bytes 1622024 | tf_op jit(solution)/shard_map/ppermute | solution.py:50
  6.5 13.7 %collective-permute-start.1 = (bf16[1,264,1024]{2,1,0:T(8,128)(2,1)S(1)}, bf16[1,264,1024]{2,1,0:T(8,128)(2,1)S(1)}, u32[]{:S(2)}, u32[]{:S(2)}) collective-permute-start(bf16[1,264,1024]{2,1,0:T(8,128)(2,1)S(1)} %maximum_bitcast_fusion), channel_id=1, source_target_pairs={{0,1},{2,0},{4,2},{6,4},{7,6},{5,7},{3,5},{1,3},{8,9},{10,8},{12,1... | collective-permute-start | bytes 1622024 | tf_op jit(solution)/shard_map/ppermute | solution.py:51
  20.3 12.8 %collective-permute-start.2 = (bf16[1,264,1024]{2,1,0:T(8,128)(2,1)S(1)}, bf16[1,264,1024]{2,1,0:T(8,128)(2,1)S(1)}, u32[]{:S(2)}, u32[]{:S(2)}) collective-permute-start(bf16[1,264,1024]{2,1,0:T(8,128)(2,1)S(1)} %collective-permute-done), channel_id=1, source_target_pairs={{0,2},{2,4},{4,6},{6,7},{7,5},{5,3},{3,1},{1,0},{8,10},{10,12},{12... | collective-permute-start | bytes 1622024 | tf_op jit(solution)/shard_map/ppermute | solution.py:50
  21.8 12.5 %collective-permute-start.3 = (bf16[1,264,1024]{2,1,0:T(8,128)(2,1)S(1)}, bf16[1,264,1024]{2,1,0:T(8,128)(2,1)S(1)}, u32[]{:S(2)}, u32[]{:S(2)}) collective-permute-start(bf16[1,264,1024]{2,1,0:T(8,128)(2,1)S(1)} %collective-permute-done.1), channel_id=1, source_target_pairs={{0,1},{2,0},{4,2},{6,4},{7,6},{5,7},{3,5},{1,3},{8,9},{10,8},{12,1... | collective-permute-start | bytes 1622024 | tf_op jit(solution)/shard_map/ppermute | solution.py:51
  34.4 11.7 %collective-permute-start.4 = (bf16[1,264,1024]{2,1,0:T(8,128)(2,1)S(1)}, bf16[1,264,1024]{2,1,0:T(8,128)(2,1)}, u32[]{:S(2)}, u32[]{:S(2)}) collective-permute-start(bf16[1,264,1024]{2,1,0:T(8,128)(2,1)S(1)} %collective-permute-done.2), channel_id=1, source_target_pairs={{0,2},{2,4},{4,6},{6,7},{7,5},{5,3},{3,1},{1,0},{8,10},{10,12},{12... | collective-permute-start | bytes 1622024 | tf_op jit(solution)/shard_map/ppermute | solution.py:50
  36.0 11.3 %collective-permute-start.5 = (bf16[1,264,1024]{2,1,0:T(8,128)(2,1)S(1)}, bf16[1,264,1024]{2,1,0:T(8,128)(2,1)S(1)}, u32[]{:S(2)}, u32[]{:S(2)}) collective-permute-start(bf16[1,264,1024]{2,1,0:T(8,128)(2,1)S(1)} %collective-permute-done.3), channel_id=1, source_target_pairs={{0,1},{2,0},{4,2},{6,4},{7,6},{5,7},{3,5},{1,3},{8,9},{10,8},{12,1... | collective-permute-start | bytes 1622024 | tf_op jit(solution)/shard_map/ppermute | solution.py:51
  47.3 10.8 %collective-permute-start.6 = (bf16[1,264,1024]{2,1,0:T(8,128)(2,1)}, bf16[1,264,1024]{2,1,0:T(8,128)(2,1)}, u32[]{:S(2)}, u32[]{:S(2)}) collective-permute-start(bf16[1,264,1024]{2,1,0:T(8,128)(2,1)} %collective-permute-done.4), channel_id=1, source_target_pairs={{0,2},{2,4},{4,6},{6,7},{7,5},{5,3},{3,1},{1,0},{8,10},{10,12},{12... | collective-permute-start | bytes 1622024 | tf_op jit(solution)/shard_map/ppermute | solution.py:46
  48.8 118.7 %collective-permute-start.28 = (bf16[1,2,384,1024]{3,2,1,0:T(8,128)(2,1)}, bf16[1,2,384,1024]{3,2,1,0:T(8,128)(2,1)}, u32[]{:S(2)}, u32[]{:S(2)}) collective-permute-start(bf16[1,2,384,1024]{3,2,1,0:T(8,128)(2,1)} %param.16), channel_id=1, source_target_pairs={{0,16},{8,24},{16,0},{24,8},{1,17},{9,25},{17,1},{25,9},{2,18},{10... | collective-permute-start | bytes 4718600 | tf_op jit(solution)/shard_map/ppermute | solution.py:21
  50.3 118.8 %collective-permute-start.29 = (bf16[1,2,384,1024]{3,2,1,0:T(8,128)(2,1)}, bf16[1,2,384,1024]{3,2,1,0:T(8,128)(2,1)}, u32[]{:S(2)}, u32[]{:S(2)}) collective-permute-start(bf16[1,2,384,1024]{3,2,1,0:T(8,128)(2,1)} %param.16), channel_id=1, source_target_pairs={{0,8},{8,16},{16,24},{24,0},{1,9},{9,17},{17,25},{25,1},{2,10},{10... | collective-permute-start | bytes 4718600 | tf_op jit(solution)/shard_map/ppermute | solution.py:21
  60.6 1.0 copy-start.6
  60.6 3.1 %copy-start.10 = (bf16[1,2,1024,384]{3,2,1,0:T(8,128)(2,1)S(1)}, bf16[1,2,1024,384]{3,2,1,0:T(8,128)(2,1)}, u32[]{:S(2)}) copy-start(bf16[1,2,1024,384]{3,2,1,0:T(8,128)(2,1)} %param.14) | copy-start | bytes 4718596
  61.7 14.3 %copy-start = (bf16[8,256,1024]{2,1,0:T(8,128)(2,1)}, bf16[8,256,1024]{2,1,0:T(8,128)(2,1)S(1)}, u32[]{:S(2)}) copy-start(bf16[8,256,1024]{2,1,0:T(8,128)(2,1)S(1)} %slice.104) | copy-start | bytes 12582916
  61.7 10.8 %collective-permute-start.7 = (bf16[256,1024]{1,0:T(8,128)(2,1)S(1)}, bf16[256,1024]{1,0:T(8,128)(2,1)S(1)}, u32[]{:S(2)}, u32[]{:S(2)}) collective-permute-start(bf16[256,1024]{1,0:T(8,128)(2,1)S(1)} %copy-done.6), channel_id=1, source_target_pairs={{0,2},{2,4},{4,6},{6,7},{7,5},{5,3},{3,1},{1,0},{8,10},{10,12},{12... | collective-permute-start | bytes 1572872 | tf_op jit(solution)/shard_map/ppermute | solution.py:50
  63.1 10.8 %collective-permute-start.8 = (bf16[256,1024]{1,0:T(8,128)(2,1)S(1)}, bf16[256,1024]{1,0:T(8,128)(2,1)S(1)}, u32[]{:S(2)}, u32[]{:S(2)}) collective-permute-start(bf16[256,1024]{1,0:T(8,128)(2,1)S(1)} %copy-done.6), channel_id=1, source_target_pairs={{0,1},{2,0},{4,2},{6,4},{7,6},{5,7},{3,5},{1,3},{8,9},{10,8},{12,1... | collective-permute-start | bytes 1572872 | tf_op jit(solution)/shard_map/ppermute | solution.py:51
  63.7 12.3 %copy-start.12 = (bf16[1,2,1024,384]{3,2,1,0:T(8,128)(2,1)S(1)}, bf16[1,2,1024,384]{3,2,1,0:T(8,128)(2,1)}, u32[]{:S(2)}) copy-start(bf16[1,2,1024,384]{3,2,1,0:T(8,128)(2,1)} %param.15) | copy-start | bytes 4718596
  67.4 15.4 %copy-start.16 = (f32[2048,2,384]{0,2,1:T(8,128)}, f32[2048,2,384]{0,2,1:T(8,128)S(1)}, u32[]{:S(2)}) copy-start(f32[2048,2,384]{0,2,1:T(8,128)S(1)} %fusion.42) | copy-start | bytes 18874372
  73.9 11.4 %collective-permute-start.9 = (bf16[256,1024]{1,0:T(8,128)(2,1)S(1)}, bf16[256,1024]{1,0:T(8,128)(2,1)}, u32[]{:S(2)}, u32[]{:S(2)}) collective-permute-start(bf16[256,1024]{1,0:T(8,128)(2,1)S(1)} %collective-permute-done.7), channel_id=1, source_target_pairs={{0,2},{2,4},{4,6},{6,7},{7,5},{5,3},{3,1},{1,0},{8,10},{10,12},{12... | collective-permute-start | bytes 1572872 | tf_op jit(solution)/shard_map/ppermute | solution.py:50
  75.5 12.1 %collective-permute-start.10 = (bf16[256,1024]{1,0:T(8,128)(2,1)S(1)}, bf16[256,1024]{1,0:T(8,128)(2,1)S(1)}, u32[]{:S(2)}, u32[]{:S(2)}) collective-permute-start(bf16[256,1024]{1,0:T(8,128)(2,1)S(1)} %collective-permute-done.8), channel_id=1, source_target_pairs={{0,1},{2,0},{4,2},{6,4},{7,6},{5,7},{3,5},{1,3},{8,9},{10,8},{12,1... | collective-permute-start | bytes 1572872 | tf_op jit(solution)/shard_map/ppermute | solution.py:51
  87.6 13.0 %collective-permute-start.11 = (bf16[256,1024]{1,0:T(8,128)(2,1)}, bf16[256,1024]{1,0:T(8,128)(2,1)}, u32[]{:S(2)}, u32[]{:S(2)}) collective-permute-start(bf16[256,1024]{1,0:T(8,128)(2,1)} %collective-permute-done.9), channel_id=1, source_target_pairs={{0,2},{2,4},{4,6},{6,7},{7,5},{5,3},{3,1},{1,0},{8,10},{10,12},{12... | collective-permute-start | bytes 1572872 | tf_op jit(solution)/shard_map/ppermute | solution.py:50
  89.1 11.5 %collective-permute-start.12 = (bf16[256,1024]{1,0:T(8,128)(2,1)S(1)}, bf16[256,1024]{1,0:T(8,128)(2,1)}, u32[]{:S(2)}, u32[]{:S(2)}) collective-permute-start(bf16[256,1024]{1,0:T(8,128)(2,1)S(1)} %collective-permute-done.10), channel_id=1, source_target_pairs={{0,1},{2,0},{4,2},{6,4},{7,6},{5,7},{3,5},{1,3},{8,9},{10,8},{12,1... | collective-permute-start | bytes 1572872 | tf_op jit(solution)/shard_map/ppermute | solution.py:51
  100.6 13.4 %collective-permute-start.13 = (bf16[256,1024]{1,0:T(8,128)(2,1)}, bf16[256,1024]{1,0:T(8,128)(2,1)S(1)}, u32[]{:S(2)}, u32[]{:S(2)}) collective-permute-start(bf16[256,1024]{1,0:T(8,128)(2,1)} %collective-permute-done.11), channel_id=1, source_target_pairs={{0,2},{2,4},{4,6},{6,7},{7,5},{5,3},{3,1},{1,0},{8,10},{10,12},{12... | collective-permute-start | bytes 1572872 | tf_op jit(solution)/shard_map/ppermute | solution.py:46
  115.1 7.8 %copy-start.14 = (bf16[1,2,384,1024]{3,2,1,0:T(8,128)(2,1)S(1)}, bf16[1,2,384,1024]{3,2,1,0:T(8,128)(2,1)}, u32[]{:S(2)}) copy-start(bf16[1,2,384,1024]{3,2,1,0:T(8,128)(2,1)} %param.16) | copy-start | bytes 4718596
  117.6 15.5 %copy-start.7 = (bf16[2048,1024]{1,0:T(8,128)(2,1)}, bf16[2048,1024]{1,0:T(8,128)(2,1)S(1)}, u32[]{:S(2)}) copy-start(bf16[2048,1024]{1,0:T(8,128)(2,1)S(1)} %constant_dynamic-update-slice_fusion.8) | copy-start | bytes 12582916
  120.8 29.5 %collective-permute-start.14 = (bf16[256,1024]{1,0:T(8,128)(2,1)S(1)}, bf16[256,1024]{1,0:T(8,128)(2,1)S(1)}, u32[]{:S(2)}, u32[]{:S(2)}) collective-permute-start(bf16[256,1024]{1,0:T(8,128)(2,1)S(1)} %get-tuple-element.90), channel_id=1, source_target_pairs={{0,2},{2,4},{4,6},{6,7},{7,5},{5,3},{3,1},{1,0},{8,10},{10,12},{12... | collective-permute-start | bytes 1572872 | tf_op jit(solution)/shard_map/ppermute | solution.py:50
  121.4 31.0 %collective-permute-start.15 = (bf16[256,1024]{1,0:T(8,128)(2,1)S(1)}, bf16[256,1024]{1,0:T(8,128)(2,1)S(1)}, u32[]{:S(2)}, u32[]{:S(2)}) collective-permute-start(bf16[256,1024]{1,0:T(8,128)(2,1)S(1)} %get-tuple-element.91), channel_id=1, source_target_pairs={{0,1},{2,0},{4,2},{6,4},{7,6},{5,7},{3,5},{1,3},{8,9},{10,8},{12,1... | collective-permute-start | bytes 1572872 | tf_op jit(solution)/shard_map/ppermute | solution.py:51
  122.9 10.2 %copy-start.11 = (bf16[1,2,1024,384]{3,2,1,0:T(8,128)(2,1)S(1)}, bf16[1,2,1024,384]{3,2,1,0:T(8,128)(2,1)}, u32[]{:S(2)}) copy-start(bf16[1,2,1024,384]{3,2,1,0:T(8,128)(2,1)} %param.14) | copy-start | bytes 4718596
  122.9 10.2 %copy-start.13 = (bf16[1,2,1024,384]{3,2,1,0:T(8,128)(2,1)S(1)}, bf16[1,2,1024,384]{3,2,1,0:T(8,128)(2,1)}, u32[]{:S(2)}) copy-start(bf16[1,2,1024,384]{3,2,1,0:T(8,128)(2,1)} %param.15) | copy-start | bytes 4718596
  147.8 21.3 %copy-start.15 = (bf16[1,2,384,1024]{3,2,1,0:T(8,128)(2,1)S(1)}, bf16[1,2,384,1024]{3,2,1,0:T(8,128)(2,1)}, u32[]{:S(2)}) copy-start(bf16[1,2,384,1024]{3,2,1,0:T(8,128)(2,1)} %param.16) | copy-start | bytes 4718596
  149.7 13.6 %collective-permute-start.21 = (bf16[256,1024]{1,0:T(8,128)(2,1)S(1)}, bf16[256,1024]{1,0:T(8,128)(2,1)S(1)}, u32[]{:S(2)}, u32[]{:S(2)}) collective-permute-start(bf16[256,1024]{1,0:T(8,128)(2,1)S(1)} %get-tuple-element.105), channel_id=1, source_target_pairs={{0,2},{2,4},{4,6},{6,7},{7,5},{5,3},{3,1},{1,0},{8,10},{10,12},{12... | collective-permute-start | bytes 1572872 | tf_op jit(solution)/shard_map/ppermute | solution.py:50
  150.3 14.9 %collective-permute-start.22 = (bf16[256,1024]{1,0:T(8,128)(2,1)S(1)}, bf16[256,1024]{1,0:T(8,128)(2,1)S(1)}, u32[]{:S(2)}, u32[]{:S(2)}) collective-permute-start(bf16[256,1024]{1,0:T(8,128)(2,1)S(1)} %get-tuple-element.106), channel_id=1, source_target_pairs={{0,1},{2,0},{4,2},{6,4},{7,6},{5,7},{3,5},{1,3},{8,9},{10,8},{12,1... | collective-permute-start | bytes 1572872 | tf_op jit(solution)/shard_map/ppermute | solution.py:51
  152.4 16.8 %copy-start.8 = (bf16[2048,1024]{1,0:T(8,128)(2,1)S(1)}, bf16[2048,1024]{1,0:T(8,128)(2,1)}, u32[]{:S(2)}) copy-start(bf16[2048,1024]{1,0:T(8,128)(2,1)} %copy-done.7) | copy-start | bytes 12582916
  152.4 16.8 %copy-start.9 = (f32[1,2,384,1024]{3,2,1,0:T(8,128)S(1)}, f32[1,2,384,1024]{3,2,1,0:T(8,128)}, u32[]{:S(2)}) copy-start(f32[1,2,384,1024]{3,2,1,0:T(8,128)} %param.18) | copy-start | bytes 9437188
  154.5 25.1 %collective-permute-start.16 = (bf16[256,1024]{1,0:T(8,128)(2,1)S(1)}, bf16[256,1024]{1,0:T(8,128)(2,1)S(1)}, u32[]{:S(2)}, u32[]{:S(2)}) collective-permute-start(bf16[256,1024]{1,0:T(8,128)(2,1)S(1)} %get-tuple-element.94), channel_id=1, source_target_pairs={{0,2},{2,4},{4,6},{6,7},{7,5},{5,3},{3,1},{1,0},{8,10},{10,12},{12... | collective-permute-start | bytes 1572872 | tf_op jit(solution)/shard_map/ppermute | solution.py:50
  163.2 16.4 %collective-permute-start.17 = (bf16[256,1024]{1,0:T(8,128)(2,1)S(1)}, bf16[256,1024]{1,0:T(8,128)(2,1)S(1)}, u32[]{:S(2)}, u32[]{:S(2)}) collective-permute-start(bf16[256,1024]{1,0:T(8,128)(2,1)S(1)} %get-tuple-element.95), channel_id=1, source_target_pairs={{0,1},{2,0},{4,2},{6,4},{7,6},{5,7},{3,5},{1,3},{8,9},{10,8},{12,1... | collective-permute-start | bytes 1572872 | tf_op jit(solution)/shard_map/ppermute | solution.py:51
  167.1 16.7 %collective-permute-start.23 = (bf16[256,1024]{1,0:T(8,128)(2,1)S(1)}, bf16[256,1024]{1,0:T(8,128)(2,1)S(1)}, u32[]{:S(2)}, u32[]{:S(2)}) collective-permute-start(bf16[256,1024]{1,0:T(8,128)(2,1)S(1)} %get-tuple-element.109), channel_id=1, source_target_pairs={{0,2},{2,4},{4,6},{6,7},{7,5},{5,3},{3,1},{1,0},{8,10},{10,12},{12... | collective-permute-start | bytes 1572872 | tf_op jit(solution)/shard_map/ppermute | solution.py:50
  167.5 21.3 %collective-permute-start.24 = (bf16[256,1024]{1,0:T(8,128)(2,1)S(1)}, bf16[256,1024]{1,0:T(8,128)(2,1)S(1)}, u32[]{:S(2)}, u32[]{:S(2)}) collective-permute-start(bf16[256,1024]{1,0:T(8,128)(2,1)S(1)} %get-tuple-element.110), channel_id=1, source_target_pairs={{0,1},{2,0},{4,2},{6,4},{7,6},{5,7},{3,5},{1,3},{8,9},{10,8},{12,1... | collective-permute-start | bytes 1572872 | tf_op jit(solution)/shard_map/ppermute | solution.py:51
  179.6 13.2 %copy-start.1 = (bf16[8,256,1024]{2,1,0:T(8,128)(2,1)S(1)}, bf16[8,256,1024]{2,1,0:T(8,128)(2,1)}, u32[]{:S(2)}) copy-start(bf16[8,256,1024]{2,1,0:T(8,128)(2,1)} %copy-done) | copy-start | bytes 12582916
  179.6 13.2 %copy-start.17 = (bf16[2,2048,384]{1,2,0:T(8,128)(2,1)S(1)}, bf16[2,2048,384]{1,2,0:T(8,128)(2,1)}, u32[]{:S(2)}) copy-start(bf16[2,2048,384]{1,2,0:T(8,128)(2,1)} %get-tuple-element.145) | copy-start | bytes 9437188
  181.7 18.3 %collective-permute-start.18 = (bf16[256,1024]{1,0:T(8,128)(2,1)S(1)}, bf16[256,1024]{1,0:T(8,128)(2,1)S(1)}, u32[]{:S(2)}, u32[]{:S(2)}) collective-permute-start(bf16[256,1024]{1,0:T(8,128)(2,1)S(1)} %get-tuple-element.98), channel_id=1, source_target_pairs={{0,2},{2,4},{4,6},{6,7},{7,5},{5,3},{3,1},{1,0},{8,10},{10,12},{12... | collective-permute-start | bytes 1572872 | tf_op jit(solution)/shard_map/ppermute | solution.py:50
  182.1 17.9 %collective-permute-start.19 = (bf16[256,1024]{1,0:T(8,128)(2,1)S(1)}, bf16[256,1024]{1,0:T(8,128)(2,1)S(1)}, u32[]{:S(2)}, u32[]{:S(2)}) collective-permute-start(bf16[256,1024]{1,0:T(8,128)(2,1)S(1)} %get-tuple-element.99), channel_id=1, source_target_pairs={{0,1},{2,0},{4,2},{6,4},{7,6},{5,7},{3,5},{1,3},{8,9},{10,8},{12,1... | collective-permute-start | bytes 1572872 | tf_op jit(solution)/shard_map/ppermute | solution.py:51
  190.7 17.1 %collective-permute-start.25 = (bf16[256,1024]{1,0:T(8,128)(2,1)S(1)}, bf16[256,1024]{1,0:T(8,128)(2,1)S(1)}, u32[]{:S(2)}, u32[]{:S(2)}) collective-permute-start(bf16[256,1024]{1,0:T(8,128)(2,1)S(1)} %get-tuple-element.113), channel_id=1, source_target_pairs={{0,2},{2,4},{4,6},{6,7},{7,5},{5,3},{3,1},{1,0},{8,10},{10,12},{12... | collective-permute-start | bytes 1572872 | tf_op jit(solution)/shard_map/ppermute | solution.py:50
  191.7 16.2 %collective-permute-start.26 = (bf16[256,1024]{1,0:T(8,128)(2,1)S(1)}, bf16[256,1024]{1,0:T(8,128)(2,1)S(1)}, u32[]{:S(2)}, u32[]{:S(2)}) collective-permute-start(bf16[256,1024]{1,0:T(8,128)(2,1)S(1)} %get-tuple-element.114), channel_id=1, source_target_pairs={{0,1},{2,0},{4,2},{6,4},{7,6},{5,7},{3,5},{1,3},{8,9},{10,8},{12,1... | collective-permute-start | bytes 1572872 | tf_op jit(solution)/shard_map/ppermute | solution.py:51
  200.0 10.9 %copy-start.3 = (bf16[256,1024]{1,0:T(8,128)(2,1)}, bf16[256,1024]{1,0:T(8,128)(2,1)S(1)}, u32[]{:S(2)}) copy-start(bf16[256,1024]{1,0:T(8,128)(2,1)S(1)} %collective-permute-done.19) | copy-start | bytes 1572868
  202.4 11.7 %collective-permute-start.20 = (bf16[256,1024]{1,0:T(8,128)(2,1)}, bf16[256,1024]{1,0:T(8,128)(2,1)}, u32[]{:S(2)}, u32[]{:S(2)}) collective-permute-start(bf16[256,1024]{1,0:T(8,128)(2,1)} %add_convert_fusion.1), channel_id=1, source_target_pairs={{0,2},{2,4},{4,6},{6,7},{7,5},{5,3},{3,1},{1,0},{8,10},{10,12},{12... | collective-permute-start | bytes 1572872 | tf_op jit(solution)/shard_map/ppermute | solution.py:46
  207.8 3.1 %copy-start.4 = (bf16[256,1024]{1,0:T(8,128)(2,1)}, bf16[256,1024]{1,0:T(8,128)(2,1)S(1)}, u32[]{:S(2)}) copy-start(bf16[256,1024]{1,0:T(8,128)(2,1)S(1)} %collective-permute-done.26) | copy-start | bytes 1572868
  210.2 9.5 %collective-permute-start.27 = (bf16[256,1024]{1,0:T(8,128)(2,1)}, bf16[256,1024]{1,0:T(8,128)(2,1)}, u32[]{:S(2)}, u32[]{:S(2)}) collective-permute-start(bf16[256,1024]{1,0:T(8,128)(2,1)} %fusion.29), channel_id=1, source_target_pairs={{0,2},{2,4},{4,6},{6,7},{7,5},{5,3},{3,1},{1,0},{8,10},{10,12},{12... | collective-permute-start | bytes 1572872 | tf_op jit(solution)/shard_map/ppermute | solution.py:46
  212.5 7.2 %copy-start.5 = (bf16[256,1024]{1,0:T(8,128)(2,1)S(1)}, bf16[256,1024]{1,0:T(8,128)(2,1)}, u32[]{:S(2)}) copy-start(bf16[256,1024]{1,0:T(8,128)(2,1)} %copy-done.4) | copy-start | bytes 1572868

commit v12 on v11

--- a/solution.py
+++ b/solution.py
@@ -131,7 +131,7 @@
     weight_flat = jnp.pad(
         weight_table.reshape(-1), (0, weight_rows * model_width - token_count * experts)
     )
-    packed_tokens = jnp.concatenate([tokens, weight_flat.reshape(weight_rows, model_width)])
+    packed_cot = jnp.concatenate([cotangent, weight_flat.reshape(weight_rows, model_width)])
     ring = ring_order(devices_exp)
     use_ring = devices_exp <= RING_MAX
 
@@ -145,15 +145,15 @@
             return ring_reduce_scatter(value, "exp", ring, jnp.bfloat16)
         return lax.psum_scatter(value, "exp", scatter_dimension=0, tiled=True)
 
-    gathered = gather(packed_tokens[None])
-    group_tokens = gathered[:, :token_count].reshape(devices_exp * token_count, model_width)
+    group_tokens = gather(tokens)
+    _, packed_cot = lax.optimization_barrier((group_tokens, packed_cot))
+    gathered = gather(packed_cot[None])
+    group_cot = gathered[:, :token_count].reshape(devices_exp * token_count, model_width)
     group_weight = (
         gathered[:, token_count:]
         .reshape(devices_exp, -1)[:, : token_count * experts]
         .reshape(devices_exp * token_count, experts)
     )
-    _, cotangent = lax.optimization_barrier((gathered, cotangent))
-    group_cot = gather(cotangent)
     local_weight = lax.dynamic_slice_in_dim(
         group_weight, my_exp * local_experts, local_experts, axis=1
     ).astype(jnp.float32)

time: 223 us -> 236 us (1.058)
  matrix products: 64.6 us -> 71.4 us
  local copies, waits for them, and re-layouts: 16.6 us -> 20.4 us
  waiting for transfers between devices: 87.7 us -> 90.7 us
    ppermute x12, waiting for transfers between devices: 62.9 us -> 68.6 us  [paired_shift(): ahead_value = lax.ppermute(ahead_value, axis, ring_pairs(ring, 1))]
    unnamed x54 -> x43, local copies, waits for them, and re-layouts: 8.66 us -> 12.5 us
    ppermute x12, waiting for transfers between devices: 13.9 us -> 11 us  [paired_shift(): behind_value = lax.ppermute(behind_value, axis, ring_pairs(ring, -1))]
  transfers between devices with their start and end apart: 30 -> 30, of which waited for: 17 -> 18; matrix products, arithmetic and copies ran while one was open for 43% -> 43% of each run, Pallas kernels for 0% -> 0%
where the time goes in v12:
time: 236 us; the launch traced here: 235 us
  waiting for transfers between devices  90.7 us (38%)
  matrix products  71.4 us (30%)
  starting transfers between devices  30.7 us (13%)
  local copies, waits for them, and re-layouts  20.4 us (9%)
  other arithmetic  20.3 us (9%)
    ppermute x12, waiting for transfers between devices, paired_shift(): ahead_value = lax.ppermute(ahead_value, axis, ring_pairs(ring, 1))  68.6 us
    dot_general x1, matrix products, chunk_pass(): jnp.einsum('eth,edh->etd', joint_cot, joint_matrix, preferred_element_typ...  14.7 us
    ppermute x12, starting transfers between devices, paired_shift(): ahead_value = lax.ppermute(ahead_value, axis, ring_pairs(ring, 1))  14.6 us
    convert_element_type x6, other arithmetic, to_wire(): return value.astype(wire_dtype)  12.7 us
    unnamed x43, local copies, waits for them, and re-layouts  12.5 us
    dot_general x1, matrix products, chunk_pass(): jnp.einsum('eth,ehd->etd', hidden, down_matrix, preferred_element_type=jn...  11.8 us
    ppermute x4, waiting for transfers between devices, paired_shift(): return (lax.ppermute(ahead_value, axis, ring_pairs(ring, 1)), None)  11.1 us
    ppermute x12, starting transfers between devices, paired_shift(): behind_value = lax.ppermute(behind_value, axis, ring_pairs(ring, -1))  11 us
  transfers between devices with their start and end apart: 30, of which 18 were waited for; matrix products, arithmetic and copies ran while one was open for 43% of the time, Pallas kernels for 0%

profile of v12, /device:TPU:0, one launch (start us, length us, event | category | flops | bytes accessed | tf_op | source)
XLA Modules:
  0.0 235.0 jit_solution(9200166102965027956)
XLA Ops:
  0.6 3.1 %collective-permute-start = (bf16[256,1024]{1,0:T(8,128)(2,1)}, bf16[256,1024]{1,0:T(8,128)(2,1)S(1)}, u32[]{:S(2)}, u32[]{:S(2)}) collective-permute-start(bf16[256,1024]{1,0:T(8,128)(2,1)} %param.10), channel_id=1, source_target_pairs={{0,2},{2,4},{4,6},{6,7},{7,5},{5,3},{3,1},{1,0},{8,10},{10,12},{12... | collective-permute-start | bytes 1572872 | tf_op jit(solution)/shard_map/ppermute | solution.py:50
  3.7 12.1 %collective-permute-done = bf16[256,1024]{1,0:T(8,128)(2,1)S(1)} collective-permute-done((bf16[256,1024]{1,0:T(8,128)(2,1)}, bf16[256,1024]{1,0:T(8,128)(2,1)S(1)}, u32[]{:S(2)}, u32[]{:S(2)}) %collective-permute-start) | collective-permute-done | bytes 524320 | tf_op jit(solution)/shard_map/ppermute | solution.py:50
  15.8 1.5 collective-permute-done.1
  17.3 1.6 collective-permute-start.2
  19.3 10.4 %collective-permute-done.2 = bf16[256,1024]{1,0:T(8,128)(2,1)S(1)} collective-permute-done((bf16[256,1024]{1,0:T(8,128)(2,1)S(1)}, bf16[256,1024]{1,0:T(8,128)(2,1)S(1)}, u32[]{:S(2)}, u32[]{:S(2)}) %collective-permute-start.2) | collective-permute-done | bytes 524320 | tf_op jit(solution)/shard_map/ppermute | solution.py:50
  29.8 1.3 collective-permute-done.3
  31.1 1.6 collective-permute-start.4
  33.1 9.4 %collective-permute-done.4 = bf16[256,1024]{1,0:T(8,128)(2,1)} collective-permute-done((bf16[256,1024]{1,0:T(8,128)(2,1)S(1)}, bf16[256,1024]{1,0:T(8,128)(2,1)}, u32[]{:S(2)}, u32[]{:S(2)}) %collective-permute-start.4) | collective-permute-done | bytes 524320 | tf_op jit(solution)/shard_map/ppermute | solution.py:50
  42.5 1.2 collective-permute-done.5
  44.4 1.5 collective-permute-start.6
  47.6 1.1 pad_maximum_fusion.5
  48.8 6.2 %collective-permute-done.6 = bf16[256,1024]{1,0:T(8,128)(2,1)} collective-permute-done((bf16[256,1024]{1,0:T(8,128)(2,1)}, bf16[256,1024]{1,0:T(8,128)(2,1)}, u32[]{:S(2)}, u32[]{:S(2)}) %collective-permute-start.6) | collective-permute-done | bytes 524320 | tf_op jit(solution)/shard_map/ppermute | solution.py:46
  54.9 1.9 constant_dynamic-update-slice_fusion.7
  56.8 1.9 constant_dynamic-update-slice_fusion.6
  59.5 0.8 constant_dynamic-update-slice_fusion.4
  60.4 0.8 constant_dynamic-update-slice_fusion.3
  62.0 0.9 constant_dynamic-update-slice_fusion.1
  62.9 0.9 constant_dynamic-update-slice_fusion
  63.8 1.5 collective-permute-start.7
  65.8 9.4 %collective-permute-done.7 = bf16[1,264,1024]{2,1,0:T(8,128)(2,1)S(1)} collective-permute-done((bf16[1,264,1024]{2,1,0:T(8,128)(2,1)S(1)}, bf16[1,264,1024]{2,1,0:T(8,128)(2,1)S(1)}, u32[]{:S(2)}, u32[]{:S(2)}) %collective-permute-start.7) | collective-permute-done | bytes 540704 | tf_op jit(solution)/shard_map/ppermute | solution.py:50
  75.2 1.7 collective-permute-done.8
  76.9 1.1 collective-permute-start.9
  78.0 0.9 collective-permute-start.10
  78.9 1.5 collective-permute-start.28
  80.4 8.3 %collective-permute-done.9 = bf16[1,264,1024]{2,1,0:T(8,128)(2,1)S(1)} collective-permute-done((bf16[1,264,1024]{2,1,0:T(8,128)(2,1)S(1)}, bf16[1,264,1024]{2,1,0:T(8,128)(2,1)S(1)}, u32[]{:S(2)}, u32[]{:S(2)}) %collective-permute-start.9) | collective-permute-done | bytes 540704 | tf_op jit(solution)/shard_map/ppermute | solution.py:50
  88.7 1.4 collective-permute-done.10
  90.9 1.2 collective-permute-start.12
  92.1 5.8 %fusion.16 = f32[2048,2,384]{0,2,1:T(8,128)S(1)} fusion(bf16[2048,1024]{1,0:T(8,128)(2,1)} %constant_dynamic-update-slice_fusion, bf16[1,2,1024,384]{3,2,1,0:T(8,128)(2,1)} %param.14), kind=kOutput, calls=%fused_computation.26 | convolution fusion | flops 3221225472 | bytes 12058624 | tf_op jit(solution)/shard_map/td,edh->eth/dot_general | solution.py:170
  98.0 4.9 %collective-permute-done.11 = bf16[1,264,1024]{2,1,0:T(8,128)(2,1)S(1)} collective-permute-done((bf16[1,264,1024]{2,1,0:T(8,128)(2,1)S(1)}, bf16[1,264,1024]{2,1,0:T(8,128)(2,1)S(1)}, u32[]{:S(2)}, u32[]{:S(2)}) %collective-permute-start.11) | collective-permute-done | bytes 540704 | tf_op jit(solution)/shard_map/ppermute | solution.py:50
  103.7 9.2 %fusion.4 = (bf16[2,2048,384]{1,2,0:T(8,128)(2,1)}, f32[2048,2,384]{0,2,1:T(8,128)}) fusion(f32[2048,2,384]{0,2,1:T(8,128)S(1)} %fusion.16, bf16[1,2,1024,384]{3,2,1,0:T(8,128)(2,1)S(1)} %copy-done.8, bf16[2048,1024]{1,0:T(8,128)(2,1)} %constant_dynamic-update-slice_fusion), kind=kOutput, calls=%fused_computation.9 | convolution fusion | flops 3230662656 | bytes 21495808 | tf_op jit(solution)/shard_map/td,edh->eth/dot_general | solution.py:173
  113.2 2.5 %slice.102 = bf16[8,256,1024]{2,1,0:T(8,128)(2,1)} slice(bf16[8,264,1024]{2,1,0:T(8,128)(2,1)S(1)} %constant_dynamic-update-slice_fusion.8), slice={[0:8], [0:256], [0:1024]} | slice | bytes 8388608 | tf_op jit(solution)/shard_map/slice | solution.py:151
  116.7 11.8 %multiply_reduce_fusion = f32[2048,1024]{1,0:T(8,128)} fusion(f32[2,2048]{1,0:T(2,128)S(1)} %bitcast_convert_fusion, bf16[2,2048,384]{1,2,0:T(8,128)(2,1)} %get-tuple-element.164, bf16[1,2,384,1024]{3,2,1,0:T(8,128)(2,1)} %param.16), kind=kOutput, calls=%fused_computation.1 | convolution fusion | flops 3231711232 | bytes 13123584 | tf_op jit(solution)/shard_map/eth,ehd->etd/dot_general | solution.py:180
  128.5 1.7 fusion.50
  130.2 0.8 collective-permute-start.14
  131.0 1.2 collective-permute-start.15
  132.2 10.6 %fusion.7 = (bf16[2,2048,384]{1,2,0:T(8,128)(2,1)}, bf16[2,2048,384]{1,2,0:T(8,128)(2,1)}) fusion(f32[2048,2,384]{0,2,1:T(8,128)} %get-tuple-element.165, f32[2048,2,384]{0,2,1:T(8,128)} %copy-done.9, bf16[1,2,384,1024]{3,2,1,0:T(8,128)(2,1)} %param.16, bf16[2048,1024]{1,0:T(8,128)(2,1)S(1)} %bitcast.102, bf16[2,2048]{1,0:T(2,128)(2,1)S(1)} %bitcast.107), kind=kOutput, calls=%fused_computation.12 | convolution fusion | flops 3245867008 | bytes 24649728 | tf_op jit(solution)/shard_map/etd,ehd->eth/dot_general | solution.py:185
  142.8 14.7 %reduce-precision_reduce_fusion = f32[2048,1024]{1,0:T(8,128)} fusion(bf16[2,2048,384]{1,2,0:T(8,128)(2,1)} %get-tuple-element.146, bf16[2,2048,384]{1,2,0:T(8,128)(2,1)} %get-tuple-element.145, bf16[2,1024,384]{2,1,0:T(8,128)(2,1)} %bitcast.110, bf16[2,1024,384]{2,1,0:T(8,128)(2,1)} %bitcast.109), kind=kOutput, calls=%fused_computation | convolution fusion | flops 6467616768 | bytes 17825792 | tf_op jit(solution)/shard_map/eth,edh->etd/dot_general | solution.py:202
  157.5 1.7 fusion.49
  159.2 0.8 collective-permute-start.21
  160.0 1.2 collective-permute-start.22
  161.9 2.1 add_convert_fusion.4
  164.9 9.2 %collective-permute-done.21 = bf16[256,1024]{1,0:T(8,128)(2,1)S(1)} collective-permute-done((bf16[256,1024]{1,0:T(8,128)(2,1)S(1)}, bf16[256,1024]{1,0:T(8,128)(2,1)S(1)}, u32[]{:S(2)}, u32[]{:S(2)}) %collective-permute-start.21) | collective-permute-done | bytes 524320 | tf_op jit(solution)/shard_map/ppermute | solution.py:50
  174.1 1.2 collective-permute-start.17
  175.3 1.9 fusion.39
  177.3 0.8 collective-permute-start.23
  178.1 1.2 collective-permute-start.24
  179.3 10.6 %fusion.44 = (f32[1,2,384,1024]{3,2,1,0:T(8,128)}, bf16[1,2,384,1024]{3,2,1,0:T(8,128)(2,1)}, f32[1,2,384,1024]{3,2,1,0:T(8,128)}) fusion(f32[1,2,384,1024]{3,2,1,0:T(8,128)S(1)} %copy-done.7, f32[1,2,384,1024]{3,2,1,0:T(8,128)} %param.17, bf16[1,2,384,1024]{3,2,1,0:T(8,128)(2,1)} %collective-permute-done.28, ...), kind=kOutput, calls=%fused_computation.70 | convolution fusion | flops 3241934848 | bytes 26222592 | tf_op jit(solution)/shard_map/eth,etd->ehd/dot_general | solution.py:192
  190.0 2.1 add_convert_fusion.2
  192.1 0.9 collective-permute-start.18
  192.9 1.2 collective-permute-start.19
  194.1 2.2 collective-permute-done.23
  196.3 3.9 %collective-permute-done.24 = bf16[256,1024]{1,0:T(8,128)(2,1)S(1)} collective-permute-done((bf16[256,1024]{1,0:T(8,128)(2,1)S(1)}, bf16[256,1024]{1,0:T(8,128)(2,1)S(1)}, u32[]{:S(2)}, u32[]{:S(2)}) %collective-permute-start.24) | collective-permute-done | bytes 524320 | tf_op jit(solution)/shard_map/ppermute | solution.py:51
  200.2 1.9 fusion.37
  202.9 1.3 collective-permute-start.26
  204.2 8.7 %convert_bitcast_fusion = bf16[2,1024,768]{1,2,0:T(8,128)(2,1)S(1)} fusion(bf16[2048,1024]{1,0:T(8,128)(2,1)} %constant_dynamic-update-slice_fusion, bf16[2,2048,384]{1,2,0:T(8,128)(2,1)S(1)} %copy-done.11, bf16[2,2048,384]{1,2,0:T(8,128)(2,1)S(1)} %copy-done.10), kind=kOutput, calls=%fused_computation.44 | convolution fusion | flops 6456606720 | bytes 13631488 | tf_op jit(solution)/shard_map/td,eth->edh/dot_general | solution.py:196
  212.9 2.4 %add_convert_fusion.1 = bf16[256,1024]{1,0:T(8,128)(2,1)} fusion(f32[2048,1024]{1,0:T(8,128)} %multiply_reduce_fusion, bf16[256,1024]{1,0:T(8,128)(2,1)S(1)} %collective-permute-done.18), kind=kLoop, calls=%fused_computation.64 | loop fusion | flops 786432 | bytes 2097152 | tf_op jit(solution)/shard_map/convert_element_type | solution.py:86
  216.1 2.7 %collective-permute-done.25 = bf16[256,1024]{1,0:T(8,128)(2,1)S(1)} collective-permute-done((bf16[256,1024]{1,0:T(8,128)(2,1)S(1)}, bf16[256,1024]{1,0:T(8,128)(2,1)S(1)}, u32[]{:S(2)}, u32[]{:S(2)}) %collective-permute-start.25) | collective-permute-done | bytes 524320 | tf_op jit(solution)/shard_map/ppermute | solution.py:50
  218.8 2.4 %fusion.36 = bf16[256,1024]{1,0:T(8,128)(2,1)} fusion(f32[2048,1024]{1,0:T(8,128)} %reduce-precision_reduce_fusion, bf16[256,1024]{1,0:T(8,128)(2,1)S(1)} %collective-permute-done.25), kind=kLoop, calls=%fused_computation.51 | loop fusion | flops 786432 | bytes 2097152 | tf_op jit(solution)/shard_map/convert_element_type | solution.py:86
  222.0 1.6 copy.50
  223.5 1.6 copy.51
  225.1 1.9 collective-permute-done.20
  227.0 2.6 %add_convert_fusion = bf16[256,1024]{1,0:T(8,128)(2,1)} fusion(bf16[256,1024]{1,0:T(8,128)(2,1)} %collective-permute-done.20, bf16[256,1024]{1,0:T(8,128)(2,1)} %copy-done.1, f32[2048,1024]{1,0:T(8,128)} %multiply_reduce_fusion), kind=kLoop, calls=%fused_computation.63 | loop fusion | flops 1310720 | bytes 2621440 | tf_op jit(solution)/shard_map/convert_element_type | solution.py:238
  229.6 3.0 %collective-permute-done.27 = bf16[256,1024]{1,0:T(8,128)(2,1)} collective-permute-done((bf16[256,1024]{1,0:T(8,128)(2,1)}, bf16[256,1024]{1,0:T(8,128)(2,1)}, u32[]{:S(2)}, u32[]{:S(2)}) %collective-permute-start.27) | collective-permute-done | bytes 524320 | tf_op jit(solution)/shard_map/ppermute | solution.py:46
  232.6 2.4 %fusion.42 = bf16[256,1024]{1,0:T(8,128)(2,1)} fusion(f32[2048,1024]{1,0:T(8,128)} %reduce-precision_reduce_fusion, bf16[256,1024]{1,0:T(8,128)(2,1)} %collective-permute-done.27, bf16[256,1024]{1,0:T(8,128)(2,1)S(1)} %copy-done.3), kind=kLoop, calls=%fused_computation.62 | loop fusion | flops 1310720 | bytes 2621440 | tf_op jit(solution)/shard_map/convert_element_type | solution.py:239
  (71 shorter events, 11.6 us)
Async XLA Ops:
  0.6 59.8 %copy-start.4 = (bf16[256,1024]{1,0:T(8,128)(2,1)S(1)}, bf16[256,1024]{1,0:T(8,128)(2,1)}, u32[]{:S(2)}) copy-start(bf16[256,1024]{1,0:T(8,128)(2,1)} %param.10) | copy-start | bytes 1572868
  0.6 15.1 %collective-permute-start = (bf16[256,1024]{1,0:T(8,128)(2,1)}, bf16[256,1024]{1,0:T(8,128)(2,1)S(1)}, u32[]{:S(2)}, u32[]{:S(2)}) collective-permute-start(bf16[256,1024]{1,0:T(8,128)(2,1)} %param.10), channel_id=1, source_target_pairs={{0,2},{2,4},{4,6},{6,7},{7,5},{5,3},{3,1},{1,0},{8,10},{10,12},{12... | collective-permute-start | bytes 1572872 | tf_op jit(solution)/shard_map/ppermute | solution.py:50
  3.7 13.6 %collective-permute-start.1 = (bf16[256,1024]{1,0:T(8,128)(2,1)}, bf16[256,1024]{1,0:T(8,128)(2,1)S(1)}, u32[]{:S(2)}, u32[]{:S(2)}) collective-permute-start(bf16[256,1024]{1,0:T(8,128)(2,1)} %param.10), channel_id=1, source_target_pairs={{0,1},{2,0},{4,2},{6,4},{7,6},{5,7},{3,5},{1,3},{8,9},{10,8},{12,1... | collective-permute-start | bytes 1572872 | tf_op jit(solution)/shard_map/ppermute | solution.py:51
  17.3 12.5 %collective-permute-start.2 = (bf16[256,1024]{1,0:T(8,128)(2,1)S(1)}, bf16[256,1024]{1,0:T(8,128)(2,1)S(1)}, u32[]{:S(2)}, u32[]{:S(2)}) collective-permute-start(bf16[256,1024]{1,0:T(8,128)(2,1)S(1)} %collective-permute-done), channel_id=1, source_target_pairs={{0,2},{2,4},{4,6},{6,7},{7,5},{5,3},{3,1},{1,0},{8,10},{10,12},{12... | collective-permute-start | bytes 1572872 | tf_op jit(solution)/shard_map/ppermute | solution.py:50
  18.9 12.2 %collective-permute-start.3 = (bf16[256,1024]{1,0:T(8,128)(2,1)S(1)}, bf16[256,1024]{1,0:T(8,128)(2,1)S(1)}, u32[]{:S(2)}, u32[]{:S(2)}) collective-permute-start(bf16[256,1024]{1,0:T(8,128)(2,1)S(1)} %collective-permute-done.1), channel_id=1, source_target_pairs={{0,1},{2,0},{4,2},{6,4},{7,6},{5,7},{3,5},{1,3},{8,9},{10,8},{12,1... | collective-permute-start | bytes 1572872 | tf_op jit(solution)/shard_map/ppermute | solution.py:51
  31.1 11.4 %collective-permute-start.4 = (bf16[256,1024]{1,0:T(8,128)(2,1)S(1)}, bf16[256,1024]{1,0:T(8,128)(2,1)}, u32[]{:S(2)}, u32[]{:S(2)}) collective-permute-start(bf16[256,1024]{1,0:T(8,128)(2,1)S(1)} %collective-permute-done.2), channel_id=1, source_target_pairs={{0,2},{2,4},{4,6},{6,7},{7,5},{5,3},{3,1},{1,0},{8,10},{10,12},{12... | collective-permute-start | bytes 1572872 | tf_op jit(solution)/shard_map/ppermute | solution.py:50
  32.7 11.0 %collective-permute-start.5 = (bf16[256,1024]{1,0:T(8,128)(2,1)S(1)}, bf16[256,1024]{1,0:T(8,128)(2,1)S(1)}, u32[]{:S(2)}, u32[]{:S(2)}) collective-permute-start(bf16[256,1024]{1,0:T(8,128)(2,1)S(1)} %collective-permute-done.3), channel_id=1, source_target_pairs={{0,1},{2,0},{4,2},{6,4},{7,6},{5,7},{3,5},{1,3},{8,9},{10,8},{12,1... | collective-permute-start | bytes 1572872 | tf_op jit(solution)/shard_map/ppermute | solution.py:51
  43.7 0.8 copy-start.5
  44.4 10.5 %collective-permute-start.6 = (bf16[256,1024]{1,0:T(8,128)(2,1)}, bf16[256,1024]{1,0:T(8,128)(2,1)}, u32[]{:S(2)}, u32[]{:S(2)}) collective-permute-start(bf16[256,1024]{1,0:T(8,128)(2,1)} %collective-permute-done.4), channel_id=1, source_target_pairs={{0,2},{2,4},{4,6},{6,7},{7,5},{5,3},{3,1},{1,0},{8,10},{10,12},{12... | collective-permute-start | bytes 1572872 | tf_op jit(solution)/shard_map/ppermute | solution.py:46
  47.6 15.3 %copy-start.6 = (bf16[256,1024]{1,0:T(8,128)(2,1)S(1)}, bf16[256,1024]{1,0:T(8,128)(2,1)}, u32[]{:S(2)}) copy-start(bf16[256,1024]{1,0:T(8,128)(2,1)} %copy-done.5) | copy-start | bytes 1572868
  63.8 11.4 %collective-permute-start.7 = (bf16[1,264,1024]{2,1,0:T(8,128)(2,1)S(1)}, bf16[1,264,1024]{2,1,0:T(8,128)(2,1)S(1)}, u32[]{:S(2)}, u32[]{:S(2)}) collective-permute-start(bf16[1,264,1024]{2,1,0:T(8,128)(2,1)S(1)} %bitcast.104), channel_id=1, source_target_pairs={{0,2},{2,4},{4,6},{6,7},{7,5},{5,3},{3,1},{1,0},{8,10},{10,12},{12... | collective-permute-start | bytes 1622024 | tf_op jit(solution)/shard_map/ppermute | solution.py:50
  65.3 11.6 %collective-permute-start.8 = (bf16[1,264,1024]{2,1,0:T(8,128)(2,1)S(1)}, bf16[1,264,1024]{2,1,0:T(8,128)(2,1)S(1)}, u32[]{:S(2)}, u32[]{:S(2)}) collective-permute-start(bf16[1,264,1024]{2,1,0:T(8,128)(2,1)S(1)} %bitcast.105), channel_id=1, source_target_pairs={{0,1},{2,0},{4,2},{6,4},{7,6},{5,7},{3,5},{1,3},{8,9},{10,8},{12,1... | collective-permute-start | bytes 1622024 | tf_op jit(solution)/shard_map/ppermute | solution.py:51
  76.9 11.8 %collective-permute-start.9 = (bf16[1,264,1024]{2,1,0:T(8,128)(2,1)S(1)}, bf16[1,264,1024]{2,1,0:T(8,128)(2,1)S(1)}, u32[]{:S(2)}, u32[]{:S(2)}) collective-permute-start(bf16[1,264,1024]{2,1,0:T(8,128)(2,1)S(1)} %collective-permute-done.7), channel_id=1, source_target_pairs={{0,2},{2,4},{4,6},{6,7},{7,5},{5,3},{3,1},{1,0},{8,10},{10,12},{12... | collective-permute-start | bytes 1622024 | tf_op jit(solution)/shard_map/ppermute | solution.py:50
  78.0 12.1 %collective-permute-start.10 = (bf16[1,264,1024]{2,1,0:T(8,128)(2,1)S(1)}, bf16[1,264,1024]{2,1,0:T(8,128)(2,1)S(1)}, u32[]{:S(2)}, u32[]{:S(2)}) collective-permute-start(bf16[1,264,1024]{2,1,0:T(8,128)(2,1)S(1)} %collective-permute-done.8), channel_id=1, source_target_pairs={{0,1},{2,0},{4,2},{6,4},{7,6},{5,7},{3,5},{1,3},{8,9},{10,8},{12,1... | collective-permute-start | bytes 1622024 | tf_op jit(solution)/shard_map/ppermute | solution.py:51
  78.9 99.2 %collective-permute-start.28 = (bf16[1,2,384,1024]{3,2,1,0:T(8,128)(2,1)}, bf16[1,2,384,1024]{3,2,1,0:T(8,128)(2,1)}, u32[]{:S(2)}, u32[]{:S(2)}) collective-permute-start(bf16[1,2,384,1024]{3,2,1,0:T(8,128)(2,1)} %param.16), channel_id=1, source_target_pairs={{0,16},{8,24},{16,0},{24,8},{1,17},{9,25},{17,1},{25,9},{2,18},{10... | collective-permute-start | bytes 4718600 | tf_op jit(solution)/shard_map/ppermute | solution.py:21
  80.4 98.9 %collective-permute-start.29 = (bf16[1,2,384,1024]{3,2,1,0:T(8,128)(2,1)}, bf16[1,2,384,1024]{3,2,1,0:T(8,128)(2,1)}, u32[]{:S(2)}, u32[]{:S(2)}) collective-permute-start(bf16[1,2,384,1024]{3,2,1,0:T(8,128)(2,1)} %param.16), channel_id=1, source_target_pairs={{0,8},{8,16},{16,24},{24,0},{1,9},{9,17},{17,25},{25,1},{2,10},{10... | collective-permute-start | bytes 4718600 | tf_op jit(solution)/shard_map/ppermute | solution.py:21
  80.4 23.3 %copy-start.8 = (bf16[1,2,1024,384]{3,2,1,0:T(8,128)(2,1)S(1)}, bf16[1,2,1024,384]{3,2,1,0:T(8,128)(2,1)}, u32[]{:S(2)}) copy-start(bf16[1,2,1024,384]{3,2,1,0:T(8,128)(2,1)} %param.15) | copy-start | bytes 4718596
  90.1 12.8 %collective-permute-start.11 = (bf16[1,264,1024]{2,1,0:T(8,128)(2,1)S(1)}, bf16[1,264,1024]{2,1,0:T(8,128)(2,1)S(1)}, u32[]{:S(2)}, u32[]{:S(2)}) collective-permute-start(bf16[1,264,1024]{2,1,0:T(8,128)(2,1)S(1)} %collective-permute-done.9), channel_id=1, source_target_pairs={{0,2},{2,4},{4,6},{6,7},{7,5},{5,3},{3,1},{1,0},{8,10},{10,12},{12... | collective-permute-start | bytes 1622024 | tf_op jit(solution)/shard_map/ppermute | solution.py:50
  90.9 12.0 %collective-permute-start.12 = (bf16[1,264,1024]{2,1,0:T(8,128)(2,1)S(1)}, bf16[1,264,1024]{2,1,0:T(8,128)(2,1)S(1)}, u32[]{:S(2)}, u32[]{:S(2)}) collective-permute-start(bf16[1,264,1024]{2,1,0:T(8,128)(2,1)S(1)} %collective-permute-done.10), channel_id=1, source_target_pairs={{0,1},{2,0},{4,2},{6,4},{7,6},{5,7},{3,5},{1,3},{8,9},{10,8},{12,1... | collective-permute-start | bytes 1622024 | tf_op jit(solution)/shard_map/ppermute | solution.py:51
  98.0 14.9 %copy-start.9 = (f32[2048,2,384]{0,2,1:T(8,128)}, f32[2048,2,384]{0,2,1:T(8,128)S(1)}, u32[]{:S(2)}) copy-start(f32[2048,2,384]{0,2,1:T(8,128)S(1)} %fusion.16) | copy-start | bytes 18874372
  102.9 10.0 %collective-permute-start.13 = (bf16[1,264,1024]{2,1,0:T(8,128)(2,1)S(1)}, bf16[1,264,1024]{2,1,0:T(8,128)(2,1)S(1)}, u32[]{:S(2)}, u32[]{:S(2)}) collective-permute-start(bf16[1,264,1024]{2,1,0:T(8,128)(2,1)S(1)} %collective-permute-done.11), channel_id=1, source_target_pairs={{0,2},{2,4},{4,6},{6,7},{7,5},{5,3},{3,1},{1,0},{8,10},{10,12},{12... | collective-permute-start | bytes 1622024 | tf_op jit(solution)/shard_map/ppermute | solution.py:46
  116.6 15.6 %copy-start = (bf16[8,256,1024]{2,1,0:T(8,128)(2,1)S(1)}, bf16[8,256,1024]{2,1,0:T(8,128)(2,1)}, u32[]{:S(2)}) copy-start(bf16[8,256,1024]{2,1,0:T(8,128)(2,1)} %slice.102) | copy-start | bytes 12582916
  130.2 29.9 %collective-permute-start.14 = (bf16[256,1024]{1,0:T(8,128)(2,1)S(1)}, bf16[256,1024]{1,0:T(8,128)(2,1)S(1)}, u32[]{:S(2)}, u32[]{:S(2)}) collective-permute-start(bf16[256,1024]{1,0:T(8,128)(2,1)S(1)} %get-tuple-element.90), channel_id=1, source_target_pairs={{0,2},{2,4},{4,6},{6,7},{7,5},{5,3},{3,1},{1,0},{8,10},{10,12},{12... | collective-permute-start | bytes 1572872 | tf_op jit(solution)/shard_map/ppermute | solution.py:50
  131.0 30.9 %collective-permute-start.15 = (bf16[256,1024]{1,0:T(8,128)(2,1)S(1)}, bf16[256,1024]{1,0:T(8,128)(2,1)S(1)}, u32[]{:S(2)}, u32[]{:S(2)}) collective-permute-start(bf16[256,1024]{1,0:T(8,128)(2,1)S(1)} %get-tuple-element.91), channel_id=1, source_target_pairs={{0,1},{2,0},{4,2},{6,4},{7,6},{5,7},{3,5},{1,3},{8,9},{10,8},{12,1... | collective-permute-start | bytes 1572872 | tf_op jit(solution)/shard_map/ppermute | solution.py:51
  159.2 14.9 %collective-permute-start.21 = (bf16[256,1024]{1,0:T(8,128)(2,1)S(1)}, bf16[256,1024]{1,0:T(8,128)(2,1)S(1)}, u32[]{:S(2)}, u32[]{:S(2)}) collective-permute-start(bf16[256,1024]{1,0:T(8,128)(2,1)S(1)} %get-tuple-element.105), channel_id=1, source_target_pairs={{0,2},{2,4},{4,6},{6,7},{7,5},{5,3},{3,1},{1,0},{8,10},{10,12},{12... | collective-permute-start | bytes 1572872 | tf_op jit(solution)/shard_map/ppermute | solution.py:50
  160.0 15.3 %collective-permute-start.22 = (bf16[256,1024]{1,0:T(8,128)(2,1)S(1)}, bf16[256,1024]{1,0:T(8,128)(2,1)S(1)}, u32[]{:S(2)}, u32[]{:S(2)}) collective-permute-start(bf16[256,1024]{1,0:T(8,128)(2,1)S(1)} %get-tuple-element.106), channel_id=1, source_target_pairs={{0,1},{2,0},{4,2},{6,4},{7,6},{5,7},{3,5},{1,3},{8,9},{10,8},{12,1... | collective-permute-start | bytes 1572872 | tf_op jit(solution)/shard_map/ppermute | solution.py:51
  161.9 17.4 %copy-start.7 = (f32[1,2,384,1024]{3,2,1,0:T(8,128)S(1)}, f32[1,2,384,1024]{3,2,1,0:T(8,128)}, u32[]{:S(2)}) copy-start(f32[1,2,384,1024]{3,2,1,0:T(8,128)} %param.18) | copy-start | bytes 9437188
  164.0 25.9 %collective-permute-start.16 = (bf16[256,1024]{1,0:T(8,128)(2,1)S(1)}, bf16[256,1024]{1,0:T(8,128)(2,1)S(1)}, u32[]{:S(2)}, u32[]{:S(2)}) collective-permute-start(bf16[256,1024]{1,0:T(8,128)(2,1)S(1)} %get-tuple-element.94), channel_id=1, source_target_pairs={{0,2},{2,4},{4,6},{6,7},{7,5},{5,3},{3,1},{1,0},{8,10},{10,12},{12... | collective-permute-start | bytes 1572872 | tf_op jit(solution)/shard_map/ppermute | solution.py:50
  174.1 15.9 %collective-permute-start.17 = (bf16[256,1024]{1,0:T(8,128)(2,1)S(1)}, bf16[256,1024]{1,0:T(8,128)(2,1)S(1)}, u32[]{:S(2)}, u32[]{:S(2)}) collective-permute-start(bf16[256,1024]{1,0:T(8,128)(2,1)S(1)} %get-tuple-element.95), channel_id=1, source_target_pairs={{0,1},{2,0},{4,2},{6,4},{7,6},{5,7},{3,5},{1,3},{8,9},{10,8},{12,1... | collective-permute-start | bytes 1572872 | tf_op jit(solution)/shard_map/ppermute | solution.py:51
  177.3 19.1 %collective-permute-start.23 = (bf16[256,1024]{1,0:T(8,128)(2,1)S(1)}, bf16[256,1024]{1,0:T(8,128)(2,1)S(1)}, u32[]{:S(2)}, u32[]{:S(2)}) collective-permute-start(bf16[256,1024]{1,0:T(8,128)(2,1)S(1)} %get-tuple-element.109), channel_id=1, source_target_pairs={{0,2},{2,4},{4,6},{6,7},{7,5},{5,3},{3,1},{1,0},{8,10},{10,12},{12... | collective-permute-start | bytes 1572872 | tf_op jit(solution)/shard_map/ppermute | solution.py:50
  178.1 22.1 %collective-permute-start.24 = (bf16[256,1024]{1,0:T(8,128)(2,1)S(1)}, bf16[256,1024]{1,0:T(8,128)(2,1)S(1)}, u32[]{:S(2)}, u32[]{:S(2)}) collective-permute-start(bf16[256,1024]{1,0:T(8,128)(2,1)S(1)} %get-tuple-element.110), channel_id=1, source_target_pairs={{0,1},{2,0},{4,2},{6,4},{7,6},{5,7},{3,5},{1,3},{8,9},{10,8},{12,1... | collective-permute-start | bytes 1572872 | tf_op jit(solution)/shard_map/ppermute | solution.py:51
  190.0 14.2 %copy-start.10 = (bf16[2,2048,384]{1,2,0:T(8,128)(2,1)S(1)}, bf16[2,2048,384]{1,2,0:T(8,128)(2,1)}, u32[]{:S(2)}) copy-start(bf16[2,2048,384]{1,2,0:T(8,128)(2,1)} %get-tuple-element.145) | copy-start | bytes 9437188
  190.0 14.2 %copy-start.11 = (bf16[2,2048,384]{1,2,0:T(8,128)(2,1)S(1)}, bf16[2,2048,384]{1,2,0:T(8,128)(2,1)}, u32[]{:S(2)}) copy-start(bf16[2,2048,384]{1,2,0:T(8,128)(2,1)} %get-tuple-element.146) | copy-start | bytes 9437188
  192.1 20.8 %collective-permute-start.18 = (bf16[256,1024]{1,0:T(8,128)(2,1)S(1)}, bf16[256,1024]{1,0:T(8,128)(2,1)S(1)}, u32[]{:S(2)}, u32[]{:S(2)}) collective-permute-start(bf16[256,1024]{1,0:T(8,128)(2,1)S(1)} %get-tuple-element.98), channel_id=1, source_target_pairs={{0,2},{2,4},{4,6},{6,7},{7,5},{5,3},{3,1},{1,0},{8,10},{10,12},{12... | collective-permute-start | bytes 1572872 | tf_op jit(solution)/shard_map/ppermute | solution.py:50
  192.9 20.0 %collective-permute-start.19 = (bf16[256,1024]{1,0:T(8,128)(2,1)S(1)}, bf16[256,1024]{1,0:T(8,128)(2,1)S(1)}, u32[]{:S(2)}, u32[]{:S(2)}) collective-permute-start(bf16[256,1024]{1,0:T(8,128)(2,1)S(1)} %get-tuple-element.99), channel_id=1, source_target_pairs={{0,1},{2,0},{4,2},{6,4},{7,6},{5,7},{3,5},{1,3},{8,9},{10,8},{12,1... | collective-permute-start | bytes 1572872 | tf_op jit(solution)/shard_map/ppermute | solution.py:51
  202.1 16.7 %collective-permute-start.25 = (bf16[256,1024]{1,0:T(8,128)(2,1)S(1)}, bf16[256,1024]{1,0:T(8,128)(2,1)S(1)}, u32[]{:S(2)}, u32[]{:S(2)}) collective-permute-start(bf16[256,1024]{1,0:T(8,128)(2,1)S(1)} %get-tuple-element.113), channel_id=1, source_target_pairs={{0,2},{2,4},{4,6},{6,7},{7,5},{5,3},{3,1},{1,0},{8,10},{10,12},{12... | collective-permute-start | bytes 1572872 | tf_op jit(solution)/shard_map/ppermute | solution.py:50
  202.9 15.9 %collective-permute-start.26 = (bf16[256,1024]{1,0:T(8,128)(2,1)S(1)}, bf16[256,1024]{1,0:T(8,128)(2,1)S(1)}, u32[]{:S(2)}, u32[]{:S(2)}) collective-permute-start(bf16[256,1024]{1,0:T(8,128)(2,1)S(1)} %get-tuple-element.114), channel_id=1, source_target_pairs={{0,1},{2,0},{4,2},{6,4},{7,6},{5,7},{3,5},{1,3},{8,9},{10,8},{12,1... | collective-permute-start | bytes 1572872 | tf_op jit(solution)/shard_map/ppermute | solution.py:51
  212.9 9.0 %copy-start.1 = (bf16[256,1024]{1,0:T(8,128)(2,1)}, bf16[256,1024]{1,0:T(8,128)(2,1)S(1)}, u32[]{:S(2)}) copy-start(bf16[256,1024]{1,0:T(8,128)(2,1)S(1)} %collective-permute-done.19) | copy-start | bytes 1572868
  215.3 11.7 %collective-permute-start.20 = (bf16[256,1024]{1,0:T(8,128)(2,1)}, bf16[256,1024]{1,0:T(8,128)(2,1)}, u32[]{:S(2)}, u32[]{:S(2)}) collective-permute-start(bf16[256,1024]{1,0:T(8,128)(2,1)} %add_convert_fusion.1), channel_id=1, source_target_pairs={{0,2},{2,4},{4,6},{6,7},{7,5},{5,3},{3,1},{1,0},{8,10},{10,12},{12... | collective-permute-start | bytes 1572872 | tf_op jit(solution)/shard_map/ppermute | solution.py:46
  218.8 3.1 %copy-start.2 = (bf16[256,1024]{1,0:T(8,128)(2,1)}, bf16[256,1024]{1,0:T(8,128)(2,1)S(1)}, u32[]{:S(2)}) copy-start(bf16[256,1024]{1,0:T(8,128)(2,1)S(1)} %collective-permute-done.26) | copy-start | bytes 1572868
  221.2 11.4 %collective-permute-start.27 = (bf16[256,1024]{1,0:T(8,128)(2,1)}, bf16[256,1024]{1,0:T(8,128)(2,1)}, u32[]{:S(2)}, u32[]{:S(2)}) collective-permute-start(bf16[256,1024]{1,0:T(8,128)(2,1)} %fusion.36), channel_id=1, source_target_pairs={{0,2},{2,4},{4,6},{6,7},{7,5},{5,3},{3,1},{1,0},{8,10},{10,12},{12... | collective-permute-start | bytes 1572872 | tf_op jit(solution)/shard_map/ppermute | solution.py:46
  223.5 9.1 %copy-start.3 = (bf16[256,1024]{1,0:T(8,128)(2,1)S(1)}, bf16[256,1024]{1,0:T(8,128)(2,1)}, u32[]{:S(2)}) copy-start(bf16[256,1024]{1,0:T(8,128)(2,1)} %copy-done.2) | copy-start | bytes 1572868

commit v13 on v11

--- a/solution.py
+++ b/solution.py
@@ -238,7 +238,8 @@
     mixed = reduce_scatter(mixed_part).astype(jnp.bfloat16)
     input_grad = reduce_scatter(input_part).astype(jnp.bfloat16)
 
-    peers = [shifted(down_weight, "rep", 1 << bit_index) for bit_index in range(ROUNDS)]
+    down_send, _ = lax.optimization_barrier((down_weight, group_cot))
+    peers = [shifted(down_send, "rep", 1 << bit_index) for bit_index in range(ROUNDS)]
     peer_down = peers[0]
     for bit_index in range(1, ROUNDS):
         peer_down = jnp.where(round_k[0] == bit_index, peers[bit_index], peer_down)

time: 223 us -> 226 us (1.013)
    unnamed x54 -> x46, local copies, waits for them, and re-layouts: 8.66 us -> 8.53 us
  transfers between devices with their start and end apart: 30 -> 30, of which waited for: 17 -> 20; matrix products, arithmetic and copies ran while one was open for 43% -> 39% of each run, Pallas kernels for 0% -> 0%
where the time goes in v13:
time: 226 us; the launch traced here: 225 us
  waiting for transfers between devices  89.2 us (39%)
  matrix products  66.3 us (29%)
  starting transfers between devices  31.7 us (14%)
  other arithmetic  20 us (9%)
  local copies, waits for them, and re-layouts  16.4 us (7%)
    ppermute x12, waiting for transfers between devices, paired_shift(): ahead_value = lax.ppermute(ahead_value, axis, ring_pairs(ring, 1))  64.2 us
    ppermute x12, starting transfers between devices, paired_shift(): ahead_value = lax.ppermute(ahead_value, axis, ring_pairs(ring, 1))  16.3 us
    dot_general x1, matrix products, chunk_pass(): jnp.einsum('eth,edh->etd', joint_cot, joint_matrix, preferred_element_typ...  14.7 us
    ppermute x4, waiting for transfers between devices, paired_shift(): return (lax.ppermute(ahead_value, axis, ring_pairs(ring, 1)), None)  12.9 us
    convert_element_type x6, other arithmetic, to_wire(): return value.astype(wire_dtype)  12.6 us
    ppermute x12, waiting for transfers between devices, paired_shift(): behind_value = lax.ppermute(behind_value, axis, ring_pairs(ring, -1))  12.2 us
    dot_general x1, matrix products, chunk_pass(): jnp.einsum('eth,ehd->etd', hidden, down_matrix, preferred_element_type=jn...  11.5 us
    dot_general x1, matrix products, chunk_pass(): jnp.einsum('eth,etd->ehd', hidden, slot_cot, preferred_element_type=jnp.f...  11.1 us
  transfers between devices with their start and end apart: 30, of which 20 were waited for; matrix products, arithmetic and copies ran while one was open for 39% of the time, Pallas kernels for 0%

profile of v13, /device:TPU:0, one launch (start us, length us, event | category | flops | bytes accessed | tf_op | source)
XLA Modules:
  0.0 225.1 jit_solution(9892930907365144287)
XLA Ops:
  0.6 0.7 convert_element_type.128
  1.4 0.7 select_reduce_fusion
  2.4 1.1 maximum_bitcast_fusion
  3.5 3.1 %collective-permute-start = (bf16[1,264,1024]{2,1,0:T(8,128)(2,1)S(1)}, bf16[1,264,1024]{2,1,0:T(8,128)(2,1)S(1)}, u32[]{:S(2)}, u32[]{:S(2)}) collective-permute-start(bf16[1,264,1024]{2,1,0:T(8,128)(2,1)S(1)} %maximum_bitcast_fusion), channel_id=1, source_target_pairs={{0,2},{2,4},{4,6},{6,7},{7,5},{5,3},{3,1},{1,0},{8,10},{10,12},{12... | collective-permute-start | bytes 1622024 | tf_op jit(solution)/shard_map/ppermute | solution.py:50
  6.5 12.2 %collective-permute-done = bf16[1,264,1024]{2,1,0:T(8,128)(2,1)S(1)} collective-permute-done((bf16[1,264,1024]{2,1,0:T(8,128)(2,1)S(1)}, bf16[1,264,1024]{2,1,0:T(8,128)(2,1)S(1)}, u32[]{:S(2)}, u32[]{:S(2)}) %collective-permute-start) | collective-permute-done | bytes 540704 | tf_op jit(solution)/shard_map/ppermute | solution.py:50
  18.7 1.5 collective-permute-done.1
  20.3 1.6 collective-permute-start.2
  22.3 10.8 %collective-permute-done.2 = bf16[1,264,1024]{2,1,0:T(8,128)(2,1)S(1)} collective-permute-done((bf16[1,264,1024]{2,1,0:T(8,128)(2,1)S(1)}, bf16[1,264,1024]{2,1,0:T(8,128)(2,1)S(1)}, u32[]{:S(2)}, u32[]{:S(2)}) %collective-permute-start.2) | collective-permute-done | bytes 540704 | tf_op jit(solution)/shard_map/ppermute | solution.py:50
  33.1 1.3 collective-permute-done.3
  34.4 1.6 collective-permute-start.4
  36.4 9.7 %collective-permute-done.4 = bf16[1,264,1024]{2,1,0:T(8,128)(2,1)} collective-permute-done((bf16[1,264,1024]{2,1,0:T(8,128)(2,1)S(1)}, bf16[1,264,1024]{2,1,0:T(8,128)(2,1)}, u32[]{:S(2)}, u32[]{:S(2)}) %collective-permute-start.4) | collective-permute-done | bytes 540704 | tf_op jit(solution)/shard_map/ppermute | solution.py:50
  46.1 1.2 collective-permute-done.5
  47.3 1.5 collective-permute-start.6
  48.8 9.4 %collective-permute-done.6 = bf16[1,264,1024]{2,1,0:T(8,128)(2,1)} collective-permute-done((bf16[1,264,1024]{2,1,0:T(8,128)(2,1)}, bf16[1,264,1024]{2,1,0:T(8,128)(2,1)}, u32[]{:S(2)}, u32[]{:S(2)}) %collective-permute-start.6) | collective-permute-done | bytes 540704 | tf_op jit(solution)/shard_map/ppermute | solution.py:46
  58.2 1.1 constant_dynamic-update-slice_fusion.7
  59.2 1.1 constant_dynamic-update-slice_fusion.6
  60.6 0.6 slice.104
  61.7 1.5 collective-permute-start.7
  63.7 3.7 %fusion.42 = f32[2048,2,384]{0,2,1:T(8,128)S(1)} fusion(bf16[2048,1024,1]{1,0,2:T(8,128)(2,1)S(1)} %bitcast.98, bf16[1,2,1024,384]{3,2,1,0:T(8,128)(2,1)S(1)} %copy-done.7), kind=kOutput, calls=%fused_computation.91 | convolution fusion | flops 3221225472 | bytes 12058624 | tf_op jit(solution)/shard_map/td,edh->eth/dot_general | solution.py:170
  67.4 5.1 %collective-permute-done.7 = bf16[256,1024]{1,0:T(8,128)(2,1)S(1)} collective-permute-done((bf16[256,1024]{1,0:T(8,128)(2,1)S(1)}, bf16[256,1024]{1,0:T(8,128)(2,1)S(1)}, u32[]{:S(2)}, u32[]{:S(2)}) %collective-permute-start.7) | collective-permute-done | bytes 524320 | tf_op jit(solution)/shard_map/ppermute | solution.py:50
  72.5 1.5 collective-permute-done.8
  74.0 1.6 collective-permute-start.9
  76.1 6.9 %fusion.4 = (bf16[2,2048,384]{1,2,0:T(8,128)(2,1)}, f32[2048,2,384]{0,2,1:T(8,128)}) fusion(f32[2048,2,384]{0,2,1:T(8,128)S(1)} %fusion.42, bf16[2048,1024,1]{1,0,2:T(8,128)(2,1)S(1)} %bitcast.99, bf16[1,2,1024,384]{3,2,1,0:T(8,128)(2,1)S(1)} %copy-done.9), kind=kOutput, calls=%fused_computation.9 | convolution fusion | flops 3230662656 | bytes 21495808 | tf_op jit(solution)/shard_map/td,edh->eth/dot_general | solution.py:173
  83.5 2.1 collective-permute-done.9
  85.5 2.3 %collective-permute-done.10 = bf16[256,1024]{1,0:T(8,128)(2,1)S(1)} collective-permute-done((bf16[256,1024]{1,0:T(8,128)(2,1)S(1)}, bf16[256,1024]{1,0:T(8,128)(2,1)S(1)}, u32[]{:S(2)}, u32[]{:S(2)}) %collective-permute-start.10) | collective-permute-done | bytes 524320 | tf_op jit(solution)/shard_map/ppermute | solution.py:51
  87.8 1.9 collective-permute-start.11
  90.3 11.2 %collective-permute-done.11 = bf16[256,1024]{1,0:T(8,128)(2,1)} collective-permute-done((bf16[256,1024]{1,0:T(8,128)(2,1)}, bf16[256,1024]{1,0:T(8,128)(2,1)}, u32[]{:S(2)}, u32[]{:S(2)}) %collective-permute-start.11) | collective-permute-done | bytes 524320 | tf_op jit(solution)/shard_map/ppermute | solution.py:50
  101.5 2.5 %collective-permute-start.13 = (bf16[256,1024]{1,0:T(8,128)(2,1)}, bf16[256,1024]{1,0:T(8,128)(2,1)S(1)}, u32[]{:S(2)}, u32[]{:S(2)}) collective-permute-start(bf16[256,1024]{1,0:T(8,128)(2,1)} %collective-permute-done.11), channel_id=1, source_target_pairs={{0,2},{2,4},{4,6},{6,7},{7,5},{5,3},{3,1},{1,0},{8,10},{10,12},{12... | collective-permute-start | bytes 1572872 | tf_op jit(solution)/shard_map/ppermute | solution.py:46
  104.0 11.5 %multiply_reduce_fusion = f32[2048,1024]{1,0:T(8,128)} fusion(f32[2,2048]{1,0:T(2,128)S(1)} %bitcast_convert_fusion, bf16[2,2048,384]{1,2,0:T(8,128)(2,1)} %get-tuple-element.166, bf16[1,2,384,1024]{3,2,1,0:T(8,128)(2,1)} %param.16), kind=kOutput, calls=%fused_computation.1 | convolution fusion | flops 3231711232 | bytes 13123584 | tf_op jit(solution)/shard_map/eth,ehd->etd/dot_general | solution.py:180
  115.5 1.1 constant_dynamic-update-slice_fusion.14
  116.6 1.1 constant_dynamic-update-slice_fusion.13
  117.8 1.1 constant_dynamic-update-slice_fusion.8
  118.9 3.2 %fusion.45 = (bf16[256,1024]{1,0:T(8,128)(2,1)S(1)}, bf16[256,1024]{1,0:T(8,128)(2,1)S(1)}) fusion(f32[2048,1024]{1,0:T(8,128)} %multiply_reduce_fusion), kind=kLoop, calls=%fused_computation.95 | loop fusion | bytes 2097152 | tf_op jit(solution)/shard_map/slice | solution.py:83
  122.1 0.6 collective-permute-start.14
  122.8 1.5 collective-permute-start.15
  124.2 10.7 %fusion.7 = (bf16[2,2048,384]{1,2,0:T(8,128)(2,1)}, bf16[2,2048,384]{1,2,0:T(8,128)(2,1)}) fusion(f32[2048,2,384]{0,2,1:T(8,128)} %get-tuple-element.167, f32[2048,2,384]{0,2,1:T(8,128)} %copy-done.11, bf16[1,2,384,1024]{3,2,1,0:T(8,128)(2,1)} %param.16, bf16[2048,1024]{1,0:T(8,128)(2,1)S(1)} %constant_dynamic-update-slice_fusion.8, ...), kind=kOutput, calls=%fused_computation.12 | convolution fusion | flops 3245867008 | bytes 24649728 | tf_op jit(solution)/shard_map/etd,ehd->eth/dot_general | solution.py:185
  134.9 14.7 %reduce-precision_reduce_fusion = f32[2048,1024]{1,0:T(8,128)} fusion(bf16[2,2048,384]{1,2,0:T(8,128)(2,1)} %get-tuple-element.148, bf16[2,2048,384]{1,2,0:T(8,128)(2,1)} %get-tuple-element.147, bf16[2,1024,384]{2,1,0:T(8,128)(2,1)S(1)} %bitcast.105, bf16[2,1024,384]{2,1,0:T(8,128)(2,1)S(1)} %bitcast.104), kind=kOutput, calls=%fused_computation | convolution fusion | flops 6467616768 | bytes 17825792 | tf_op jit(solution)/shard_map/eth,edh->etd/dot_general | solution.py:202
  149.7 1.7 fusion.44
  152.0 1.5 collective-permute-start.22
  153.5 2.0 add_convert_fusion.4
  156.1 1.5 collective-permute-start.17
  158.2 1.6 collective-permute-start.28
  159.8 0.8 collective-permute-done.21
  161.2 1.9 fusion.32
  163.5 2.7 %collective-permute-done.16 = bf16[256,1024]{1,0:T(8,128)(2,1)S(1)} collective-permute-done((bf16[256,1024]{1,0:T(8,128)(2,1)S(1)}, bf16[256,1024]{1,0:T(8,128)(2,1)S(1)}, u32[]{:S(2)}, u32[]{:S(2)}) %collective-permute-start.16) | collective-permute-done | bytes 524320 | tf_op jit(solution)/shard_map/ppermute | solution.py:50
  166.8 2.7 %add_convert_fusion.2 = (bf16[256,1024]{1,0:T(8,128)(2,1)}, bf16[256,1024]{1,0:T(8,128)(2,1)S(1)}) fusion(f32[2048,1024]{1,0:T(8,128)} %multiply_reduce_fusion, bf16[256,1024]{1,0:T(8,128)(2,1)S(1)} %collective-permute-done.17, bf16[256,1024]{1,0:T(8,128)(2,1)S(1)} %collective-permute-done.16), kind=kLoop, calls=%fused_computation.60 | loop fusion | flops 1572864 | bytes 4194304 | tf_op jit(solution)/shard_map/convert_element_type | solution.py:86
  169.5 1.5 collective-permute-start.18
  170.9 7.7 %convert_bitcast_fusion = bf16[2,1024,768]{1,2,0:T(8,128)(2,1)S(1)} fusion(bf16[2048,1024,1]{1,0,2:T(8,128)(2,1)S(1)} %bitcast.100, bf16[2,2048,384]{1,2,0:T(8,128)(2,1)S(1)} %copy-done.13, bf16[2,2048,384]{1,2,0:T(8,128)(2,1)S(1)} %copy-done.12), kind=kOutput, calls=%fused_computation.39 | convolution fusion | flops 6456606720 | bytes 13631488 | tf_op jit(solution)/shard_map/td,eth->edh/dot_general | solution.py:196
  178.7 0.8 collective-permute-start.19
  179.4 2.8 %fusion.30 = (bf16[256,1024]{1,0:T(8,128)(2,1)}, bf16[256,1024]{1,0:T(8,128)(2,1)}) fusion(f32[2048,1024]{1,0:T(8,128)} %reduce-precision_reduce_fusion, bf16[256,1024]{1,0:T(8,128)(2,1)S(1)} %collective-permute-done.24, bf16[256,1024]{1,0:T(8,128)(2,1)S(1)} %collective-permute-done.23), kind=kLoop, calls=%fused_computation.48 | loop fusion | flops 1572864 | bytes 4194304 | tf_op jit(solution)/shard_map/convert_element_type | solution.py:86
  182.3 1.3 collective-permute-start.25
  183.6 5.4 %collective-permute-done.18 = bf16[256,1024]{1,0:T(8,128)(2,1)S(1)} collective-permute-done((bf16[256,1024]{1,0:T(8,128)(2,1)S(1)}, bf16[256,1024]{1,0:T(8,128)(2,1)S(1)}, u32[]{:S(2)}, u32[]{:S(2)}) %collective-permute-start.18) | collective-permute-done | bytes 524320 | tf_op jit(solution)/shard_map/ppermute | solution.py:50
  189.1 1.6 collective-permute-start.26
  191.0 1.6 copy.50
  192.6 1.6 copy.51
  194.1 1.7 add_convert_fusion.1
  196.2 4.1 %collective-permute-done.25 = bf16[256,1024]{1,0:T(8,128)(2,1)} collective-permute-done((bf16[256,1024]{1,0:T(8,128)(2,1)}, bf16[256,1024]{1,0:T(8,128)(2,1)}, u32[]{:S(2)}, u32[]{:S(2)}) %collective-permute-start.25) | collective-permute-done | bytes 524320 | tf_op jit(solution)/shard_map/ppermute | solution.py:50
  200.4 3.2 %collective-permute-done.26 = bf16[256,1024]{1,0:T(8,128)(2,1)} collective-permute-done((bf16[256,1024]{1,0:T(8,128)(2,1)}, bf16[256,1024]{1,0:T(8,128)(2,1)}, u32[]{:S(2)}, u32[]{:S(2)}) %collective-permute-start.26) | collective-permute-done | bytes 524320 | tf_op jit(solution)/shard_map/ppermute | solution.py:51
  203.6 1.5 fusion.29
  205.1 0.6 collective-permute-start.27
  205.8 11.1 %fusion.37 = (f32[1,2,384,1024]{3,2,1,0:T(8,128)}, bf16[1,2,384,1024]{3,2,1,0:T(8,128)(2,1)}, f32[1,2,384,1024]{3,2,1,0:T(8,128)}) fusion(f32[1,2,384,1024]{3,2,1,0:T(8,128)} %param.18, f32[1,2,384,1024]{3,2,1,0:T(8,128)} %param.17, bf16[1,2,384,1024]{3,2,1,0:T(8,128)(2,1)} %collective-permute-done.28, ...), kind=kOutput, calls=%fused_computation.65 | convolution fusion | flops 3241934848 | bytes 26222592 | tf_op jit(solution)/shard_map/eth,etd->ehd/dot_general | solution.py:192
  216.9 2.4 %add_convert_fusion = bf16[256,1024]{1,0:T(8,128)(2,1)} fusion(bf16[256,1024]{1,0:T(8,128)(2,1)S(1)} %collective-permute-done.20, bf16[256,1024]{1,0:T(8,128)(2,1)} %collective-permute-done.19, f32[2048,1024]{1,0:T(8,128)} %multiply_reduce_fusion), kind=kLoop, calls=%fused_computation.58 | loop fusion | flops 1310720 | bytes 2621440 | tf_op jit(solution)/shard_map/convert_element_type | solution.py:238
  219.3 3.5 %collective-permute-done.27 = bf16[256,1024]{1,0:T(8,128)(2,1)S(1)} collective-permute-done((bf16[256,1024]{1,0:T(8,128)(2,1)S(1)}, bf16[256,1024]{1,0:T(8,128)(2,1)S(1)}, u32[]{:S(2)}, u32[]{:S(2)}) %collective-permute-start.27) | collective-permute-done | bytes 524320 | tf_op jit(solution)/shard_map/ppermute | solution.py:46
  222.8 2.4 %fusion.35 = bf16[256,1024]{1,0:T(8,128)(2,1)} fusion(f32[2048,1024]{1,0:T(8,128)} %reduce-precision_reduce_fusion, bf16[256,1024]{1,0:T(8,128)(2,1)S(1)} %collective-permute-done.27, bf16[256,1024]{1,0:T(8,128)(2,1)} %collective-permute-done.26), kind=kLoop, calls=%fused_computation.57 | loop fusion | flops 1310720 | bytes 2621440 | tf_op jit(solution)/shard_map/convert_element_type | solution.py:239
  (75 shorter events, 7.5 us)
Async XLA Ops:
  0.6 59.8 %copy-start.2 = (bf16[256,1024]{1,0:T(8,128)(2,1)S(1)}, bf16[256,1024]{1,0:T(8,128)(2,1)}, u32[]{:S(2)}) copy-start(bf16[256,1024]{1,0:T(8,128)(2,1)} %param.10) | copy-start | bytes 1572868
  3.5 15.3 %collective-permute-start = (bf16[1,264,1024]{2,1,0:T(8,128)(2,1)S(1)}, bf16[1,264,1024]{2,1,0:T(8,128)(2,1)S(1)}, u32[]{:S(2)}, u32[]{:S(2)}) collective-permute-start(bf16[1,264,1024]{2,1,0:T(8,128)(2,1)S(1)} %maximum_bitcast_fusion), channel_id=1, source_target_pairs={{0,2},{2,4},{4,6},{6,7},{7,5},{5,3},{3,1},{1,0},{8,10},{10,12},{12... | collective-permute-start | bytes 1622024 | tf_op jit(solution)/shard_map/ppermute | solution.py:50
  6.5 13.7 %collective-permute-start.1 = (bf16[1,264,1024]{2,1,0:T(8,128)(2,1)S(1)}, bf16[1,264,1024]{2,1,0:T(8,128)(2,1)S(1)}, u32[]{:S(2)}, u32[]{:S(2)}) collective-permute-start(bf16[1,264,1024]{2,1,0:T(8,128)(2,1)S(1)} %maximum_bitcast_fusion), channel_id=1, source_target_pairs={{0,1},{2,0},{4,2},{6,4},{7,6},{5,7},{3,5},{1,3},{8,9},{10,8},{12,1... | collective-permute-start | bytes 1622024 | tf_op jit(solution)/shard_map/ppermute | solution.py:51
  20.3 12.8 %collective-permute-start.2 = (bf16[1,264,1024]{2,1,0:T(8,128)(2,1)S(1)}, bf16[1,264,1024]{2,1,0:T(8,128)(2,1)S(1)}, u32[]{:S(2)}, u32[]{:S(2)}) collective-permute-start(bf16[1,264,1024]{2,1,0:T(8,128)(2,1)S(1)} %collective-permute-done), channel_id=1, source_target_pairs={{0,2},{2,4},{4,6},{6,7},{7,5},{5,3},{3,1},{1,0},{8,10},{10,12},{12... | collective-permute-start | bytes 1622024 | tf_op jit(solution)/shard_map/ppermute | solution.py:50
  21.8 12.5 %collective-permute-start.3 = (bf16[1,264,1024]{2,1,0:T(8,128)(2,1)S(1)}, bf16[1,264,1024]{2,1,0:T(8,128)(2,1)S(1)}, u32[]{:S(2)}, u32[]{:S(2)}) collective-permute-start(bf16[1,264,1024]{2,1,0:T(8,128)(2,1)S(1)} %collective-permute-done.1), channel_id=1, source_target_pairs={{0,1},{2,0},{4,2},{6,4},{7,6},{5,7},{3,5},{1,3},{8,9},{10,8},{12,1... | collective-permute-start | bytes 1622024 | tf_op jit(solution)/shard_map/ppermute | solution.py:51
  34.4 11.7 %collective-permute-start.4 = (bf16[1,264,1024]{2,1,0:T(8,128)(2,1)S(1)}, bf16[1,264,1024]{2,1,0:T(8,128)(2,1)}, u32[]{:S(2)}, u32[]{:S(2)}) collective-permute-start(bf16[1,264,1024]{2,1,0:T(8,128)(2,1)S(1)} %collective-permute-done.2), channel_id=1, source_target_pairs={{0,2},{2,4},{4,6},{6,7},{7,5},{5,3},{3,1},{1,0},{8,10},{10,12},{12... | collective-permute-start | bytes 1622024 | tf_op jit(solution)/shard_map/ppermute | solution.py:50
  36.0 11.3 %collective-permute-start.5 = (bf16[1,264,1024]{2,1,0:T(8,128)(2,1)S(1)}, bf16[1,264,1024]{2,1,0:T(8,128)(2,1)S(1)}, u32[]{:S(2)}, u32[]{:S(2)}) collective-permute-start(bf16[1,264,1024]{2,1,0:T(8,128)(2,1)S(1)} %collective-permute-done.3), channel_id=1, source_target_pairs={{0,1},{2,0},{4,2},{6,4},{7,6},{5,7},{3,5},{1,3},{8,9},{10,8},{12,1... | collective-permute-start | bytes 1622024 | tf_op jit(solution)/shard_map/ppermute | solution.py:51
  47.3 10.8 %collective-permute-start.6 = (bf16[1,264,1024]{2,1,0:T(8,128)(2,1)}, bf16[1,264,1024]{2,1,0:T(8,128)(2,1)}, u32[]{:S(2)}, u32[]{:S(2)}) collective-permute-start(bf16[1,264,1024]{2,1,0:T(8,128)(2,1)} %collective-permute-done.4), channel_id=1, source_target_pairs={{0,2},{2,4},{4,6},{6,7},{7,5},{5,3},{3,1},{1,0},{8,10},{10,12},{12... | collective-permute-start | bytes 1622024 | tf_op jit(solution)/shard_map/ppermute | solution.py:46
  60.6 1.0 copy-start.3
  60.6 3.1 %copy-start.7 = (bf16[1,2,1024,384]{3,2,1,0:T(8,128)(2,1)S(1)}, bf16[1,2,1024,384]{3,2,1,0:T(8,128)(2,1)}, u32[]{:S(2)}) copy-start(bf16[1,2,1024,384]{3,2,1,0:T(8,128)(2,1)} %param.14) | copy-start | bytes 4718596
  61.7 14.4 %copy-start = (bf16[8,256,1024]{2,1,0:T(8,128)(2,1)}, bf16[8,256,1024]{2,1,0:T(8,128)(2,1)S(1)}, u32[]{:S(2)}) copy-start(bf16[8,256,1024]{2,1,0:T(8,128)(2,1)S(1)} %slice.104) | copy-start | bytes 12582916
  61.7 10.9 %collective-permute-start.7 = (bf16[256,1024]{1,0:T(8,128)(2,1)S(1)}, bf16[256,1024]{1,0:T(8,128)(2,1)S(1)}, u32[]{:S(2)}, u32[]{:S(2)}) collective-permute-start(bf16[256,1024]{1,0:T(8,128)(2,1)S(1)} %copy-done.3), channel_id=1, source_target_pairs={{0,2},{2,4},{4,6},{6,7},{7,5},{5,3},{3,1},{1,0},{8,10},{10,12},{12... | collective-permute-start | bytes 1572872 | tf_op jit(solution)/shard_map/ppermute | solution.py:50
  63.2 10.9 %collective-permute-start.8 = (bf16[256,1024]{1,0:T(8,128)(2,1)S(1)}, bf16[256,1024]{1,0:T(8,128)(2,1)S(1)}, u32[]{:S(2)}, u32[]{:S(2)}) collective-permute-start(bf16[256,1024]{1,0:T(8,128)(2,1)S(1)} %copy-done.3), channel_id=1, source_target_pairs={{0,1},{2,0},{4,2},{6,4},{7,6},{5,7},{3,5},{1,3},{8,9},{10,8},{12,1... | collective-permute-start | bytes 1572872 | tf_op jit(solution)/shard_map/ppermute | solution.py:51
  63.7 12.4 %copy-start.9 = (bf16[1,2,1024,384]{3,2,1,0:T(8,128)(2,1)S(1)}, bf16[1,2,1024,384]{3,2,1,0:T(8,128)(2,1)}, u32[]{:S(2)}) copy-start(bf16[1,2,1024,384]{3,2,1,0:T(8,128)(2,1)} %param.15) | copy-start | bytes 4718596
  67.4 15.5 %copy-start.11 = (f32[2048,2,384]{0,2,1:T(8,128)}, f32[2048,2,384]{0,2,1:T(8,128)S(1)}, u32[]{:S(2)}) copy-start(f32[2048,2,384]{0,2,1:T(8,128)S(1)} %fusion.42) | copy-start | bytes 18874372
  74.0 11.5 %collective-permute-start.9 = (bf16[256,1024]{1,0:T(8,128)(2,1)S(1)}, bf16[256,1024]{1,0:T(8,128)(2,1)}, u32[]{:S(2)}, u32[]{:S(2)}) collective-permute-start(bf16[256,1024]{1,0:T(8,128)(2,1)S(1)} %collective-permute-done.7), channel_id=1, source_target_pairs={{0,2},{2,4},{4,6},{6,7},{7,5},{5,3},{3,1},{1,0},{8,10},{10,12},{12... | collective-permute-start | bytes 1572872 | tf_op jit(solution)/shard_map/ppermute | solution.py:50
  75.6 12.2 %collective-permute-start.10 = (bf16[256,1024]{1,0:T(8,128)(2,1)S(1)}, bf16[256,1024]{1,0:T(8,128)(2,1)S(1)}, u32[]{:S(2)}, u32[]{:S(2)}) collective-permute-start(bf16[256,1024]{1,0:T(8,128)(2,1)S(1)} %collective-permute-done.8), channel_id=1, source_target_pairs={{0,1},{2,0},{4,2},{6,4},{7,6},{5,7},{3,5},{1,3},{8,9},{10,8},{12,1... | collective-permute-start | bytes 1572872 | tf_op jit(solution)/shard_map/ppermute | solution.py:51
  87.8 13.7 %collective-permute-start.11 = (bf16[256,1024]{1,0:T(8,128)(2,1)}, bf16[256,1024]{1,0:T(8,128)(2,1)}, u32[]{:S(2)}, u32[]{:S(2)}) collective-permute-start(bf16[256,1024]{1,0:T(8,128)(2,1)} %collective-permute-done.9), channel_id=1, source_target_pairs={{0,2},{2,4},{4,6},{6,7},{7,5},{5,3},{3,1},{1,0},{8,10},{10,12},{12... | collective-permute-start | bytes 1572872 | tf_op jit(solution)/shard_map/ppermute | solution.py:50
  89.7 11.8 %collective-permute-start.12 = (bf16[256,1024]{1,0:T(8,128)(2,1)S(1)}, bf16[256,1024]{1,0:T(8,128)(2,1)}, u32[]{:S(2)}, u32[]{:S(2)}) collective-permute-start(bf16[256,1024]{1,0:T(8,128)(2,1)S(1)} %collective-permute-done.10), channel_id=1, source_target_pairs={{0,1},{2,0},{4,2},{6,4},{7,6},{5,7},{3,5},{1,3},{8,9},{10,8},{12,1... | collective-permute-start | bytes 1572872 | tf_op jit(solution)/shard_map/ppermute | solution.py:51
  101.5 14.0 %collective-permute-start.13 = (bf16[256,1024]{1,0:T(8,128)(2,1)}, bf16[256,1024]{1,0:T(8,128)(2,1)S(1)}, u32[]{:S(2)}, u32[]{:S(2)}) collective-permute-start(bf16[256,1024]{1,0:T(8,128)(2,1)} %collective-permute-done.11), channel_id=1, source_target_pairs={{0,2},{2,4},{4,6},{6,7},{7,5},{5,3},{3,1},{1,0},{8,10},{10,12},{12... | collective-permute-start | bytes 1572872 | tf_op jit(solution)/shard_map/ppermute | solution.py:46
  118.9 16.0 %copy-start.5 = (bf16[2048,1024]{1,0:T(8,128)(2,1)}, bf16[2048,1024]{1,0:T(8,128)(2,1)S(1)}, u32[]{:S(2)}) copy-start(bf16[2048,1024]{1,0:T(8,128)(2,1)S(1)} %constant_dynamic-update-slice_fusion.8) | copy-start | bytes 12582916
  122.1 31.3 %collective-permute-start.14 = (bf16[256,1024]{1,0:T(8,128)(2,1)S(1)}, bf16[256,1024]{1,0:T(8,128)(2,1)S(1)}, u32[]{:S(2)}, u32[]{:S(2)}) collective-permute-start(bf16[256,1024]{1,0:T(8,128)(2,1)S(1)} %get-tuple-element.91), channel_id=1, source_target_pairs={{0,2},{2,4},{4,6},{6,7},{7,5},{5,3},{3,1},{1,0},{8,10},{10,12},{12... | collective-permute-start | bytes 1572872 | tf_op jit(solution)/shard_map/ppermute | solution.py:50
  122.8 30.7 %collective-permute-start.15 = (bf16[256,1024]{1,0:T(8,128)(2,1)S(1)}, bf16[256,1024]{1,0:T(8,128)(2,1)S(1)}, u32[]{:S(2)}, u32[]{:S(2)}) collective-permute-start(bf16[256,1024]{1,0:T(8,128)(2,1)S(1)} %get-tuple-element.92), channel_id=1, source_target_pairs={{0,1},{2,0},{4,2},{6,4},{7,6},{5,7},{3,5},{1,3},{8,9},{10,8},{12,1... | collective-permute-start | bytes 1572872 | tf_op jit(solution)/shard_map/ppermute | solution.py:51
  124.2 10.7 %copy-start.8 = (bf16[1,2,1024,384]{3,2,1,0:T(8,128)(2,1)S(1)}, bf16[1,2,1024,384]{3,2,1,0:T(8,128)(2,1)}, u32[]{:S(2)}) copy-start(bf16[1,2,1024,384]{3,2,1,0:T(8,128)(2,1)} %param.14) | copy-start | bytes 4718596
  124.2 10.7 %copy-start.10 = (bf16[1,2,1024,384]{3,2,1,0:T(8,128)(2,1)S(1)}, bf16[1,2,1024,384]{3,2,1,0:T(8,128)(2,1)}, u32[]{:S(2)}) copy-start(bf16[1,2,1024,384]{3,2,1,0:T(8,128)(2,1)} %param.15) | copy-start | bytes 4718596
  151.4 9.2 %collective-permute-start.21 = (bf16[256,1024]{1,0:T(8,128)(2,1)S(1)}, bf16[256,1024]{1,0:T(8,128)(2,1)S(1)}, u32[]{:S(2)}, u32[]{:S(2)}) collective-permute-start(bf16[256,1024]{1,0:T(8,128)(2,1)S(1)} %get-tuple-element.106), channel_id=1, source_target_pairs={{0,2},{2,4},{4,6},{6,7},{7,5},{5,3},{3,1},{1,0},{8,10},{10,12},{12... | collective-permute-start | bytes 1572872 | tf_op jit(solution)/shard_map/ppermute | solution.py:50
  152.0 9.2 %collective-permute-start.22 = (bf16[256,1024]{1,0:T(8,128)(2,1)S(1)}, bf16[256,1024]{1,0:T(8,128)(2,1)S(1)}, u32[]{:S(2)}, u32[]{:S(2)}) collective-permute-start(bf16[256,1024]{1,0:T(8,128)(2,1)S(1)} %get-tuple-element.107), channel_id=1, source_target_pairs={{0,1},{2,0},{4,2},{6,4},{7,6},{5,7},{3,5},{1,3},{8,9},{10,8},{12,1... | collective-permute-start | bytes 1572872 | tf_op jit(solution)/shard_map/ppermute | solution.py:51
  153.5 17.5 %copy-start.13 = (bf16[2,2048,384]{1,2,0:T(8,128)(2,1)S(1)}, bf16[2,2048,384]{1,2,0:T(8,128)(2,1)}, u32[]{:S(2)}) copy-start(bf16[2,2048,384]{1,2,0:T(8,128)(2,1)} %get-tuple-element.148) | copy-start | bytes 9437188
  155.5 10.7 %collective-permute-start.16 = (bf16[256,1024]{1,0:T(8,128)(2,1)S(1)}, bf16[256,1024]{1,0:T(8,128)(2,1)S(1)}, u32[]{:S(2)}, u32[]{:S(2)}) collective-permute-start(bf16[256,1024]{1,0:T(8,128)(2,1)S(1)} %get-tuple-element.95), channel_id=1, source_target_pairs={{0,2},{2,4},{4,6},{6,7},{7,5},{5,3},{3,1},{1,0},{8,10},{10,12},{12... | collective-permute-start | bytes 1572872 | tf_op jit(solution)/shard_map/ppermute | solution.py:50
  156.1 10.7 %collective-permute-start.17 = (bf16[256,1024]{1,0:T(8,128)(2,1)S(1)}, bf16[256,1024]{1,0:T(8,128)(2,1)S(1)}, u32[]{:S(2)}, u32[]{:S(2)}) collective-permute-start(bf16[256,1024]{1,0:T(8,128)(2,1)S(1)} %get-tuple-element.96), channel_id=1, source_target_pairs={{0,1},{2,0},{4,2},{6,4},{7,6},{5,7},{3,5},{1,3},{8,9},{10,8},{12,1... | collective-permute-start | bytes 1572872 | tf_op jit(solution)/shard_map/ppermute | solution.py:51
  158.2 12.7 %copy-start.1 = (bf16[8,256,1024]{2,1,0:T(8,128)(2,1)S(1)}, bf16[8,256,1024]{2,1,0:T(8,128)(2,1)}, u32[]{:S(2)}) copy-start(bf16[8,256,1024]{2,1,0:T(8,128)(2,1)} %copy-done) | copy-start | bytes 12582916
  158.2 12.7 %copy-start.12 = (bf16[2,2048,384]{1,2,0:T(8,128)(2,1)S(1)}, bf16[2,2048,384]{1,2,0:T(8,128)(2,1)}, u32[]{:S(2)}) copy-start(bf16[2,2048,384]{1,2,0:T(8,128)(2,1)} %get-tuple-element.147) | copy-start | bytes 9437188
  158.2 47.5 %collective-permute-start.28 = (bf16[1,2,384,1024]{3,2,1,0:T(8,128)(2,1)}, bf16[1,2,384,1024]{3,2,1,0:T(8,128)(2,1)}, u32[]{:S(2)}, u32[]{:S(2)}) collective-permute-start(bf16[1,2,384,1024]{3,2,1,0:T(8,128)(2,1)} %param.16), channel_id=1, source_target_pairs={{0,16},{8,24},{16,0},{24,8},{1,17},{9,25},{17,1},{25,9},{2,18},{10... | collective-permute-start | bytes 4718600 | tf_op jit(solution)/shard_map/ppermute | solution.py:21
  160.6 45.2 %collective-permute-start.29 = (bf16[1,2,384,1024]{3,2,1,0:T(8,128)(2,1)}, bf16[1,2,384,1024]{3,2,1,0:T(8,128)(2,1)}, u32[]{:S(2)}, u32[]{:S(2)}) collective-permute-start(bf16[1,2,384,1024]{3,2,1,0:T(8,128)(2,1)} %param.16), channel_id=1, source_target_pairs={{0,8},{8,16},{16,24},{24,0},{1,9},{9,17},{17,25},{25,1},{2,10},{10... | collective-permute-start | bytes 4718600 | tf_op jit(solution)/shard_map/ppermute | solution.py:21
  163.1 15.6 %collective-permute-start.23 = (bf16[256,1024]{1,0:T(8,128)(2,1)S(1)}, bf16[256,1024]{1,0:T(8,128)(2,1)S(1)}, u32[]{:S(2)}, u32[]{:S(2)}) collective-permute-start(bf16[256,1024]{1,0:T(8,128)(2,1)S(1)} %get-tuple-element.110), channel_id=1, source_target_pairs={{0,2},{2,4},{4,6},{6,7},{7,5},{5,3},{3,1},{1,0},{8,10},{10,12},{12... | collective-permute-start | bytes 1572872 | tf_op jit(solution)/shard_map/ppermute | solution.py:50
  166.2 13.2 %collective-permute-start.24 = (bf16[256,1024]{1,0:T(8,128)(2,1)S(1)}, bf16[256,1024]{1,0:T(8,128)(2,1)S(1)}, u32[]{:S(2)}, u32[]{:S(2)}) collective-permute-start(bf16[256,1024]{1,0:T(8,128)(2,1)S(1)} %get-tuple-element.111), channel_id=1, source_target_pairs={{0,1},{2,0},{4,2},{6,4},{7,6},{5,7},{3,5},{1,3},{8,9},{10,8},{12,1... | collective-permute-start | bytes 1572872 | tf_op jit(solution)/shard_map/ppermute | solution.py:51
  169.5 19.6 %collective-permute-start.18 = (bf16[256,1024]{1,0:T(8,128)(2,1)S(1)}, bf16[256,1024]{1,0:T(8,128)(2,1)S(1)}, u32[]{:S(2)}, u32[]{:S(2)}) collective-permute-start(bf16[256,1024]{1,0:T(8,128)(2,1)S(1)} %get-tuple-element.99), channel_id=1, source_target_pairs={{0,2},{2,4},{4,6},{6,7},{7,5},{5,3},{3,1},{1,0},{8,10},{10,12},{12... | collective-permute-start | bytes 1572872 | tf_op jit(solution)/shard_map/ppermute | solution.py:50
  178.7 15.4 %collective-permute-start.19 = (bf16[256,1024]{1,0:T(8,128)(2,1)}, bf16[256,1024]{1,0:T(8,128)(2,1)}, u32[]{:S(2)}, u32[]{:S(2)}) collective-permute-start(bf16[256,1024]{1,0:T(8,128)(2,1)} %get-tuple-element.100), channel_id=1, source_target_pairs={{0,1},{2,0},{4,2},{6,4},{7,6},{5,7},{3,5},{1,3},{8,9},{10,8},{12,1... | collective-permute-start | bytes 1572872 | tf_op jit(solution)/shard_map/ppermute | solution.py:51
  182.3 18.1 %collective-permute-start.25 = (bf16[256,1024]{1,0:T(8,128)(2,1)}, bf16[256,1024]{1,0:T(8,128)(2,1)}, u32[]{:S(2)}, u32[]{:S(2)}) collective-permute-start(bf16[256,1024]{1,0:T(8,128)(2,1)} %get-tuple-element.114), channel_id=1, source_target_pairs={{0,2},{2,4},{4,6},{6,7},{7,5},{5,3},{3,1},{1,0},{8,10},{10,12},{12... | collective-permute-start | bytes 1572872 | tf_op jit(solution)/shard_map/ppermute | solution.py:50
  189.1 1.9 copy-start.4
  189.1 14.6 %collective-permute-start.26 = (bf16[256,1024]{1,0:T(8,128)(2,1)}, bf16[256,1024]{1,0:T(8,128)(2,1)}, u32[]{:S(2)}, u32[]{:S(2)}) collective-permute-start(bf16[256,1024]{1,0:T(8,128)(2,1)} %get-tuple-element.115), channel_id=1, source_target_pairs={{0,1},{2,0},{4,2},{6,4},{7,6},{5,7},{3,5},{1,3},{8,9},{10,8},{12,1... | collective-permute-start | bytes 1572872 | tf_op jit(solution)/shard_map/ppermute | solution.py:51
  194.1 11.6 %copy-start.6 = (bf16[2048,1024]{1,0:T(8,128)(2,1)S(1)}, bf16[2048,1024]{1,0:T(8,128)(2,1)}, u32[]{:S(2)}) copy-start(bf16[2048,1024]{1,0:T(8,128)(2,1)} %copy-done.5) | copy-start | bytes 12582916
  195.8 21.1 %collective-permute-start.20 = (bf16[256,1024]{1,0:T(8,128)(2,1)S(1)}, bf16[256,1024]{1,0:T(8,128)(2,1)S(1)}, u32[]{:S(2)}, u32[]{:S(2)}) collective-permute-start(bf16[256,1024]{1,0:T(8,128)(2,1)S(1)} %add_convert_fusion.1), channel_id=1, source_target_pairs={{0,2},{2,4},{4,6},{6,7},{7,5},{5,3},{3,1},{1,0},{8,10},{10,12},{12... | collective-permute-start | bytes 1572872 | tf_op jit(solution)/shard_map/ppermute | solution.py:46
  205.1 17.6 %collective-permute-start.27 = (bf16[256,1024]{1,0:T(8,128)(2,1)S(1)}, bf16[256,1024]{1,0:T(8,128)(2,1)S(1)}, u32[]{:S(2)}, u32[]{:S(2)}) collective-permute-start(bf16[256,1024]{1,0:T(8,128)(2,1)S(1)} %fusion.29), channel_id=1, source_target_pairs={{0,2},{2,4},{4,6},{6,7},{7,5},{5,3},{3,1},{1,0},{8,10},{10,12},{12... | collective-permute-start | bytes 1572872 | tf_op jit(solution)/shard_map/ppermute | solution.py:46

commit v14 on v11

--- a/solution.py
+++ b/solution.py
@@ -152,7 +152,6 @@
         .reshape(devices_exp, -1)[:, : token_count * experts]
         .reshape(devices_exp * token_count, experts)
     )
-    _, cotangent = lax.optimization_barrier((gathered, cotangent))
     group_cot = gather(cotangent)
     local_weight = lax.dynamic_slice_in_dim(
         group_weight, my_exp * local_experts, local_experts, axis=1

time: 223 us -> 240 us (1.076)
  waiting for transfers between devices: 87.7 us -> 96.3 us
  matrix products: 64.6 us -> 70.3 us
  starting transfers between devices: 31.2 us -> 35.2 us
    ppermute x4, waiting for transfers between devices: 10.9 us -> 25.3 us  [paired_shift(): return (lax.ppermute(ahead_value, axis, ring_pairs(ring, 1)), None)]
    ppermute x12, waiting for transfers between devices: 62.9 us -> 56 us  [paired_shift(): ahead_value = lax.ppermute(ahead_value, axis, ring_pairs(ring, 1))]
    ppermute x12, starting transfers between devices: 14.5 us -> 19.4 us  [paired_shift(): ahead_value = lax.ppermute(ahead_value, axis, ring_pairs(ring, 1))]
    ppermute x12, starting transfers between devices: 10.6 us -> 7.76 us  [paired_shift(): behind_value = lax.ppermute(behind_value, axis, ring_pairs(ring, -1))]
    dot_general x1, matrix products: 3.72 us -> 6.16 us  [chunk_pass(): jnp.einsum('td,edh->eth', chunk_tokens, gate_matrix, preferred_element_ty...]
    unnamed x54 -> x58, local copies, waits for them, and re-layouts: 8.66 us -> 8.16 us
  transfers between devices with their start and end apart: 30 -> 30, of which waited for: 17 -> 20; matrix products, arithmetic and copies ran while one was open for 43% -> 43% of each run, Pallas kernels for 0% -> 0%
where the time goes in v14:
time: 240 us; the launch traced here: 239 us
  waiting for transfers between devices  96.3 us (40%)
  matrix products  70.3 us (29%)
  starting transfers between devices  35.2 us (15%)
  other arithmetic  20.3 us (8%)
  local copies, waits for them, and re-layouts  15.2 us (6%)
    ppermute x12, waiting for transfers between devices, paired_shift(): ahead_value = lax.ppermute(ahead_value, axis, ring_pairs(ring, 1))  56 us
    ppermute x4, waiting for transfers between devices, paired_shift(): return (lax.ppermute(ahead_value, axis, ring_pairs(ring, 1)), None)  25.3 us
    ppermute x12, starting transfers between devices, paired_shift(): ahead_value = lax.ppermute(ahead_value, axis, ring_pairs(ring, 1))  19.4 us
    ppermute x12, waiting for transfers between devices, paired_shift(): behind_value = lax.ppermute(behind_value, axis, ring_pairs(ring, -1))  15.1 us
    dot_general x1, matrix products, chunk_pass(): jnp.einsum('eth,edh->etd', joint_cot, joint_matrix, preferred_element_typ...  14.7 us
    convert_element_type x6, other arithmetic, to_wire(): return value.astype(wire_dtype)  12.8 us
    dot_general x1, matrix products, chunk_pass(): jnp.einsum('etd,ehd->eth', slot_cot, down_matrix, preferred_element_type=...  12 us
    dot_general x1, matrix products, chunk_pass(): jnp.einsum('eth,ehd->etd', hidden, down_matrix, preferred_element_type=jn...  11.5 us
  transfers between devices with their start and end apart: 30, of which 20 were waited for; matrix products, arithmetic and copies ran while one was open for 43% of the time, Pallas kernels for 0%

profile of v14, /device:TPU:0, one launch (start us, length us, event | category | flops | bytes accessed | tf_op | source)
XLA Modules:
  0.0 238.9 jit_solution(6437438805723275751)
XLA Ops:
  0.6 3.1 %collective-permute-start = (bf16[256,1024]{1,0:T(8,128)(2,1)}, bf16[256,1024]{1,0:T(8,128)(2,1)S(1)}, u32[]{:S(2)}, u32[]{:S(2)}) collective-permute-start(bf16[256,1024]{1,0:T(8,128)(2,1)} %param.11), channel_id=1, source_target_pairs={{0,2},{2,4},{4,6},{6,7},{7,5},{5,3},{3,1},{1,0},{8,10},{10,12},{12... | collective-permute-start | bytes 1572872 | tf_op jit(solution)/shard_map/ppermute | solution.py:50
  4.4 0.7 select_reduce_fusion
  5.4 1.1 maximum_bitcast_fusion
  6.5 2.1 collective-permute-start.7
  8.5 8.0 %collective-permute-done = bf16[256,1024]{1,0:T(8,128)(2,1)S(1)} collective-permute-done((bf16[256,1024]{1,0:T(8,128)(2,1)}, bf16[256,1024]{1,0:T(8,128)(2,1)S(1)}, u32[]{:S(2)}, u32[]{:S(2)}) %collective-permute-start) | collective-permute-done | bytes 524320 | tf_op jit(solution)/shard_map/ppermute | solution.py:50
  16.6 2.2 collective-permute-done.1
  18.8 1.6 collective-permute-start.2
  20.8 7.4 %collective-permute-done.7 = bf16[1,264,1024]{2,1,0:T(8,128)(2,1)S(1)} collective-permute-done((bf16[1,264,1024]{2,1,0:T(8,128)(2,1)S(1)}, bf16[1,264,1024]{2,1,0:T(8,128)(2,1)S(1)}, u32[]{:S(2)}, u32[]{:S(2)}) %collective-permute-start.7) | collective-permute-done | bytes 540704 | tf_op jit(solution)/shard_map/ppermute | solution.py:50
  28.2 2.2 collective-permute-done.8
  30.4 1.6 collective-permute-start.9
  32.4 7.0 %collective-permute-done.2 = bf16[256,1024]{1,0:T(8,128)(2,1)S(1)} collective-permute-done((bf16[256,1024]{1,0:T(8,128)(2,1)S(1)}, bf16[256,1024]{1,0:T(8,128)(2,1)S(1)}, u32[]{:S(2)}, u32[]{:S(2)}) %collective-permute-start.2) | collective-permute-done | bytes 524320 | tf_op jit(solution)/shard_map/ppermute | solution.py:50
  39.4 2.2 collective-permute-done.3
  41.6 1.6 collective-permute-start.4
  43.6 7.4 %collective-permute-done.9 = bf16[1,264,1024]{2,1,0:T(8,128)(2,1)S(1)} collective-permute-done((bf16[1,264,1024]{2,1,0:T(8,128)(2,1)S(1)}, bf16[1,264,1024]{2,1,0:T(8,128)(2,1)S(1)}, u32[]{:S(2)}, u32[]{:S(2)}) %collective-permute-start.9) | collective-permute-done | bytes 540704 | tf_op jit(solution)/shard_map/ppermute | solution.py:50
  51.0 2.2 collective-permute-done.10
  53.2 1.6 collective-permute-start.11
  55.2 7.1 %collective-permute-done.4 = bf16[256,1024]{1,0:T(8,128)(2,1)} collective-permute-done((bf16[256,1024]{1,0:T(8,128)(2,1)S(1)}, bf16[256,1024]{1,0:T(8,128)(2,1)}, u32[]{:S(2)}, u32[]{:S(2)}) %collective-permute-start.4) | collective-permute-done | bytes 524320 | tf_op jit(solution)/shard_map/ppermute | solution.py:50
  62.3 2.1 collective-permute-done.5
  64.4 1.6 collective-permute-start.6
  66.0 1.5 collective-permute-start.28
  67.5 6.3 %collective-permute-done.11 = bf16[1,264,1024]{2,1,0:T(8,128)(2,1)S(1)} collective-permute-done((bf16[1,264,1024]{2,1,0:T(8,128)(2,1)S(1)}, bf16[1,264,1024]{2,1,0:T(8,128)(2,1)S(1)}, u32[]{:S(2)}, u32[]{:S(2)}) %collective-permute-start.11) | collective-permute-done | bytes 540704 | tf_op jit(solution)/shard_map/ppermute | solution.py:50
  73.8 0.7 collective-permute-done.12
  74.5 1.6 collective-permute-start.13
  76.1 9.0 %collective-permute-done.6 = bf16[256,1024]{1,0:T(8,128)(2,1)} collective-permute-done((bf16[256,1024]{1,0:T(8,128)(2,1)}, bf16[256,1024]{1,0:T(8,128)(2,1)}, u32[]{:S(2)}, u32[]{:S(2)}) %collective-permute-start.6) | collective-permute-done | bytes 524320 | tf_op jit(solution)/shard_map/ppermute | solution.py:46
  85.2 1.1 constant_dynamic-update-slice_fusion.7
  86.2 1.1 constant_dynamic-update-slice_fusion.6
  87.3 1.1 constant_dynamic-update-slice_fusion.5
  88.4 1.1 constant_dynamic-update-slice_fusion.4
  89.7 6.1 %collective-permute-done.13 = bf16[1,264,1024]{2,1,0:T(8,128)(2,1)S(1)} collective-permute-done((bf16[1,264,1024]{2,1,0:T(8,128)(2,1)S(1)}, bf16[1,264,1024]{2,1,0:T(8,128)(2,1)S(1)}, u32[]{:S(2)}, u32[]{:S(2)}) %collective-permute-start.13) | collective-permute-done | bytes 540704 | tf_op jit(solution)/shard_map/ppermute | solution.py:46
  96.2 2.4 %slice.104 = bf16[8,256,1024]{2,1,0:T(8,128)(2,1)} slice(bf16[8,264,1024]{2,1,0:T(8,128)(2,1)S(1)} %constant_dynamic-update-slice_fusion.8), slice={[0:8], [0:256], [0:1024]} | slice | bytes 8388608 | tf_op jit(solution)/shard_map/slice | solution.py:149
  99.6 6.2 %fusion.42 = f32[2048,2,384]{0,2,1:T(8,128)S(1)} fusion(bf16[2048,1024,1]{1,0,2:T(8,128)(2,1)} %bitcast.98, bf16[1,2,1024,384]{3,2,1,0:T(8,128)(2,1)} %param.14), kind=kOutput, calls=%fused_computation.91 | convolution fusion | flops 3221225472 | bytes 12058624 | tf_op jit(solution)/shard_map/td,edh->eth/dot_general | solution.py:169
  105.8 6.9 %fusion.4 = (bf16[2,2048,384]{1,2,0:T(8,128)(2,1)}, f32[2048,2,384]{0,2,1:T(8,128)}) fusion(f32[2048,2,384]{0,2,1:T(8,128)S(1)} %fusion.42, bf16[2048,1024,1]{1,0,2:T(8,128)(2,1)S(1)} %bitcast.99, bf16[1,2,1024,384]{3,2,1,0:T(8,128)(2,1)S(1)} %copy-done.16), kind=kOutput, calls=%fused_computation.9 | convolution fusion | flops 3230662656 | bytes 21495808 | tf_op jit(solution)/shard_map/td,edh->eth/dot_general | solution.py:172
  112.7 11.5 %multiply_reduce_fusion = f32[2048,1024]{1,0:T(8,128)} fusion(f32[2,2048]{1,0:T(2,128)S(1)} %bitcast_convert_fusion, bf16[2,2048,384]{1,2,0:T(8,128)(2,1)} %get-tuple-element.162, bf16[1,2,384,1024]{3,2,1,0:T(8,128)(2,1)} %param.16), kind=kOutput, calls=%fused_computation.1 | convolution fusion | flops 3231711232 | bytes 13123584 | tf_op jit(solution)/shard_map/eth,ehd->etd/dot_general | solution.py:179
  124.3 1.7 fusion.45
  126.0 1.9 collective-permute-start.14
  128.0 12.0 %fusion.7 = (bf16[2,2048,384]{1,2,0:T(8,128)(2,1)}, bf16[2,2048,384]{1,2,0:T(8,128)(2,1)}) fusion(f32[2048,2,384]{0,2,1:T(8,128)} %get-tuple-element.163, f32[2048,2,384]{0,2,1:T(8,128)} %copy-done.17, bf16[1,2,384,1024]{3,2,1,0:T(8,128)(2,1)} %param.16, bf16[2048,1024]{1,0:T(8,128)(2,1)} %copy-done.14, bf16[2,2048]{1,0:T(2,128)(2,1)S(1)} %bitcast.102), kind=kOutput, calls=%fused_computation.12 | convolution fusion | flops 3245867008 | bytes 24649728 | tf_op jit(solution)/shard_map/etd,ehd->eth/dot_general | solution.py:184
  140.0 14.7 %reduce-precision_reduce_fusion = f32[2048,1024]{1,0:T(8,128)} fusion(bf16[2,2048,384]{1,2,0:T(8,128)(2,1)} %get-tuple-element.144, bf16[2,2048,384]{1,2,0:T(8,128)(2,1)} %get-tuple-element.143, bf16[2,1024,384]{2,1,0:T(8,128)(2,1)} %bitcast.105, bf16[2,1024,384]{2,1,0:T(8,128)(2,1)} %bitcast.104), kind=kOutput, calls=%fused_computation | convolution fusion | flops 6467616768 | bytes 17825792 | tf_op jit(solution)/shard_map/eth,edh->etd/dot_general | solution.py:201
  154.7 1.7 fusion.44
  156.4 1.8 collective-permute-start.21
  159.1 2.1 add_convert_fusion.4
  161.2 1.8 collective-permute-start.16
  163.0 8.2 %collective-permute-done.21 = bf16[256,1024]{1,0:T(8,128)(2,1)S(1)} collective-permute-done((bf16[256,1024]{1,0:T(8,128)(2,1)S(1)}, bf16[256,1024]{1,0:T(8,128)(2,1)S(1)}, u32[]{:S(2)}, u32[]{:S(2)}) %collective-permute-start.21) | collective-permute-done | bytes 524320 | tf_op jit(solution)/shard_map/ppermute | solution.py:50
  171.3 1.7 collective-permute-start.17
  173.0 1.9 fusion.32
  175.3 1.7 collective-permute-start.24
  177.0 11.0 %fusion.37 = (f32[1,2,384,1024]{3,2,1,0:T(8,128)}, bf16[1,2,384,1024]{3,2,1,0:T(8,128)(2,1)}, f32[1,2,384,1024]{3,2,1,0:T(8,128)}) fusion(f32[1,2,384,1024]{3,2,1,0:T(8,128)} %param.18, f32[1,2,384,1024]{3,2,1,0:T(8,128)} %param.17, bf16[1,2,384,1024]{3,2,1,0:T(8,128)(2,1)} %collective-permute-done.28, ...), kind=kOutput, calls=%fused_computation.65 | convolution fusion | flops 3241934848 | bytes 26222592 | tf_op jit(solution)/shard_map/eth,etd->ehd/dot_general | solution.py:191
  188.1 2.1 add_convert_fusion.2
  190.5 1.7 collective-permute-start.19
  192.2 1.5 collective-permute-done.23
  193.7 3.5 %collective-permute-done.24 = bf16[256,1024]{1,0:T(8,128)(2,1)S(1)} collective-permute-done((bf16[256,1024]{1,0:T(8,128)(2,1)S(1)}, bf16[256,1024]{1,0:T(8,128)(2,1)S(1)}, u32[]{:S(2)}, u32[]{:S(2)}) %collective-permute-start.24) | collective-permute-done | bytes 524320 | tf_op jit(solution)/shard_map/ppermute | solution.py:51
  197.3 1.9 fusion.30
  199.2 1.7 collective-permute-start.25
  201.3 8.0 %convert_bitcast_fusion = bf16[2,1024,768]{1,2,0:T(8,128)(2,1)S(1)} fusion(bf16[2048,1024,1]{1,0,2:T(8,128)(2,1)S(1)} %bitcast.100, bf16[2,2048,384]{1,2,0:T(8,128)(2,1)S(1)} %copy-done.19, bf16[2,2048,384]{1,2,0:T(8,128)(2,1)S(1)} %copy-done.18), kind=kOutput, calls=%fused_computation.39 | convolution fusion | flops 6456606720 | bytes 13631488 | tf_op jit(solution)/shard_map/td,eth->edh/dot_general | solution.py:195
  209.3 2.4 add_convert_fusion.1
  211.7 1.6 collective-permute-start.20
  213.3 3.0 %collective-permute-done.25 = bf16[256,1024]{1,0:T(8,128)(2,1)S(1)} collective-permute-done((bf16[256,1024]{1,0:T(8,128)(2,1)S(1)}, bf16[256,1024]{1,0:T(8,128)(2,1)S(1)}, u32[]{:S(2)}, u32[]{:S(2)}) %collective-permute-start.25) | collective-permute-done | bytes 524320 | tf_op jit(solution)/shard_map/ppermute | solution.py:50
  216.3 2.4 fusion.29
  218.7 1.7 collective-permute-start.27
  220.7 1.6 copy.50
  222.3 1.6 copy.51
  223.8 3.8 %collective-permute-done.20 = bf16[256,1024]{1,0:T(8,128)(2,1)} collective-permute-done((bf16[256,1024]{1,0:T(8,128)(2,1)}, bf16[256,1024]{1,0:T(8,128)(2,1)}, u32[]{:S(2)}, u32[]{:S(2)}) %collective-permute-start.20) | collective-permute-done | bytes 524320 | tf_op jit(solution)/shard_map/ppermute | solution.py:46
  227.6 2.6 %add_convert_fusion = bf16[256,1024]{1,0:T(8,128)(2,1)} fusion(bf16[256,1024]{1,0:T(8,128)(2,1)} %collective-permute-done.20, bf16[256,1024]{1,0:T(8,128)(2,1)} %copy-done.2, f32[2048,1024]{1,0:T(8,128)} %multiply_reduce_fusion), kind=kLoop, calls=%fused_computation.58 | loop fusion | flops 1310720 | bytes 2621440 | tf_op jit(solution)/shard_map/convert_element_type | solution.py:237
  230.2 6.3 %collective-permute-done.27 = bf16[256,1024]{1,0:T(8,128)(2,1)} collective-permute-done((bf16[256,1024]{1,0:T(8,128)(2,1)}, bf16[256,1024]{1,0:T(8,128)(2,1)}, u32[]{:S(2)}, u32[]{:S(2)}) %collective-permute-start.27) | collective-permute-done | bytes 524320 | tf_op jit(solution)/shard_map/ppermute | solution.py:46
  236.5 2.4 %fusion.35 = bf16[256,1024]{1,0:T(8,128)(2,1)} fusion(f32[2048,1024]{1,0:T(8,128)} %reduce-precision_reduce_fusion, bf16[256,1024]{1,0:T(8,128)(2,1)} %collective-permute-done.27, bf16[256,1024]{1,0:T(8,128)(2,1)S(1)} %copy-done.4), kind=kLoop, calls=%fused_computation.57 | loop fusion | flops 1310720 | bytes 2621440 | tf_op jit(solution)/shard_map/convert_element_type | solution.py:238
  (87 shorter events, 6.1 us)
Async XLA Ops:
  0.6 16.0 %collective-permute-start = (bf16[256,1024]{1,0:T(8,128)(2,1)}, bf16[256,1024]{1,0:T(8,128)(2,1)S(1)}, u32[]{:S(2)}, u32[]{:S(2)}) collective-permute-start(bf16[256,1024]{1,0:T(8,128)(2,1)} %param.11), channel_id=1, source_target_pairs={{0,2},{2,4},{4,6},{6,7},{7,5},{5,3},{3,1},{1,0},{8,10},{10,12},{12... | collective-permute-start | bytes 1572872 | tf_op jit(solution)/shard_map/ppermute | solution.py:50
  3.7 15.1 %collective-permute-start.1 = (bf16[256,1024]{1,0:T(8,128)(2,1)}, bf16[256,1024]{1,0:T(8,128)(2,1)S(1)}, u32[]{:S(2)}, u32[]{:S(2)}) collective-permute-start(bf16[256,1024]{1,0:T(8,128)(2,1)} %param.11), channel_id=1, source_target_pairs={{0,1},{2,0},{4,2},{6,4},{7,6},{5,7},{3,5},{1,3},{8,9},{10,8},{12,1... | collective-permute-start | bytes 1572872 | tf_op jit(solution)/shard_map/ppermute | solution.py:51
  6.5 21.7 %collective-permute-start.7 = (bf16[1,264,1024]{2,1,0:T(8,128)(2,1)S(1)}, bf16[1,264,1024]{2,1,0:T(8,128)(2,1)S(1)}, u32[]{:S(2)}, u32[]{:S(2)}) collective-permute-start(bf16[1,264,1024]{2,1,0:T(8,128)(2,1)S(1)} %maximum_bitcast_fusion), channel_id=1, source_target_pairs={{0,2},{2,4},{4,6},{6,7},{7,5},{5,3},{3,1},{1,0},{8,10},{10,12},{12... | collective-permute-start | bytes 1622024 | tf_op jit(solution)/shard_map/ppermute | solution.py:50
  8.5 21.8 %collective-permute-start.8 = (bf16[1,264,1024]{2,1,0:T(8,128)(2,1)S(1)}, bf16[1,264,1024]{2,1,0:T(8,128)(2,1)S(1)}, u32[]{:S(2)}, u32[]{:S(2)}) collective-permute-start(bf16[1,264,1024]{2,1,0:T(8,128)(2,1)S(1)} %maximum_bitcast_fusion), channel_id=1, source_target_pairs={{0,1},{2,0},{4,2},{6,4},{7,6},{5,7},{3,5},{1,3},{8,9},{10,8},{12,1... | collective-permute-start | bytes 1622024 | tf_op jit(solution)/shard_map/ppermute | solution.py:51
  16.6 34.4 %copy-start.8 = (bf16[256,1024]{1,0:T(8,128)(2,1)}, bf16[256,1024]{1,0:T(8,128)(2,1)S(1)}, u32[]{:S(2)}) copy-start(bf16[256,1024]{1,0:T(8,128)(2,1)S(1)} %collective-permute-done) | copy-start | bytes 1572868
  18.8 34.4 %copy-start.6 = (bf16[256,1024]{1,0:T(8,128)(2,1)}, bf16[256,1024]{1,0:T(8,128)(2,1)S(1)}, u32[]{:S(2)}) copy-start(bf16[256,1024]{1,0:T(8,128)(2,1)S(1)} %collective-permute-done.1) | copy-start | bytes 1572868
  18.8 20.6 %collective-permute-start.2 = (bf16[256,1024]{1,0:T(8,128)(2,1)S(1)}, bf16[256,1024]{1,0:T(8,128)(2,1)S(1)}, u32[]{:S(2)}, u32[]{:S(2)}) collective-permute-start(bf16[256,1024]{1,0:T(8,128)(2,1)S(1)} %collective-permute-done), channel_id=1, source_target_pairs={{0,2},{2,4},{4,6},{6,7},{7,5},{5,3},{3,1},{1,0},{8,10},{10,12},{12... | collective-permute-start | bytes 1572872 | tf_op jit(solution)/shard_map/ppermute | solution.py:50
  20.3 21.2 %collective-permute-start.3 = (bf16[256,1024]{1,0:T(8,128)(2,1)S(1)}, bf16[256,1024]{1,0:T(8,128)(2,1)S(1)}, u32[]{:S(2)}, u32[]{:S(2)}) collective-permute-start(bf16[256,1024]{1,0:T(8,128)(2,1)S(1)} %collective-permute-done.1), channel_id=1, source_target_pairs={{0,1},{2,0},{4,2},{6,4},{7,6},{5,7},{3,5},{1,3},{8,9},{10,8},{12,1... | collective-permute-start | bytes 1572872 | tf_op jit(solution)/shard_map/ppermute | solution.py:51
  30.4 20.6 %collective-permute-start.9 = (bf16[1,264,1024]{2,1,0:T(8,128)(2,1)S(1)}, bf16[1,264,1024]{2,1,0:T(8,128)(2,1)S(1)}, u32[]{:S(2)}, u32[]{:S(2)}) collective-permute-start(bf16[1,264,1024]{2,1,0:T(8,128)(2,1)S(1)} %collective-permute-done.7), channel_id=1, source_target_pairs={{0,2},{2,4},{4,6},{6,7},{7,5},{5,3},{3,1},{1,0},{8,10},{10,12},{12... | collective-permute-start | bytes 1622024 | tf_op jit(solution)/shard_map/ppermute | solution.py:50
  31.9 21.2 %collective-permute-start.10 = (bf16[1,264,1024]{2,1,0:T(8,128)(2,1)S(1)}, bf16[1,264,1024]{2,1,0:T(8,128)(2,1)S(1)}, u32[]{:S(2)}, u32[]{:S(2)}) collective-permute-start(bf16[1,264,1024]{2,1,0:T(8,128)(2,1)S(1)} %collective-permute-done.8), channel_id=1, source_target_pairs={{0,1},{2,0},{4,2},{6,4},{7,6},{5,7},{3,5},{1,3},{8,9},{10,8},{12,1... | collective-permute-start | bytes 1622024 | tf_op jit(solution)/shard_map/ppermute | solution.py:51
  39.4 25.0 %copy-start.11 = (bf16[256,1024]{1,0:T(8,128)(2,1)}, bf16[256,1024]{1,0:T(8,128)(2,1)S(1)}, u32[]{:S(2)}) copy-start(bf16[256,1024]{1,0:T(8,128)(2,1)S(1)} %collective-permute-done.2) | copy-start | bytes 1572868
  41.6 13.2 %copy-start.9 = (bf16[256,1024]{1,0:T(8,128)(2,1)}, bf16[256,1024]{1,0:T(8,128)(2,1)S(1)}, u32[]{:S(2)}) copy-start(bf16[256,1024]{1,0:T(8,128)(2,1)S(1)} %collective-permute-done.3) | copy-start | bytes 1572868
  41.6 20.7 %collective-permute-start.4 = (bf16[256,1024]{1,0:T(8,128)(2,1)S(1)}, bf16[256,1024]{1,0:T(8,128)(2,1)}, u32[]{:S(2)}, u32[]{:S(2)}) collective-permute-start(bf16[256,1024]{1,0:T(8,128)(2,1)S(1)} %collective-permute-done.2), channel_id=1, source_target_pairs={{0,2},{2,4},{4,6},{6,7},{7,5},{5,3},{3,1},{1,0},{8,10},{10,12},{12... | collective-permute-start | bytes 1572872 | tf_op jit(solution)/shard_map/ppermute | solution.py:50
  43.2 21.2 %collective-permute-start.5 = (bf16[256,1024]{1,0:T(8,128)(2,1)S(1)}, bf16[256,1024]{1,0:T(8,128)(2,1)S(1)}, u32[]{:S(2)}, u32[]{:S(2)}) collective-permute-start(bf16[256,1024]{1,0:T(8,128)(2,1)S(1)} %collective-permute-done.3), channel_id=1, source_target_pairs={{0,1},{2,0},{4,2},{6,4},{7,6},{5,7},{3,5},{1,3},{8,9},{10,8},{12,1... | collective-permute-start | bytes 1572872 | tf_op jit(solution)/shard_map/ppermute | solution.py:51
  53.2 20.6 %collective-permute-start.11 = (bf16[1,264,1024]{2,1,0:T(8,128)(2,1)S(1)}, bf16[1,264,1024]{2,1,0:T(8,128)(2,1)S(1)}, u32[]{:S(2)}, u32[]{:S(2)}) collective-permute-start(bf16[1,264,1024]{2,1,0:T(8,128)(2,1)S(1)} %collective-permute-done.9), channel_id=1, source_target_pairs={{0,2},{2,4},{4,6},{6,7},{7,5},{5,3},{3,1},{1,0},{8,10},{10,12},{12... | collective-permute-start | bytes 1622024 | tf_op jit(solution)/shard_map/ppermute | solution.py:50
  54.8 19.8 %collective-permute-start.12 = (bf16[1,264,1024]{2,1,0:T(8,128)(2,1)S(1)}, bf16[1,264,1024]{2,1,0:T(8,128)(2,1)S(1)}, u32[]{:S(2)}, u32[]{:S(2)}) collective-permute-start(bf16[1,264,1024]{2,1,0:T(8,128)(2,1)S(1)} %collective-permute-done.10), channel_id=1, source_target_pairs={{0,1},{2,0},{4,2},{6,4},{7,6},{5,7},{3,5},{1,3},{8,9},{10,8},{12,1... | collective-permute-start | bytes 1622024 | tf_op jit(solution)/shard_map/ppermute | solution.py:51
  64.4 1.6 copy-start.12
  64.4 20.7 %collective-permute-start.6 = (bf16[256,1024]{1,0:T(8,128)(2,1)}, bf16[256,1024]{1,0:T(8,128)(2,1)}, u32[]{:S(2)}, u32[]{:S(2)}) collective-permute-start(bf16[256,1024]{1,0:T(8,128)(2,1)} %collective-permute-done.4), channel_id=1, source_target_pairs={{0,2},{2,4},{4,6},{6,7},{7,5},{5,3},{3,1},{1,0},{8,10},{10,12},{12... | collective-permute-start | bytes 1572872 | tf_op jit(solution)/shard_map/ppermute | solution.py:46
  66.0 109.3 %collective-permute-start.28 = (bf16[1,2,384,1024]{3,2,1,0:T(8,128)(2,1)}, bf16[1,2,384,1024]{3,2,1,0:T(8,128)(2,1)}, u32[]{:S(2)}, u32[]{:S(2)}) collective-permute-start(bf16[1,2,384,1024]{3,2,1,0:T(8,128)(2,1)} %param.16), channel_id=1, source_target_pairs={{0,16},{8,24},{16,0},{24,8},{1,17},{9,25},{17,1},{25,9},{2,18},{10... | collective-permute-start | bytes 4718600 | tf_op jit(solution)/shard_map/ppermute | solution.py:21
  67.5 109.5 %collective-permute-start.29 = (bf16[1,2,384,1024]{3,2,1,0:T(8,128)(2,1)}, bf16[1,2,384,1024]{3,2,1,0:T(8,128)(2,1)}, u32[]{:S(2)}, u32[]{:S(2)}) collective-permute-start(bf16[1,2,384,1024]{3,2,1,0:T(8,128)(2,1)} %param.16), channel_id=1, source_target_pairs={{0,8},{8,16},{16,24},{24,0},{1,9},{9,17},{17,25},{25,1},{2,10},{10... | collective-permute-start | bytes 4718600 | tf_op jit(solution)/shard_map/ppermute | solution.py:21
  67.5 22.0 %copy-start.5 = (bf16[256,1024]{1,0:T(8,128)(2,1)S(1)}, bf16[256,1024]{1,0:T(8,128)(2,1)}, u32[]{:S(2)}) copy-start(bf16[256,1024]{1,0:T(8,128)(2,1)} %param.11) | copy-start | bytes 1572868
  67.5 22.0 %copy-start.7 = (bf16[256,1024]{1,0:T(8,128)(2,1)S(1)}, bf16[256,1024]{1,0:T(8,128)(2,1)}, u32[]{:S(2)}) copy-start(bf16[256,1024]{1,0:T(8,128)(2,1)} %copy-done.6) | copy-start | bytes 1572868
  67.5 22.1 %copy-start.10 = (bf16[256,1024]{1,0:T(8,128)(2,1)S(1)}, bf16[256,1024]{1,0:T(8,128)(2,1)}, u32[]{:S(2)}) copy-start(bf16[256,1024]{1,0:T(8,128)(2,1)} %copy-done.9) | copy-start | bytes 1572868
  67.5 22.1 %copy-start.13 = (bf16[256,1024]{1,0:T(8,128)(2,1)S(1)}, bf16[256,1024]{1,0:T(8,128)(2,1)}, u32[]{:S(2)}) copy-start(bf16[256,1024]{1,0:T(8,128)(2,1)} %copy-done.12) | copy-start | bytes 1572868
  74.5 21.3 %collective-permute-start.13 = (bf16[1,264,1024]{2,1,0:T(8,128)(2,1)S(1)}, bf16[1,264,1024]{2,1,0:T(8,128)(2,1)S(1)}, u32[]{:S(2)}, u32[]{:S(2)}) collective-permute-start(bf16[1,264,1024]{2,1,0:T(8,128)(2,1)S(1)} %collective-permute-done.11), channel_id=1, source_target_pairs={{0,2},{2,4},{4,6},{6,7},{7,5},{5,3},{3,1},{1,0},{8,10},{10,12},{12... | collective-permute-start | bytes 1622024 | tf_op jit(solution)/shard_map/ppermute | solution.py:46
  89.5 6.5 %copy-start.1 = (bf16[256,1024]{1,0:T(8,128)(2,1)S(1)}, bf16[256,1024]{1,0:T(8,128)(2,1)}, u32[]{:S(2)}) copy-start(bf16[256,1024]{1,0:T(8,128)(2,1)} %param.10) | copy-start | bytes 1572868
  89.7 6.5 %copy-start.14 = (bf16[2048,1024]{1,0:T(8,128)(2,1)}, bf16[2048,1024]{1,0:T(8,128)(2,1)S(1)}, u32[]{:S(2)}) copy-start(bf16[2048,1024]{1,0:T(8,128)(2,1)S(1)} %constant_dynamic-update-slice_fusion) | copy-start | bytes 12582916
  99.6 6.2 %copy-start = (bf16[8,256,1024]{2,1,0:T(8,128)(2,1)S(1)}, bf16[8,256,1024]{2,1,0:T(8,128)(2,1)}, u32[]{:S(2)}) copy-start(bf16[8,256,1024]{2,1,0:T(8,128)(2,1)} %slice.104) | copy-start | bytes 12582916
  99.6 6.2 %copy-start.16 = (bf16[1,2,1024,384]{3,2,1,0:T(8,128)(2,1)S(1)}, bf16[1,2,1024,384]{3,2,1,0:T(8,128)(2,1)}, u32[]{:S(2)}) copy-start(bf16[1,2,1024,384]{3,2,1,0:T(8,128)(2,1)} %param.15) | copy-start | bytes 4718596
  105.8 6.9 %copy-start.17 = (f32[2048,2,384]{0,2,1:T(8,128)}, f32[2048,2,384]{0,2,1:T(8,128)S(1)}, u32[]{:S(2)}) copy-start(f32[2048,2,384]{0,2,1:T(8,128)S(1)} %fusion.42) | copy-start | bytes 18874372
  126.0 32.2 %collective-permute-start.14 = (bf16[256,1024]{1,0:T(8,128)(2,1)S(1)}, bf16[256,1024]{1,0:T(8,128)(2,1)S(1)}, u32[]{:S(2)}, u32[]{:S(2)}) collective-permute-start(bf16[256,1024]{1,0:T(8,128)(2,1)S(1)} %get-tuple-element.88), channel_id=1, source_target_pairs={{0,2},{2,4},{4,6},{6,7},{7,5},{5,3},{3,1},{1,0},{8,10},{10,12},{12... | collective-permute-start | bytes 1572872 | tf_op jit(solution)/shard_map/ppermute | solution.py:50
  127.8 31.3 %collective-permute-start.15 = (bf16[256,1024]{1,0:T(8,128)(2,1)S(1)}, bf16[256,1024]{1,0:T(8,128)(2,1)S(1)}, u32[]{:S(2)}, u32[]{:S(2)}) collective-permute-start(bf16[256,1024]{1,0:T(8,128)(2,1)S(1)} %get-tuple-element.89), channel_id=1, source_target_pairs={{0,1},{2,0},{4,2},{6,4},{7,6},{5,7},{3,5},{1,3},{8,9},{10,8},{12,1... | collective-permute-start | bytes 1572872 | tf_op jit(solution)/shard_map/ppermute | solution.py:51
  156.4 14.9 %collective-permute-start.21 = (bf16[256,1024]{1,0:T(8,128)(2,1)S(1)}, bf16[256,1024]{1,0:T(8,128)(2,1)S(1)}, u32[]{:S(2)}, u32[]{:S(2)}) collective-permute-start(bf16[256,1024]{1,0:T(8,128)(2,1)S(1)} %get-tuple-element.103), channel_id=1, source_target_pairs={{0,2},{2,4},{4,6},{6,7},{7,5},{5,3},{3,1},{1,0},{8,10},{10,12},{12... | collective-permute-start | bytes 1572872 | tf_op jit(solution)/shard_map/ppermute | solution.py:50
  158.2 14.8 %collective-permute-start.22 = (bf16[256,1024]{1,0:T(8,128)(2,1)S(1)}, bf16[256,1024]{1,0:T(8,128)(2,1)S(1)}, u32[]{:S(2)}, u32[]{:S(2)}) collective-permute-start(bf16[256,1024]{1,0:T(8,128)(2,1)S(1)} %get-tuple-element.104), channel_id=1, source_target_pairs={{0,1},{2,0},{4,2},{6,4},{7,6},{5,7},{3,5},{1,3},{8,9},{10,8},{12,1... | collective-permute-start | bytes 1572872 | tf_op jit(solution)/shard_map/ppermute | solution.py:51
  159.1 17.9 %copy-start.15 = (bf16[2048,1024]{1,0:T(8,128)(2,1)S(1)}, bf16[2048,1024]{1,0:T(8,128)(2,1)}, u32[]{:S(2)}) copy-start(bf16[2048,1024]{1,0:T(8,128)(2,1)} %copy-done.14) | copy-start | bytes 12582916
  161.2 26.8 %collective-permute-start.16 = (bf16[256,1024]{1,0:T(8,128)(2,1)S(1)}, bf16[256,1024]{1,0:T(8,128)(2,1)S(1)}, u32[]{:S(2)}, u32[]{:S(2)}) collective-permute-start(bf16[256,1024]{1,0:T(8,128)(2,1)S(1)} %get-tuple-element.92), channel_id=1, source_target_pairs={{0,2},{2,4},{4,6},{6,7},{7,5},{5,3},{3,1},{1,0},{8,10},{10,12},{12... | collective-permute-start | bytes 1572872 | tf_op jit(solution)/shard_map/ppermute | solution.py:50
  171.3 16.8 %collective-permute-start.17 = (bf16[256,1024]{1,0:T(8,128)(2,1)S(1)}, bf16[256,1024]{1,0:T(8,128)(2,1)S(1)}, u32[]{:S(2)}, u32[]{:S(2)}) collective-permute-start(bf16[256,1024]{1,0:T(8,128)(2,1)S(1)} %get-tuple-element.93), channel_id=1, source_target_pairs={{0,1},{2,0},{4,2},{6,4},{7,6},{5,7},{3,5},{1,3},{8,9},{10,8},{12,1... | collective-permute-start | bytes 1572872 | tf_op jit(solution)/shard_map/ppermute | solution.py:51
  174.9 18.8 %collective-permute-start.23 = (bf16[256,1024]{1,0:T(8,128)(2,1)S(1)}, bf16[256,1024]{1,0:T(8,128)(2,1)S(1)}, u32[]{:S(2)}, u32[]{:S(2)}) collective-permute-start(bf16[256,1024]{1,0:T(8,128)(2,1)S(1)} %get-tuple-element.107), channel_id=1, source_target_pairs={{0,2},{2,4},{4,6},{6,7},{7,5},{5,3},{3,1},{1,0},{8,10},{10,12},{12... | collective-permute-start | bytes 1572872 | tf_op jit(solution)/shard_map/ppermute | solution.py:50
  175.3 22.0 %collective-permute-start.24 = (bf16[256,1024]{1,0:T(8,128)(2,1)S(1)}, bf16[256,1024]{1,0:T(8,128)(2,1)S(1)}, u32[]{:S(2)}, u32[]{:S(2)}) collective-permute-start(bf16[256,1024]{1,0:T(8,128)(2,1)S(1)} %get-tuple-element.108), channel_id=1, source_target_pairs={{0,1},{2,0},{4,2},{6,4},{7,6},{5,7},{3,5},{1,3},{8,9},{10,8},{12,1... | collective-permute-start | bytes 1572872 | tf_op jit(solution)/shard_map/ppermute | solution.py:51
  188.0 13.3 %copy-start.18 = (bf16[2,2048,384]{1,2,0:T(8,128)(2,1)S(1)}, bf16[2,2048,384]{1,2,0:T(8,128)(2,1)}, u32[]{:S(2)}) copy-start(bf16[2,2048,384]{1,2,0:T(8,128)(2,1)} %get-tuple-element.143) | copy-start | bytes 9437188
  188.0 13.3 %copy-start.19 = (bf16[2,2048,384]{1,2,0:T(8,128)(2,1)S(1)}, bf16[2,2048,384]{1,2,0:T(8,128)(2,1)}, u32[]{:S(2)}) copy-start(bf16[2,2048,384]{1,2,0:T(8,128)(2,1)} %get-tuple-element.144) | copy-start | bytes 9437188
  190.1 19.1 %collective-permute-start.18 = (bf16[256,1024]{1,0:T(8,128)(2,1)S(1)}, bf16[256,1024]{1,0:T(8,128)(2,1)S(1)}, u32[]{:S(2)}, u32[]{:S(2)}) collective-permute-start(bf16[256,1024]{1,0:T(8,128)(2,1)S(1)} %get-tuple-element.96), channel_id=1, source_target_pairs={{0,2},{2,4},{4,6},{6,7},{7,5},{5,3},{3,1},{1,0},{8,10},{10,12},{12... | collective-permute-start | bytes 1572872 | tf_op jit(solution)/shard_map/ppermute | solution.py:50
  190.5 18.7 %collective-permute-start.19 = (bf16[256,1024]{1,0:T(8,128)(2,1)S(1)}, bf16[256,1024]{1,0:T(8,128)(2,1)S(1)}, u32[]{:S(2)}, u32[]{:S(2)}) collective-permute-start(bf16[256,1024]{1,0:T(8,128)(2,1)S(1)} %get-tuple-element.97), channel_id=1, source_target_pairs={{0,1},{2,0},{4,2},{6,4},{7,6},{5,7},{3,5},{1,3},{8,9},{10,8},{12,1... | collective-permute-start | bytes 1572872 | tf_op jit(solution)/shard_map/ppermute | solution.py:51
  199.2 17.1 %collective-permute-start.25 = (bf16[256,1024]{1,0:T(8,128)(2,1)S(1)}, bf16[256,1024]{1,0:T(8,128)(2,1)S(1)}, u32[]{:S(2)}, u32[]{:S(2)}) collective-permute-start(bf16[256,1024]{1,0:T(8,128)(2,1)S(1)} %get-tuple-element.111), channel_id=1, source_target_pairs={{0,2},{2,4},{4,6},{6,7},{7,5},{5,3},{3,1},{1,0},{8,10},{10,12},{12... | collective-permute-start | bytes 1572872 | tf_op jit(solution)/shard_map/ppermute | solution.py:50
  200.9 15.4 %collective-permute-start.26 = (bf16[256,1024]{1,0:T(8,128)(2,1)S(1)}, bf16[256,1024]{1,0:T(8,128)(2,1)S(1)}, u32[]{:S(2)}, u32[]{:S(2)}) collective-permute-start(bf16[256,1024]{1,0:T(8,128)(2,1)S(1)} %get-tuple-element.112), channel_id=1, source_target_pairs={{0,1},{2,0},{4,2},{6,4},{7,6},{5,7},{3,5},{1,3},{8,9},{10,8},{12,1... | collective-permute-start | bytes 1572872 | tf_op jit(solution)/shard_map/ppermute | solution.py:51
  209.3 11.4 %copy-start.2 = (bf16[256,1024]{1,0:T(8,128)(2,1)}, bf16[256,1024]{1,0:T(8,128)(2,1)S(1)}, u32[]{:S(2)}) copy-start(bf16[256,1024]{1,0:T(8,128)(2,1)S(1)} %collective-permute-done.19) | copy-start | bytes 1572868
  211.7 16.0 %collective-permute-start.20 = (bf16[256,1024]{1,0:T(8,128)(2,1)}, bf16[256,1024]{1,0:T(8,128)(2,1)}, u32[]{:S(2)}, u32[]{:S(2)}) collective-permute-start(bf16[256,1024]{1,0:T(8,128)(2,1)} %add_convert_fusion.1), channel_id=1, source_target_pairs={{0,2},{2,4},{4,6},{6,7},{7,5},{5,3},{3,1},{1,0},{8,10},{10,12},{12... | collective-permute-start | bytes 1572872 | tf_op jit(solution)/shard_map/ppermute | solution.py:46
  216.3 4.4 %copy-start.3 = (bf16[256,1024]{1,0:T(8,128)(2,1)}, bf16[256,1024]{1,0:T(8,128)(2,1)S(1)}, u32[]{:S(2)}) copy-start(bf16[256,1024]{1,0:T(8,128)(2,1)S(1)} %collective-permute-done.26) | copy-start | bytes 1572868
  218.7 17.9 %collective-permute-start.27 = (bf16[256,1024]{1,0:T(8,128)(2,1)}, bf16[256,1024]{1,0:T(8,128)(2,1)}, u32[]{:S(2)}, u32[]{:S(2)}) collective-permute-start(bf16[256,1024]{1,0:T(8,128)(2,1)} %fusion.29), channel_id=1, source_target_pairs={{0,2},{2,4},{4,6},{6,7},{7,5},{5,3},{3,1},{1,0},{8,10},{10,12},{12... | collective-permute-start | bytes 1572872 | tf_op jit(solution)/shard_map/ppermute | solution.py:46
  222.3 14.3 %copy-start.4 = (bf16[256,1024]{1,0:T(8,128)(2,1)S(1)}, bf16[256,1024]{1,0:T(8,128)(2,1)}, u32[]{:S(2)}) copy-start(bf16[256,1024]{1,0:T(8,128)(2,1)} %copy-done.3) | copy-start | bytes 1572868
